TPU v7x, 32 devices: a whole 2x2x4 slice. The times are simulated.
32 devices in a mesh: sta: 2 (over y), evt: 2 (over core), mode: 8 (over z, x).
Axes of the slice: x: 2, y: 2, z: 4, core: 2. Of those that a mesh axis runs over, the one named last changes fastest.
Arguments:
- receivers: bfloat16 [768, 32768], P('sta', ('mode', 'evt')), may hold values from -6 to 6
- excitations: bfloat16 [32768, 512], P(('mode', 'sta'), 'evt'), may hold values from -0.00390625 to 0.00390625
- mode_freqs: float32 [32768], P('mode'), may hold values from 0 to 1
- mode_damping: float32 [32768], P('mode'), may hold values from 0.02 to 0.2
- sample_freqs: float32 [8], replicated, may hold values from 0.2 to 0.8
Outputs:
- spectra: float32 [768, 2, 8, 512], P(('sta', 'mode'), None, None, 'evt')
All inputs are finite; a program needn't handle non-finite values.
Results may differ from a plain program's by a relative error of at most 0.0029.
Values may be sent and summed in bfloat16 or wider, within the bound.
No kernel may reach another device: no remote copies, remote signals or barrier semaphores. Data moves between devices by JAX's collectives and lax.ppermute only.
A program may use at most 128 MiB of HBM per device.

v0:
```python
import jax
import jax.numpy as jnp
from jax import lax
from jax.sharding import PartitionSpec as P


def resonance(mode_freqs, mode_damping, frequency):
    offset = mode_freqs - frequency
    denominator = offset * offset + mode_damping * mode_damping
    return (mode_damping / denominator, -offset / denominator)


def synthesize(row_block, sources, mode_freqs, mode_damping, sample_freqs):
    row_count = row_block.shape[0]
    widened = row_block.astype(jnp.float32)
    results = []
    for position in range(sample_freqs.shape[0]):
        real_weight, imag_weight = resonance(mode_freqs, mode_damping, sample_freqs[position])
        weighted = jnp.stack([widened * real_weight, widened * imag_weight], axis=1).astype(
            jnp.bfloat16
        )
        product = jnp.dot(
            weighted.reshape(2 * row_count, row_block.shape[1]),
            sources,
            preferred_element_type=jnp.float32,
        )
        results.append(product.reshape(row_count, 2, sources.shape[1]))
    return jnp.stack(results, axis=2)


def per_device(receivers, excitations, mode_freqs, mode_damping, sample_freqs):
    receiver_block = lax.all_gather(receivers, "evt", axis=1, tiled=True)
    source_block = lax.all_gather(excitations, "sta", axis=0, tiled=True)
    receiver_rows = lax.all_to_all(receiver_block, "mode", split_axis=0, concat_axis=1, tiled=True)
    source_whole = lax.all_gather(source_block, "mode", axis=0, tiled=True)
    freqs_whole, damping_whole = (
        lax.all_gather(mode_freqs, "mode", axis=0, tiled=True),
        lax.all_gather(mode_damping, "mode", axis=0, tiled=True),
    )
    return synthesize(receiver_rows, source_whole, freqs_whole, damping_whole, sample_freqs)


def solution(mesh):
    placed = (P("sta", ("mode", "evt")), P(("mode", "sta"), "evt"), P("mode"), P("mode"), P())
    return jax.shard_map(
        per_device,
        mesh=mesh,
        in_specs=placed,
        out_specs=P(("sta", "mode"), None, None, "evt"),
        check_vma=False,
    )
```

profile of v0, /device:TPU:0, one launch (start us, length us, event | category | flops | bytes accessed | tf_op | source)
XLA Modules:
  0.0 423.6 jit_solution(11411845319753619724)
XLA Ops:
  6.5 0.7 all-gather.6.cloned.1.call-update
  7.3 0.0 all-gather.4.cloned.1.call-start
  7.3 0.7 all-gather.4.cloned.1.call-update
  8.0 0.0 all-gather.8.cloned.1.call-start
  8.1 36.7 %all-gather.6.cloned.1.call-done = bf16[4096,256]{1,0:T(8,128)(2,1)} async-done(((bf16[2048,256]{1,0:T(8,128)(2,1)}), bf16[4096,256]{1,0:T(8,128)(2,1)}) %all-gather.6.cloned.1.call-update) | async-done | bytes 2097168 | tf_op jit(solution)/shard_map/all_gather | solution.py:33
  44.8 0.0 all-gather.8.cloned.1.call-update
  44.8 13.7 %all-gather.4.cloned.1.call-done = bf16[384,4096]{1,0:T(8,128)(2,1)} async-done(((bf16[384,2048]{1,0:T(8,128)(2,1)}), bf16[384,4096]{1,0:T(8,128)(2,1)}) %all-gather.4.cloned.1.call-update) | async-done | bytes 3145744 | tf_op jit(solution)/shard_map/all_gather | solution.py:32
  58.5 5.8 %all-to-all-start = ((bf16[8,48,4096]{2,1,0:T(8,128)(2,1)}), bf16[8,48,4096]{2,1,0:T(8,128)(2,1)S(1)}, u32[]{:S(2)}, u32[]{:S(2)}) async-start(bf16[8,48,4096]{2,1,0:T(8,128)(2,1)} %bitcast.92), calls=%async_computation | async-start | bytes 6291456 | tf_op jit(solution)/shard_map/all_to_all | solution.py:34
  64.2 162.1 %all_gather.16 = f32[32768]{0:T(1024)S(1)} all-gather(f32[4096]{0:T(1024)S(1)} %copy-done.14), channel_id=1, replica_groups=mesh['sta'=2,'evt'=2,'mode'=8] {'mode'}, dimensions={0}, use_global_device_ids=true | all-gather | bytes 147456 | tf_op jit(solution)/shard_map/all_gather | solution.py:38
  226.3 31.6 %all_gather.17 = f32[32768]{0:T(1024)S(1)} all-gather(f32[4096]{0:T(1024)S(1)} %copy-done.15), channel_id=1, replica_groups=mesh['sta'=2,'evt'=2,'mode'=8] {'mode'}, dimensions={0}, use_global_device_ids=true | all-gather | bytes 147456 | tf_op jit(solution)/shard_map/all_gather | solution.py:37
  257.9 0.7 fusion.136
  258.6 6.3 %fusion.127 = (f32[32768]{0:T(1024)S(1)}, f32[32768]{0:T(1024)S(1)}, f32[32768]{0:T(1024)S(1)}, f32[32768]{0:T(1024)}, f32[32768]{0:T(1024)}, /*index=5*/f32[327...) fusion(f32[32768]{0:T(1024)S(1)} %all_gather.16, ...), kind=kLoop, calls=%fused_computation.96 | loop fusion | flops 1605632 | bytes 2359328 | tf_op jit(solution)/shard_map/div | solution.py:10
  264.9 0.0 all-to-all-done
  264.9 0.8 convert_bitcast_fusion
  265.6 6.3 %copy.8 = f32[48,8,4096]{2,1,0:T(8,128)} copy(f32[48,8,4096]{2,0,1:T(8,128)S(1)} %convert_bitcast_fusion) | data formatting | bytes 12582912 | tf_op jit(solution)/shard_map/convert_element_type | solution.py:15
  271.9 7.2 %reshape.467 = f32[48,1,32768]{2,0,1:T(8,128)} reshape(f32[48,8,4096]{2,1,0:T(8,128)} %copy.8) | data formatting | bytes 12582912 | tf_op jit(solution)/shard_map/convert_element_type | solution.py:15
  279.1 17.7 %multiply_convert_fusion.1 = (bf16[48,1,32768]{2,0,1:T(8,128)(2,1)S(1)}, bf16[48,1,32768]{2,0,1:T(8,128)(2,1)}, bf16[48,1,32768]{2,0,1:T(8,128)(2,1)}, bf16[48,1...) fusion(f32[48,1,32768]{2,0,1:T(8,128)} %reshape.467, ...), kind=kLoop, calls=%fused_computation.42 | loop fusion | flops 50331648 | bytes 58720256 | tf_op jit(solution)/shard_map/convert.2
  296.8 55.5 %all-gather.8.cloned.1.call-done = bf16[32768,256]{1,0:T(8,128)(2,1)} async-done(((bf16[4096,256]{1,0:T(8,128)(2,1)}), bf16[32768,256]{1,0:T(8,128)(2,1)}) %all-gather.8.cloned.1.call-update) | async-done | bytes 16777232 | tf_op jit(solution)/shard_map/all_gather | solution.py:35
  352.3 10.5 %fusion.45 = f32[48,2,8,256]{3,0,1,2:T(8,128)S(1)} fusion(bf16[32768,256]{1,0:T(8,128)(2,1)} %all-gather.8.cloned.1.call-done, bf16[48,1,32768]{2,0,1:T(8,128)(2,1)} %get-tuple-element.19, bf16[48,1,32768]{2,0,1:T(8,128)(2,1)} %get-tuple-element.20), kind=kOutput, calls=%fused_computation.58 | convolution fusion | flops 1613758464 | bytes 23166976 | tf_op jit(solution)/shard_map/dot_general | solution.py:22
  362.8 7.5 %fusion.55 = f32[48,2,8,256]{3,0,1,2:T(8,128)S(1)} fusion(f32[48,2,8,256]{3,0,1,2:T(8,128)S(1)} %fusion.45, bf16[32768,256]{1,0:T(8,128)(2,1)} %all-gather.8.cloned.1.call-done, bf16[48,1,32768]{2,0,1:T(8,128)(2,1)S(1)} %copy-done.11, bf16[48,1,32768]{2,0,1:T(8,128)(2,1)S(1)} %copy-done.12), kind=kOutput, calls=%fused_computation.60 | convolution fusion | flops 1613758464 | bytes 23166976 | tf_op jit(solution)/shard_map/dot_general | solution.py:22
  370.3 0.1 copy-done.10
  370.4 7.5 %fusion.65 = f32[48,2,8,256]{3,0,1,2:T(8,128)S(1)} fusion(f32[48,2,8,256]{3,0,1,2:T(8,128)S(1)} %fusion.55, bf16[32768,256]{1,0:T(8,128)(2,1)} %all-gather.8.cloned.1.call-done, bf16[48,1,32768]{2,0,1:T(8,128)(2,1)S(1)} %copy-done.9, bf16[48,1,32768]{2,0,1:T(8,128)(2,1)S(1)} %copy-done.10), kind=kOutput, calls=%fused_computation.62 | convolution fusion | flops 1613758464 | bytes 23166976 | tf_op jit(solution)/shard_map/dot_general | solution.py:22
  377.9 0.1 copy-done.8
  378.1 7.5 %fusion.75 = f32[48,2,8,256]{3,0,1,2:T(8,128)S(1)} fusion(f32[48,2,8,256]{3,0,1,2:T(8,128)S(1)} %fusion.65, bf16[32768,256]{1,0:T(8,128)(2,1)} %all-gather.8.cloned.1.call-done, bf16[48,1,32768]{2,0,1:T(8,128)(2,1)S(1)} %copy-done.7, bf16[48,1,32768]{2,0,1:T(8,128)(2,1)S(1)} %copy-done.8), kind=kOutput, calls=%fused_computation.64 | convolution fusion | flops 1613758464 | bytes 23166976 | tf_op jit(solution)/shard_map/dot_general | solution.py:22
  385.6 0.1 copy-done.6
  385.7 7.5 %fusion.85 = f32[48,2,8,256]{3,0,1,2:T(8,128)S(1)} fusion(f32[48,2,8,256]{3,0,1,2:T(8,128)S(1)} %fusion.75, bf16[32768,256]{1,0:T(8,128)(2,1)} %all-gather.8.cloned.1.call-done, bf16[48,1,32768]{2,0,1:T(8,128)(2,1)S(1)} %copy-done.5, bf16[48,1,32768]{2,0,1:T(8,128)(2,1)S(1)} %copy-done.6), kind=kOutput, calls=%fused_computation.66 | convolution fusion | flops 1613758464 | bytes 23166976 | tf_op jit(solution)/shard_map/dot_general | solution.py:22
  393.2 0.1 copy-done.4
  393.3 7.5 %fusion.95 = f32[48,2,8,256]{3,0,1,2:T(8,128)S(1)} fusion(f32[48,2,8,256]{3,0,1,2:T(8,128)S(1)} %fusion.85, bf16[32768,256]{1,0:T(8,128)(2,1)} %all-gather.8.cloned.1.call-done, bf16[48,1,32768]{2,0,1:T(8,128)(2,1)S(1)} %copy-done.3, bf16[48,1,32768]{2,0,1:T(8,128)(2,1)S(1)} %copy-done.4), kind=kOutput, calls=%fused_computation.68 | convolution fusion | flops 1613758464 | bytes 23166976 | tf_op jit(solution)/shard_map/dot_general | solution.py:22
  400.8 0.1 copy-done.2
  400.9 7.5 %fusion.105 = f32[48,2,8,256]{3,0,1,2:T(8,128)S(1)} fusion(f32[48,2,8,256]{3,0,1,2:T(8,128)S(1)} %fusion.95, bf16[32768,256]{1,0:T(8,128)(2,1)} %all-gather.8.cloned.1.call-done, bf16[48,1,32768]{2,0,1:T(8,128)(2,1)S(1)} %copy-done.1, bf16[48,1,32768]{2,0,1:T(8,128)(2,1)S(1)} %copy-done.2), kind=kOutput, calls=%fused_computation.70 | convolution fusion | flops 1613758464 | bytes 23166976 | tf_op jit(solution)/shard_map/dot_general | solution.py:22
  408.4 7.3 %fusion.115 = f32[48,2,8,256]{3,0,1,2:T(8,128)S(1)} fusion(f32[48,2,8,256]{3,0,1,2:T(8,128)S(1)} %fusion.105, bf16[32768,256]{1,0:T(8,128)(2,1)} %all-gather.8.cloned.1.call-done, bf16[48,1,32768]{2,0,1:T(8,128)(2,1)S(1)} %copy-done, bf16[48,1,32768]{2,0,1:T(8,128)(2,1)S(1)} %get-tuple-element.5), kind=kOutput, calls=%fused_computation.72 | convolution fusion | flops 1613758464 | bytes 23166976 | tf_op jit(solution)/shard_map/dot_general | solution.py:22
  415.7 1.3 copy.9
  (28 shorter events, 0.1 us)
Async XLA Ops:
  6.5 57.7 %copy-start.14 = (f32[4096]{0:T(1024)S(1)}, f32[4096]{0:T(1024)}, u32[]{:S(2)}) copy-start(f32[4096]{0:T(1024)} %param.8) | copy-start | bytes 49156
  6.5 219.8 %copy-start.15 = (f32[4096]{0:T(1024)S(1)}, f32[4096]{0:T(1024)}, u32[]{:S(2)}) copy-start(f32[4096]{0:T(1024)} %param.7) | copy-start | bytes 49156
  6.5 251.4 %copy-start.13 = (f32[8]{0:T(128)S(1)}, f32[8]{0:T(128)}, u32[]{:S(2)}) copy-start(f32[8]{0:T(128)} %param.9) | copy-start | bytes 100
  6.5 38.2 %all-gather.6.cloned.1.call-start = ((), (), s32[]{:S(2)}) async-start(), calls=%async_computation.2 | async-start | bytes 3145728 | tf_op jit(solution)/shard_map/all_gather | solution.py:33
  7.3 51.2 %all-gather.4.cloned.1.call-start = ((), (), s32[]{:S(2)}) async-start(), calls=%async_computation.1 | async-start | bytes 4718592 | tf_op jit(solution)/shard_map/all_gather | solution.py:32
  8.0 344.2 %all-gather.8.cloned.1.call-start = ((), (), s32[]{:S(2)}) async-start(), calls=%async_computation.3 | async-start | bytes 18874368 | tf_op jit(solution)/shard_map/all_gather | solution.py:35
  58.5 206.4 %all-to-all-start = ((bf16[8,48,4096]{2,1,0:T(8,128)(2,1)}), bf16[8,48,4096]{2,1,0:T(8,128)(2,1)S(1)}, u32[]{:S(2)}, u32[]{:S(2)}) async-start(bf16[8,48,4096]{2,1,0:T(8,128)(2,1)} %bitcast.92), calls=%async_computation | async-start | bytes 6291456 | tf_op jit(solution)/shard_map/all_to_all | solution.py:34
  352.3 10.5 %copy-start.11 = (bf16[48,1,32768]{2,0,1:T(8,128)(2,1)S(1)}, bf16[48,1,32768]{2,0,1:T(8,128)(2,1)}, u32[]{:S(2)}) copy-start(bf16[48,1,32768]{2,0,1:T(8,128)(2,1)} %get-tuple-element.17) | copy-start | bytes 9437188
  352.3 10.6 %copy-start.12 = (bf16[48,1,32768]{2,0,1:T(8,128)(2,1)S(1)}, bf16[48,1,32768]{2,0,1:T(8,128)(2,1)}, u32[]{:S(2)}) copy-start(bf16[48,1,32768]{2,0,1:T(8,128)(2,1)} %get-tuple-element.18) | copy-start | bytes 9437188
  362.8 7.5 %copy-start.9 = (bf16[48,1,32768]{2,0,1:T(8,128)(2,1)S(1)}, bf16[48,1,32768]{2,0,1:T(8,128)(2,1)}, u32[]{:S(2)}) copy-start(bf16[48,1,32768]{2,0,1:T(8,128)(2,1)} %get-tuple-element.15) | copy-start | bytes 9437188
  362.8 7.6 %copy-start.10 = (bf16[48,1,32768]{2,0,1:T(8,128)(2,1)S(1)}, bf16[48,1,32768]{2,0,1:T(8,128)(2,1)}, u32[]{:S(2)}) copy-start(bf16[48,1,32768]{2,0,1:T(8,128)(2,1)} %get-tuple-element.16) | copy-start | bytes 9437188
  370.4 7.5 %copy-start.7 = (bf16[48,1,32768]{2,0,1:T(8,128)(2,1)S(1)}, bf16[48,1,32768]{2,0,1:T(8,128)(2,1)}, u32[]{:S(2)}) copy-start(bf16[48,1,32768]{2,0,1:T(8,128)(2,1)} %get-tuple-element.13) | copy-start | bytes 9437188
  370.4 7.6 %copy-start.8 = (bf16[48,1,32768]{2,0,1:T(8,128)(2,1)S(1)}, bf16[48,1,32768]{2,0,1:T(8,128)(2,1)}, u32[]{:S(2)}) copy-start(bf16[48,1,32768]{2,0,1:T(8,128)(2,1)} %get-tuple-element.14) | copy-start | bytes 9437188
  378.1 7.5 %copy-start.5 = (bf16[48,1,32768]{2,0,1:T(8,128)(2,1)S(1)}, bf16[48,1,32768]{2,0,1:T(8,128)(2,1)}, u32[]{:S(2)}) copy-start(bf16[48,1,32768]{2,0,1:T(8,128)(2,1)} %get-tuple-element.11) | copy-start | bytes 9437188
  378.1 7.6 %copy-start.6 = (bf16[48,1,32768]{2,0,1:T(8,128)(2,1)S(1)}, bf16[48,1,32768]{2,0,1:T(8,128)(2,1)}, u32[]{:S(2)}) copy-start(bf16[48,1,32768]{2,0,1:T(8,128)(2,1)} %get-tuple-element.12) | copy-start | bytes 9437188
  385.7 7.5 %copy-start.3 = (bf16[48,1,32768]{2,0,1:T(8,128)(2,1)S(1)}, bf16[48,1,32768]{2,0,1:T(8,128)(2,1)}, u32[]{:S(2)}) copy-start(bf16[48,1,32768]{2,0,1:T(8,128)(2,1)} %get-tuple-element.9) | copy-start | bytes 9437188
  385.7 7.6 %copy-start.4 = (bf16[48,1,32768]{2,0,1:T(8,128)(2,1)S(1)}, bf16[48,1,32768]{2,0,1:T(8,128)(2,1)}, u32[]{:S(2)}) copy-start(bf16[48,1,32768]{2,0,1:T(8,128)(2,1)} %get-tuple-element.10) | copy-start | bytes 9437188
  393.3 7.5 %copy-start.1 = (bf16[48,1,32768]{2,0,1:T(8,128)(2,1)S(1)}, bf16[48,1,32768]{2,0,1:T(8,128)(2,1)}, u32[]{:S(2)}) copy-start(bf16[48,1,32768]{2,0,1:T(8,128)(2,1)} %get-tuple-element.7) | copy-start | bytes 9437188
  393.3 7.6 %copy-start.2 = (bf16[48,1,32768]{2,0,1:T(8,128)(2,1)S(1)}, bf16[48,1,32768]{2,0,1:T(8,128)(2,1)}, u32[]{:S(2)}) copy-start(bf16[48,1,32768]{2,0,1:T(8,128)(2,1)} %get-tuple-element.8) | copy-start | bytes 9437188
  400.9 7.5 %copy-start = (bf16[48,1,32768]{2,0,1:T(8,128)(2,1)S(1)}, bf16[48,1,32768]{2,0,1:T(8,128)(2,1)}, u32[]{:S(2)}) copy-start(bf16[48,1,32768]{2,0,1:T(8,128)(2,1)} %get-tuple-element.6) | copy-start | bytes 9437188
Sparse Core Ops, SparseCore 0:
  8.9 35.8 all-gather.5
  46.3 12.1 all-gather.3
  60.6 291.6 all-gather.7
where the time goes:
time: 424 us
  blocking collectives  194 us (46%)
  waiting for transfers between devices  107 us (25%)
  matrix products  62.7 us (15%)
  other arithmetic  24.7 us (6%)
  local copies, waits for them, and re-layouts  16.1 us (4%)
  between operations  13.3 us (3%)
  starting transfers between devices  5.85 us (1%)
    all_gather x1, blocking collectives, per_device(): lax.all_gather(mode_damping, 'mode', axis=0, tiled=True)  162 us
    dot_general x8, matrix products, synthesize(): jnp.dot(weighted.reshape(2 * row_count, row_block.shape[1]), sources, pre...  62.7 us
    all_gather x1, waiting for transfers between devices, per_device(): source_whole = lax.all_gather(source_block, 'mode', axis=0, tiled=True)  55.5 us
    all_gather x1, waiting for transfers between devices, per_device(): source_block = lax.all_gather(excitations, 'sta', axis=0, tiled=True)  36.7 us
    all_gather x1, blocking collectives, per_device(): lax.all_gather(mode_freqs, 'mode', axis=0, tiled=True)  31.6 us
    another operation x1, other arithmetic  17.7 us
    all_gather x1, waiting for transfers between devices, per_device(): receiver_block = lax.all_gather(receivers, 'evt', axis=1, tiled=True)  13.7 us
    convert_element_type x2, local copies, waits for them, and re-layouts, synthesize(): widened = row_block.astype(jnp.float32)  13.5 us
  transfers between devices with their start and end apart: 4, of which 3 were waited for; matrix products, arithmetic and copies ran while one was open for 9% of the time, Pallas kernels for 0%

commit v1 on v0

v1 whole, which is shorter than its diff:
```python
import jax
import jax.numpy as jnp
from jax import lax
from jax.sharding import PartitionSpec as P


def resonance(mode_freqs, mode_damping, frequency):
    offset = mode_freqs - frequency
    denominator = offset * offset + mode_damping * mode_damping
    return (mode_damping / denominator, -offset / denominator)


def per_device(receivers, excitations, mode_freqs, mode_damping, sample_freqs):
    receiver_block = lax.all_gather(receivers, "evt", axis=1, tiled=True)
    source_block = lax.all_gather(excitations, "sta", axis=0, tiled=True)
    row_count, mode_count = receiver_block.shape
    real_weight, imag_weight = resonance(
        mode_freqs[None, :], mode_damping[None, :], sample_freqs[:, None]
    )
    weights = jnp.stack([real_weight, imag_weight], axis=0)
    widened = receiver_block.astype(jnp.float32)
    weighted = (widened[:, None, None, :] * weights[None]).astype(jnp.bfloat16)
    partial = jnp.dot(
        weighted.reshape(-1, mode_count), source_block, preferred_element_type=jnp.float32
    )
    partial = partial.reshape(row_count, 2, sample_freqs.shape[0], source_block.shape[1])
    return lax.psum_scatter(partial, "mode", scatter_dimension=0, tiled=True)


def solution(mesh):
    placed = (P("sta", ("mode", "evt")), P(("mode", "sta"), "evt"), P("mode"), P("mode"), P())
    return jax.shard_map(
        per_device,
        mesh=mesh,
        in_specs=placed,
        out_specs=P(("sta", "mode"), None, None, "evt"),
        check_vma=False,
    )
```

time: 424 us -> 205 us (0.48)
  blocking collectives: 194 us -> 0 us
  waiting for transfers between devices: 107 us -> 164 us
  matrix products: 62.7 us -> 17.8 us
  other arithmetic: 24.7 us -> 6.99 us
  local copies, waits for them, and re-layouts: 16.1 us -> 2.47 us
  starting transfers between devices: 5.85 us -> 0.08 us
    all_gather x2 -> x0, blocking collectives: 194 us -> none  [the longest x1 162 us: per_device(): lax.all_gather(mode_damping, 'mode', axis=0, tiled=True)]
    reduce_scatter x0 -> x1, waiting for transfers between devices: none -> 118 us  [per_device(): return lax.psum_scatter(partial, 'mode', scatter_dimension=0, tiled=True)]
    all_gather x1 -> x0, waiting for transfers between devices: 55.5 us -> none  [per_device(): source_whole = lax.all_gather(source_block, 'mode', axis=0, tiled=True)]
    dot_general x8 -> x1, matrix products: 62.7 us -> 17.8 us  [per_device(): jnp.dot(weighted.reshape(-1, mode_count), source_block, preferred_element...]
    another operation x1, other arithmetic: 17.7 us -> 0.02 us  [per_device(): weights = jnp.stack([real_weight, imag_weight], axis=0)]
    convert_element_type x2 -> x0, local copies, waits for them, and re-layouts: 13.5 us -> none  [synthesize(): widened = row_block.astype(jnp.float32)]
    all_gather x1, waiting for transfers between devices: 36.7 us -> 30.5 us  [per_device(): source_block = lax.all_gather(excitations, 'sta', axis=0, tiled=True)]
    all_to_all x1 -> x0, starting transfers between devices: 5.77 us -> none  [per_device(): lax.all_to_all(receiver_block, 'mode', split_axis=0, concat_axis=1, tiled...]
  transfers between devices with their start and end apart: 4 -> 3, of which waited for: 3 -> 3; matrix products, arithmetic and copies ran while one was open for 9% -> 3% of each run, Pallas kernels for 0% -> 0%
where the time goes in v1:
time: 205 us
  waiting for transfers between devices  164 us (80%)
  matrix products  17.8 us (9%)
  between operations  13.1 us (6%)
  other arithmetic  6.99 us (3%)
  local copies, waits for them, and re-layouts  2.47 us (1%)
    reduce_scatter x1, waiting for transfers between devices, per_device(): return lax.psum_scatter(partial, 'mode', scatter_dimension=0, tiled=True)  118 us
    all_gather x1, waiting for transfers between devices, per_device(): source_block = lax.all_gather(excitations, 'sta', axis=0, tiled=True)  30.5 us
    dot_general x1, matrix products, per_device(): jnp.dot(weighted.reshape(-1, mode_count), source_block, preferred_element...  17.8 us
    all_gather x1, waiting for transfers between devices, per_device(): receiver_block = lax.all_gather(receivers, 'evt', axis=1, tiled=True)  14.1 us
    convert_element_type x1, other arithmetic, per_device(): widened = receiver_block.astype(jnp.float32)  5.32 us
  transfers between devices with their start and end apart: 3, of which 3 were waited for; matrix products, arithmetic and copies ran while one was open for 3% of the time, Pallas kernels for 0%

profile of v1, /device:TPU:0, one launch (start us, length us, event | category | flops | bytes accessed | tf_op | source)
XLA Modules:
  0.0 204.6 jit_solution(1197653298187763293)
XLA Ops:
  6.5 0.0 all-gather.3.cloned.1.call-start
  6.5 0.7 all-gather.3.cloned.1.call-update
  7.3 0.0 all-gather.5.cloned.1.call-start
  7.3 0.7 all-gather.5.cloned.1.call-update
  8.0 0.0 reduce-scatter.2.cloned.1.call-start
  8.1 0.8 mul.35
  8.9 0.9 fusion.6
  9.7 14.1 %all-gather.3.cloned.1.call-done = bf16[384,4096]{1,0:T(8,128)(2,1)} async-done(((bf16[384,2048]{1,0:T(8,128)(2,1)}), bf16[384,4096]{1,0:T(8,128)(2,1)}) %all-gather.3.cloned.1.call-update) | async-done | bytes 3145744 | tf_op jit(solution)/shard_map/all_gather | solution.py:14
  23.8 5.3 %convert_element_type.8 = f32[384,4096]{1,0:T(8,128)} convert(bf16[384,4096]{1,0:T(8,128)(2,1)} %all-gather.3.cloned.1.call-done) | non-fusion elementwise | flops 1572864 | bytes 9437184 | tf_op jit(solution)/shard_map/convert_element_type | solution.py:21
  29.1 30.5 %all-gather.5.cloned.1.call-done = bf16[4096,256]{1,0:T(8,128)(2,1)} async-done(((bf16[2048,256]{1,0:T(8,128)(2,1)}), bf16[4096,256]{1,0:T(8,128)(2,1)}) %all-gather.5.cloned.1.call-update) | async-done | bytes 2097168 | tf_op jit(solution)/shard_map/all_gather | solution.py:15
  59.7 17.8 %fusion = f32[384,2,8,256]{3,0,2,1:T(8,128)} fusion(f32[2,8,4096]{2,1,0:T(8,128)S(1)} %pad_maximum_fusion, f32[384,4096]{1,0:T(8,128)} %convert_element_type.8, bf16[4096,256]{1,0:T(8,128)(2,1)} %all-gather.5.cloned.1.call-done), kind=kOutput, calls=%fused_computation.1 | convolution fusion | flops 12935233536 | bytes 14942208 | tf_op jit(solution)/shard_map/dot_general | solution.py:23
  77.5 0.0 reduce-scatter.2.cloned.1.call-update
  77.5 118.1 %reduce-scatter.2.cloned.1.call-done = f32[48,2,8,256]{3,0,2,1:T(8,128)} async-done(((f32[384,2,8,256]{3,0,2,1:T(8,128)}), f32[48,2,8,256]{3,0,2,1:T(8,128)}) %reduce-scatter.2.cloned.1.call-update) | async-done | bytes 786448 | tf_op jit(solution)/shard_map/reduce_scatter | solution.py:27
  195.6 2.5 %copy.6 = f32[48,2,8,256]{3,2,1,0:T(8,128)} copy(f32[48,2,8,256]{3,0,2,1:T(8,128)} %reduce-scatter.2.cloned.1.call-done) | data formatting | bytes 1572864 | tf_op jit(solution)/shard_map/reduce_scatter | solution.py:27
  (1 shorter events, 0.0 us)
Async XLA Ops:
  6.5 17.3 %all-gather.3.cloned.1.call-start = ((), (), s32[]{:S(2)}) async-start(), calls=%async_computation.1 | async-start | bytes 4718592 | tf_op jit(solution)/shard_map/all_gather | solution.py:14
  7.3 52.4 %all-gather.5.cloned.1.call-start = ((), (), s32[]{:S(2)}) async-start(), calls=%async_computation.2 | async-start | bytes 3145728 | tf_op jit(solution)/shard_map/all_gather | solution.py:15
  8.0 187.6 %reduce-scatter.2.cloned.1.call-start = ((), (), s32[]{:S(2)}) async-start(), calls=%async_computation.3 | async-start | bytes 7077888 | tf_op jit(solution)/shard_map/reduce_scatter | solution.py:27
Sparse Core Ops, SparseCore 0:
  8.9 14.8 all-gather.2
  25.4 34.2 all-gather.4
  77.7 117.9 reduce-scatter.1

commit v2 on v1

v2 whole, which is shorter than its diff:
```python
import jax
import jax.numpy as jnp
from jax import lax
from jax.sharding import PartitionSpec as P


def resonance(mode_freqs, mode_damping, frequency):
    offset = mode_freqs - frequency
    denominator = offset * offset + mode_damping * mode_damping
    return (mode_damping / denominator, -offset / denominator)


def ring_order(count):
    if count % 2:
        return list(range(count))
    return [2 * i for i in range(count // 2)] + [2 * i + 1 for i in reversed(range(count // 2))]


def swap_pair(local, axis_name):
    return lax.ppermute(local, axis_name, [(0, 1), (1, 0)])


def gather_blocks(local, axis_name, size, axis):
    if size != 2:
        return lax.all_gather(local, axis_name, axis=axis, tiled=True)
    other = swap_pair(local, axis_name)
    index = lax.axis_index(axis_name)
    first = jnp.where(index == 0, local, other)
    second = jnp.where(index == 0, other, local)
    return jnp.concatenate([first, second], axis=axis)


def make_per_device(sizes):
    mode_count = sizes["mode"]
    order = ring_order(mode_count)
    position_of = [0] * mode_count
    for position, device in enumerate(order):
        position_of[device] = position
    clockwise = [(order[i], order[(i + 1) % mode_count]) for i in range(mode_count)]
    counter = [(order[(i + 1) % mode_count], order[i]) for i in range(mode_count)]

    def per_device(receivers, excitations, mode_freqs, mode_damping, sample_freqs):
        mode = lax.axis_index("mode")
        receiver_block = gather_blocks(receivers, "evt", sizes["evt"], 1)
        source_block = gather_blocks(excitations, "sta", sizes["sta"], 0)
        row_count, block_modes = receiver_block.shape
        real_weight, imag_weight = resonance(
            mode_freqs[None, :], mode_damping[None, :], sample_freqs[:, None]
        )
        weights = jnp.stack([real_weight, imag_weight], axis=0)
        chunk = row_count // mode_count
        half = chunk // 2
        order_table = jnp.asarray(order, dtype=jnp.int32)
        position = jnp.asarray(position_of, dtype=jnp.int32)[mode]

        def partial_rows(owner, part):
            start = owner * chunk + part * half
            rows = lax.dynamic_slice_in_dim(receiver_block, start, half, axis=0)
            widened = rows.astype(jnp.float32)
            weighted = (widened[:, None, None, :] * weights[None]).astype(jnp.bfloat16)
            product = jnp.dot(
                weighted.reshape(-1, block_modes), source_block, preferred_element_type=jnp.float32
            )
            return product.reshape(half, 2, sample_freqs.shape[0], source_block.shape[1])

        def owner_at(offset):
            return order_table[(position + offset) % mode_count]

        ahead = partial_rows(owner_at(-1), 0)
        behind = partial_rows(owner_at(1), 1)
        for step in range(mode_count - 1):
            ahead = lax.ppermute(ahead, "mode", clockwise)
            behind = lax.ppermute(behind, "mode", counter)
            ahead = ahead + partial_rows(owner_at(-step - 2), 0)
            behind = behind + partial_rows(owner_at(step + 2), 1)
        return jnp.concatenate([ahead, behind], axis=0)

    return per_device


def solution(mesh):
    placed = (P("sta", ("mode", "evt")), P(("mode", "sta"), "evt"), P("mode"), P("mode"), P())
    return jax.shard_map(
        make_per_device(dict(mesh.shape)),
        mesh=mesh,
        in_specs=placed,
        out_specs=P(("sta", "mode"), None, None, "evt"),
        check_vma=False,
    )
```

time: 205 us -> 104 us (0.51)
  waiting for transfers between devices: 164 us -> 39.3 us
  starting transfers between devices: 0.08 us -> 18.4 us
  between operations: 13.1 us -> 20.9 us
  matrix products: 17.8 us -> 15.6 us
    reduce_scatter x1 -> x0, waiting for transfers between devices: 118 us -> none  [per_device(): return lax.psum_scatter(partial, 'mode', scatter_dimension=0, tiled=True)]
    all_gather x2 -> x0, waiting for transfers between devices: 44.6 us -> none  [the longest x1 30.5 us: per_device(): source_block = lax.all_gather(excitations, 'sta', axis=0, tiled=True)]
    ppermute x0 -> x16, waiting for transfers between devices: none -> 39.3 us  [the longest x7 34.9 us: per_device(): ahead = lax.ppermute(ahead, 'mode', clockwise)]
    ppermute x0 -> x16, starting transfers between devices: none -> 18.4 us  [the longest x7 11.5 us: per_device(): ahead = lax.ppermute(ahead, 'mode', clockwise)]
    convert_element_type x1 -> x3, other arithmetic: 5.32 us -> 0.61 us  [partial_rows(): widened = rows.astype(jnp.float32)]
    dynamic_slice x0 -> x2, local copies, waits for them, and re-layouts: none -> 3.23 us  [the longest x1 2 us: owner_at(): return order_table[(position + offset) % mode_count]]
    reduce_scatter x1 -> x0, local copies, waits for them, and re-layouts: 2.47 us -> none  [per_device(): return lax.psum_scatter(partial, 'mode', scatter_dimension=0, tiled=True)]
    dot_general x1 -> x16, matrix products: 17.8 us -> 15.6 us  [partial_rows(): jnp.dot(weighted.reshape(-1, block_modes), source_block, preferred_elemen...]
  transfers between devices with their start and end apart: 3 -> 16, of which waited for: 3 -> 14; matrix products, arithmetic and copies ran while one was open for 3% -> 21% of each run, Pallas kernels for 0% -> 0%
where the time goes in v2:
time: 104 us; the launch traced here: 103 us
  waiting for transfers between devices  39.3 us (38%)
  between operations  20.9 us (20%)
  starting transfers between devices  18.4 us (18%)
  matrix products  15.6 us (15%)
  other arithmetic  5.67 us (5%)
  local copies, waits for them, and re-layouts  3.44 us (3%)
    ppermute x7, waiting for transfers between devices, per_device(): ahead = lax.ppermute(ahead, 'mode', clockwise)  34.9 us
    dot_general x16, matrix products, partial_rows(): jnp.dot(weighted.reshape(-1, block_modes), source_block, preferred_elemen...  15.6 us
    ppermute x7, starting transfers between devices, per_device(): ahead = lax.ppermute(ahead, 'mode', clockwise)  11.5 us
    ppermute x7, waiting for transfers between devices, per_device(): behind = lax.ppermute(behind, 'mode', counter)  4.46 us
    ppermute x7, starting transfers between devices, per_device(): behind = lax.ppermute(behind, 'mode', counter)  3.89 us
    ppermute x2, starting transfers between devices, swap_pair(): return lax.ppermute(local, axis_name, [(0, 1), (1, 0)])  3.03 us
  transfers between devices with their start and end apart: 16, of which 14 were waited for; matrix products, arithmetic and copies ran while one was open for 21% of the time, Pallas kernels for 0%

profile of v2, /device:TPU:0, one launch (start us, length us, event | category | flops | bytes accessed | tf_op | source)
XLA Modules:
  0.0 103.4 jit_solution(3274299407792414619)
XLA Ops:
  0.5 2.6 %collective-permute-start.1 = (bf16[2048,256]{1,0:T(8,128)(2,1)}, bf16[2048,256]{1,0:T(8,128)(2,1)}, u32[]{:S(2)}, u32[]{:S(2)}) collective-permute-start(bf16[2048,256]{1,0:T(8,128)(2,1)} %param.8), channel_id=1, source_target_pairs={{0,16},{16,0},{1,17},{17,1},{2,18},{18,2},{3,19},{19,3},{4,20},{20... | collective-permute-start | bytes 3145736 | tf_op jit(solution)/shard_map/ppermute | solution.py:20
  3.0 1.2 %dynamic_slice.99 = s32[1]{0:T(128)} dynamic-slice(s32[8]{0:T(128)} %constant.186.clone, s32[]{:T(128)S(6)} %select_n.193), dynamic_slice_sizes={1} | dynamic-slice | bytes 12 | tf_op jit(solution)/shard_map/dynamic_slice | solution.py:54
  14.9 2.0 %fusion.83 = (s32[1]{0:T(128)}, s32[1]{0:T(128)}, s32[1]{0:T(128)}, s32[1]{0:T(128)}, s32[1]{0:T(128)}, /*index=5*/s32[1]{0:T(128)}, s32[1]{0:T(128)}, s32[1]{0:...) fusion(s32[8]{0:T(128)} %constant.185.clone, ...), kind=kLoop, calls=%fused_computation.140 | loop fusion | bytes 192 | tf_op jit(solution)/shard_map/dynamic_slice | solution.py:67
  28.6 1.5 %broadcast_select_fusion.3 = (bf16[2048,256]{1,0:T(8,128)(2,1)S(1)}, bf16[2048,256]{1,0:T(8,128)(2,1)S(1)}) fusion(bf16[2048,256]{1,0:T(8,128)(2,1)S(1)} %copy-done.1, bf16[2048,256]{1,0:T(8,128)(2,1)} %collective-permute-done.1, pred[]{:T(512)S(6)} %eq.26), kind=kLoop, calls=%fused_computation.100 | loop fusion | flops 1048576 | bytes 4194305 | tf_op jit(solution)/shard_map/jit(_where)/select_n | solution.py:28
  30.8 1.0 fusion
  31.8 1.6 %collective-permute-start.2 = (f32[24,2,8,256]{3,2,1,0:T(8,128)S(1)}, f32[24,2,8,256]{3,2,1,0:T(8,128)S(1)}, u32[]{:S(2)}, u32[]{:S(2)}) collective-permute-start(f32[24,2,8,256]{3,2,1,0:T(8,128)S(1)} %fusion), channel_id=1, source_target_pairs={{0,2},{2,4},{4,6},{6,7},{7,5},{5,3},{3,1},{1,0},{8,10},{10,12},{12... | collective-permute-start | bytes 1179656 | tf_op jit(solution)/shard_map/ppermute | solution.py:72
  33.6 1.0 fusion.8
  35.3 1.0 fusion.1
  36.3 1.0 fusion.9
  37.3 5.8 %collective-permute-done.2 = f32[24,2,8,256]{3,2,1,0:T(8,128)S(1)} collective-permute-done((f32[24,2,8,256]{3,2,1,0:T(8,128)S(1)}, f32[24,2,8,256]{3,2,1,0:T(8,128)S(1)}, u32[]{:S(2)}, u32[]{:S(2)}) %collective-permute-start.2) | collective-permute-done | bytes 393248 | tf_op jit(solution)/shard_map/ppermute | solution.py:72
  43.1 1.6 %collective-permute-start.3 = (f32[24,2,8,256]{3,2,1,0:T(8,128)S(1)}, f32[24,2,8,256]{3,2,1,0:T(8,128)S(1)}, u32[]{:S(2)}, u32[]{:S(2)}) collective-permute-start(f32[24,2,8,256]{3,2,1,0:T(8,128)S(1)} %add.406), channel_id=1, source_target_pairs={{0,2},{2,4},{4,6},{6,7},{7,5},{5,3},{3,1},{1,0},{8,10},{10,12},{12... | collective-permute-start | bytes 1179656 | tf_op jit(solution)/shard_map/ppermute | solution.py:72
  46.2 1.0 fusion.2
  47.1 1.0 fusion.10
  48.1 5.4 %collective-permute-done.3 = f32[24,2,8,256]{3,2,1,0:T(8,128)S(1)} collective-permute-done((f32[24,2,8,256]{3,2,1,0:T(8,128)S(1)}, f32[24,2,8,256]{3,2,1,0:T(8,128)S(1)}, u32[]{:S(2)}, u32[]{:S(2)}) %collective-permute-start.3) | collective-permute-done | bytes 393248 | tf_op jit(solution)/shard_map/ppermute | solution.py:72
  53.5 1.6 %collective-permute-start.4 = (f32[24,2,8,256]{3,2,1,0:T(8,128)S(1)}, f32[24,2,8,256]{3,2,1,0:T(8,128)S(1)}, u32[]{:S(2)}, u32[]{:S(2)}) collective-permute-start(f32[24,2,8,256]{3,2,1,0:T(8,128)S(1)} %add.412), channel_id=1, source_target_pairs={{0,2},{2,4},{4,6},{6,7},{7,5},{5,3},{3,1},{1,0},{8,10},{10,12},{12... | collective-permute-start | bytes 1179656 | tf_op jit(solution)/shard_map/ppermute | solution.py:72
  56.3 1.0 fusion.3
  57.3 1.0 fusion.11
  58.3 4.8 %collective-permute-done.4 = f32[24,2,8,256]{3,2,1,0:T(8,128)S(1)} collective-permute-done((f32[24,2,8,256]{3,2,1,0:T(8,128)S(1)}, f32[24,2,8,256]{3,2,1,0:T(8,128)S(1)}, u32[]{:S(2)}, u32[]{:S(2)}) %collective-permute-start.4) | collective-permute-done | bytes 393248 | tf_op jit(solution)/shard_map/ppermute | solution.py:72
  63.1 1.7 %collective-permute-start.5 = (f32[24,2,8,256]{3,2,1,0:T(8,128)S(1)}, f32[24,2,8,256]{3,2,1,0:T(8,128)S(1)}, u32[]{:S(2)}, u32[]{:S(2)}) collective-permute-start(f32[24,2,8,256]{3,2,1,0:T(8,128)S(1)} %add.418), channel_id=1, source_target_pairs={{0,2},{2,4},{4,6},{6,7},{7,5},{5,3},{3,1},{1,0},{8,10},{10,12},{12... | collective-permute-start | bytes 1179656 | tf_op jit(solution)/shard_map/ppermute | solution.py:72
  66.7 1.0 fusion.12
  67.7 4.6 %collective-permute-done.5 = f32[24,2,8,256]{3,2,1,0:T(8,128)S(1)} collective-permute-done((f32[24,2,8,256]{3,2,1,0:T(8,128)S(1)}, f32[24,2,8,256]{3,2,1,0:T(8,128)S(1)}, u32[]{:S(2)}, u32[]{:S(2)}) %collective-permute-start.5) | collective-permute-done | bytes 393248 | tf_op jit(solution)/shard_map/ppermute | solution.py:72
  72.4 1.7 %collective-permute-start.6 = (f32[24,2,8,256]{3,2,1,0:T(8,128)S(1)}, f32[24,2,8,256]{3,2,1,0:T(8,128)S(1)}, u32[]{:S(2)}, u32[]{:S(2)}) collective-permute-start(f32[24,2,8,256]{3,2,1,0:T(8,128)S(1)} %add.424), channel_id=1, source_target_pairs={{0,2},{2,4},{4,6},{6,7},{7,5},{5,3},{3,1},{1,0},{8,10},{10,12},{12... | collective-permute-start | bytes 1179656 | tf_op jit(solution)/shard_map/ppermute | solution.py:72
  76.0 1.0 fusion.13
  77.0 5.0 %collective-permute-done.6 = f32[24,2,8,256]{3,2,1,0:T(8,128)S(1)} collective-permute-done((f32[24,2,8,256]{3,2,1,0:T(8,128)S(1)}, f32[24,2,8,256]{3,2,1,0:T(8,128)S(1)}, u32[]{:S(2)}, u32[]{:S(2)}) %collective-permute-start.6) | collective-permute-done | bytes 393248 | tf_op jit(solution)/shard_map/ppermute | solution.py:72
  82.0 1.6 %collective-permute-start.7 = (f32[24,2,8,256]{3,2,1,0:T(8,128)S(1)}, f32[24,2,8,256]{3,2,1,0:T(8,128)S(1)}, u32[]{:S(2)}, u32[]{:S(2)}) collective-permute-start(f32[24,2,8,256]{3,2,1,0:T(8,128)S(1)} %add.430), channel_id=1, source_target_pairs={{0,2},{2,4},{4,6},{6,7},{7,5},{5,3},{3,1},{1,0},{8,10},{10,12},{12... | collective-permute-start | bytes 1179656 | tf_op jit(solution)/shard_map/ppermute | solution.py:72
  85.6 1.0 fusion.14
  86.6 6.1 %collective-permute-done.7 = f32[24,2,8,256]{3,2,1,0:T(8,128)S(1)} collective-permute-done((f32[24,2,8,256]{3,2,1,0:T(8,128)S(1)}, f32[24,2,8,256]{3,2,1,0:T(8,128)S(1)}, u32[]{:S(2)}, u32[]{:S(2)}) %collective-permute-start.7) | collective-permute-done | bytes 393248 | tf_op jit(solution)/shard_map/ppermute | solution.py:72
  92.7 1.6 %collective-permute-start.8 = (f32[24,2,8,256]{3,2,1,0:T(8,128)S(1)}, f32[24,2,8,256]{3,2,1,0:T(8,128)S(1)}, u32[]{:S(2)}, u32[]{:S(2)}) collective-permute-start(f32[24,2,8,256]{3,2,1,0:T(8,128)S(1)} %add.436), channel_id=1, source_target_pairs={{0,2},{2,4},{4,6},{6,7},{7,5},{5,3},{3,1},{1,0},{8,10},{10,12},{12... | collective-permute-start | bytes 1179656 | tf_op jit(solution)/shard_map/ppermute | solution.py:72
  95.2 1.0 fusion.7
  96.2 1.0 fusion.15
  97.2 3.3 %collective-permute-done.8 = f32[24,2,8,256]{3,2,1,0:T(8,128)S(1)} collective-permute-done((f32[24,2,8,256]{3,2,1,0:T(8,128)S(1)}, f32[24,2,8,256]{3,2,1,0:T(8,128)S(1)}, u32[]{:S(2)}, u32[]{:S(2)}) %collective-permute-start.8) | collective-permute-done | bytes 393248 | tf_op jit(solution)/shard_map/ppermute | solution.py:72
  100.6 1.8 %collective-permute-done.15 = f32[24,2,8,256]{3,2,1,0:T(8,128)S(1)} collective-permute-done((f32[24,2,8,256]{3,2,1,0:T(8,128)S(1)}, f32[24,2,8,256]{3,2,1,0:T(8,128)S(1)}, u32[]{:S(2)}, u32[]{:S(2)}) %collective-permute-start.15) | collective-permute-done | bytes 393248 | tf_op jit(solution)/shard_map/ppermute | solution.py:73
  (45 shorter events, 14.3 us)
Async XLA Ops:
  0.0 28.6 %copy-start.1 = (bf16[2048,256]{1,0:T(8,128)(2,1)S(1)}, bf16[2048,256]{1,0:T(8,128)(2,1)}, u32[]{:S(2)}) copy-start(bf16[2048,256]{1,0:T(8,128)(2,1)} %param.8) | copy-start | bytes 3145732
  0.0 30.1 %collective-permute-start = (bf16[384,2048]{1,0:T(8,128)(2,1)}, bf16[384,2048]{1,0:T(8,128)(2,1)S(1)}, u32[]{:S(2)}, u32[]{:S(2)}) collective-permute-start(bf16[384,2048]{1,0:T(8,128)(2,1)} %param.7), channel_id=1, source_target_pairs={{0,8},{8,0},{1,9},{9,1},{2,10},{10,2},{3,11},{11,3},{4,12},{12,4},... | collective-permute-start | bytes 4718600 | tf_op jit(solution)/shard_map/ppermute | solution.py:20
  0.5 28.2 %collective-permute-start.1 = (bf16[2048,256]{1,0:T(8,128)(2,1)}, bf16[2048,256]{1,0:T(8,128)(2,1)}, u32[]{:S(2)}, u32[]{:S(2)}) collective-permute-start(bf16[2048,256]{1,0:T(8,128)(2,1)} %param.8), channel_id=1, source_target_pairs={{0,16},{16,0},{1,17},{17,1},{2,18},{18,2},{3,19},{19,3},{4,20},{20... | collective-permute-start | bytes 3145736 | tf_op jit(solution)/shard_map/ppermute | solution.py:20
  28.6 1.7 %copy-start = (bf16[384,2048]{1,0:T(8,128)(2,1)S(1)}, bf16[384,2048]{1,0:T(8,128)(2,1)}, u32[]{:S(2)}) copy-start(bf16[384,2048]{1,0:T(8,128)(2,1)} %param.7) | copy-start | bytes 4718596
  31.8 11.2 %collective-permute-start.2 = (f32[24,2,8,256]{3,2,1,0:T(8,128)S(1)}, f32[24,2,8,256]{3,2,1,0:T(8,128)S(1)}, u32[]{:S(2)}, u32[]{:S(2)}) collective-permute-start(f32[24,2,8,256]{3,2,1,0:T(8,128)S(1)} %fusion), channel_id=1, source_target_pairs={{0,2},{2,4},{4,6},{6,7},{7,5},{5,3},{3,1},{1,0},{8,10},{10,12},{12... | collective-permute-start | bytes 1179656 | tf_op jit(solution)/shard_map/ppermute | solution.py:72
  34.6 11.0 %collective-permute-start.9 = (f32[24,2,8,256]{3,2,1,0:T(8,128)S(1)}, f32[24,2,8,256]{3,2,1,0:T(8,128)S(1)}, u32[]{:S(2)}, u32[]{:S(2)}) collective-permute-start(f32[24,2,8,256]{3,2,1,0:T(8,128)S(1)} %fusion.8), channel_id=1, source_target_pairs={{2,0},{4,2},{6,4},{7,6},{5,7},{3,5},{1,3},{0,1},{10,8},{12,10},{14... | collective-permute-start | bytes 1179656 | tf_op jit(solution)/shard_map/ppermute | solution.py:73
  43.1 10.4 %collective-permute-start.3 = (f32[24,2,8,256]{3,2,1,0:T(8,128)S(1)}, f32[24,2,8,256]{3,2,1,0:T(8,128)S(1)}, u32[]{:S(2)}, u32[]{:S(2)}) collective-permute-start(f32[24,2,8,256]{3,2,1,0:T(8,128)S(1)} %add.406), channel_id=1, source_target_pairs={{0,2},{2,4},{4,6},{6,7},{7,5},{5,3},{3,1},{1,0},{8,10},{10,12},{12... | collective-permute-start | bytes 1179656 | tf_op jit(solution)/shard_map/ppermute | solution.py:72
  45.6 10.1 %collective-permute-start.10 = (f32[24,2,8,256]{3,2,1,0:T(8,128)S(1)}, f32[24,2,8,256]{3,2,1,0:T(8,128)S(1)}, u32[]{:S(2)}, u32[]{:S(2)}) collective-permute-start(f32[24,2,8,256]{3,2,1,0:T(8,128)S(1)} %add.459), channel_id=1, source_target_pairs={{2,0},{4,2},{6,4},{7,6},{5,7},{3,5},{1,3},{0,1},{10,8},{12,10},{14... | collective-permute-start | bytes 1179656 | tf_op jit(solution)/shard_map/ppermute | solution.py:73
  53.5 9.5 %collective-permute-start.4 = (f32[24,2,8,256]{3,2,1,0:T(8,128)S(1)}, f32[24,2,8,256]{3,2,1,0:T(8,128)S(1)}, u32[]{:S(2)}, u32[]{:S(2)}) collective-permute-start(f32[24,2,8,256]{3,2,1,0:T(8,128)S(1)} %add.412), channel_id=1, source_target_pairs={{0,2},{2,4},{4,6},{6,7},{7,5},{5,3},{3,1},{1,0},{8,10},{10,12},{12... | collective-permute-start | bytes 1179656 | tf_op jit(solution)/shard_map/ppermute | solution.py:72
  55.8 9.2 %collective-permute-start.11 = (f32[24,2,8,256]{3,2,1,0:T(8,128)S(1)}, f32[24,2,8,256]{3,2,1,0:T(8,128)S(1)}, u32[]{:S(2)}, u32[]{:S(2)}) collective-permute-start(f32[24,2,8,256]{3,2,1,0:T(8,128)S(1)} %add.468), channel_id=1, source_target_pairs={{2,0},{4,2},{6,4},{7,6},{5,7},{3,5},{1,3},{0,1},{10,8},{12,10},{14... | collective-permute-start | bytes 1179656 | tf_op jit(solution)/shard_map/ppermute | solution.py:73
  63.1 9.2 %collective-permute-start.5 = (f32[24,2,8,256]{3,2,1,0:T(8,128)S(1)}, f32[24,2,8,256]{3,2,1,0:T(8,128)S(1)}, u32[]{:S(2)}, u32[]{:S(2)}) collective-permute-start(f32[24,2,8,256]{3,2,1,0:T(8,128)S(1)} %add.418), channel_id=1, source_target_pairs={{0,2},{2,4},{4,6},{6,7},{7,5},{5,3},{3,1},{1,0},{8,10},{10,12},{12... | collective-permute-start | bytes 1179656 | tf_op jit(solution)/shard_map/ppermute | solution.py:72
  65.0 9.4 %collective-permute-start.12 = (f32[24,2,8,256]{3,2,1,0:T(8,128)S(1)}, f32[24,2,8,256]{3,2,1,0:T(8,128)S(1)}, u32[]{:S(2)}, u32[]{:S(2)}) collective-permute-start(f32[24,2,8,256]{3,2,1,0:T(8,128)S(1)} %add.477), channel_id=1, source_target_pairs={{2,0},{4,2},{6,4},{7,6},{5,7},{3,5},{1,3},{0,1},{10,8},{12,10},{14... | collective-permute-start | bytes 1179656 | tf_op jit(solution)/shard_map/ppermute | solution.py:73
  72.4 9.6 %collective-permute-start.6 = (f32[24,2,8,256]{3,2,1,0:T(8,128)S(1)}, f32[24,2,8,256]{3,2,1,0:T(8,128)S(1)}, u32[]{:S(2)}, u32[]{:S(2)}) collective-permute-start(f32[24,2,8,256]{3,2,1,0:T(8,128)S(1)} %add.424), channel_id=1, source_target_pairs={{0,2},{2,4},{4,6},{6,7},{7,5},{5,3},{3,1},{1,0},{8,10},{10,12},{12... | collective-permute-start | bytes 1179656 | tf_op jit(solution)/shard_map/ppermute | solution.py:72
  74.5 9.6 %collective-permute-start.13 = (f32[24,2,8,256]{3,2,1,0:T(8,128)S(1)}, f32[24,2,8,256]{3,2,1,0:T(8,128)S(1)}, u32[]{:S(2)}, u32[]{:S(2)}) collective-permute-start(f32[24,2,8,256]{3,2,1,0:T(8,128)S(1)} %add.486), channel_id=1, source_target_pairs={{2,0},{4,2},{6,4},{7,6},{5,7},{3,5},{1,3},{0,1},{10,8},{12,10},{14... | collective-permute-start | bytes 1179656 | tf_op jit(solution)/shard_map/ppermute | solution.py:73
  82.0 10.7 %collective-permute-start.7 = (f32[24,2,8,256]{3,2,1,0:T(8,128)S(1)}, f32[24,2,8,256]{3,2,1,0:T(8,128)S(1)}, u32[]{:S(2)}, u32[]{:S(2)}) collective-permute-start(f32[24,2,8,256]{3,2,1,0:T(8,128)S(1)} %add.430), channel_id=1, source_target_pairs={{0,2},{2,4},{4,6},{6,7},{7,5},{5,3},{3,1},{1,0},{8,10},{10,12},{12... | collective-permute-start | bytes 1179656 | tf_op jit(solution)/shard_map/ppermute | solution.py:72
  84.1 10.4 %collective-permute-start.14 = (f32[24,2,8,256]{3,2,1,0:T(8,128)S(1)}, f32[24,2,8,256]{3,2,1,0:T(8,128)S(1)}, u32[]{:S(2)}, u32[]{:S(2)}) collective-permute-start(f32[24,2,8,256]{3,2,1,0:T(8,128)S(1)} %add.495), channel_id=1, source_target_pairs={{2,0},{4,2},{6,4},{7,6},{5,7},{3,5},{1,3},{0,1},{10,8},{12,10},{14... | collective-permute-start | bytes 1179656 | tf_op jit(solution)/shard_map/ppermute | solution.py:73
  92.7 7.8 %collective-permute-start.8 = (f32[24,2,8,256]{3,2,1,0:T(8,128)S(1)}, f32[24,2,8,256]{3,2,1,0:T(8,128)S(1)}, u32[]{:S(2)}, u32[]{:S(2)}) collective-permute-start(f32[24,2,8,256]{3,2,1,0:T(8,128)S(1)} %add.436), channel_id=1, source_target_pairs={{0,2},{2,4},{4,6},{6,7},{7,5},{5,3},{3,1},{1,0},{8,10},{10,12},{12... | collective-permute-start | bytes 1179656 | tf_op jit(solution)/shard_map/ppermute | solution.py:72
  94.6 7.8 %collective-permute-start.15 = (f32[24,2,8,256]{3,2,1,0:T(8,128)S(1)}, f32[24,2,8,256]{3,2,1,0:T(8,128)S(1)}, u32[]{:S(2)}, u32[]{:S(2)}) collective-permute-start(f32[24,2,8,256]{3,2,1,0:T(8,128)S(1)} %add.504), channel_id=1, source_target_pairs={{2,0},{4,2},{6,4},{7,6},{5,7},{3,5},{1,3},{0,1},{10,8},{12,10},{14... | collective-permute-start | bytes 1179656 | tf_op jit(solution)/shard_map/ppermute | solution.py:73

commit v3 on v2

--- a/solution.py
+++ b/solution.py
@@ -42,7 +42,12 @@
     def per_device(receivers, excitations, mode_freqs, mode_damping, sample_freqs):
         mode = lax.axis_index("mode")
         receiver_block = gather_blocks(receivers, "evt", sizes["evt"], 1)
-        source_block = gather_blocks(excitations, "sta", sizes["sta"], 0)
+        pieces = 2
+        width = excitations.shape[1] // pieces
+        source_blocks = [
+            gather_blocks(excitations[:, q * width : (q + 1) * width], "sta", sizes["sta"], 0)
+            for q in range(pieces)
+        ]
         row_count, block_modes = receiver_block.shape
         real_weight, imag_weight = resonance(
             mode_freqs[None, :], mode_damping[None, :], sample_freqs[:, None]
@@ -53,7 +58,7 @@
         order_table = jnp.asarray(order, dtype=jnp.int32)
         position = jnp.asarray(position_of, dtype=jnp.int32)[mode]
 
-        def partial_rows(owner, part):
+        def partial_rows(owner, part, source_block):
             start = owner * chunk + part * half
             rows = lax.dynamic_slice_in_dim(receiver_block, start, half, axis=0)
             widened = rows.astype(jnp.float32)
@@ -66,14 +71,16 @@
         def owner_at(offset):
             return order_table[(position + offset) % mode_count]
 
-        ahead = partial_rows(owner_at(-1), 0)
-        behind = partial_rows(owner_at(1), 1)
+        ahead = [partial_rows(owner_at(-1), 0, source) for source in source_blocks]
+        behind = [partial_rows(owner_at(1), 1, source) for source in source_blocks]
         for step in range(mode_count - 1):
-            ahead = lax.ppermute(ahead, "mode", clockwise)
-            behind = lax.ppermute(behind, "mode", counter)
-            ahead = ahead + partial_rows(owner_at(-step - 2), 0)
-            behind = behind + partial_rows(owner_at(step + 2), 1)
-        return jnp.concatenate([ahead, behind], axis=0)
+            for q, source in enumerate(source_blocks):
+                ahead[q] = lax.ppermute(ahead[q], "mode", clockwise)
+                behind[q] = lax.ppermute(behind[q], "mode", counter)
+                ahead[q] = ahead[q] + partial_rows(owner_at(-step - 2), 0, source)
+                behind[q] = behind[q] + partial_rows(owner_at(step + 2), 1, source)
+        rows = [jnp.concatenate(parts, axis=3) for parts in (ahead, behind)]
+        return jnp.concatenate(rows, axis=0)
 
     return per_device
 

time: 104 us -> 131 us (1.26)
  starting transfers between devices: 18.4 us -> 35.1 us
  matrix products: 15.6 us -> 31.4 us
  waiting for transfers between devices: 39.3 us -> 35.6 us
    dot_general x16 -> x32, matrix products: 15.6 us -> 31.4 us  [partial_rows(): jnp.dot(weighted.reshape(-1, block_modes), source_block, preferred_elemen...]
    ppermute x14 -> x28, starting transfers between devices: 15.4 us -> 30.3 us  [the longest x14 19 us: per_device(): behind[q] = lax.ppermute(behind[q], 'mode', counter)]
    ppermute x14 -> x28, waiting for transfers between devices: 39.3 us -> 24.5 us  [the longest x14 17 us: per_device(): ahead[q] = lax.ppermute(ahead[q], 'mode', clockwise)]
    ppermute x2 -> x3, waiting for transfers between devices: 0.01 us -> 11.1 us  [swap_pair(): return lax.ppermute(local, axis_name, [(0, 1), (1, 0)])]
    ppermute x2 -> x3, starting transfers between devices: 3.03 us -> 4.77 us  [swap_pair(): return lax.ppermute(local, axis_name, [(0, 1), (1, 0)])]
    select_n x2 -> x3, other arithmetic: 1.69 us -> 2.95 us  [gather_blocks(): first = jnp.where(index == 0, local, other)]
  transfers between devices with their start and end apart: 16 -> 31, of which waited for: 14 -> 17; matrix products, arithmetic and copies ran while one was open for 21% -> 12% of each run, Pallas kernels for 0% -> 0%
where the time goes in v3:
time: 131 us
  waiting for transfers between devices  35.6 us (27%)
  starting transfers between devices  35.1 us (27%)
  matrix products  31.4 us (24%)
  between operations  20 us (15%)
  other arithmetic  6.07 us (5%)
  local copies, waits for them, and re-layouts  2.77 us (2%)
    dot_general x32, matrix products, partial_rows(): jnp.dot(weighted.reshape(-1, block_modes), source_block, preferred_elemen...  31.4 us
    ppermute x14, starting transfers between devices, per_device(): behind[q] = lax.ppermute(behind[q], 'mode', counter)  19 us
    ppermute x14, waiting for transfers between devices, per_device(): ahead[q] = lax.ppermute(ahead[q], 'mode', clockwise)  17 us
    ppermute x14, starting transfers between devices, per_device(): ahead[q] = lax.ppermute(ahead[q], 'mode', clockwise)  11.3 us
    ppermute x3, waiting for transfers between devices, swap_pair(): return lax.ppermute(local, axis_name, [(0, 1), (1, 0)])  11.1 us
    ppermute x14, waiting for transfers between devices, per_device(): behind[q] = lax.ppermute(behind[q], 'mode', counter)  7.5 us
    ppermute x3, starting transfers between devices, swap_pair(): return lax.ppermute(local, axis_name, [(0, 1), (1, 0)])  4.77 us
    select_n x3, other arithmetic, gather_blocks(): first = jnp.where(index == 0, local, other)  2.95 us
  transfers between devices with their start and end apart: 31, of which 17 were waited for; matrix products, arithmetic and copies ran while one was open for 12% of the time, Pallas kernels for 0%

profile of v3, /device:TPU:0, one launch (start us, length us, event | category | flops | bytes accessed | tf_op | source)
XLA Modules:
  0.0 130.9 jit_solution(2983077008417433127)
XLA Ops:
  0.0 1.2 slice.6
  1.2 3.0 %collective-permute-start.1 = (bf16[2048,128]{1,0:T(8,128)(2,1)S(1)}, bf16[2048,128]{1,0:T(8,128)(2,1)S(1)}, u32[]{:S(2)}, u32[]{:S(2)}) collective-permute-start(bf16[2048,128]{1,0:T(8,128)(2,1)S(1)} %slice.6), channel_id=1, source_target_pairs={{0,16},{16,0},{1,17},{17,1},{2,18},{18,2},{3,19},{19,3},{4,20},{20... | collective-permute-start | bytes 1572872 | tf_op jit(solution)/shard_map/ppermute | solution.py:20
  5.0 11.1 %collective-permute-done.1 = bf16[2048,128]{1,0:T(8,128)(2,1)S(1)} collective-permute-done((bf16[2048,128]{1,0:T(8,128)(2,1)S(1)}, bf16[2048,128]{1,0:T(8,128)(2,1)S(1)}, u32[]{:S(2)}, u32[]{:S(2)}) %collective-permute-start.1) | collective-permute-done | bytes 524320 | tf_op jit(solution)/shard_map/ppermute | solution.py:20
  16.1 1.3 broadcast_select_fusion.5
  17.4 1.7 %collective-permute-start.9 = (bf16[2048,128]{1,0:T(8,128)(2,1)}, bf16[2048,128]{1,0:T(8,128)(2,1)S(1)}, u32[]{:S(2)}, u32[]{:S(2)}) collective-permute-start(bf16[2048,128]{1,0:T(8,128)(2,1)} %get-tuple-element.27), channel_id=1, source_target_pairs={{0,16},{16,0},{1,17},{17,1},{2,18},{18,2},{3,19},{19,3},{4,20},{20... | collective-permute-start | bytes 1572872 | tf_op jit(solution)/shard_map/ppermute | solution.py:20
  40.2 1.6 %broadcast_select_fusion.1 = (bf16[384,2048]{1,0:T(8,128)(2,1)S(1)}, bf16[384,2048]{1,0:T(8,128)(2,1)S(1)}) fusion(bf16[384,2048]{1,0:T(8,128)(2,1)S(1)} %copy-done.1, bf16[384,2048]{1,0:T(8,128)(2,1)} %collective-permute-done, pred[]{:T(512)S(6)} %eq.43), kind=kLoop, calls=%fused_computation.145 | loop fusion | flops 1572864 | bytes 6291457 | tf_op jit(solution)/shard_map/jit(_where)/select_n | solution.py:28
  53.3 1.2 fusion.29
  62.6 1.5 %collective-permute-start.24 = (f32[24,2,8,128]{3,2,1,0:T(8,128)S(1)}, f32[24,2,8,128]{3,2,1,0:T(8,128)S(1)}, u32[]{:S(2)}, u32[]{:S(2)}) collective-permute-start(f32[24,2,8,128]{3,2,1,0:T(8,128)S(1)} %fusion.16), channel_id=1, source_target_pairs={{2,0},{4,2},{6,4},{7,6},{5,7},{3,5},{1,3},{0,1},{10,8},{12,10},{14... | collective-permute-start | bytes 589832 | tf_op jit(solution)/shard_map/ppermute | solution.py:79
  64.2 1.6 %collective-permute-start.17 = (f32[24,2,8,128]{3,2,1,0:T(8,128)S(1)}, f32[24,2,8,128]{3,2,1,0:T(8,128)S(1)}, u32[]{:S(2)}, u32[]{:S(2)}) collective-permute-start(f32[24,2,8,128]{3,2,1,0:T(8,128)S(1)} %fusion.17), channel_id=1, source_target_pairs={{2,0},{4,2},{6,4},{7,6},{5,7},{3,5},{1,3},{0,1},{10,8},{12,10},{14... | collective-permute-start | bytes 589832 | tf_op jit(solution)/shard_map/ppermute | solution.py:79
  68.7 1.8 %collective-permute-done.24 = f32[24,2,8,128]{3,2,1,0:T(8,128)S(1)} collective-permute-done((f32[24,2,8,128]{3,2,1,0:T(8,128)S(1)}, f32[24,2,8,128]{3,2,1,0:T(8,128)S(1)}, u32[]{:S(2)}, u32[]{:S(2)}) %collective-permute-start.24) | collective-permute-done | bytes 196640 | tf_op jit(solution)/shard_map/ppermute | solution.py:79
  71.5 1.5 %collective-permute-start.25 = (f32[24,2,8,128]{3,2,1,0:T(8,128)S(1)}, f32[24,2,8,128]{3,2,1,0:T(8,128)S(1)}, u32[]{:S(2)}, u32[]{:S(2)}) collective-permute-start(f32[24,2,8,128]{3,2,1,0:T(8,128)S(1)} %fusion.97), channel_id=1, source_target_pairs={{2,0},{4,2},{6,4},{7,6},{5,7},{3,5},{1,3},{0,1},{10,8},{12,10},{14... | collective-permute-start | bytes 589832 | tf_op jit(solution)/shard_map/ppermute | solution.py:79
  73.0 1.7 %collective-permute-done.17 = f32[24,2,8,128]{3,2,1,0:T(8,128)S(1)} collective-permute-done((f32[24,2,8,128]{3,2,1,0:T(8,128)S(1)}, f32[24,2,8,128]{3,2,1,0:T(8,128)S(1)}, u32[]{:S(2)}, u32[]{:S(2)}) %collective-permute-start.17) | collective-permute-done | bytes 196640 | tf_op jit(solution)/shard_map/ppermute | solution.py:79
  75.7 1.8 %collective-permute-start.18 = (f32[24,2,8,128]{3,2,1,0:T(8,128)S(1)}, f32[24,2,8,128]{3,2,1,0:T(8,128)S(1)}, u32[]{:S(2)}, u32[]{:S(2)}) collective-permute-start(f32[24,2,8,128]{3,2,1,0:T(8,128)S(1)} %fusion.96), channel_id=1, source_target_pairs={{2,0},{4,2},{6,4},{7,6},{5,7},{3,5},{1,3},{0,1},{10,8},{12,10},{14... | collective-permute-start | bytes 589832 | tf_op jit(solution)/shard_map/ppermute | solution.py:79
  80.0 1.6 %collective-permute-start.3 = (f32[24,2,8,128]{3,2,1,0:T(8,128)S(1)}, f32[24,2,8,128]{3,2,1,0:T(8,128)S(1)}, u32[]{:S(2)}, u32[]{:S(2)}) collective-permute-start(f32[24,2,8,128]{3,2,1,0:T(8,128)S(1)} %fusion.98), channel_id=1, source_target_pairs={{0,2},{2,4},{4,6},{6,7},{7,5},{5,3},{3,1},{1,0},{8,10},{10,12},{12... | collective-permute-start | bytes 589832 | tf_op jit(solution)/shard_map/ppermute | solution.py:78
  83.4 1.8 %collective-permute-start.19 = (f32[24,2,8,128]{3,2,1,0:T(8,128)S(1)}, f32[24,2,8,128]{3,2,1,0:T(8,128)S(1)}, u32[]{:S(2)}, u32[]{:S(2)}) collective-permute-start(f32[24,2,8,128]{3,2,1,0:T(8,128)S(1)} %add.589), channel_id=1, source_target_pairs={{2,0},{4,2},{6,4},{7,6},{5,7},{3,5},{1,3},{0,1},{10,8},{12,10},{14... | collective-permute-start | bytes 589832 | tf_op jit(solution)/shard_map/ppermute | solution.py:79
  86.9 3.6 %collective-permute-done.3 = f32[24,2,8,128]{3,2,1,0:T(8,128)S(1)} collective-permute-done((f32[24,2,8,128]{3,2,1,0:T(8,128)S(1)}, f32[24,2,8,128]{3,2,1,0:T(8,128)S(1)}, u32[]{:S(2)}, u32[]{:S(2)}) %collective-permute-start.3) | collective-permute-done | bytes 196640 | tf_op jit(solution)/shard_map/ppermute | solution.py:78
  92.1 1.5 %collective-permute-start.27 = (f32[24,2,8,128]{3,2,1,0:T(8,128)S(1)}, f32[24,2,8,128]{3,2,1,0:T(8,128)S(1)}, u32[]{:S(2)}, u32[]{:S(2)}) collective-permute-start(f32[24,2,8,128]{3,2,1,0:T(8,128)S(1)} %add.637), channel_id=1, source_target_pairs={{2,0},{4,2},{6,4},{7,6},{5,7},{3,5},{1,3},{0,1},{10,8},{12,10},{14... | collective-permute-start | bytes 589832 | tf_op jit(solution)/shard_map/ppermute | solution.py:79
  95.4 1.3 %collective-permute-start.13 = (f32[24,2,8,128]{3,2,1,0:T(8,128)S(1)}, f32[24,2,8,128]{3,2,1,0:T(8,128)S(1)}, u32[]{:S(2)}, u32[]{:S(2)}) collective-permute-start(f32[24,2,8,128]{3,2,1,0:T(8,128)S(1)} %add.559), channel_id=1, source_target_pairs={{0,2},{2,4},{4,6},{6,7},{7,5},{5,3},{3,1},{1,0},{8,10},{10,12},{12... | collective-permute-start | bytes 589832 | tf_op jit(solution)/shard_map/ppermute | solution.py:78
  96.7 2.2 %collective-permute-done.4 = f32[24,2,8,128]{3,2,1,0:T(8,128)S(1)} collective-permute-done((f32[24,2,8,128]{3,2,1,0:T(8,128)S(1)}, f32[24,2,8,128]{3,2,1,0:T(8,128)S(1)}, u32[]{:S(2)}, u32[]{:S(2)}) %collective-permute-start.4) | collective-permute-done | bytes 196640 | tf_op jit(solution)/shard_map/ppermute | solution.py:78
  100.6 1.5 %collective-permute-start.28 = (f32[24,2,8,128]{3,2,1,0:T(8,128)S(1)}, f32[24,2,8,128]{3,2,1,0:T(8,128)S(1)}, u32[]{:S(2)}, u32[]{:S(2)}) collective-permute-start(f32[24,2,8,128]{3,2,1,0:T(8,128)S(1)} %add.638), channel_id=1, source_target_pairs={{2,0},{4,2},{6,4},{7,6},{5,7},{3,5},{1,3},{0,1},{10,8},{12,10},{14... | collective-permute-start | bytes 589832 | tf_op jit(solution)/shard_map/ppermute | solution.py:79
  102.1 1.1 collective-permute-done.20
  103.3 1.4 %collective-permute-start.21 = (f32[24,2,8,128]{3,2,1,0:T(8,128)S(1)}, f32[24,2,8,128]{3,2,1,0:T(8,128)S(1)}, u32[]{:S(2)}, u32[]{:S(2)}) collective-permute-start(f32[24,2,8,128]{3,2,1,0:T(8,128)S(1)} %add.607), channel_id=1, source_target_pairs={{2,0},{4,2},{6,4},{7,6},{5,7},{3,5},{1,3},{0,1},{10,8},{12,10},{14... | collective-permute-start | bytes 589832 | tf_op jit(solution)/shard_map/ppermute | solution.py:79
  105.4 2.1 %collective-permute-done.5 = f32[24,2,8,128]{3,2,1,0:T(8,128)S(1)} collective-permute-done((f32[24,2,8,128]{3,2,1,0:T(8,128)S(1)}, f32[24,2,8,128]{3,2,1,0:T(8,128)S(1)}, u32[]{:S(2)}, u32[]{:S(2)}) %collective-permute-start.5) | collective-permute-done | bytes 196640 | tf_op jit(solution)/shard_map/ppermute | solution.py:78
  107.5 1.3 %collective-permute-start.6 = (f32[24,2,8,128]{3,2,1,0:T(8,128)S(1)}, f32[24,2,8,128]{3,2,1,0:T(8,128)S(1)}, u32[]{:S(2)}, u32[]{:S(2)}) collective-permute-start(f32[24,2,8,128]{3,2,1,0:T(8,128)S(1)} %add.538), channel_id=1, source_target_pairs={{0,2},{2,4},{4,6},{6,7},{7,5},{5,3},{3,1},{1,0},{8,10},{10,12},{12... | collective-permute-start | bytes 589832 | tf_op jit(solution)/shard_map/ppermute | solution.py:78
  110.7 1.3 %collective-permute-done.21 = f32[24,2,8,128]{3,2,1,0:T(8,128)S(1)} collective-permute-done((f32[24,2,8,128]{3,2,1,0:T(8,128)S(1)}, f32[24,2,8,128]{3,2,1,0:T(8,128)S(1)}, u32[]{:S(2)}, u32[]{:S(2)}) %collective-permute-start.21) | collective-permute-done | bytes 196640 | tf_op jit(solution)/shard_map/ppermute | solution.py:79
  112.0 1.1 collective-permute-start.22
  113.2 1.1 collective-permute-start.15
  114.3 2.5 %collective-permute-done.6 = f32[24,2,8,128]{3,2,1,0:T(8,128)S(1)} collective-permute-done((f32[24,2,8,128]{3,2,1,0:T(8,128)S(1)}, f32[24,2,8,128]{3,2,1,0:T(8,128)S(1)}, u32[]{:S(2)}, u32[]{:S(2)}) %collective-permute-start.6) | collective-permute-done | bytes 196640 | tf_op jit(solution)/shard_map/ppermute | solution.py:78
  118.5 1.5 %collective-permute-start.30 = (f32[24,2,8,128]{3,2,1,0:T(8,128)S(1)}, f32[24,2,8,128]{3,2,1,0:T(8,128)S(1)}, u32[]{:S(2)}, u32[]{:S(2)}) collective-permute-start(f32[24,2,8,128]{3,2,1,0:T(8,128)S(1)} %add.640), channel_id=1, source_target_pairs={{2,0},{4,2},{6,4},{7,6},{5,7},{3,5},{1,3},{0,1},{10,8},{12,10},{14... | collective-permute-start | bytes 589832 | tf_op jit(solution)/shard_map/ppermute | solution.py:79
  120.1 1.6 %collective-permute-start.23 = (f32[24,2,8,128]{3,2,1,0:T(8,128)S(1)}, f32[24,2,8,128]{3,2,1,0:T(8,128)S(1)}, u32[]{:S(2)}, u32[]{:S(2)}) collective-permute-start(f32[24,2,8,128]{3,2,1,0:T(8,128)S(1)} %add.625), channel_id=1, source_target_pairs={{2,0},{4,2},{6,4},{7,6},{5,7},{3,5},{1,3},{0,1},{10,8},{12,10},{14... | collective-permute-start | bytes 589832 | tf_op jit(solution)/shard_map/ppermute | solution.py:79
  122.2 2.0 %collective-permute-done.7 = f32[24,2,8,128]{3,2,1,0:T(8,128)S(1)} collective-permute-done((f32[24,2,8,128]{3,2,1,0:T(8,128)S(1)}, f32[24,2,8,128]{3,2,1,0:T(8,128)S(1)}, u32[]{:S(2)}, u32[]{:S(2)}) %collective-permute-start.7) | collective-permute-done | bytes 196640 | tf_op jit(solution)/shard_map/ppermute | solution.py:78
  127.4 2.6 %collective-permute-done.8 = f32[24,2,8,128]{3,2,1,0:T(8,128)S(1)} collective-permute-done((f32[24,2,8,128]{3,2,1,0:T(8,128)S(1)}, f32[24,2,8,128]{3,2,1,0:T(8,128)S(1)}, u32[]{:S(2)}, u32[]{:S(2)}) %collective-permute-start.8) | collective-permute-done | bytes 196640 | tf_op jit(solution)/shard_map/ppermute | solution.py:78
  (117 shorter events, 46.8 us)
Async XLA Ops:
  1.2 15.0 %collective-permute-start.1 = (bf16[2048,128]{1,0:T(8,128)(2,1)S(1)}, bf16[2048,128]{1,0:T(8,128)(2,1)S(1)}, u32[]{:S(2)}, u32[]{:S(2)}) collective-permute-start(bf16[2048,128]{1,0:T(8,128)(2,1)S(1)} %slice.6), channel_id=1, source_target_pairs={{0,16},{16,0},{1,17},{17,1},{2,18},{18,2},{3,19},{19,3},{4,20},{20... | collective-permute-start | bytes 1572872 | tf_op jit(solution)/shard_map/ppermute | solution.py:20
  4.2 36.0 %collective-permute-start = (bf16[384,2048]{1,0:T(8,128)(2,1)}, bf16[384,2048]{1,0:T(8,128)(2,1)}, u32[]{:S(2)}, u32[]{:S(2)}) collective-permute-start(bf16[384,2048]{1,0:T(8,128)(2,1)} %param.7), channel_id=1, source_target_pairs={{0,8},{8,0},{1,9},{9,1},{2,10},{10,2},{3,11},{11,3},{4,12},{12,4},... | collective-permute-start | bytes 4718600 | tf_op jit(solution)/shard_map/ppermute | solution.py:20
  5.0 24.2 %copy-start.5 = (s32[8]{0:T(128)S(1)}, s32[8]{0:T(128)}, u32[]{:S(2)}) copy-start(s32[8]{0:T(128)} %constant.217.clone) | copy-start | bytes 100
  17.4 22.7 %collective-permute-start.9 = (bf16[2048,128]{1,0:T(8,128)(2,1)}, bf16[2048,128]{1,0:T(8,128)(2,1)S(1)}, u32[]{:S(2)}, u32[]{:S(2)}) collective-permute-start(bf16[2048,128]{1,0:T(8,128)(2,1)} %get-tuple-element.27), channel_id=1, source_target_pairs={{0,16},{16,0},{1,17},{17,1},{2,18},{18,2},{3,19},{19,3},{4,20},{20... | collective-permute-start | bytes 1572872 | tf_op jit(solution)/shard_map/ppermute | solution.py:20
  62.6 7.9 %collective-permute-start.24 = (f32[24,2,8,128]{3,2,1,0:T(8,128)S(1)}, f32[24,2,8,128]{3,2,1,0:T(8,128)S(1)}, u32[]{:S(2)}, u32[]{:S(2)}) collective-permute-start(f32[24,2,8,128]{3,2,1,0:T(8,128)S(1)} %fusion.16), channel_id=1, source_target_pairs={{2,0},{4,2},{6,4},{7,6},{5,7},{3,5},{1,3},{0,1},{10,8},{12,10},{14... | collective-permute-start | bytes 589832 | tf_op jit(solution)/shard_map/ppermute | solution.py:79
  64.2 10.6 %collective-permute-start.17 = (f32[24,2,8,128]{3,2,1,0:T(8,128)S(1)}, f32[24,2,8,128]{3,2,1,0:T(8,128)S(1)}, u32[]{:S(2)}, u32[]{:S(2)}) collective-permute-start(f32[24,2,8,128]{3,2,1,0:T(8,128)S(1)} %fusion.17), channel_id=1, source_target_pairs={{2,0},{4,2},{6,4},{7,6},{5,7},{3,5},{1,3},{0,1},{10,8},{12,10},{14... | collective-permute-start | bytes 589832 | tf_op jit(solution)/shard_map/ppermute | solution.py:79
  65.7 11.7 %collective-permute-start.10 = (f32[24,2,8,128]{3,2,1,0:T(8,128)S(1)}, f32[24,2,8,128]{3,2,1,0:T(8,128)S(1)}, u32[]{:S(2)}, u32[]{:S(2)}) collective-permute-start(f32[24,2,8,128]{3,2,1,0:T(8,128)S(1)} %fusion), channel_id=1, source_target_pairs={{0,2},{2,4},{4,6},{6,7},{7,5},{5,3},{3,1},{1,0},{8,10},{10,12},{12... | collective-permute-start | bytes 589832 | tf_op jit(solution)/shard_map/ppermute | solution.py:78
  67.2 11.9 %collective-permute-start.2 = (f32[24,2,8,128]{3,2,1,0:T(8,128)S(1)}, f32[24,2,8,128]{3,2,1,0:T(8,128)S(1)}, u32[]{:S(2)}, u32[]{:S(2)}) collective-permute-start(f32[24,2,8,128]{3,2,1,0:T(8,128)S(1)} %fusion.1), channel_id=1, source_target_pairs={{0,2},{2,4},{4,6},{6,7},{7,5},{5,3},{3,1},{1,0},{8,10},{10,12},{12... | collective-permute-start | bytes 589832 | tf_op jit(solution)/shard_map/ppermute | solution.py:78
  71.5 11.2 %collective-permute-start.25 = (f32[24,2,8,128]{3,2,1,0:T(8,128)S(1)}, f32[24,2,8,128]{3,2,1,0:T(8,128)S(1)}, u32[]{:S(2)}, u32[]{:S(2)}) collective-permute-start(f32[24,2,8,128]{3,2,1,0:T(8,128)S(1)} %fusion.97), channel_id=1, source_target_pairs={{2,0},{4,2},{6,4},{7,6},{5,7},{3,5},{1,3},{0,1},{10,8},{12,10},{14... | collective-permute-start | bytes 589832 | tf_op jit(solution)/shard_map/ppermute | solution.py:79
  75.7 7.7 %collective-permute-start.18 = (f32[24,2,8,128]{3,2,1,0:T(8,128)S(1)}, f32[24,2,8,128]{3,2,1,0:T(8,128)S(1)}, u32[]{:S(2)}, u32[]{:S(2)}) collective-permute-start(f32[24,2,8,128]{3,2,1,0:T(8,128)S(1)} %fusion.96), channel_id=1, source_target_pairs={{2,0},{4,2},{6,4},{7,6},{5,7},{3,5},{1,3},{0,1},{10,8},{12,10},{14... | collective-permute-start | bytes 589832 | tf_op jit(solution)/shard_map/ppermute | solution.py:79
  78.5 7.8 %collective-permute-start.11 = (f32[24,2,8,128]{3,2,1,0:T(8,128)S(1)}, f32[24,2,8,128]{3,2,1,0:T(8,128)S(1)}, u32[]{:S(2)}, u32[]{:S(2)}) collective-permute-start(f32[24,2,8,128]{3,2,1,0:T(8,128)S(1)} %fusion.99), channel_id=1, source_target_pairs={{0,2},{2,4},{4,6},{6,7},{7,5},{5,3},{3,1},{1,0},{8,10},{10,12},{12... | collective-permute-start | bytes 589832 | tf_op jit(solution)/shard_map/ppermute | solution.py:78
  80.0 10.5 %collective-permute-start.3 = (f32[24,2,8,128]{3,2,1,0:T(8,128)S(1)}, f32[24,2,8,128]{3,2,1,0:T(8,128)S(1)}, u32[]{:S(2)}, u32[]{:S(2)}) collective-permute-start(f32[24,2,8,128]{3,2,1,0:T(8,128)S(1)} %fusion.98), channel_id=1, source_target_pairs={{0,2},{2,4},{4,6},{6,7},{7,5},{5,3},{3,1},{1,0},{8,10},{10,12},{12... | collective-permute-start | bytes 589832 | tf_op jit(solution)/shard_map/ppermute | solution.py:78
  82.7 9.4 %collective-permute-start.26 = (f32[24,2,8,128]{3,2,1,0:T(8,128)S(1)}, f32[24,2,8,128]{3,2,1,0:T(8,128)S(1)}, u32[]{:S(2)}, u32[]{:S(2)}) collective-permute-start(f32[24,2,8,128]{3,2,1,0:T(8,128)S(1)} %add.636), channel_id=1, source_target_pairs={{2,0},{4,2},{6,4},{7,6},{5,7},{3,5},{1,3},{0,1},{10,8},{12,10},{14... | collective-permute-start | bytes 589832 | tf_op jit(solution)/shard_map/ppermute | solution.py:79
  83.4 11.1 %collective-permute-start.19 = (f32[24,2,8,128]{3,2,1,0:T(8,128)S(1)}, f32[24,2,8,128]{3,2,1,0:T(8,128)S(1)}, u32[]{:S(2)}, u32[]{:S(2)}) collective-permute-start(f32[24,2,8,128]{3,2,1,0:T(8,128)S(1)} %add.589), channel_id=1, source_target_pairs={{2,0},{4,2},{6,4},{7,6},{5,7},{3,5},{1,3},{0,1},{10,8},{12,10},{14... | collective-permute-start | bytes 589832 | tf_op jit(solution)/shard_map/ppermute | solution.py:79
  86.3 9.0 %collective-permute-start.12 = (f32[24,2,8,128]{3,2,1,0:T(8,128)S(1)}, f32[24,2,8,128]{3,2,1,0:T(8,128)S(1)}, u32[]{:S(2)}, u32[]{:S(2)}) collective-permute-start(f32[24,2,8,128]{3,2,1,0:T(8,128)S(1)} %add.558), channel_id=1, source_target_pairs={{0,2},{2,4},{4,6},{6,7},{7,5},{5,3},{3,1},{1,0},{8,10},{10,12},{12... | collective-permute-start | bytes 589832 | tf_op jit(solution)/shard_map/ppermute | solution.py:78
  90.5 8.4 %collective-permute-start.4 = (f32[24,2,8,128]{3,2,1,0:T(8,128)S(1)}, f32[24,2,8,128]{3,2,1,0:T(8,128)S(1)}, u32[]{:S(2)}, u32[]{:S(2)}) collective-permute-start(f32[24,2,8,128]{3,2,1,0:T(8,128)S(1)} %add.526), channel_id=1, source_target_pairs={{0,2},{2,4},{4,6},{6,7},{7,5},{5,3},{3,1},{1,0},{8,10},{10,12},{12... | collective-permute-start | bytes 589832 | tf_op jit(solution)/shard_map/ppermute | solution.py:78
  92.1 8.4 %collective-permute-start.27 = (f32[24,2,8,128]{3,2,1,0:T(8,128)S(1)}, f32[24,2,8,128]{3,2,1,0:T(8,128)S(1)}, u32[]{:S(2)}, u32[]{:S(2)}) collective-permute-start(f32[24,2,8,128]{3,2,1,0:T(8,128)S(1)} %add.637), channel_id=1, source_target_pairs={{2,0},{4,2},{6,4},{7,6},{5,7},{3,5},{1,3},{0,1},{10,8},{12,10},{14... | collective-permute-start | bytes 589832 | tf_op jit(solution)/shard_map/ppermute | solution.py:79
  94.5 8.7 %collective-permute-start.20 = (f32[24,2,8,128]{3,2,1,0:T(8,128)S(1)}, f32[24,2,8,128]{3,2,1,0:T(8,128)S(1)}, u32[]{:S(2)}, u32[]{:S(2)}) collective-permute-start(f32[24,2,8,128]{3,2,1,0:T(8,128)S(1)} %add.598), channel_id=1, source_target_pairs={{2,0},{4,2},{6,4},{7,6},{5,7},{3,5},{1,3},{0,1},{10,8},{12,10},{14... | collective-permute-start | bytes 589832 | tf_op jit(solution)/shard_map/ppermute | solution.py:79
  95.4 9.2 %collective-permute-start.13 = (f32[24,2,8,128]{3,2,1,0:T(8,128)S(1)}, f32[24,2,8,128]{3,2,1,0:T(8,128)S(1)}, u32[]{:S(2)}, u32[]{:S(2)}) collective-permute-start(f32[24,2,8,128]{3,2,1,0:T(8,128)S(1)} %add.559), channel_id=1, source_target_pairs={{0,2},{2,4},{4,6},{6,7},{7,5},{5,3},{3,1},{1,0},{8,10},{10,12},{12... | collective-permute-start | bytes 589832 | tf_op jit(solution)/shard_map/ppermute | solution.py:78
  99.0 8.5 %collective-permute-start.5 = (f32[24,2,8,128]{3,2,1,0:T(8,128)S(1)}, f32[24,2,8,128]{3,2,1,0:T(8,128)S(1)}, u32[]{:S(2)}, u32[]{:S(2)}) collective-permute-start(f32[24,2,8,128]{3,2,1,0:T(8,128)S(1)} %add.532), channel_id=1, source_target_pairs={{0,2},{2,4},{4,6},{6,7},{7,5},{5,3},{3,1},{1,0},{8,10},{10,12},{12... | collective-permute-start | bytes 589832 | tf_op jit(solution)/shard_map/ppermute | solution.py:78
  100.6 9.3 %collective-permute-start.28 = (f32[24,2,8,128]{3,2,1,0:T(8,128)S(1)}, f32[24,2,8,128]{3,2,1,0:T(8,128)S(1)}, u32[]{:S(2)}, u32[]{:S(2)}) collective-permute-start(f32[24,2,8,128]{3,2,1,0:T(8,128)S(1)} %add.638), channel_id=1, source_target_pairs={{2,0},{4,2},{6,4},{7,6},{5,7},{3,5},{1,3},{0,1},{10,8},{12,10},{14... | collective-permute-start | bytes 589832 | tf_op jit(solution)/shard_map/ppermute | solution.py:79
  103.3 8.8 %collective-permute-start.21 = (f32[24,2,8,128]{3,2,1,0:T(8,128)S(1)}, f32[24,2,8,128]{3,2,1,0:T(8,128)S(1)}, u32[]{:S(2)}, u32[]{:S(2)}) collective-permute-start(f32[24,2,8,128]{3,2,1,0:T(8,128)S(1)} %add.607), channel_id=1, source_target_pairs={{2,0},{4,2},{6,4},{7,6},{5,7},{3,5},{1,3},{0,1},{10,8},{12,10},{14... | collective-permute-start | bytes 589832 | tf_op jit(solution)/shard_map/ppermute | solution.py:79
  104.7 8.5 %collective-permute-start.14 = (f32[24,2,8,128]{3,2,1,0:T(8,128)S(1)}, f32[24,2,8,128]{3,2,1,0:T(8,128)S(1)}, u32[]{:S(2)}, u32[]{:S(2)}) collective-permute-start(f32[24,2,8,128]{3,2,1,0:T(8,128)S(1)} %add.560), channel_id=1, source_target_pairs={{0,2},{2,4},{4,6},{6,7},{7,5},{5,3},{3,1},{1,0},{8,10},{10,12},{12... | collective-permute-start | bytes 589832 | tf_op jit(solution)/shard_map/ppermute | solution.py:78
  107.5 9.2 %collective-permute-start.6 = (f32[24,2,8,128]{3,2,1,0:T(8,128)S(1)}, f32[24,2,8,128]{3,2,1,0:T(8,128)S(1)}, u32[]{:S(2)}, u32[]{:S(2)}) collective-permute-start(f32[24,2,8,128]{3,2,1,0:T(8,128)S(1)} %add.538), channel_id=1, source_target_pairs={{0,2},{2,4},{4,6},{6,7},{7,5},{5,3},{3,1},{1,0},{8,10},{10,12},{12... | collective-permute-start | bytes 589832 | tf_op jit(solution)/shard_map/ppermute | solution.py:78
  109.9 8.6 %collective-permute-start.29 = (f32[24,2,8,128]{3,2,1,0:T(8,128)S(1)}, f32[24,2,8,128]{3,2,1,0:T(8,128)S(1)}, u32[]{:S(2)}, u32[]{:S(2)}) collective-permute-start(f32[24,2,8,128]{3,2,1,0:T(8,128)S(1)} %add.639), channel_id=1, source_target_pairs={{2,0},{4,2},{6,4},{7,6},{5,7},{3,5},{1,3},{0,1},{10,8},{12,10},{14... | collective-permute-start | bytes 589832 | tf_op jit(solution)/shard_map/ppermute | solution.py:79
  112.0 8.0 %collective-permute-start.22 = (f32[24,2,8,128]{3,2,1,0:T(8,128)S(1)}, f32[24,2,8,128]{3,2,1,0:T(8,128)S(1)}, u32[]{:S(2)}, u32[]{:S(2)}) collective-permute-start(f32[24,2,8,128]{3,2,1,0:T(8,128)S(1)} %add.616), channel_id=1, source_target_pairs={{2,0},{4,2},{6,4},{7,6},{5,7},{3,5},{1,3},{0,1},{10,8},{12,10},{14... | collective-permute-start | bytes 589832 | tf_op jit(solution)/shard_map/ppermute | solution.py:79
  113.2 8.5 %collective-permute-start.15 = (f32[24,2,8,128]{3,2,1,0:T(8,128)S(1)}, f32[24,2,8,128]{3,2,1,0:T(8,128)S(1)}, u32[]{:S(2)}, u32[]{:S(2)}) collective-permute-start(f32[24,2,8,128]{3,2,1,0:T(8,128)S(1)} %add.561), channel_id=1, source_target_pairs={{0,2},{2,4},{4,6},{6,7},{7,5},{5,3},{3,1},{1,0},{8,10},{10,12},{12... | collective-permute-start | bytes 589832 | tf_op jit(solution)/shard_map/ppermute | solution.py:78
  116.8 7.4 %collective-permute-start.7 = (f32[24,2,8,128]{3,2,1,0:T(8,128)S(1)}, f32[24,2,8,128]{3,2,1,0:T(8,128)S(1)}, u32[]{:S(2)}, u32[]{:S(2)}) collective-permute-start(f32[24,2,8,128]{3,2,1,0:T(8,128)S(1)} %add.544), channel_id=1, source_target_pairs={{0,2},{2,4},{4,6},{6,7},{7,5},{5,3},{3,1},{1,0},{8,10},{10,12},{12... | collective-permute-start | bytes 589832 | tf_op jit(solution)/shard_map/ppermute | solution.py:78
  118.5 7.3 %collective-permute-start.30 = (f32[24,2,8,128]{3,2,1,0:T(8,128)S(1)}, f32[24,2,8,128]{3,2,1,0:T(8,128)S(1)}, u32[]{:S(2)}, u32[]{:S(2)}) collective-permute-start(f32[24,2,8,128]{3,2,1,0:T(8,128)S(1)} %add.640), channel_id=1, source_target_pairs={{2,0},{4,2},{6,4},{7,6},{5,7},{3,5},{1,3},{0,1},{10,8},{12,10},{14... | collective-permute-start | bytes 589832 | tf_op jit(solution)/shard_map/ppermute | solution.py:79
  120.1 6.3 %collective-permute-start.23 = (f32[24,2,8,128]{3,2,1,0:T(8,128)S(1)}, f32[24,2,8,128]{3,2,1,0:T(8,128)S(1)}, u32[]{:S(2)}, u32[]{:S(2)}) collective-permute-start(f32[24,2,8,128]{3,2,1,0:T(8,128)S(1)} %add.625), channel_id=1, source_target_pairs={{2,0},{4,2},{6,4},{7,6},{5,7},{3,5},{1,3},{0,1},{10,8},{12,10},{14... | collective-permute-start | bytes 589832 | tf_op jit(solution)/shard_map/ppermute | solution.py:79
  121.6 5.7 %collective-permute-start.16 = (f32[24,2,8,128]{3,2,1,0:T(8,128)S(1)}, f32[24,2,8,128]{3,2,1,0:T(8,128)S(1)}, u32[]{:S(2)}, u32[]{:S(2)}) collective-permute-start(f32[24,2,8,128]{3,2,1,0:T(8,128)S(1)} %add.562), channel_id=1, source_target_pairs={{0,2},{2,4},{4,6},{6,7},{7,5},{5,3},{3,1},{1,0},{8,10},{10,12},{12... | collective-permute-start | bytes 589832 | tf_op jit(solution)/shard_map/ppermute | solution.py:78
  124.2 5.7 %collective-permute-start.8 = (f32[24,2,8,128]{3,2,1,0:T(8,128)S(1)}, f32[24,2,8,128]{3,2,1,0:T(8,128)S(1)}, u32[]{:S(2)}, u32[]{:S(2)}) collective-permute-start(f32[24,2,8,128]{3,2,1,0:T(8,128)S(1)} %add.550), channel_id=1, source_target_pairs={{0,2},{2,4},{4,6},{6,7},{7,5},{5,3},{3,1},{1,0},{8,10},{10,12},{12... | collective-permute-start | bytes 589832 | tf_op jit(solution)/shard_map/ppermute | solution.py:78
  (8 other events, 90.7 us)

commit v4 on v3

--- a/solution.py
+++ b/solution.py
@@ -58,7 +58,7 @@
         order_table = jnp.asarray(order, dtype=jnp.int32)
         position = jnp.asarray(position_of, dtype=jnp.int32)[mode]
 
-        def partial_rows(owner, part, source_block):
+        def partial_rows(owner, part, source_block, receiver_block=receiver_block):
             start = owner * chunk + part * half
             rows = lax.dynamic_slice_in_dim(receiver_block, start, half, axis=0)
             widened = rows.astype(jnp.float32)
@@ -75,10 +75,13 @@
         behind = [partial_rows(owner_at(1), 1, source) for source in source_blocks]
         for step in range(mode_count - 1):
             for q, source in enumerate(source_blocks):
-                ahead[q] = lax.ppermute(ahead[q], "mode", clockwise)
-                behind[q] = lax.ppermute(behind[q], "mode", counter)
-                ahead[q] = ahead[q] + partial_rows(owner_at(-step - 2), 0, source)
-                behind[q] = behind[q] + partial_rows(owner_at(step + 2), 1, source)
+                held, gated, sent_ahead, sent_behind = lax.optimization_barrier(
+                    (receiver_block, source, ahead[q], behind[q])
+                )
+                ahead[q] = lax.ppermute(sent_ahead, "mode", clockwise)
+                behind[q] = lax.ppermute(sent_behind, "mode", counter)
+                ahead[q] = ahead[q] + partial_rows(owner_at(-step - 2), 0, gated, held)
+                behind[q] = behind[q] + partial_rows(owner_at(step + 2), 1, gated, held)
         rows = [jnp.concatenate(parts, axis=3) for parts in (ahead, behind)]
         return jnp.concatenate(rows, axis=0)
 

time: 131 us -> 122 us (0.931)
  waiting for transfers between devices: 35.6 us -> 23.8 us
  between operations: 20 us -> 21.8 us
  starting transfers between devices: 35.1 us -> 33.5 us
  other arithmetic: 6.07 us -> 7.59 us
    ppermute x28, waiting for transfers between devices: 24.5 us -> 12.9 us  [the longest x14 9.66 us: per_device(): behind[q] = lax.ppermute(sent_behind, 'mode', counter)]
    ppermute x28, starting transfers between devices: 30.3 us -> 28.6 us  [the longest x14 22.1 us: per_device(): behind[q] = lax.ppermute(sent_behind, 'mode', counter)]
  transfers between devices with their start and end apart: 31 -> 31, of which waited for: 17 -> 13; matrix products, arithmetic and copies ran while one was open for 12% -> 28% of each run, Pallas kernels for 0% -> 0%
where the time goes in v4:
time: 122 us
  starting transfers between devices  33.5 us (27%)
  matrix products  31.4 us (26%)
  waiting for transfers between devices  23.8 us (20%)
  between operations  21.8 us (18%)
  other arithmetic  7.59 us (6%)
  local copies, waits for them, and re-layouts  3.59 us (3%)
    dot_general x32, matrix products, partial_rows(): jnp.dot(weighted.reshape(-1, block_modes), source_block, preferred_elemen...  31.4 us
    ppermute x14, starting transfers between devices, per_device(): behind[q] = lax.ppermute(sent_behind, 'mode', counter)  22.1 us
    ppermute x3, waiting for transfers between devices, swap_pair(): return lax.ppermute(local, axis_name, [(0, 1), (1, 0)])  10.9 us
    ppermute x14, waiting for transfers between devices, per_device(): behind[q] = lax.ppermute(sent_behind, 'mode', counter)  9.66 us
    ppermute x14, starting transfers between devices, per_device(): ahead[q] = lax.ppermute(sent_ahead, 'mode', clockwise)  6.51 us
    ppermute x3, starting transfers between devices, swap_pair(): return lax.ppermute(local, axis_name, [(0, 1), (1, 0)])  4.86 us
    ppermute x14, waiting for transfers between devices, per_device(): ahead[q] = lax.ppermute(sent_ahead, 'mode', clockwise)  3.25 us
    select_n x3, other arithmetic, gather_blocks(): first = jnp.where(index == 0, local, other)  2.99 us
  transfers between devices with their start and end apart: 31, of which 13 were waited for; matrix products, arithmetic and copies ran while one was open for 28% of the time, Pallas kernels for 0%

profile of v4, /device:TPU:0, one launch (start us, length us, event | category | flops | bytes accessed | tf_op | source)
XLA Modules:
  0.0 121.8 jit_solution(16258484951497382766)
XLA Ops:
  0.5 1.1 slice.6
  1.5 2.6 %collective-permute-start.1 = (bf16[2048,128]{1,0:T(8,128)(2,1)S(1)}, bf16[2048,128]{1,0:T(8,128)(2,1)S(1)}, u32[]{:S(2)}, u32[]{:S(2)}) collective-permute-start(bf16[2048,128]{1,0:T(8,128)(2,1)S(1)} %slice.6), channel_id=1, source_target_pairs={{0,16},{16,0},{1,17},{17,1},{2,18},{18,2},{3,19},{19,3},{4,20},{20... | collective-permute-start | bytes 1572872 | tf_op jit(solution)/shard_map/ppermute | solution.py:20
  5.8 10.9 %collective-permute-done.1 = bf16[2048,128]{1,0:T(8,128)(2,1)S(1)} collective-permute-done((bf16[2048,128]{1,0:T(8,128)(2,1)S(1)}, bf16[2048,128]{1,0:T(8,128)(2,1)S(1)}, u32[]{:S(2)}, u32[]{:S(2)}) %collective-permute-start.1) | collective-permute-done | bytes 524320 | tf_op jit(solution)/shard_map/ppermute | solution.py:20
  16.7 1.3 %broadcast_select_fusion.5 = (bf16[2048,128]{1,0:T(8,128)(2,1)S(1)}, bf16[2048,128]{1,0:T(8,128)(2,1)S(1)}, bf16[2048,128]{1,0:T(8,128)(2,1)S(1)}) fusion(bf16[2048,128]{1,0:T(8,128)(2,1)S(1)} %collective-permute-done.1, pred[]{:T(512)S(6)} %eq.44, bf16[2048,256]{1,0:T(8,128)(2,1)} %param.8), kind=kLoop, calls=%fused_computation.175 | loop fusion | flops 524288 | bytes 3145729 | tf_op jit(solution)/shard_map/jit(_where)/select_n | solution.py:28
  18.0 1.8 %collective-permute-start.15 = (bf16[2048,128]{1,0:T(8,128)(2,1)S(1)}, bf16[2048,128]{1,0:T(8,128)(2,1)S(1)}, u32[]{:S(2)}, u32[]{:S(2)}) collective-permute-start(bf16[2048,128]{1,0:T(8,128)(2,1)S(1)} %get-tuple-element.153), channel_id=1, source_target_pairs={{0,16},{16,0},{1,17},{17,1},{2,18},{18,2},{3,19},{19,3},{4,20},{20... | collective-permute-start | bytes 1572872 | tf_op jit(solution)/shard_map/ppermute | solution.py:20
  42.6 1.1 copy-done.1
  43.8 1.6 %broadcast_select_fusion.1 = (bf16[384,2048]{1,0:T(8,128)(2,1)S(1)}, bf16[384,2048]{1,0:T(8,128)(2,1)S(1)}) fusion(bf16[384,2048]{1,0:T(8,128)(2,1)S(1)} %copy-done.1, bf16[384,2048]{1,0:T(8,128)(2,1)} %collective-permute-done, pred[]{:T(512)S(6)} %eq.43), kind=kLoop, calls=%fused_computation.132 | loop fusion | flops 1572864 | bytes 6291457 | tf_op jit(solution)/shard_map/jit(_where)/select_n | solution.py:28
  45.8 1.0 fusion.3
  47.8 1.0 fusion.1
  49.8 1.5 %collective-permute-start.3 = (f32[24,2,8,128]{3,2,1,0:T(8,128)S(1)}, f32[24,2,8,128]{3,2,1,0:T(8,128)S(1)}, u32[]{:S(2)}, u32[]{:S(2)}) collective-permute-start(f32[24,2,8,128]{3,2,1,0:T(8,128)S(1)} %fusion.3), channel_id=1, source_target_pairs={{2,0},{4,2},{6,4},{7,6},{5,7},{3,5},{1,3},{0,1},{10,8},{12,10},{14... | collective-permute-start | bytes 589832 | tf_op jit(solution)/shard_map/ppermute | solution.py:82
  52.0 1.5 %collective-permute-start.17 = (f32[24,2,8,128]{3,2,1,0:T(8,128)S(1)}, f32[24,2,8,128]{3,2,1,0:T(8,128)S(1)}, u32[]{:S(2)}, u32[]{:S(2)}) collective-permute-start(f32[24,2,8,128]{3,2,1,0:T(8,128)S(1)} %fusion.2), channel_id=1, source_target_pairs={{2,0},{4,2},{6,4},{7,6},{5,7},{3,5},{1,3},{0,1},{10,8},{12,10},{14... | collective-permute-start | bytes 589832 | tf_op jit(solution)/shard_map/ppermute | solution.py:82
  54.1 3.6 %collective-permute-done.3 = f32[24,2,8,128]{3,2,1,0:T(8,128)S(1)} collective-permute-done((f32[24,2,8,128]{3,2,1,0:T(8,128)S(1)}, f32[24,2,8,128]{3,2,1,0:T(8,128)S(1)}, u32[]{:S(2)}, u32[]{:S(2)}) %collective-permute-start.3) | collective-permute-done | bytes 196640 | tf_op jit(solution)/shard_map/ppermute | solution.py:82
  57.7 1.0 fusion.98
  59.2 1.0 fusion.99
  60.2 1.6 %collective-permute-start.5 = (f32[24,2,8,128]{3,2,1,0:T(8,128)S(1)}, f32[24,2,8,128]{3,2,1,0:T(8,128)S(1)}, u32[]{:S(2)}, u32[]{:S(2)}) collective-permute-start(f32[24,2,8,128]{3,2,1,0:T(8,128)S(1)} %fusion.98), channel_id=1, source_target_pairs={{2,0},{4,2},{6,4},{7,6},{5,7},{3,5},{1,3},{0,1},{10,8},{12,10},{14... | collective-permute-start | bytes 589832 | tf_op jit(solution)/shard_map/ppermute | solution.py:82
  63.3 1.0 fusion.96
  65.3 1.0 fusion.97
  66.4 1.6 %collective-permute-start.19 = (f32[24,2,8,128]{3,2,1,0:T(8,128)S(1)}, f32[24,2,8,128]{3,2,1,0:T(8,128)S(1)}, u32[]{:S(2)}, u32[]{:S(2)}) collective-permute-start(f32[24,2,8,128]{3,2,1,0:T(8,128)S(1)} %fusion.96), channel_id=1, source_target_pairs={{2,0},{4,2},{6,4},{7,6},{5,7},{3,5},{1,3},{0,1},{10,8},{12,10},{14... | collective-permute-start | bytes 589832 | tf_op jit(solution)/shard_map/ppermute | solution.py:82
  70.5 1.6 %collective-permute-start.7 = (f32[24,2,8,128]{3,2,1,0:T(8,128)S(1)}, f32[24,2,8,128]{3,2,1,0:T(8,128)S(1)}, u32[]{:S(2)}, u32[]{:S(2)}) collective-permute-start(f32[24,2,8,128]{3,2,1,0:T(8,128)S(1)} %add.552), channel_id=1, source_target_pairs={{2,0},{4,2},{6,4},{7,6},{5,7},{3,5},{1,3},{0,1},{10,8},{12,10},{14... | collective-permute-start | bytes 589832 | tf_op jit(solution)/shard_map/ppermute | solution.py:82
  74.8 1.6 %collective-permute-start.21 = (f32[24,2,8,128]{3,2,1,0:T(8,128)S(1)}, f32[24,2,8,128]{3,2,1,0:T(8,128)S(1)}, u32[]{:S(2)}, u32[]{:S(2)}) collective-permute-start(f32[24,2,8,128]{3,2,1,0:T(8,128)S(1)} %add.622), channel_id=1, source_target_pairs={{2,0},{4,2},{6,4},{7,6},{5,7},{3,5},{1,3},{0,1},{10,8},{12,10},{14... | collective-permute-start | bytes 589832 | tf_op jit(solution)/shard_map/ppermute | solution.py:82
  79.2 1.6 %collective-permute-start.9 = (f32[24,2,8,128]{3,2,1,0:T(8,128)S(1)}, f32[24,2,8,128]{3,2,1,0:T(8,128)S(1)}, u32[]{:S(2)}, u32[]{:S(2)}) collective-permute-start(f32[24,2,8,128]{3,2,1,0:T(8,128)S(1)} %add.567), channel_id=1, source_target_pairs={{2,0},{4,2},{6,4},{7,6},{5,7},{3,5},{1,3},{0,1},{10,8},{12,10},{14... | collective-permute-start | bytes 589832 | tf_op jit(solution)/shard_map/ppermute | solution.py:82
  82.6 1.0 fusion.10
  84.1 1.6 %collective-permute-start.23 = (f32[24,2,8,128]{3,2,1,0:T(8,128)S(1)}, f32[24,2,8,128]{3,2,1,0:T(8,128)S(1)}, u32[]{:S(2)}, u32[]{:S(2)}) collective-permute-start(f32[24,2,8,128]{3,2,1,0:T(8,128)S(1)} %add.624), channel_id=1, source_target_pairs={{2,0},{4,2},{6,4},{7,6},{5,7},{3,5},{1,3},{0,1},{10,8},{12,10},{14... | collective-permute-start | bytes 589832 | tf_op jit(solution)/shard_map/ppermute | solution.py:82
  88.6 1.3 %collective-permute-start.11 = (f32[24,2,8,128]{3,2,1,0:T(8,128)S(1)}, f32[24,2,8,128]{3,2,1,0:T(8,128)S(1)}, u32[]{:S(2)}, u32[]{:S(2)}) collective-permute-start(f32[24,2,8,128]{3,2,1,0:T(8,128)S(1)} %add.582), channel_id=1, source_target_pairs={{2,0},{4,2},{6,4},{7,6},{5,7},{3,5},{1,3},{0,1},{10,8},{12,10},{14... | collective-permute-start | bytes 589832 | tf_op jit(solution)/shard_map/ppermute | solution.py:82
  93.0 1.7 %collective-permute-start.25 = (f32[24,2,8,128]{3,2,1,0:T(8,128)S(1)}, f32[24,2,8,128]{3,2,1,0:T(8,128)S(1)}, u32[]{:S(2)}, u32[]{:S(2)}) collective-permute-start(f32[24,2,8,128]{3,2,1,0:T(8,128)S(1)} %add.626), channel_id=1, source_target_pairs={{2,0},{4,2},{6,4},{7,6},{5,7},{3,5},{1,3},{0,1},{10,8},{12,10},{14... | collective-permute-start | bytes 589832 | tf_op jit(solution)/shard_map/ppermute | solution.py:82
  97.1 2.0 %collective-permute-start.13 = (f32[24,2,8,128]{3,2,1,0:T(8,128)S(1)}, f32[24,2,8,128]{3,2,1,0:T(8,128)S(1)}, u32[]{:S(2)}, u32[]{:S(2)}) collective-permute-start(f32[24,2,8,128]{3,2,1,0:T(8,128)S(1)} %add.597), channel_id=1, source_target_pairs={{2,0},{4,2},{6,4},{7,6},{5,7},{3,5},{1,3},{0,1},{10,8},{12,10},{14... | collective-permute-start | bytes 589832 | tf_op jit(solution)/shard_map/ppermute | solution.py:82
  101.3 1.2 collective-permute-done.24
  102.6 1.3 %collective-permute-start.27 = (f32[24,2,8,128]{3,2,1,0:T(8,128)S(1)}, f32[24,2,8,128]{3,2,1,0:T(8,128)S(1)}, u32[]{:S(2)}, u32[]{:S(2)}) collective-permute-start(f32[24,2,8,128]{3,2,1,0:T(8,128)S(1)} %add.628), channel_id=1, source_target_pairs={{2,0},{4,2},{6,4},{7,6},{5,7},{3,5},{1,3},{0,1},{10,8},{12,10},{14... | collective-permute-start | bytes 589832 | tf_op jit(solution)/shard_map/ppermute | solution.py:82
  107.1 3.0 %collective-permute-done.27 = f32[24,2,8,128]{3,2,1,0:T(8,128)S(1)} collective-permute-done((f32[24,2,8,128]{3,2,1,0:T(8,128)S(1)}, f32[24,2,8,128]{3,2,1,0:T(8,128)S(1)}, u32[]{:S(2)}, u32[]{:S(2)}) %collective-permute-start.27) | collective-permute-done | bytes 196640 | tf_op jit(solution)/shard_map/ppermute | solution.py:82
  113.0 1.4 %collective-permute-start.29 = (f32[24,2,8,128]{3,2,1,0:T(8,128)S(1)}, f32[24,2,8,128]{3,2,1,0:T(8,128)S(1)}, u32[]{:S(2)}, u32[]{:S(2)}) collective-permute-start(f32[24,2,8,128]{3,2,1,0:T(8,128)S(1)} %add.612), channel_id=1, source_target_pairs={{2,0},{4,2},{6,4},{7,6},{5,7},{3,5},{1,3},{0,1},{10,8},{12,10},{14... | collective-permute-start | bytes 589832 | tf_op jit(solution)/shard_map/ppermute | solution.py:82
  114.4 1.5 %collective-permute-start.30 = (f32[24,2,8,128]{3,2,1,0:T(8,128)S(1)}, f32[24,2,8,128]{3,2,1,0:T(8,128)S(1)}, u32[]{:S(2)}, u32[]{:S(2)}) collective-permute-start(f32[24,2,8,128]{3,2,1,0:T(8,128)S(1)} %add.630), channel_id=1, source_target_pairs={{2,0},{4,2},{6,4},{7,6},{5,7},{3,5},{1,3},{0,1},{10,8},{12,10},{14... | collective-permute-start | bytes 589832 | tf_op jit(solution)/shard_map/ppermute | solution.py:82
  118.7 2.1 %collective-permute-done.30 = f32[24,2,8,128]{3,2,1,0:T(8,128)S(1)} collective-permute-done((f32[24,2,8,128]{3,2,1,0:T(8,128)S(1)}, f32[24,2,8,128]{3,2,1,0:T(8,128)S(1)}, u32[]{:S(2)}, u32[]{:S(2)}) %collective-permute-start.30) | collective-permute-done | bytes 196640 | tf_op jit(solution)/shard_map/ppermute | solution.py:82
  (122 shorter events, 40.6 us)
Async XLA Ops:
  0.0 42.6 %collective-permute-start = (bf16[384,2048]{1,0:T(8,128)(2,1)}, bf16[384,2048]{1,0:T(8,128)(2,1)}, u32[]{:S(2)}, u32[]{:S(2)}) collective-permute-start(bf16[384,2048]{1,0:T(8,128)(2,1)} %param.7), channel_id=1, source_target_pairs={{0,8},{8,0},{1,9},{9,1},{2,10},{10,2},{3,11},{11,3},{4,12},{12,4},... | collective-permute-start | bytes 4718600 | tf_op jit(solution)/shard_map/ppermute | solution.py:20
  1.5 15.2 %collective-permute-start.1 = (bf16[2048,128]{1,0:T(8,128)(2,1)S(1)}, bf16[2048,128]{1,0:T(8,128)(2,1)S(1)}, u32[]{:S(2)}, u32[]{:S(2)}) collective-permute-start(bf16[2048,128]{1,0:T(8,128)(2,1)S(1)} %slice.6), channel_id=1, source_target_pairs={{0,16},{16,0},{1,17},{17,1},{2,18},{18,2},{3,19},{19,3},{4,20},{20... | collective-permute-start | bytes 1572872 | tf_op jit(solution)/shard_map/ppermute | solution.py:20
  5.8 36.7 %copy-start = (bf16[2048,256]{1,0:T(8,128)(2,1)S(1)}, bf16[2048,256]{1,0:T(8,128)(2,1)}, u32[]{:S(2)}) copy-start(bf16[2048,256]{1,0:T(8,128)(2,1)} %param.8) | copy-start | bytes 3145732
  18.0 24.4 %collective-permute-start.15 = (bf16[2048,128]{1,0:T(8,128)(2,1)S(1)}, bf16[2048,128]{1,0:T(8,128)(2,1)S(1)}, u32[]{:S(2)}, u32[]{:S(2)}) collective-permute-start(bf16[2048,128]{1,0:T(8,128)(2,1)S(1)} %get-tuple-element.153), channel_id=1, source_target_pairs={{0,16},{16,0},{1,17},{17,1},{2,18},{18,2},{3,19},{19,3},{4,20},{20... | collective-permute-start | bytes 1572872 | tf_op jit(solution)/shard_map/ppermute | solution.py:20
  49.8 7.9 %collective-permute-start.3 = (f32[24,2,8,128]{3,2,1,0:T(8,128)S(1)}, f32[24,2,8,128]{3,2,1,0:T(8,128)S(1)}, u32[]{:S(2)}, u32[]{:S(2)}) collective-permute-start(f32[24,2,8,128]{3,2,1,0:T(8,128)S(1)} %fusion.3), channel_id=1, source_target_pairs={{2,0},{4,2},{6,4},{7,6},{5,7},{3,5},{1,3},{0,1},{10,8},{12,10},{14... | collective-permute-start | bytes 589832 | tf_op jit(solution)/shard_map/ppermute | solution.py:82
  51.3 7.8 %collective-permute-start.2 = (f32[24,2,8,128]{3,2,1,0:T(8,128)S(1)}, f32[24,2,8,128]{3,2,1,0:T(8,128)S(1)}, u32[]{:S(2)}, u32[]{:S(2)}) collective-permute-start(f32[24,2,8,128]{3,2,1,0:T(8,128)S(1)} %fusion.1), channel_id=1, source_target_pairs={{0,2},{2,4},{4,6},{6,7},{7,5},{5,3},{3,1},{1,0},{8,10},{10,12},{12... | collective-permute-start | bytes 589832 | tf_op jit(solution)/shard_map/ppermute | solution.py:81
  52.0 11.3 %collective-permute-start.17 = (f32[24,2,8,128]{3,2,1,0:T(8,128)S(1)}, f32[24,2,8,128]{3,2,1,0:T(8,128)S(1)}, u32[]{:S(2)}, u32[]{:S(2)}) collective-permute-start(f32[24,2,8,128]{3,2,1,0:T(8,128)S(1)} %fusion.2), channel_id=1, source_target_pairs={{2,0},{4,2},{6,4},{7,6},{5,7},{3,5},{1,3},{0,1},{10,8},{12,10},{14... | collective-permute-start | bytes 589832 | tf_op jit(solution)/shard_map/ppermute | solution.py:82
  53.5 11.8 %collective-permute-start.16 = (f32[24,2,8,128]{3,2,1,0:T(8,128)S(1)}, f32[24,2,8,128]{3,2,1,0:T(8,128)S(1)}, u32[]{:S(2)}, u32[]{:S(2)}) collective-permute-start(f32[24,2,8,128]{3,2,1,0:T(8,128)S(1)} %fusion), channel_id=1, source_target_pairs={{0,2},{2,4},{4,6},{6,7},{7,5},{5,3},{3,1},{1,0},{8,10},{10,12},{12... | collective-permute-start | bytes 589832 | tf_op jit(solution)/shard_map/ppermute | solution.py:81
  60.2 10.3 %collective-permute-start.5 = (f32[24,2,8,128]{3,2,1,0:T(8,128)S(1)}, f32[24,2,8,128]{3,2,1,0:T(8,128)S(1)}, u32[]{:S(2)}, u32[]{:S(2)}) collective-permute-start(f32[24,2,8,128]{3,2,1,0:T(8,128)S(1)} %fusion.98), channel_id=1, source_target_pairs={{2,0},{4,2},{6,4},{7,6},{5,7},{3,5},{1,3},{0,1},{10,8},{12,10},{14... | collective-permute-start | bytes 589832 | tf_op jit(solution)/shard_map/ppermute | solution.py:82
  61.8 8.7 %collective-permute-start.4 = (f32[24,2,8,128]{3,2,1,0:T(8,128)S(1)}, f32[24,2,8,128]{3,2,1,0:T(8,128)S(1)}, u32[]{:S(2)}, u32[]{:S(2)}) collective-permute-start(f32[24,2,8,128]{3,2,1,0:T(8,128)S(1)} %fusion.99), channel_id=1, source_target_pairs={{0,2},{2,4},{4,6},{6,7},{7,5},{5,3},{3,1},{1,0},{8,10},{10,12},{12... | collective-permute-start | bytes 589832 | tf_op jit(solution)/shard_map/ppermute | solution.py:81
  66.4 7.3 %collective-permute-start.19 = (f32[24,2,8,128]{3,2,1,0:T(8,128)S(1)}, f32[24,2,8,128]{3,2,1,0:T(8,128)S(1)}, u32[]{:S(2)}, u32[]{:S(2)}) collective-permute-start(f32[24,2,8,128]{3,2,1,0:T(8,128)S(1)} %fusion.96), channel_id=1, source_target_pairs={{2,0},{4,2},{6,4},{7,6},{5,7},{3,5},{1,3},{0,1},{10,8},{12,10},{14... | collective-permute-start | bytes 589832 | tf_op jit(solution)/shard_map/ppermute | solution.py:82
  68.0 6.7 %collective-permute-start.18 = (f32[24,2,8,128]{3,2,1,0:T(8,128)S(1)}, f32[24,2,8,128]{3,2,1,0:T(8,128)S(1)}, u32[]{:S(2)}, u32[]{:S(2)}) collective-permute-start(f32[24,2,8,128]{3,2,1,0:T(8,128)S(1)} %fusion.97), channel_id=1, source_target_pairs={{0,2},{2,4},{4,6},{6,7},{7,5},{5,3},{3,1},{1,0},{8,10},{10,12},{12... | collective-permute-start | bytes 589832 | tf_op jit(solution)/shard_map/ppermute | solution.py:81
  70.5 8.3 %collective-permute-start.7 = (f32[24,2,8,128]{3,2,1,0:T(8,128)S(1)}, f32[24,2,8,128]{3,2,1,0:T(8,128)S(1)}, u32[]{:S(2)}, u32[]{:S(2)}) collective-permute-start(f32[24,2,8,128]{3,2,1,0:T(8,128)S(1)} %add.552), channel_id=1, source_target_pairs={{2,0},{4,2},{6,4},{7,6},{5,7},{3,5},{1,3},{0,1},{10,8},{12,10},{14... | collective-permute-start | bytes 589832 | tf_op jit(solution)/shard_map/ppermute | solution.py:82
  72.2 7.0 %collective-permute-start.6 = (f32[24,2,8,128]{3,2,1,0:T(8,128)S(1)}, f32[24,2,8,128]{3,2,1,0:T(8,128)S(1)}, u32[]{:S(2)}, u32[]{:S(2)}) collective-permute-start(f32[24,2,8,128]{3,2,1,0:T(8,128)S(1)} %add.543), channel_id=1, source_target_pairs={{0,2},{2,4},{4,6},{6,7},{7,5},{5,3},{3,1},{1,0},{8,10},{10,12},{12... | collective-permute-start | bytes 589832 | tf_op jit(solution)/shard_map/ppermute | solution.py:81
  74.8 7.8 %collective-permute-start.21 = (f32[24,2,8,128]{3,2,1,0:T(8,128)S(1)}, f32[24,2,8,128]{3,2,1,0:T(8,128)S(1)}, u32[]{:S(2)}, u32[]{:S(2)}) collective-permute-start(f32[24,2,8,128]{3,2,1,0:T(8,128)S(1)} %add.622), channel_id=1, source_target_pairs={{2,0},{4,2},{6,4},{7,6},{5,7},{3,5},{1,3},{0,1},{10,8},{12,10},{14... | collective-permute-start | bytes 589832 | tf_op jit(solution)/shard_map/ppermute | solution.py:82
  76.4 7.5 %collective-permute-start.20 = (f32[24,2,8,128]{3,2,1,0:T(8,128)S(1)}, f32[24,2,8,128]{3,2,1,0:T(8,128)S(1)}, u32[]{:S(2)}, u32[]{:S(2)}) collective-permute-start(f32[24,2,8,128]{3,2,1,0:T(8,128)S(1)} %add.621), channel_id=1, source_target_pairs={{0,2},{2,4},{4,6},{6,7},{7,5},{5,3},{3,1},{1,0},{8,10},{10,12},{12... | collective-permute-start | bytes 589832 | tf_op jit(solution)/shard_map/ppermute | solution.py:81
  79.2 8.9 %collective-permute-start.9 = (f32[24,2,8,128]{3,2,1,0:T(8,128)S(1)}, f32[24,2,8,128]{3,2,1,0:T(8,128)S(1)}, u32[]{:S(2)}, u32[]{:S(2)}) collective-permute-start(f32[24,2,8,128]{3,2,1,0:T(8,128)S(1)} %add.567), channel_id=1, source_target_pairs={{2,0},{4,2},{6,4},{7,6},{5,7},{3,5},{1,3},{0,1},{10,8},{12,10},{14... | collective-permute-start | bytes 589832 | tf_op jit(solution)/shard_map/ppermute | solution.py:82
  80.8 7.8 %collective-permute-start.8 = (f32[24,2,8,128]{3,2,1,0:T(8,128)S(1)}, f32[24,2,8,128]{3,2,1,0:T(8,128)S(1)}, u32[]{:S(2)}, u32[]{:S(2)}) collective-permute-start(f32[24,2,8,128]{3,2,1,0:T(8,128)S(1)} %add.558), channel_id=1, source_target_pairs={{0,2},{2,4},{4,6},{6,7},{7,5},{5,3},{3,1},{1,0},{8,10},{10,12},{12... | collective-permute-start | bytes 589832 | tf_op jit(solution)/shard_map/ppermute | solution.py:81
  84.1 7.7 %collective-permute-start.23 = (f32[24,2,8,128]{3,2,1,0:T(8,128)S(1)}, f32[24,2,8,128]{3,2,1,0:T(8,128)S(1)}, u32[]{:S(2)}, u32[]{:S(2)}) collective-permute-start(f32[24,2,8,128]{3,2,1,0:T(8,128)S(1)} %add.624), channel_id=1, source_target_pairs={{2,0},{4,2},{6,4},{7,6},{5,7},{3,5},{1,3},{0,1},{10,8},{12,10},{14... | collective-permute-start | bytes 589832 | tf_op jit(solution)/shard_map/ppermute | solution.py:82
  85.6 7.3 %collective-permute-start.22 = (f32[24,2,8,128]{3,2,1,0:T(8,128)S(1)}, f32[24,2,8,128]{3,2,1,0:T(8,128)S(1)}, u32[]{:S(2)}, u32[]{:S(2)}) collective-permute-start(f32[24,2,8,128]{3,2,1,0:T(8,128)S(1)} %add.623), channel_id=1, source_target_pairs={{0,2},{2,4},{4,6},{6,7},{7,5},{5,3},{3,1},{1,0},{8,10},{10,12},{12... | collective-permute-start | bytes 589832 | tf_op jit(solution)/shard_map/ppermute | solution.py:81
  88.6 8.4 %collective-permute-start.11 = (f32[24,2,8,128]{3,2,1,0:T(8,128)S(1)}, f32[24,2,8,128]{3,2,1,0:T(8,128)S(1)}, u32[]{:S(2)}, u32[]{:S(2)}) collective-permute-start(f32[24,2,8,128]{3,2,1,0:T(8,128)S(1)} %add.582), channel_id=1, source_target_pairs={{2,0},{4,2},{6,4},{7,6},{5,7},{3,5},{1,3},{0,1},{10,8},{12,10},{14... | collective-permute-start | bytes 589832 | tf_op jit(solution)/shard_map/ppermute | solution.py:82
  90.0 7.2 %collective-permute-start.10 = (f32[24,2,8,128]{3,2,1,0:T(8,128)S(1)}, f32[24,2,8,128]{3,2,1,0:T(8,128)S(1)}, u32[]{:S(2)}, u32[]{:S(2)}) collective-permute-start(f32[24,2,8,128]{3,2,1,0:T(8,128)S(1)} %add.573), channel_id=1, source_target_pairs={{0,2},{2,4},{4,6},{6,7},{7,5},{5,3},{3,1},{1,0},{8,10},{10,12},{12... | collective-permute-start | bytes 589832 | tf_op jit(solution)/shard_map/ppermute | solution.py:81
  93.0 7.3 %collective-permute-start.25 = (f32[24,2,8,128]{3,2,1,0:T(8,128)S(1)}, f32[24,2,8,128]{3,2,1,0:T(8,128)S(1)}, u32[]{:S(2)}, u32[]{:S(2)}) collective-permute-start(f32[24,2,8,128]{3,2,1,0:T(8,128)S(1)} %add.626), channel_id=1, source_target_pairs={{2,0},{4,2},{6,4},{7,6},{5,7},{3,5},{1,3},{0,1},{10,8},{12,10},{14... | collective-permute-start | bytes 589832 | tf_op jit(solution)/shard_map/ppermute | solution.py:82
  94.7 7.8 %collective-permute-start.24 = (f32[24,2,8,128]{3,2,1,0:T(8,128)S(1)}, f32[24,2,8,128]{3,2,1,0:T(8,128)S(1)}, u32[]{:S(2)}, u32[]{:S(2)}) collective-permute-start(f32[24,2,8,128]{3,2,1,0:T(8,128)S(1)} %add.625), channel_id=1, source_target_pairs={{0,2},{2,4},{4,6},{6,7},{7,5},{5,3},{3,1},{1,0},{8,10},{10,12},{12... | collective-permute-start | bytes 589832 | tf_op jit(solution)/shard_map/ppermute | solution.py:81
  97.1 9.5 %collective-permute-start.13 = (f32[24,2,8,128]{3,2,1,0:T(8,128)S(1)}, f32[24,2,8,128]{3,2,1,0:T(8,128)S(1)}, u32[]{:S(2)}, u32[]{:S(2)}) collective-permute-start(f32[24,2,8,128]{3,2,1,0:T(8,128)S(1)} %add.597), channel_id=1, source_target_pairs={{2,0},{4,2},{6,4},{7,6},{5,7},{3,5},{1,3},{0,1},{10,8},{12,10},{14... | collective-permute-start | bytes 589832 | tf_op jit(solution)/shard_map/ppermute | solution.py:82
  99.2 7.8 %collective-permute-start.12 = (f32[24,2,8,128]{3,2,1,0:T(8,128)S(1)}, f32[24,2,8,128]{3,2,1,0:T(8,128)S(1)}, u32[]{:S(2)}, u32[]{:S(2)}) collective-permute-start(f32[24,2,8,128]{3,2,1,0:T(8,128)S(1)} %add.588), channel_id=1, source_target_pairs={{0,2},{2,4},{4,6},{6,7},{7,5},{5,3},{3,1},{1,0},{8,10},{10,12},{12... | collective-permute-start | bytes 589832 | tf_op jit(solution)/shard_map/ppermute | solution.py:81
  102.6 7.5 %collective-permute-start.27 = (f32[24,2,8,128]{3,2,1,0:T(8,128)S(1)}, f32[24,2,8,128]{3,2,1,0:T(8,128)S(1)}, u32[]{:S(2)}, u32[]{:S(2)}) collective-permute-start(f32[24,2,8,128]{3,2,1,0:T(8,128)S(1)} %add.628), channel_id=1, source_target_pairs={{2,0},{4,2},{6,4},{7,6},{5,7},{3,5},{1,3},{0,1},{10,8},{12,10},{14... | collective-permute-start | bytes 589832 | tf_op jit(solution)/shard_map/ppermute | solution.py:82
  103.9 6.2 %collective-permute-start.26 = (f32[24,2,8,128]{3,2,1,0:T(8,128)S(1)}, f32[24,2,8,128]{3,2,1,0:T(8,128)S(1)}, u32[]{:S(2)}, u32[]{:S(2)}) collective-permute-start(f32[24,2,8,128]{3,2,1,0:T(8,128)S(1)} %add.627), channel_id=1, source_target_pairs={{0,2},{2,4},{4,6},{6,7},{7,5},{5,3},{3,1},{1,0},{8,10},{10,12},{12... | collective-permute-start | bytes 589832 | tf_op jit(solution)/shard_map/ppermute | solution.py:81
  107.0 10.8 %collective-permute-start.14 = (f32[24,2,8,128]{3,2,1,0:T(8,128)S(1)}, f32[24,2,8,128]{3,2,1,0:T(8,128)S(1)}, u32[]{:S(2)}, u32[]{:S(2)}) collective-permute-start(f32[24,2,8,128]{3,2,1,0:T(8,128)S(1)} %add.603), channel_id=1, source_target_pairs={{0,2},{2,4},{4,6},{6,7},{7,5},{5,3},{3,1},{1,0},{8,10},{10,12},{12... | collective-permute-start | bytes 589832 | tf_op jit(solution)/shard_map/ppermute | solution.py:81
  110.3 7.6 %collective-permute-start.28 = (f32[24,2,8,128]{3,2,1,0:T(8,128)S(1)}, f32[24,2,8,128]{3,2,1,0:T(8,128)S(1)}, u32[]{:S(2)}, u32[]{:S(2)}) collective-permute-start(f32[24,2,8,128]{3,2,1,0:T(8,128)S(1)} %add.629), channel_id=1, source_target_pairs={{0,2},{2,4},{4,6},{6,7},{7,5},{5,3},{3,1},{1,0},{8,10},{10,12},{12... | collective-permute-start | bytes 589832 | tf_op jit(solution)/shard_map/ppermute | solution.py:81
  113.0 5.7 %collective-permute-start.29 = (f32[24,2,8,128]{3,2,1,0:T(8,128)S(1)}, f32[24,2,8,128]{3,2,1,0:T(8,128)S(1)}, u32[]{:S(2)}, u32[]{:S(2)}) collective-permute-start(f32[24,2,8,128]{3,2,1,0:T(8,128)S(1)} %add.612), channel_id=1, source_target_pairs={{2,0},{4,2},{6,4},{7,6},{5,7},{3,5},{1,3},{0,1},{10,8},{12,10},{14... | collective-permute-start | bytes 589832 | tf_op jit(solution)/shard_map/ppermute | solution.py:82
  114.4 6.4 %collective-permute-start.30 = (f32[24,2,8,128]{3,2,1,0:T(8,128)S(1)}, f32[24,2,8,128]{3,2,1,0:T(8,128)S(1)}, u32[]{:S(2)}, u32[]{:S(2)}) collective-permute-start(f32[24,2,8,128]{3,2,1,0:T(8,128)S(1)} %add.630), channel_id=1, source_target_pairs={{2,0},{4,2},{6,4},{7,6},{5,7},{3,5},{1,3},{0,1},{10,8},{12,10},{14... | collective-permute-start | bytes 589832 | tf_op jit(solution)/shard_map/ppermute | solution.py:82
  (3 other events, 52.4 us)

commit v5 on v2

--- a/solution.py
+++ b/solution.py
@@ -41,7 +41,7 @@
 
     def per_device(receivers, excitations, mode_freqs, mode_damping, sample_freqs):
         mode = lax.axis_index("mode")
-        receiver_block = gather_blocks(receivers, "evt", sizes["evt"], 1)
+        receiver_block = lax.all_gather(receivers, "evt", axis=1, tiled=True)
         source_block = gather_blocks(excitations, "sta", sizes["sta"], 0)
         row_count, block_modes = receiver_block.shape
         real_weight, imag_weight = resonance(

time: 104 us -> 119 us (1.14)
  between operations: 20.9 us -> 34.2 us
  other arithmetic: 5.67 us -> 7.01 us
    convert_element_type x3 -> x1, other arithmetic: 0.61 us -> 2.54 us  [partial_rows(): widened = rows.astype(jnp.float32)]
    ppermute x2 -> x1, starting transfers between devices: 3.03 us -> 3.03 us  [swap_pair(): return lax.ppermute(local, axis_name, [(0, 1), (1, 0)])]
  transfers between devices with their start and end apart: 16 -> 16, of which waited for: 14 -> 14; matrix products, arithmetic and copies ran while one was open for 21% -> 18% of each run, Pallas kernels for 0% -> 0%
where the time goes in v5:
time: 119 us
  waiting for transfers between devices  40.1 us (34%)
  between operations  34.2 us (29%)
  starting transfers between devices  18.3 us (15%)
  matrix products  15.6 us (13%)
  other arithmetic  7.01 us (6%)
  local copies, waits for them, and re-layouts  3.25 us (3%)
    ppermute x7, waiting for transfers between devices, per_device(): ahead = lax.ppermute(ahead, 'mode', clockwise)  35.1 us
    dot_general x16, matrix products, partial_rows(): jnp.dot(weighted.reshape(-1, block_modes), source_block, preferred_elemen...  15.6 us
    ppermute x7, starting transfers between devices, per_device(): ahead = lax.ppermute(ahead, 'mode', clockwise)  11.2 us
    ppermute x7, waiting for transfers between devices, per_device(): behind = lax.ppermute(behind, 'mode', counter)  4.3 us
    ppermute x7, starting transfers between devices, per_device(): behind = lax.ppermute(behind, 'mode', counter)  4.08 us
    ppermute x1, starting transfers between devices, swap_pair(): return lax.ppermute(local, axis_name, [(0, 1), (1, 0)])  3.03 us
    convert_element_type x1, other arithmetic, partial_rows(): widened = rows.astype(jnp.float32)  2.54 us
  transfers between devices with their start and end apart: 16, of which 14 were waited for; matrix products, arithmetic and copies ran while one was open for 18% of the time, Pallas kernels for 0%

profile of v5, /device:TPU:0, one launch (start us, length us, event | category | flops | bytes accessed | tf_op | source)
XLA Modules:
  0.0 118.6 jit_solution(13191183507887679492)
XLA Ops:
  7.3 3.0 %collective-permute-start = (bf16[2048,256]{1,0:T(8,128)(2,1)}, bf16[2048,256]{1,0:T(8,128)(2,1)S(1)}, u32[]{:S(2)}, u32[]{:S(2)}) collective-permute-start(bf16[2048,256]{1,0:T(8,128)(2,1)} %param.8), channel_id=1, source_target_pairs={{0,16},{16,0},{1,17},{17,1},{2,18},{18,2},{3,19},{19,3},{4,20},{20... | collective-permute-start | bytes 3145736 | tf_op jit(solution)/shard_map/ppermute | solution.py:20
  10.3 1.2 %dynamic_slice.99 = s32[1]{0:T(128)} dynamic-slice(s32[8]{0:T(128)} %constant.183.clone, s32[]{:T(128)S(6)} %select_n.178), dynamic_slice_sizes={1} | dynamic-slice | bytes 12 | tf_op jit(solution)/shard_map/dynamic_slice | solution.py:54
  22.2 2.0 %fusion.51 = (s32[1]{0:T(128)}, s32[1]{0:T(128)}, s32[1]{0:T(128)}, s32[1]{0:T(128)}, s32[1]{0:T(128)}, /*index=5*/s32[1]{0:T(128)}, s32[1]{0:T(128)}, s32[1]{0:...) fusion(s32[8]{0:T(128)} %constant.182.clone, ...), kind=kLoop, calls=%fused_computation.90 | loop fusion | bytes 192 | tf_op jit(solution)/shard_map/dynamic_slice | solution.py:67
  35.9 1.1 broadcast_select_fusion.1
  37.0 2.5 %dynamic-slice_convert_fusion.8 = (f32[24,4096]{1,0:T(8,128)S(1)}, f32[24,4096]{1,0:T(8,128)S(1)}, f32[24,4096]{1,0:T(8,128)S(1)}, f32[24,4096]{1,0:T(8,128)S(1)...) fusion(bf16[384,4096]{1,0:T(8,128)(2,1)} %all-gather.2.cloned.1, ...), kind=kLoop, calls=%fused_computation.77 | loop fusion | flops 1572864 | bytes 9437248 | tf_op jit(solution)/shard_map/convert_element_type | solution.py:59
  39.5 1.0 fusion
  40.5 1.6 %collective-permute-start.1 = (f32[24,2,8,256]{3,2,1,0:T(8,128)S(1)}, f32[24,2,8,256]{3,2,1,0:T(8,128)S(1)}, u32[]{:S(2)}, u32[]{:S(2)}) collective-permute-start(f32[24,2,8,256]{3,2,1,0:T(8,128)S(1)} %fusion), channel_id=1, source_target_pairs={{0,2},{2,4},{4,6},{6,7},{7,5},{5,3},{3,1},{1,0},{8,10},{10,12},{12... | collective-permute-start | bytes 1179656 | tf_op jit(solution)/shard_map/ppermute | solution.py:72
  44.6 1.0 fusion.9
  45.6 5.5 %collective-permute-done.1 = f32[24,2,8,256]{3,2,1,0:T(8,128)S(1)} collective-permute-done((f32[24,2,8,256]{3,2,1,0:T(8,128)S(1)}, f32[24,2,8,256]{3,2,1,0:T(8,128)S(1)}, u32[]{:S(2)}, u32[]{:S(2)}) %collective-permute-start.1) | collective-permute-done | bytes 393248 | tf_op jit(solution)/shard_map/ppermute | solution.py:72
  51.2 1.6 %collective-permute-start.2 = (f32[24,2,8,256]{3,2,1,0:T(8,128)S(1)}, f32[24,2,8,256]{3,2,1,0:T(8,128)S(1)}, u32[]{:S(2)}, u32[]{:S(2)}) collective-permute-start(f32[24,2,8,256]{3,2,1,0:T(8,128)S(1)} %add.406), channel_id=1, source_target_pairs={{0,2},{2,4},{4,6},{6,7},{7,5},{5,3},{3,1},{1,0},{8,10},{10,12},{12... | collective-permute-start | bytes 1179656 | tf_op jit(solution)/shard_map/ppermute | solution.py:72
  55.0 1.0 fusion.10
  56.0 4.9 %collective-permute-done.2 = f32[24,2,8,256]{3,2,1,0:T(8,128)S(1)} collective-permute-done((f32[24,2,8,256]{3,2,1,0:T(8,128)S(1)}, f32[24,2,8,256]{3,2,1,0:T(8,128)S(1)}, u32[]{:S(2)}, u32[]{:S(2)}) %collective-permute-start.2) | collective-permute-done | bytes 393248 | tf_op jit(solution)/shard_map/ppermute | solution.py:72
  61.0 1.6 %collective-permute-start.3 = (f32[24,2,8,256]{3,2,1,0:T(8,128)S(1)}, f32[24,2,8,256]{3,2,1,0:T(8,128)S(1)}, u32[]{:S(2)}, u32[]{:S(2)}) collective-permute-start(f32[24,2,8,256]{3,2,1,0:T(8,128)S(1)} %add.412), channel_id=1, source_target_pairs={{0,2},{2,4},{4,6},{6,7},{7,5},{5,3},{3,1},{1,0},{8,10},{10,12},{12... | collective-permute-start | bytes 1179656 | tf_op jit(solution)/shard_map/ppermute | solution.py:72
  63.5 1.0 fusion.3
  64.5 1.0 fusion.11
  65.5 4.7 %collective-permute-done.3 = f32[24,2,8,256]{3,2,1,0:T(8,128)S(1)} collective-permute-done((f32[24,2,8,256]{3,2,1,0:T(8,128)S(1)}, f32[24,2,8,256]{3,2,1,0:T(8,128)S(1)}, u32[]{:S(2)}, u32[]{:S(2)}) %collective-permute-start.3) | collective-permute-done | bytes 393248 | tf_op jit(solution)/shard_map/ppermute | solution.py:72
  70.3 1.6 %collective-permute-start.4 = (f32[24,2,8,256]{3,2,1,0:T(8,128)S(1)}, f32[24,2,8,256]{3,2,1,0:T(8,128)S(1)}, u32[]{:S(2)}, u32[]{:S(2)}) collective-permute-start(f32[24,2,8,256]{3,2,1,0:T(8,128)S(1)} %add.418), channel_id=1, source_target_pairs={{0,2},{2,4},{4,6},{6,7},{7,5},{5,3},{3,1},{1,0},{8,10},{10,12},{12... | collective-permute-start | bytes 1179656 | tf_op jit(solution)/shard_map/ppermute | solution.py:72
  72.8 1.0 fusion.4
  73.8 1.0 fusion.12
  74.8 4.7 %collective-permute-done.4 = f32[24,2,8,256]{3,2,1,0:T(8,128)S(1)} collective-permute-done((f32[24,2,8,256]{3,2,1,0:T(8,128)S(1)}, f32[24,2,8,256]{3,2,1,0:T(8,128)S(1)}, u32[]{:S(2)}, u32[]{:S(2)}) %collective-permute-start.4) | collective-permute-done | bytes 393248 | tf_op jit(solution)/shard_map/ppermute | solution.py:72
  79.5 1.6 %collective-permute-start.5 = (f32[24,2,8,256]{3,2,1,0:T(8,128)S(1)}, f32[24,2,8,256]{3,2,1,0:T(8,128)S(1)}, u32[]{:S(2)}, u32[]{:S(2)}) collective-permute-start(f32[24,2,8,256]{3,2,1,0:T(8,128)S(1)} %add.424), channel_id=1, source_target_pairs={{0,2},{2,4},{4,6},{6,7},{7,5},{5,3},{3,1},{1,0},{8,10},{10,12},{12... | collective-permute-start | bytes 1179656 | tf_op jit(solution)/shard_map/ppermute | solution.py:72
  82.2 1.0 fusion.5
  83.2 1.0 fusion.13
  84.2 5.6 %collective-permute-done.5 = f32[24,2,8,256]{3,2,1,0:T(8,128)S(1)} collective-permute-done((f32[24,2,8,256]{3,2,1,0:T(8,128)S(1)}, f32[24,2,8,256]{3,2,1,0:T(8,128)S(1)}, u32[]{:S(2)}, u32[]{:S(2)}) %collective-permute-start.5) | collective-permute-done | bytes 393248 | tf_op jit(solution)/shard_map/ppermute | solution.py:72
  89.8 1.6 %collective-permute-start.6 = (f32[24,2,8,256]{3,2,1,0:T(8,128)S(1)}, f32[24,2,8,256]{3,2,1,0:T(8,128)S(1)}, u32[]{:S(2)}, u32[]{:S(2)}) collective-permute-start(f32[24,2,8,256]{3,2,1,0:T(8,128)S(1)} %add.430), channel_id=1, source_target_pairs={{0,2},{2,4},{4,6},{6,7},{7,5},{5,3},{3,1},{1,0},{8,10},{10,12},{12... | collective-permute-start | bytes 1179656 | tf_op jit(solution)/shard_map/ppermute | solution.py:72
  93.4 1.0 fusion.14
  94.3 6.5 %collective-permute-done.6 = f32[24,2,8,256]{3,2,1,0:T(8,128)S(1)} collective-permute-done((f32[24,2,8,256]{3,2,1,0:T(8,128)S(1)}, f32[24,2,8,256]{3,2,1,0:T(8,128)S(1)}, u32[]{:S(2)}, u32[]{:S(2)}) %collective-permute-start.6) | collective-permute-done | bytes 393248 | tf_op jit(solution)/shard_map/ppermute | solution.py:72
  100.9 1.6 %collective-permute-start.7 = (f32[24,2,8,256]{3,2,1,0:T(8,128)S(1)}, f32[24,2,8,256]{3,2,1,0:T(8,128)S(1)}, u32[]{:S(2)}, u32[]{:S(2)}) collective-permute-start(f32[24,2,8,256]{3,2,1,0:T(8,128)S(1)} %add.436), channel_id=1, source_target_pairs={{0,2},{2,4},{4,6},{6,7},{7,5},{5,3},{3,1},{1,0},{8,10},{10,12},{12... | collective-permute-start | bytes 1179656 | tf_op jit(solution)/shard_map/ppermute | solution.py:72
  103.6 1.0 fusion.7
  104.6 1.0 fusion.15
  105.6 3.1 %collective-permute-done.7 = f32[24,2,8,256]{3,2,1,0:T(8,128)S(1)} collective-permute-done((f32[24,2,8,256]{3,2,1,0:T(8,128)S(1)}, f32[24,2,8,256]{3,2,1,0:T(8,128)S(1)}, u32[]{:S(2)}, u32[]{:S(2)}) %collective-permute-start.7) | collective-permute-done | bytes 393248 | tf_op jit(solution)/shard_map/ppermute | solution.py:72
  108.8 1.9 %collective-permute-done.14 = f32[24,2,8,256]{3,2,1,0:T(8,128)S(1)} collective-permute-done((f32[24,2,8,256]{3,2,1,0:T(8,128)S(1)}, f32[24,2,8,256]{3,2,1,0:T(8,128)S(1)}, u32[]{:S(2)}, u32[]{:S(2)}) %collective-permute-start.14) | collective-permute-done | bytes 393248 | tf_op jit(solution)/shard_map/ppermute | solution.py:73
  (43 shorter events, 14.4 us)
Async XLA Ops:
  6.5 29.3 %copy-start = (bf16[2048,256]{1,0:T(8,128)(2,1)S(1)}, bf16[2048,256]{1,0:T(8,128)(2,1)}, u32[]{:S(2)}) copy-start(bf16[2048,256]{1,0:T(8,128)(2,1)} %param.8) | copy-start | bytes 3145732
  6.5 30.4 %all-gather.2.cloned.1.call-start = ((), (), s32[]{:S(2)}) async-start(), calls=%async_computation | async-start | bytes 4718592 | tf_op jit(solution)/shard_map/all_gather | solution.py:44
  7.3 28.6 %collective-permute-start = (bf16[2048,256]{1,0:T(8,128)(2,1)}, bf16[2048,256]{1,0:T(8,128)(2,1)S(1)}, u32[]{:S(2)}, u32[]{:S(2)}) collective-permute-start(bf16[2048,256]{1,0:T(8,128)(2,1)} %param.8), channel_id=1, source_target_pairs={{0,16},{16,0},{1,17},{17,1},{2,18},{18,2},{3,19},{19,3},{4,20},{20... | collective-permute-start | bytes 3145736 | tf_op jit(solution)/shard_map/ppermute | solution.py:20
  37.0 2.6 %copy-start.1 = (bf16[2048,256]{1,0:T(8,128)(2,1)S(1)}, bf16[2048,256]{1,0:T(8,128)(2,1)}, u32[]{:S(2)}) copy-start(bf16[2048,256]{1,0:T(8,128)(2,1)} %get-tuple-element.22) | copy-start | bytes 3145732
  40.5 10.6 %collective-permute-start.1 = (f32[24,2,8,256]{3,2,1,0:T(8,128)S(1)}, f32[24,2,8,256]{3,2,1,0:T(8,128)S(1)}, u32[]{:S(2)}, u32[]{:S(2)}) collective-permute-start(f32[24,2,8,256]{3,2,1,0:T(8,128)S(1)} %fusion), channel_id=1, source_target_pairs={{0,2},{2,4},{4,6},{6,7},{7,5},{5,3},{3,1},{1,0},{8,10},{10,12},{12... | collective-permute-start | bytes 1179656 | tf_op jit(solution)/shard_map/ppermute | solution.py:72
  43.1 10.3 %collective-permute-start.8 = (f32[24,2,8,256]{3,2,1,0:T(8,128)S(1)}, f32[24,2,8,256]{3,2,1,0:T(8,128)S(1)}, u32[]{:S(2)}, u32[]{:S(2)}) collective-permute-start(f32[24,2,8,256]{3,2,1,0:T(8,128)S(1)} %fusion.8), channel_id=1, source_target_pairs={{2,0},{4,2},{6,4},{7,6},{5,7},{3,5},{1,3},{0,1},{10,8},{12,10},{14... | collective-permute-start | bytes 1179656 | tf_op jit(solution)/shard_map/ppermute | solution.py:73
  51.2 9.7 %collective-permute-start.2 = (f32[24,2,8,256]{3,2,1,0:T(8,128)S(1)}, f32[24,2,8,256]{3,2,1,0:T(8,128)S(1)}, u32[]{:S(2)}, u32[]{:S(2)}) collective-permute-start(f32[24,2,8,256]{3,2,1,0:T(8,128)S(1)} %add.406), channel_id=1, source_target_pairs={{0,2},{2,4},{4,6},{6,7},{7,5},{5,3},{3,1},{1,0},{8,10},{10,12},{12... | collective-permute-start | bytes 1179656 | tf_op jit(solution)/shard_map/ppermute | solution.py:72
  53.5 9.4 %collective-permute-start.9 = (f32[24,2,8,256]{3,2,1,0:T(8,128)S(1)}, f32[24,2,8,256]{3,2,1,0:T(8,128)S(1)}, u32[]{:S(2)}, u32[]{:S(2)}) collective-permute-start(f32[24,2,8,256]{3,2,1,0:T(8,128)S(1)} %add.459), channel_id=1, source_target_pairs={{2,0},{4,2},{6,4},{7,6},{5,7},{3,5},{1,3},{0,1},{10,8},{12,10},{14... | collective-permute-start | bytes 1179656 | tf_op jit(solution)/shard_map/ppermute | solution.py:73
  61.0 9.2 %collective-permute-start.3 = (f32[24,2,8,256]{3,2,1,0:T(8,128)S(1)}, f32[24,2,8,256]{3,2,1,0:T(8,128)S(1)}, u32[]{:S(2)}, u32[]{:S(2)}) collective-permute-start(f32[24,2,8,256]{3,2,1,0:T(8,128)S(1)} %add.412), channel_id=1, source_target_pairs={{0,2},{2,4},{4,6},{6,7},{7,5},{5,3},{3,1},{1,0},{8,10},{10,12},{12... | collective-permute-start | bytes 1179656 | tf_op jit(solution)/shard_map/ppermute | solution.py:72
  63.0 9.0 %collective-permute-start.10 = (f32[24,2,8,256]{3,2,1,0:T(8,128)S(1)}, f32[24,2,8,256]{3,2,1,0:T(8,128)S(1)}, u32[]{:S(2)}, u32[]{:S(2)}) collective-permute-start(f32[24,2,8,256]{3,2,1,0:T(8,128)S(1)} %add.468), channel_id=1, source_target_pairs={{2,0},{4,2},{6,4},{7,6},{5,7},{3,5},{1,3},{0,1},{10,8},{12,10},{14... | collective-permute-start | bytes 1179656 | tf_op jit(solution)/shard_map/ppermute | solution.py:73
  70.3 9.2 %collective-permute-start.4 = (f32[24,2,8,256]{3,2,1,0:T(8,128)S(1)}, f32[24,2,8,256]{3,2,1,0:T(8,128)S(1)}, u32[]{:S(2)}, u32[]{:S(2)}) collective-permute-start(f32[24,2,8,256]{3,2,1,0:T(8,128)S(1)} %add.418), channel_id=1, source_target_pairs={{0,2},{2,4},{4,6},{6,7},{7,5},{5,3},{3,1},{1,0},{8,10},{10,12},{12... | collective-permute-start | bytes 1179656 | tf_op jit(solution)/shard_map/ppermute | solution.py:72
  72.1 9.5 %collective-permute-start.11 = (f32[24,2,8,256]{3,2,1,0:T(8,128)S(1)}, f32[24,2,8,256]{3,2,1,0:T(8,128)S(1)}, u32[]{:S(2)}, u32[]{:S(2)}) collective-permute-start(f32[24,2,8,256]{3,2,1,0:T(8,128)S(1)} %add.477), channel_id=1, source_target_pairs={{2,0},{4,2},{6,4},{7,6},{5,7},{3,5},{1,3},{0,1},{10,8},{12,10},{14... | collective-permute-start | bytes 1179656 | tf_op jit(solution)/shard_map/ppermute | solution.py:73
  79.5 10.2 %collective-permute-start.5 = (f32[24,2,8,256]{3,2,1,0:T(8,128)S(1)}, f32[24,2,8,256]{3,2,1,0:T(8,128)S(1)}, u32[]{:S(2)}, u32[]{:S(2)}) collective-permute-start(f32[24,2,8,256]{3,2,1,0:T(8,128)S(1)} %add.424), channel_id=1, source_target_pairs={{0,2},{2,4},{4,6},{6,7},{7,5},{5,3},{3,1},{1,0},{8,10},{10,12},{12... | collective-permute-start | bytes 1179656 | tf_op jit(solution)/shard_map/ppermute | solution.py:72
  81.7 10.1 %collective-permute-start.12 = (f32[24,2,8,256]{3,2,1,0:T(8,128)S(1)}, f32[24,2,8,256]{3,2,1,0:T(8,128)S(1)}, u32[]{:S(2)}, u32[]{:S(2)}) collective-permute-start(f32[24,2,8,256]{3,2,1,0:T(8,128)S(1)} %add.486), channel_id=1, source_target_pairs={{2,0},{4,2},{6,4},{7,6},{5,7},{3,5},{1,3},{0,1},{10,8},{12,10},{14... | collective-permute-start | bytes 1179656 | tf_op jit(solution)/shard_map/ppermute | solution.py:73
  89.8 11.0 %collective-permute-start.6 = (f32[24,2,8,256]{3,2,1,0:T(8,128)S(1)}, f32[24,2,8,256]{3,2,1,0:T(8,128)S(1)}, u32[]{:S(2)}, u32[]{:S(2)}) collective-permute-start(f32[24,2,8,256]{3,2,1,0:T(8,128)S(1)} %add.430), channel_id=1, source_target_pairs={{0,2},{2,4},{4,6},{6,7},{7,5},{5,3},{3,1},{1,0},{8,10},{10,12},{12... | collective-permute-start | bytes 1179656 | tf_op jit(solution)/shard_map/ppermute | solution.py:72
  91.9 11.0 %collective-permute-start.13 = (f32[24,2,8,256]{3,2,1,0:T(8,128)S(1)}, f32[24,2,8,256]{3,2,1,0:T(8,128)S(1)}, u32[]{:S(2)}, u32[]{:S(2)}) collective-permute-start(f32[24,2,8,256]{3,2,1,0:T(8,128)S(1)} %add.495), channel_id=1, source_target_pairs={{2,0},{4,2},{6,4},{7,6},{5,7},{3,5},{1,3},{0,1},{10,8},{12,10},{14... | collective-permute-start | bytes 1179656 | tf_op jit(solution)/shard_map/ppermute | solution.py:73
  100.9 7.8 %collective-permute-start.7 = (f32[24,2,8,256]{3,2,1,0:T(8,128)S(1)}, f32[24,2,8,256]{3,2,1,0:T(8,128)S(1)}, u32[]{:S(2)}, u32[]{:S(2)}) collective-permute-start(f32[24,2,8,256]{3,2,1,0:T(8,128)S(1)} %add.436), channel_id=1, source_target_pairs={{0,2},{2,4},{4,6},{6,7},{7,5},{5,3},{3,1},{1,0},{8,10},{10,12},{12... | collective-permute-start | bytes 1179656 | tf_op jit(solution)/shard_map/ppermute | solution.py:72
  102.9 7.8 %collective-permute-start.14 = (f32[24,2,8,256]{3,2,1,0:T(8,128)S(1)}, f32[24,2,8,256]{3,2,1,0:T(8,128)S(1)}, u32[]{:S(2)}, u32[]{:S(2)}) collective-permute-start(f32[24,2,8,256]{3,2,1,0:T(8,128)S(1)} %add.504), channel_id=1, source_target_pairs={{2,0},{4,2},{6,4},{7,6},{5,7},{3,5},{1,3},{0,1},{10,8},{12,10},{14... | collective-permute-start | bytes 1179656 | tf_op jit(solution)/shard_map/ppermute | solution.py:73
Sparse Core Ops, SparseCore 0:
  8.9 14.8 all-gather.1

commit v6 on v2

--- a/solution.py
+++ b/solution.py
@@ -42,7 +42,13 @@
     def per_device(receivers, excitations, mode_freqs, mode_damping, sample_freqs):
         mode = lax.axis_index("mode")
         receiver_block = gather_blocks(receivers, "evt", sizes["evt"], 1)
-        source_block = gather_blocks(excitations, "sta", sizes["sta"], 0)
+        width = excitations.shape[1] // 2
+        first_source = gather_blocks(excitations[:, :width], "sta", sizes["sta"], 0)
+        second_local, _ = lax.optimization_barrier((excitations[:, width:], first_source))
+        if sizes["sta"] == 2:
+            second_far = swap_pair(second_local, "sta")
+        else:
+            second_far = lax.all_gather(second_local, "sta", axis=0, tiled=True)
         row_count, block_modes = receiver_block.shape
         real_weight, imag_weight = resonance(
             mode_freqs[None, :], mode_damping[None, :], sample_freqs[:, None]
@@ -53,7 +59,7 @@
         order_table = jnp.asarray(order, dtype=jnp.int32)
         position = jnp.asarray(position_of, dtype=jnp.int32)[mode]
 
-        def partial_rows(owner, part):
+        def partial_rows(owner, part, source_block, receiver_block=receiver_block):
             start = owner * chunk + part * half
             rows = lax.dynamic_slice_in_dim(receiver_block, start, half, axis=0)
             widened = rows.astype(jnp.float32)
@@ -66,14 +72,46 @@
         def owner_at(offset):
             return order_table[(position + offset) % mode_count]
 
-        ahead = partial_rows(owner_at(-1), 0)
-        behind = partial_rows(owner_at(1), 1)
-        for step in range(mode_count - 1):
-            ahead = lax.ppermute(ahead, "mode", clockwise)
-            behind = lax.ppermute(behind, "mode", counter)
-            ahead = ahead + partial_rows(owner_at(-step - 2), 0)
-            behind = behind + partial_rows(owner_at(step + 2), 1)
-        return jnp.concatenate([ahead, behind], axis=0)
+        def start(source, held=receiver_block):
+            return (
+                partial_rows(owner_at(-1), 0, source, held),
+                partial_rows(owner_at(1), 1, source, held),
+            )
+
+        def ring_step(step, sums, source):
+            held, gated, sent_ahead, sent_behind = lax.optimization_barrier(
+                (receiver_block, source, sums[0], sums[1])
+            )
+            ahead = lax.ppermute(sent_ahead, "mode", clockwise)
+            behind = lax.ppermute(sent_behind, "mode", counter)
+            return (
+                ahead + partial_rows(owner_at(-step - 2), 0, gated, held),
+                behind + partial_rows(owner_at(step + 2), 1, gated, held),
+            )
+
+        steps = mode_count - 1
+        first = ring_step(0, start(first_source), first_source)
+        held, second_far, _, _ = lax.optimization_barrier(
+            (receiver_block, second_far, first[0], first[1])
+        )
+        if sizes["sta"] == 2:
+            index = lax.axis_index("sta")
+            second_source = jnp.concatenate(
+                [
+                    jnp.where(index == 0, second_local, second_far),
+                    jnp.where(index == 0, second_far, second_local),
+                ],
+                axis=0,
+            )
+        else:
+            second_source = second_far
+        second = start(second_source, held)
+        for step in range(1, steps):
+            first = ring_step(step, first, first_source)
+            second = ring_step(step - 1, second, second_source)
+        second = ring_step(steps - 1, second, second_source)
+        rows = [jnp.concatenate(parts, axis=3) for parts in zip(first, second)]
+        return jnp.concatenate(rows, axis=0)
 
     return per_device
 

time: 104 us -> 112 us (1.077)
  waiting for transfers between devices: 39.3 us -> 15.4 us
  matrix products: 15.6 us -> 31.2 us
  starting transfers between devices: 18.4 us -> 31.8 us
  other arithmetic: 5.67 us -> 7.48 us
    ppermute x14 -> x28, waiting for transfers between devices: 39.3 us -> 15.4 us  [the longest x14 8.59 us: ring_step(): behind = lax.ppermute(sent_behind, 'mode', counter)]
    dot_general x16 -> x32, matrix products: 15.6 us -> 31.2 us  [partial_rows(): jnp.dot(weighted.reshape(-1, block_modes), source_block, preferred_elemen...]
    ppermute x14 -> x28, starting transfers between devices: 15.4 us -> 28.6 us  [the longest x14 21.4 us: ring_step(): behind = lax.ppermute(sent_behind, 'mode', counter)]
    ppermute x2 -> x3, starting transfers between devices: 3.03 us -> 3.21 us  [swap_pair(): return lax.ppermute(local, axis_name, [(0, 1), (1, 0)])]
  transfers between devices with their start and end apart: 16 -> 31, of which waited for: 14 -> 12; matrix products, arithmetic and copies ran while one was open for 21% -> 38% of each run, Pallas kernels for 0% -> 0%
where the time goes in v6:
time: 112 us
  starting transfers between devices  31.8 us (28%)
  matrix products  31.2 us (28%)
  between operations  21.4 us (19%)
  waiting for transfers between devices  15.4 us (14%)
  other arithmetic  7.48 us (7%)
  local copies, waits for them, and re-layouts  4.35 us (4%)
    dot_general x32, matrix products, partial_rows(): jnp.dot(weighted.reshape(-1, block_modes), source_block, preferred_elemen...  31.2 us
    ppermute x14, starting transfers between devices, ring_step(): behind = lax.ppermute(sent_behind, 'mode', counter)  21.4 us
    ppermute x14, waiting for transfers between devices, ring_step(): behind = lax.ppermute(sent_behind, 'mode', counter)  8.59 us
    ppermute x14, starting transfers between devices, ring_step(): ahead = lax.ppermute(sent_ahead, 'mode', clockwise)  7.23 us
    ppermute x14, waiting for transfers between devices, ring_step(): ahead = lax.ppermute(sent_ahead, 'mode', clockwise)  6.78 us
    ppermute x3, starting transfers between devices, swap_pair(): return lax.ppermute(local, axis_name, [(0, 1), (1, 0)])  3.21 us
    select_n x2, other arithmetic, gather_blocks(): first = jnp.where(index == 0, local, other)  2.77 us
  transfers between devices with their start and end apart: 31, of which 12 were waited for; matrix products, arithmetic and copies ran while one was open for 38% of the time, Pallas kernels for 0%

profile of v6, /device:TPU:0, one launch (start us, length us, event | category | flops | bytes accessed | tf_op | source)
XLA Modules:
  0.0 111.6 jit_solution(991934322370342290)
XLA Ops:
  0.5 1.1 slice.6
  1.5 2.7 %collective-permute-start.1 = (bf16[2048,128]{1,0:T(8,128)(2,1)S(1)}, bf16[2048,128]{1,0:T(8,128)(2,1)}, u32[]{:S(2)}, u32[]{:S(2)}) collective-permute-start(bf16[2048,128]{1,0:T(8,128)(2,1)S(1)} %slice.6), channel_id=1, source_target_pairs={{0,16},{16,0},{1,17},{17,1},{2,18},{18,2},{3,19},{19,3},{4,20},{20... | collective-permute-start | bytes 1572872 | tf_op jit(solution)/shard_map/ppermute | solution.py:20
  5.9 1.2 %dynamic_slice.163 = s32[1]{0:T(128)} dynamic-slice(s32[8]{0:T(128)} %constant.218.clone, s32[]{:T(128)S(6)} %select_n.268), dynamic_slice_sizes={1} | dynamic-slice | bytes 12 | tf_op jit(solution)/shard_map/dynamic_slice | solution.py:60
  17.9 2.0 %fusion.139 = (s32[1]{0:T(128)}, s32[1]{0:T(128)}, s32[1]{0:T(128)}, s32[1]{0:T(128)}, s32[1]{0:T(128)}, /*index=5*/s32[1]{0:T(128)}, s32[1]{0:T(128)}, s32[1]{0...) fusion(s32[8]{0:T(128)} %constant.217.clone, ...), kind=kLoop, calls=%fused_computation.218 | loop fusion | bytes 192 | tf_op jit(solution)/shard_map/dynamic_slice | solution.py:73
  29.8 1.1 %broadcast_select_fusion.5 = (bf16[2048,128]{1,0:T(8,128)(2,1)S(1)}, bf16[2048,128]{1,0:T(8,128)(2,1)S(1)}, bf16[2048,128]{1,0:T(8,128)(2,1)S(1)}) fusion(bf16[2048,128]{1,0:T(8,128)(2,1)} %collective-permute-done.1, pred[]{:T(512)S(6)} %eq.44, bf16[2048,256]{1,0:T(8,128)(2,1)S(1)} %copy-done), kind=kLoop, calls=%fused_computation.177 | loop fusion | flops 524288 | bytes 3145729 | tf_op jit(solution)/shard_map/jit(_where)/select_n | solution.py:28
  31.2 1.6 %broadcast_select_fusion.1 = (bf16[384,2048]{1,0:T(8,128)(2,1)S(1)}, bf16[384,2048]{1,0:T(8,128)(2,1)S(1)}) fusion(bf16[384,2048]{1,0:T(8,128)(2,1)S(1)} %copy-done.1, bf16[384,2048]{1,0:T(8,128)(2,1)} %collective-permute-done, pred[]{:T(512)S(6)} %eq.43), kind=kLoop, calls=%fused_computation.134 | loop fusion | flops 1572864 | bytes 6291457 | tf_op jit(solution)/shard_map/jit(_where)/select_n | solution.py:28
  33.2 1.0 fusion.1
  34.2 1.0 fusion
  35.2 2.0 %collective-permute-start.3 = (f32[24,2,8,128]{3,2,1,0:T(8,128)S(1)}, f32[24,2,8,128]{3,2,1,0:T(8,128)S(1)}, u32[]{:S(2)}, u32[]{:S(2)}) collective-permute-start(f32[24,2,8,128]{3,2,1,0:T(8,128)S(1)} %fusion.1), channel_id=1, source_target_pairs={{2,0},{4,2},{6,4},{7,6},{5,7},{3,5},{1,3},{0,1},{10,8},{12,10},{14... | collective-permute-start | bytes 589832 | tf_op jit(solution)/shard_map/ppermute | solution.py:86
  37.4 4.8 %collective-permute-done.3 = f32[24,2,8,128]{3,2,1,0:T(8,128)S(1)} collective-permute-done((f32[24,2,8,128]{3,2,1,0:T(8,128)S(1)}, f32[24,2,8,128]{3,2,1,0:T(8,128)S(1)}, u32[]{:S(2)}, u32[]{:S(2)}) %collective-permute-start.3) | collective-permute-done | bytes 196640 | tf_op jit(solution)/shard_map/ppermute | solution.py:86
  42.2 1.0 fusion.98
  43.6 1.0 fusion.99
  44.6 1.6 %collective-permute-start.5 = (f32[24,2,8,128]{3,2,1,0:T(8,128)S(1)}, f32[24,2,8,128]{3,2,1,0:T(8,128)S(1)}, u32[]{:S(2)}, u32[]{:S(2)}) collective-permute-start(f32[24,2,8,128]{3,2,1,0:T(8,128)S(1)} %fusion.98), channel_id=1, source_target_pairs={{2,0},{4,2},{6,4},{7,6},{5,7},{3,5},{1,3},{0,1},{10,8},{12,10},{14... | collective-permute-start | bytes 589832 | tf_op jit(solution)/shard_map/ppermute | solution.py:86
  46.9 1.0 fusion.16
  47.9 1.0 fusion.15
  48.9 1.6 %collective-permute-start.17 = (f32[24,2,8,128]{3,2,1,0:T(8,128)S(1)}, f32[24,2,8,128]{3,2,1,0:T(8,128)S(1)}, u32[]{:S(2)}, u32[]{:S(2)}) collective-permute-start(f32[24,2,8,128]{3,2,1,0:T(8,128)S(1)} %fusion.16), channel_id=1, source_target_pairs={{2,0},{4,2},{6,4},{7,6},{5,7},{3,5},{1,3},{0,1},{10,8},{12,10},{14... | collective-permute-start | bytes 589832 | tf_op jit(solution)/shard_map/ppermute | solution.py:86
  53.1 1.6 %collective-permute-start.7 = (f32[24,2,8,128]{3,2,1,0:T(8,128)S(1)}, f32[24,2,8,128]{3,2,1,0:T(8,128)S(1)}, u32[]{:S(2)}, u32[]{:S(2)}) collective-permute-start(f32[24,2,8,128]{3,2,1,0:T(8,128)S(1)} %add.552), channel_id=1, source_target_pairs={{2,0},{4,2},{6,4},{7,6},{5,7},{3,5},{1,3},{0,1},{10,8},{12,10},{14... | collective-permute-start | bytes 589832 | tf_op jit(solution)/shard_map/ppermute | solution.py:86
  56.3 1.0 fusion.96
  58.2 1.0 fusion.97
  59.3 1.6 %collective-permute-start.19 = (f32[24,2,8,128]{3,2,1,0:T(8,128)S(1)}, f32[24,2,8,128]{3,2,1,0:T(8,128)S(1)}, u32[]{:S(2)}, u32[]{:S(2)}) collective-permute-start(f32[24,2,8,128]{3,2,1,0:T(8,128)S(1)} %fusion.96), channel_id=1, source_target_pairs={{2,0},{4,2},{6,4},{7,6},{5,7},{3,5},{1,3},{0,1},{10,8},{12,10},{14... | collective-permute-start | bytes 589832 | tf_op jit(solution)/shard_map/ppermute | solution.py:86
  63.4 1.6 %collective-permute-start.9 = (f32[24,2,8,128]{3,2,1,0:T(8,128)S(1)}, f32[24,2,8,128]{3,2,1,0:T(8,128)S(1)}, u32[]{:S(2)}, u32[]{:S(2)}) collective-permute-start(f32[24,2,8,128]{3,2,1,0:T(8,128)S(1)} %add.567), channel_id=1, source_target_pairs={{2,0},{4,2},{6,4},{7,6},{5,7},{3,5},{1,3},{0,1},{10,8},{12,10},{14... | collective-permute-start | bytes 589832 | tf_op jit(solution)/shard_map/ppermute | solution.py:86
  68.6 1.6 %collective-permute-start.21 = (f32[24,2,8,128]{3,2,1,0:T(8,128)S(1)}, f32[24,2,8,128]{3,2,1,0:T(8,128)S(1)}, u32[]{:S(2)}, u32[]{:S(2)}) collective-permute-start(f32[24,2,8,128]{3,2,1,0:T(8,128)S(1)} %add.622), channel_id=1, source_target_pairs={{2,0},{4,2},{6,4},{7,6},{5,7},{3,5},{1,3},{0,1},{10,8},{12,10},{14... | collective-permute-start | bytes 589832 | tf_op jit(solution)/shard_map/ppermute | solution.py:86
  72.9 1.6 %collective-permute-start.11 = (f32[24,2,8,128]{3,2,1,0:T(8,128)S(1)}, f32[24,2,8,128]{3,2,1,0:T(8,128)S(1)}, u32[]{:S(2)}, u32[]{:S(2)}) collective-permute-start(f32[24,2,8,128]{3,2,1,0:T(8,128)S(1)} %add.582), channel_id=1, source_target_pairs={{2,0},{4,2},{6,4},{7,6},{5,7},{3,5},{1,3},{0,1},{10,8},{12,10},{14... | collective-permute-start | bytes 589832 | tf_op jit(solution)/shard_map/ppermute | solution.py:86
  77.2 1.6 %collective-permute-start.23 = (f32[24,2,8,128]{3,2,1,0:T(8,128)S(1)}, f32[24,2,8,128]{3,2,1,0:T(8,128)S(1)}, u32[]{:S(2)}, u32[]{:S(2)}) collective-permute-start(f32[24,2,8,128]{3,2,1,0:T(8,128)S(1)} %add.624), channel_id=1, source_target_pairs={{2,0},{4,2},{6,4},{7,6},{5,7},{3,5},{1,3},{0,1},{10,8},{12,10},{14... | collective-permute-start | bytes 589832 | tf_op jit(solution)/shard_map/ppermute | solution.py:86
  82.0 1.5 %collective-permute-start.13 = (f32[24,2,8,128]{3,2,1,0:T(8,128)S(1)}, f32[24,2,8,128]{3,2,1,0:T(8,128)S(1)}, u32[]{:S(2)}, u32[]{:S(2)}) collective-permute-start(f32[24,2,8,128]{3,2,1,0:T(8,128)S(1)} %add.597), channel_id=1, source_target_pairs={{2,0},{4,2},{6,4},{7,6},{5,7},{3,5},{1,3},{0,1},{10,8},{12,10},{14... | collective-permute-start | bytes 589832 | tf_op jit(solution)/shard_map/ppermute | solution.py:86
  86.6 1.2 %collective-permute-start.25 = (f32[24,2,8,128]{3,2,1,0:T(8,128)S(1)}, f32[24,2,8,128]{3,2,1,0:T(8,128)S(1)}, u32[]{:S(2)}, u32[]{:S(2)}) collective-permute-start(f32[24,2,8,128]{3,2,1,0:T(8,128)S(1)} %add.626), channel_id=1, source_target_pairs={{2,0},{4,2},{6,4},{7,6},{5,7},{3,5},{1,3},{0,1},{10,8},{12,10},{14... | collective-permute-start | bytes 589832 | tf_op jit(solution)/shard_map/ppermute | solution.py:86
  91.6 2.9 %collective-permute-done.25 = f32[24,2,8,128]{3,2,1,0:T(8,128)S(1)} collective-permute-done((f32[24,2,8,128]{3,2,1,0:T(8,128)S(1)}, f32[24,2,8,128]{3,2,1,0:T(8,128)S(1)}, u32[]{:S(2)}, u32[]{:S(2)}) %collective-permute-start.25) | collective-permute-done | bytes 196640 | tf_op jit(solution)/shard_map/ppermute | solution.py:86
  94.6 1.0 collective-permute-start.27
  97.6 1.1 collective-permute-start.26
  101.7 2.7 %collective-permute-done.26 = f32[24,2,8,128]{3,2,1,0:T(8,128)S(1)} collective-permute-done((f32[24,2,8,128]{3,2,1,0:T(8,128)S(1)}, f32[24,2,8,128]{3,2,1,0:T(8,128)S(1)}, u32[]{:S(2)}, u32[]{:S(2)}) %collective-permute-start.26) | collective-permute-done | bytes 196640 | tf_op jit(solution)/shard_map/ppermute | solution.py:85
  105.0 1.8 %collective-permute-start.30 = (f32[24,2,8,128]{3,2,1,0:T(8,128)S(1)}, f32[24,2,8,128]{3,2,1,0:T(8,128)S(1)}, u32[]{:S(2)}, u32[]{:S(2)}) collective-permute-start(f32[24,2,8,128]{3,2,1,0:T(8,128)S(1)} %add.630), channel_id=1, source_target_pairs={{2,0},{4,2},{6,4},{7,6},{5,7},{3,5},{1,3},{0,1},{10,8},{12,10},{14... | collective-permute-start | bytes 589832 | tf_op jit(solution)/shard_map/ppermute | solution.py:86
  108.8 1.5 %collective-permute-done.28 = f32[24,2,8,128]{3,2,1,0:T(8,128)S(1)} collective-permute-done((f32[24,2,8,128]{3,2,1,0:T(8,128)S(1)}, f32[24,2,8,128]{3,2,1,0:T(8,128)S(1)}, u32[]{:S(2)}, u32[]{:S(2)}) %collective-permute-start.28) | collective-permute-done | bytes 196640 | tf_op jit(solution)/shard_map/ppermute | solution.py:85
  (119 shorter events, 39.2 us)
Async XLA Ops:
  0.0 29.8 %copy-start = (bf16[2048,256]{1,0:T(8,128)(2,1)S(1)}, bf16[2048,256]{1,0:T(8,128)(2,1)}, u32[]{:S(2)}) copy-start(bf16[2048,256]{1,0:T(8,128)(2,1)} %param.8) | copy-start | bytes 3145732
  0.0 31.2 %collective-permute-start = (bf16[384,2048]{1,0:T(8,128)(2,1)}, bf16[384,2048]{1,0:T(8,128)(2,1)}, u32[]{:S(2)}, u32[]{:S(2)}) collective-permute-start(bf16[384,2048]{1,0:T(8,128)(2,1)} %param.7), channel_id=1, source_target_pairs={{0,8},{8,0},{1,9},{9,1},{2,10},{10,2},{3,11},{11,3},{4,12},{12,4},... | collective-permute-start | bytes 4718600 | tf_op jit(solution)/shard_map/ppermute | solution.py:20
  1.5 28.3 %collective-permute-start.1 = (bf16[2048,128]{1,0:T(8,128)(2,1)S(1)}, bf16[2048,128]{1,0:T(8,128)(2,1)}, u32[]{:S(2)}, u32[]{:S(2)}) collective-permute-start(bf16[2048,128]{1,0:T(8,128)(2,1)S(1)} %slice.6), channel_id=1, source_target_pairs={{0,16},{16,0},{1,17},{17,1},{2,18},{18,2},{3,19},{19,3},{4,20},{20... | collective-permute-start | bytes 1572872 | tf_op jit(solution)/shard_map/ppermute | solution.py:20
  31.1 15.6 %collective-permute-start.15 = (bf16[2048,128]{1,0:T(8,128)(2,1)S(1)}, bf16[2048,128]{1,0:T(8,128)(2,1)S(1)}, u32[]{:S(2)}, u32[]{:S(2)}) collective-permute-start(bf16[2048,128]{1,0:T(8,128)(2,1)S(1)} %get-tuple-element.91), channel_id=1, source_target_pairs={{0,16},{16,0},{1,17},{17,1},{2,18},{18,2},{3,19},{19,3},{4,20},{20... | collective-permute-start | bytes 1572872 | tf_op jit(solution)/shard_map/ppermute | solution.py:20
  35.2 7.0 %collective-permute-start.3 = (f32[24,2,8,128]{3,2,1,0:T(8,128)S(1)}, f32[24,2,8,128]{3,2,1,0:T(8,128)S(1)}, u32[]{:S(2)}, u32[]{:S(2)}) collective-permute-start(f32[24,2,8,128]{3,2,1,0:T(8,128)S(1)} %fusion.1), channel_id=1, source_target_pairs={{2,0},{4,2},{6,4},{7,6},{5,7},{3,5},{1,3},{0,1},{10,8},{12,10},{14... | collective-permute-start | bytes 589832 | tf_op jit(solution)/shard_map/ppermute | solution.py:86
  37.2 6.4 %collective-permute-start.2 = (f32[24,2,8,128]{3,2,1,0:T(8,128)S(1)}, f32[24,2,8,128]{3,2,1,0:T(8,128)S(1)}, u32[]{:S(2)}, u32[]{:S(2)}) collective-permute-start(f32[24,2,8,128]{3,2,1,0:T(8,128)S(1)} %fusion), channel_id=1, source_target_pairs={{0,2},{2,4},{4,6},{6,7},{7,5},{5,3},{3,1},{1,0},{8,10},{10,12},{12... | collective-permute-start | bytes 589832 | tf_op jit(solution)/shard_map/ppermute | solution.py:85
  44.6 8.4 %collective-permute-start.5 = (f32[24,2,8,128]{3,2,1,0:T(8,128)S(1)}, f32[24,2,8,128]{3,2,1,0:T(8,128)S(1)}, u32[]{:S(2)}, u32[]{:S(2)}) collective-permute-start(f32[24,2,8,128]{3,2,1,0:T(8,128)S(1)} %fusion.98), channel_id=1, source_target_pairs={{2,0},{4,2},{6,4},{7,6},{5,7},{3,5},{1,3},{0,1},{10,8},{12,10},{14... | collective-permute-start | bytes 589832 | tf_op jit(solution)/shard_map/ppermute | solution.py:86
  46.2 6.9 %collective-permute-start.4 = (f32[24,2,8,128]{3,2,1,0:T(8,128)S(1)}, f32[24,2,8,128]{3,2,1,0:T(8,128)S(1)}, u32[]{:S(2)}, u32[]{:S(2)}) collective-permute-start(f32[24,2,8,128]{3,2,1,0:T(8,128)S(1)} %fusion.99), channel_id=1, source_target_pairs={{0,2},{2,4},{4,6},{6,7},{7,5},{5,3},{3,1},{1,0},{8,10},{10,12},{12... | collective-permute-start | bytes 589832 | tf_op jit(solution)/shard_map/ppermute | solution.py:85
  48.9 7.3 %collective-permute-start.17 = (f32[24,2,8,128]{3,2,1,0:T(8,128)S(1)}, f32[24,2,8,128]{3,2,1,0:T(8,128)S(1)}, u32[]{:S(2)}, u32[]{:S(2)}) collective-permute-start(f32[24,2,8,128]{3,2,1,0:T(8,128)S(1)} %fusion.16), channel_id=1, source_target_pairs={{2,0},{4,2},{6,4},{7,6},{5,7},{3,5},{1,3},{0,1},{10,8},{12,10},{14... | collective-permute-start | bytes 589832 | tf_op jit(solution)/shard_map/ppermute | solution.py:86
  50.6 7.7 %collective-permute-start.16 = (f32[24,2,8,128]{3,2,1,0:T(8,128)S(1)}, f32[24,2,8,128]{3,2,1,0:T(8,128)S(1)}, u32[]{:S(2)}, u32[]{:S(2)}) collective-permute-start(f32[24,2,8,128]{3,2,1,0:T(8,128)S(1)} %fusion.15), channel_id=1, source_target_pairs={{0,2},{2,4},{4,6},{6,7},{7,5},{5,3},{3,1},{1,0},{8,10},{10,12},{12... | collective-permute-start | bytes 589832 | tf_op jit(solution)/shard_map/ppermute | solution.py:85
  53.1 10.2 %collective-permute-start.7 = (f32[24,2,8,128]{3,2,1,0:T(8,128)S(1)}, f32[24,2,8,128]{3,2,1,0:T(8,128)S(1)}, u32[]{:S(2)}, u32[]{:S(2)}) collective-permute-start(f32[24,2,8,128]{3,2,1,0:T(8,128)S(1)} %add.552), channel_id=1, source_target_pairs={{2,0},{4,2},{6,4},{7,6},{5,7},{3,5},{1,3},{0,1},{10,8},{12,10},{14... | collective-permute-start | bytes 589832 | tf_op jit(solution)/shard_map/ppermute | solution.py:86
  54.7 8.6 %collective-permute-start.6 = (f32[24,2,8,128]{3,2,1,0:T(8,128)S(1)}, f32[24,2,8,128]{3,2,1,0:T(8,128)S(1)}, u32[]{:S(2)}, u32[]{:S(2)}) collective-permute-start(f32[24,2,8,128]{3,2,1,0:T(8,128)S(1)} %add.543), channel_id=1, source_target_pairs={{0,2},{2,4},{4,6},{6,7},{7,5},{5,3},{3,1},{1,0},{8,10},{10,12},{12... | collective-permute-start | bytes 589832 | tf_op jit(solution)/shard_map/ppermute | solution.py:85
  59.3 7.8 %collective-permute-start.19 = (f32[24,2,8,128]{3,2,1,0:T(8,128)S(1)}, f32[24,2,8,128]{3,2,1,0:T(8,128)S(1)}, u32[]{:S(2)}, u32[]{:S(2)}) collective-permute-start(f32[24,2,8,128]{3,2,1,0:T(8,128)S(1)} %fusion.96), channel_id=1, source_target_pairs={{2,0},{4,2},{6,4},{7,6},{5,7},{3,5},{1,3},{0,1},{10,8},{12,10},{14... | collective-permute-start | bytes 589832 | tf_op jit(solution)/shard_map/ppermute | solution.py:86
  60.9 7.6 %collective-permute-start.18 = (f32[24,2,8,128]{3,2,1,0:T(8,128)S(1)}, f32[24,2,8,128]{3,2,1,0:T(8,128)S(1)}, u32[]{:S(2)}, u32[]{:S(2)}) collective-permute-start(f32[24,2,8,128]{3,2,1,0:T(8,128)S(1)} %fusion.97), channel_id=1, source_target_pairs={{0,2},{2,4},{4,6},{6,7},{7,5},{5,3},{3,1},{1,0},{8,10},{10,12},{12... | collective-permute-start | bytes 589832 | tf_op jit(solution)/shard_map/ppermute | solution.py:85
  63.4 9.2 %collective-permute-start.9 = (f32[24,2,8,128]{3,2,1,0:T(8,128)S(1)}, f32[24,2,8,128]{3,2,1,0:T(8,128)S(1)}, u32[]{:S(2)}, u32[]{:S(2)}) collective-permute-start(f32[24,2,8,128]{3,2,1,0:T(8,128)S(1)} %add.567), channel_id=1, source_target_pairs={{2,0},{4,2},{6,4},{7,6},{5,7},{3,5},{1,3},{0,1},{10,8},{12,10},{14... | collective-permute-start | bytes 589832 | tf_op jit(solution)/shard_map/ppermute | solution.py:86
  65.0 7.8 %collective-permute-start.8 = (f32[24,2,8,128]{3,2,1,0:T(8,128)S(1)}, f32[24,2,8,128]{3,2,1,0:T(8,128)S(1)}, u32[]{:S(2)}, u32[]{:S(2)}) collective-permute-start(f32[24,2,8,128]{3,2,1,0:T(8,128)S(1)} %add.558), channel_id=1, source_target_pairs={{0,2},{2,4},{4,6},{6,7},{7,5},{5,3},{3,1},{1,0},{8,10},{10,12},{12... | collective-permute-start | bytes 589832 | tf_op jit(solution)/shard_map/ppermute | solution.py:85
  68.6 7.4 %collective-permute-start.21 = (f32[24,2,8,128]{3,2,1,0:T(8,128)S(1)}, f32[24,2,8,128]{3,2,1,0:T(8,128)S(1)}, u32[]{:S(2)}, u32[]{:S(2)}) collective-permute-start(f32[24,2,8,128]{3,2,1,0:T(8,128)S(1)} %add.622), channel_id=1, source_target_pairs={{2,0},{4,2},{6,4},{7,6},{5,7},{3,5},{1,3},{0,1},{10,8},{12,10},{14... | collective-permute-start | bytes 589832 | tf_op jit(solution)/shard_map/ppermute | solution.py:86
  70.2 6.8 %collective-permute-start.20 = (f32[24,2,8,128]{3,2,1,0:T(8,128)S(1)}, f32[24,2,8,128]{3,2,1,0:T(8,128)S(1)}, u32[]{:S(2)}, u32[]{:S(2)}) collective-permute-start(f32[24,2,8,128]{3,2,1,0:T(8,128)S(1)} %add.621), channel_id=1, source_target_pairs={{0,2},{2,4},{4,6},{6,7},{7,5},{5,3},{3,1},{1,0},{8,10},{10,12},{12... | collective-permute-start | bytes 589832 | tf_op jit(solution)/shard_map/ppermute | solution.py:85
  72.9 8.3 %collective-permute-start.11 = (f32[24,2,8,128]{3,2,1,0:T(8,128)S(1)}, f32[24,2,8,128]{3,2,1,0:T(8,128)S(1)}, u32[]{:S(2)}, u32[]{:S(2)}) collective-permute-start(f32[24,2,8,128]{3,2,1,0:T(8,128)S(1)} %add.582), channel_id=1, source_target_pairs={{2,0},{4,2},{6,4},{7,6},{5,7},{3,5},{1,3},{0,1},{10,8},{12,10},{14... | collective-permute-start | bytes 589832 | tf_op jit(solution)/shard_map/ppermute | solution.py:86
  74.5 7.4 %collective-permute-start.10 = (f32[24,2,8,128]{3,2,1,0:T(8,128)S(1)}, f32[24,2,8,128]{3,2,1,0:T(8,128)S(1)}, u32[]{:S(2)}, u32[]{:S(2)}) collective-permute-start(f32[24,2,8,128]{3,2,1,0:T(8,128)S(1)} %add.573), channel_id=1, source_target_pairs={{0,2},{2,4},{4,6},{6,7},{7,5},{5,3},{3,1},{1,0},{8,10},{10,12},{12... | collective-permute-start | bytes 589832 | tf_op jit(solution)/shard_map/ppermute | solution.py:85
  77.2 7.9 %collective-permute-start.23 = (f32[24,2,8,128]{3,2,1,0:T(8,128)S(1)}, f32[24,2,8,128]{3,2,1,0:T(8,128)S(1)}, u32[]{:S(2)}, u32[]{:S(2)}) collective-permute-start(f32[24,2,8,128]{3,2,1,0:T(8,128)S(1)} %add.624), channel_id=1, source_target_pairs={{2,0},{4,2},{6,4},{7,6},{5,7},{3,5},{1,3},{0,1},{10,8},{12,10},{14... | collective-permute-start | bytes 589832 | tf_op jit(solution)/shard_map/ppermute | solution.py:86
  78.8 7.8 %collective-permute-start.22 = (f32[24,2,8,128]{3,2,1,0:T(8,128)S(1)}, f32[24,2,8,128]{3,2,1,0:T(8,128)S(1)}, u32[]{:S(2)}, u32[]{:S(2)}) collective-permute-start(f32[24,2,8,128]{3,2,1,0:T(8,128)S(1)} %add.623), channel_id=1, source_target_pairs={{0,2},{2,4},{4,6},{6,7},{7,5},{5,3},{3,1},{1,0},{8,10},{10,12},{12... | collective-permute-start | bytes 589832 | tf_op jit(solution)/shard_map/ppermute | solution.py:85
  82.0 8.7 %collective-permute-start.13 = (f32[24,2,8,128]{3,2,1,0:T(8,128)S(1)}, f32[24,2,8,128]{3,2,1,0:T(8,128)S(1)}, u32[]{:S(2)}, u32[]{:S(2)}) collective-permute-start(f32[24,2,8,128]{3,2,1,0:T(8,128)S(1)} %add.597), channel_id=1, source_target_pairs={{2,0},{4,2},{6,4},{7,6},{5,7},{3,5},{1,3},{0,1},{10,8},{12,10},{14... | collective-permute-start | bytes 589832 | tf_op jit(solution)/shard_map/ppermute | solution.py:86
  83.4 7.8 %collective-permute-start.12 = (f32[24,2,8,128]{3,2,1,0:T(8,128)S(1)}, f32[24,2,8,128]{3,2,1,0:T(8,128)S(1)}, u32[]{:S(2)}, u32[]{:S(2)}) collective-permute-start(f32[24,2,8,128]{3,2,1,0:T(8,128)S(1)} %add.588), channel_id=1, source_target_pairs={{0,2},{2,4},{4,6},{6,7},{7,5},{5,3},{3,1},{1,0},{8,10},{10,12},{12... | collective-permute-start | bytes 589832 | tf_op jit(solution)/shard_map/ppermute | solution.py:85
  86.6 7.8 %collective-permute-start.25 = (f32[24,2,8,128]{3,2,1,0:T(8,128)S(1)}, f32[24,2,8,128]{3,2,1,0:T(8,128)S(1)}, u32[]{:S(2)}, u32[]{:S(2)}) collective-permute-start(f32[24,2,8,128]{3,2,1,0:T(8,128)S(1)} %add.626), channel_id=1, source_target_pairs={{2,0},{4,2},{6,4},{7,6},{5,7},{3,5},{1,3},{0,1},{10,8},{12,10},{14... | collective-permute-start | bytes 589832 | tf_op jit(solution)/shard_map/ppermute | solution.py:86
  87.8 6.7 %collective-permute-start.24 = (f32[24,2,8,128]{3,2,1,0:T(8,128)S(1)}, f32[24,2,8,128]{3,2,1,0:T(8,128)S(1)}, u32[]{:S(2)}, u32[]{:S(2)}) collective-permute-start(f32[24,2,8,128]{3,2,1,0:T(8,128)S(1)} %add.625), channel_id=1, source_target_pairs={{0,2},{2,4},{4,6},{6,7},{7,5},{5,3},{3,1},{1,0},{8,10},{10,12},{12... | collective-permute-start | bytes 589832 | tf_op jit(solution)/shard_map/ppermute | solution.py:85
  91.2 15.5 %collective-permute-start.14 = (f32[24,2,8,128]{3,2,1,0:T(8,128)S(1)}, f32[24,2,8,128]{3,2,1,0:T(8,128)S(1)}, u32[]{:S(2)}, u32[]{:S(2)}) collective-permute-start(f32[24,2,8,128]{3,2,1,0:T(8,128)S(1)} %add.603), channel_id=1, source_target_pairs={{0,2},{2,4},{4,6},{6,7},{7,5},{5,3},{3,1},{1,0},{8,10},{10,12},{12... | collective-permute-start | bytes 589832 | tf_op jit(solution)/shard_map/ppermute | solution.py:85
  94.6 7.1 %collective-permute-start.27 = (f32[24,2,8,128]{3,2,1,0:T(8,128)S(1)}, f32[24,2,8,128]{3,2,1,0:T(8,128)S(1)}, u32[]{:S(2)}, u32[]{:S(2)}) collective-permute-start(f32[24,2,8,128]{3,2,1,0:T(8,128)S(1)} %add.628), channel_id=1, source_target_pairs={{2,0},{4,2},{6,4},{7,6},{5,7},{3,5},{1,3},{0,1},{10,8},{12,10},{14... | collective-permute-start | bytes 589832 | tf_op jit(solution)/shard_map/ppermute | solution.py:86
  97.6 6.8 %collective-permute-start.26 = (f32[24,2,8,128]{3,2,1,0:T(8,128)S(1)}, f32[24,2,8,128]{3,2,1,0:T(8,128)S(1)}, u32[]{:S(2)}, u32[]{:S(2)}) collective-permute-start(f32[24,2,8,128]{3,2,1,0:T(8,128)S(1)} %add.627), channel_id=1, source_target_pairs={{0,2},{2,4},{4,6},{6,7},{7,5},{5,3},{3,1},{1,0},{8,10},{10,12},{12... | collective-permute-start | bytes 589832 | tf_op jit(solution)/shard_map/ppermute | solution.py:85
  98.7 9.1 %collective-permute-start.29 = (f32[24,2,8,128]{3,2,1,0:T(8,128)S(1)}, f32[24,2,8,128]{3,2,1,0:T(8,128)S(1)}, u32[]{:S(2)}, u32[]{:S(2)}) collective-permute-start(f32[24,2,8,128]{3,2,1,0:T(8,128)S(1)} %add.612), channel_id=1, source_target_pairs={{2,0},{4,2},{6,4},{7,6},{5,7},{3,5},{1,3},{0,1},{10,8},{12,10},{14... | collective-permute-start | bytes 589832 | tf_op jit(solution)/shard_map/ppermute | solution.py:86
  104.5 5.8 %collective-permute-start.28 = (f32[24,2,8,128]{3,2,1,0:T(8,128)S(1)}, f32[24,2,8,128]{3,2,1,0:T(8,128)S(1)}, u32[]{:S(2)}, u32[]{:S(2)}) collective-permute-start(f32[24,2,8,128]{3,2,1,0:T(8,128)S(1)} %add.629), channel_id=1, source_target_pairs={{0,2},{2,4},{4,6},{6,7},{7,5},{5,3},{3,1},{1,0},{8,10},{10,12},{12... | collective-permute-start | bytes 589832 | tf_op jit(solution)/shard_map/ppermute | solution.py:85
  105.0 5.7 %collective-permute-start.30 = (f32[24,2,8,128]{3,2,1,0:T(8,128)S(1)}, f32[24,2,8,128]{3,2,1,0:T(8,128)S(1)}, u32[]{:S(2)}, u32[]{:S(2)}) collective-permute-start(f32[24,2,8,128]{3,2,1,0:T(8,128)S(1)} %add.630), channel_id=1, source_target_pairs={{2,0},{4,2},{6,4},{7,6},{5,7},{3,5},{1,3},{0,1},{10,8},{12,10},{14... | collective-permute-start | bytes 589832 | tf_op jit(solution)/shard_map/ppermute | solution.py:86
  (1 other events, 18.1 us)

commit v7 on v2

--- a/solution.py
+++ b/solution.py
@@ -49,7 +49,7 @@
         )
         weights = jnp.stack([real_weight, imag_weight], axis=0)
         chunk = row_count // mode_count
-        half = chunk // 2
+        half = chunk // 3
         order_table = jnp.asarray(order, dtype=jnp.int32)
         position = jnp.asarray(position_of, dtype=jnp.int32)[mode]
 
@@ -66,6 +66,15 @@
         def owner_at(offset):
             return order_table[(position + offset) % mode_count]
 
+        offloaded_rows = receiver_block.reshape(mode_count, chunk, block_modes)[:, 2 * half :]
+        widened = offloaded_rows.reshape(-1, block_modes).astype(jnp.float32)
+        weighted = (widened[:, None, None, :] * weights[None]).astype(jnp.bfloat16)
+        offloaded = jnp.dot(
+            weighted.reshape(-1, block_modes), source_block, preferred_element_type=jnp.float32
+        )
+        offloaded = offloaded.reshape(-1, 2, sample_freqs.shape[0], source_block.shape[1])
+        offloaded = lax.psum_scatter(offloaded, "mode", scatter_dimension=0, tiled=True)
+
         ahead = partial_rows(owner_at(-1), 0)
         behind = partial_rows(owner_at(1), 1)
         for step in range(mode_count - 1):
@@ -73,7 +82,7 @@
             behind = lax.ppermute(behind, "mode", counter)
             ahead = ahead + partial_rows(owner_at(-step - 2), 0)
             behind = behind + partial_rows(owner_at(step + 2), 1)
-        return jnp.concatenate([ahead, behind], axis=0)
+        return jnp.concatenate([ahead, behind, offloaded], axis=0)
 
     return per_device
 

time: 104 us -> 141 us (1.36)
  between operations: 20.9 us -> 34.7 us
  waiting for transfers between devices: 39.3 us -> 46.6 us
  other arithmetic: 5.67 us -> 12.6 us
  local copies, waits for them, and re-layouts: 3.44 us -> 7.45 us
  matrix products: 15.6 us -> 19.4 us
    ppermute x7, waiting for transfers between devices: 34.9 us -> 39.6 us  [per_device(): ahead = lax.ppermute(ahead, 'mode', clockwise)]
    dot_general x0 -> x1, matrix products: none -> 4.76 us  [per_device(): jnp.dot(weighted.reshape(-1, block_modes), source_block, preferred_elemen...]
    ppermute x7, starting transfers between devices: 3.89 us -> 7.64 us  [per_device(): behind = lax.ppermute(behind, 'mode', counter)]
    dot_general x0 -> x1, local copies, waits for them, and re-layouts: none -> 2.59 us  [per_device(): jnp.dot(weighted.reshape(-1, block_modes), source_block, preferred_elemen...]
    ppermute x7, starting transfers between devices: 11.5 us -> 9.08 us  [per_device(): ahead = lax.ppermute(ahead, 'mode', clockwise)]
    ppermute x7, waiting for transfers between devices: 4.46 us -> 6.67 us  [per_device(): behind = lax.ppermute(behind, 'mode', counter)]
    select_n x2, other arithmetic: 1.69 us -> 3.81 us  [gather_blocks(): first = jnp.where(index == 0, local, other)]
    convert_element_type x3, other arithmetic: 0.61 us -> 2.26 us  [partial_rows(): widened = rows.astype(jnp.float32)]
  transfers between devices with their start and end apart: 16 -> 17, of which waited for: 14 -> 11; matrix products, arithmetic and copies ran while one was open for 21% -> 22% of each run, Pallas kernels for 0% -> 0%
where the time goes in v7:
time: 141 us; the launch traced here: 140 us
  waiting for transfers between devices  46.6 us (33%)
  between operations  34.7 us (25%)
  starting transfers between devices  19.7 us (14%)
  matrix products  19.4 us (14%)
  other arithmetic  12.6 us (9%)
  local copies, waits for them, and re-layouts  7.45 us (5%)
    ppermute x7, waiting for transfers between devices, per_device(): ahead = lax.ppermute(ahead, 'mode', clockwise)  39.6 us
    dot_general x16, matrix products, partial_rows(): jnp.dot(weighted.reshape(-1, block_modes), source_block, preferred_elemen...  14.6 us
    ppermute x7, starting transfers between devices, per_device(): ahead = lax.ppermute(ahead, 'mode', clockwise)  9.08 us
    ppermute x7, starting transfers between devices, per_device(): behind = lax.ppermute(behind, 'mode', counter)  7.64 us
    ppermute x7, waiting for transfers between devices, per_device(): behind = lax.ppermute(behind, 'mode', counter)  6.67 us
    dot_general x1, matrix products, per_device(): jnp.dot(weighted.reshape(-1, block_modes), source_block, preferred_elemen...  4.76 us
    select_n x2, other arithmetic, gather_blocks(): first = jnp.where(index == 0, local, other)  3.81 us
    ppermute x2, starting transfers between devices, swap_pair(): return lax.ppermute(local, axis_name, [(0, 1), (1, 0)])  2.97 us
  transfers between devices with their start and end apart: 17, of which 11 were waited for; matrix products, arithmetic and copies ran while one was open for 22% of the time, Pallas kernels for 0%

profile of v7, /device:TPU:0, one launch (start us, length us, event | category | flops | bytes accessed | tf_op | source)
XLA Modules:
  0.0 140.4 jit_solution(7473029733300611614)
XLA Ops:
  7.0 2.5 %collective-permute-start.1 = (bf16[2048,256]{1,0:T(8,128)(2,1)}, bf16[2048,256]{1,0:T(8,128)(2,1)S(1)}, u32[]{:S(2)}, u32[]{:S(2)}) collective-permute-start(bf16[2048,256]{1,0:T(8,128)(2,1)} %param.8), channel_id=1, source_target_pairs={{0,16},{16,0},{1,17},{17,1},{2,18},{18,2},{3,19},{19,3},{4,20},{20... | collective-permute-start | bytes 3145736 | tf_op jit(solution)/shard_map/ppermute | solution.py:20
  9.5 1.2 dynamic_slice.99
  21.4 2.0 %fusion.86 = (s32[1]{0:T(128)}, s32[1]{0:T(128)}, s32[1]{0:T(128)}, s32[1]{0:T(128)}, s32[1]{0:T(128)}, /*index=5*/s32[1]{0:T(128)}, s32[1]{0:T(128)}, s32[1]{0:...) fusion(s32[8]{0:T(128)} %constant.185.clone, ...), kind=kLoop, calls=%fused_computation.146 | loop fusion | bytes 192 | tf_op jit(solution)/shard_map/dynamic_slice | solution.py:67
  34.3 1.0 fusion.69
  35.4 1.5 %broadcast_select_fusion.3 = (bf16[2048,256]{1,0:T(8,128)(2,1)S(1)}, bf16[2048,256]{1,0:T(8,128)(2,1)S(1)}) fusion(bf16[2048,256]{1,0:T(8,128)(2,1)} %param.8, bf16[2048,256]{1,0:T(8,128)(2,1)S(1)} %collective-permute-done.1, pred[]{:T(512)S(6)} %eq.26), kind=kLoop, calls=%fused_computation.106 | loop fusion | flops 1048576 | bytes 4194305 | tf_op jit(solution)/shard_map/jit(_where)/select_n | solution.py:28
  36.9 2.3 %broadcast_select_fusion.1 = (bf16[384,2048]{1,0:T(8,128)(2,1)S(1)}, bf16[384,2048]{1,0:T(8,128)(2,1)S(1)}) fusion(bf16[384,2048]{1,0:T(8,128)(2,1)S(1)} %copy-done, bf16[384,2048]{1,0:T(8,128)(2,1)} %collective-permute-done, pred[]{:T(512)S(6)} %eq.25), kind=kLoop, calls=%fused_computation.103 | loop fusion | flops 1572864 | bytes 6291457 | tf_op jit(solution)/shard_map/jit(_where)/select_n | solution.py:28
  39.4 1.2 fusion.78
  40.6 1.4 %fusion.3 = f32[16,2,8,256]{3,2,1,0:T(8,128)} fusion(f32[2,8,4096]{2,1,0:T(8,128)S(1)} %pad_maximum_fusion.2, f32[16,4096]{1,0:T(8,128)S(1)} %get-tuple-element.6, bf16[2048,256]{1,0:T(8,128)(2,1)S(1)} %get-tuple-element.24, bf16[2048,256]{1,0:T(8,128)(2,1)S(1)} %get-tuple-element.23), kind=kOutput, calls=%fused_computation.53 | convolution fusion | flops 543162368 | bytes 2883584 | tf_op jit(solution)/shard_map/dot_general | solution.py:61
  42.0 1.6 %collective-permute-start.2 = (f32[16,2,8,256]{3,2,1,0:T(8,128)}, f32[16,2,8,256]{3,2,1,0:T(8,128)}, u32[]{:S(2)}, u32[]{:S(2)}) collective-permute-start(f32[16,2,8,256]{3,2,1,0:T(8,128)} %fusion.3), channel_id=1, source_target_pairs={{0,2},{2,4},{4,6},{6,7},{7,5},{5,3},{3,1},{1,0},{8,10},{10,12},{12... | collective-permute-start | bytes 786440 | tf_op jit(solution)/shard_map/ppermute | solution.py:81
  43.6 1.0 fusion.79
  44.6 1.4 %fusion.11 = f32[16,2,8,256]{3,2,1,0:T(8,128)} fusion(f32[16,4096]{1,0:T(8,128)S(1)} %get-tuple-element.13, f32[2,8,4096]{2,1,0:T(8,128)S(1)} %pad_maximum_fusion.2, bf16[2048,256]{1,0:T(8,128)(2,1)S(1)} %get-tuple-element.24, bf16[2048,256]{1,0:T(8,128)(2,1)S(1)} %get-tuple-element.23), kind=kOutput, calls=%fused_computation.61 | convolution fusion | flops 543162368 | bytes 2883584 | tf_op jit(solution)/shard_map/dot_general | solution.py:61
  46.9 4.8 %fusion = f32[128,2,8,256]{3,0,2,1:T(8,128)S(1)} fusion(f32[2,8,4096]{2,1,0:T(8,128)S(1)} %pad_maximum_fusion.2, f32[128,4096]{1,0:T(8,128)S(1)} %bitcast_convert_fusion, bf16[2048,256]{1,0:T(8,128)(2,1)S(1)} %get-tuple-element.24, bf16[2048,256]{1,0:T(8,128)(2,1)S(1)} %get-tuple-element.23), kind=kOutput, calls=%fused_computation.1 | convolution fusion | flops 4315938816 | bytes 6553600 | tf_op jit(solution)/shard_map/dot_general | solution.py:72
  51.6 2.6 %copy.8 = f32[128,2,8,256]{3,2,1,0:T(8,128)} copy(f32[128,2,8,256]{3,0,2,1:T(8,128)S(1)} %fusion) | data formatting | bytes 4194304 | tf_op jit(solution)/shard_map/dot_general | solution.py:72
  54.3 2.6 %fusion.10 = f32[16,2,8,256]{3,2,1,0:T(8,128)S(1)} fusion(f32[16,4096]{1,0:T(8,128)} %get-tuple-element.5, f32[2,8,4096]{2,1,0:T(8,128)} %copy-done.13, bf16[2048,256]{1,0:T(8,128)(2,1)} %copy-done.3, bf16[2048,256]{1,0:T(8,128)(2,1)} %copy-done.1), kind=kOutput, calls=%fused_computation.60 | convolution fusion | flops 543162368 | bytes 2883584 | tf_op jit(solution)/shard_map/dot_general | solution.py:61
  63.6 1.0 add.408
  64.6 1.9 %collective-permute-start.3 = (f32[16,2,8,256]{3,2,1,0:T(8,128)S(1)}, f32[16,2,8,256]{3,2,1,0:T(8,128)S(1)}, u32[]{:S(2)}, u32[]{:S(2)}) collective-permute-start(f32[16,2,8,256]{3,2,1,0:T(8,128)S(1)} %add.408), channel_id=1, source_target_pairs={{0,2},{2,4},{4,6},{6,7},{7,5},{5,3},{3,1},{1,0},{8,10},{10,12},{12... | collective-permute-start | bytes 786440 | tf_op jit(solution)/shard_map/ppermute | solution.py:81
  66.4 1.0 add.461
  68.6 9.4 %collective-permute-done.3 = f32[16,2,8,256]{3,2,1,0:T(8,128)S(1)} collective-permute-done((f32[16,2,8,256]{3,2,1,0:T(8,128)S(1)}, f32[16,2,8,256]{3,2,1,0:T(8,128)S(1)}, u32[]{:S(2)}, u32[]{:S(2)}) %collective-permute-start.3) | collective-permute-done | bytes 262176 | tf_op jit(solution)/shard_map/ppermute | solution.py:81
  78.1 2.9 %collective-permute-start.4 = (f32[16,2,8,256]{3,2,1,0:T(8,128)S(1)}, f32[16,2,8,256]{3,2,1,0:T(8,128)S(1)}, u32[]{:S(2)}, u32[]{:S(2)}) collective-permute-start(f32[16,2,8,256]{3,2,1,0:T(8,128)S(1)} %add.414), channel_id=1, source_target_pairs={{0,2},{2,4},{4,6},{6,7},{7,5},{5,3},{3,1},{1,0},{8,10},{10,12},{12... | collective-permute-start | bytes 786440 | tf_op jit(solution)/shard_map/ppermute | solution.py:81
  81.0 2.5 %collective-permute-done.10 = f32[16,2,8,256]{3,2,1,0:T(8,128)S(1)} collective-permute-done((f32[16,2,8,256]{3,2,1,0:T(8,128)S(1)}, f32[16,2,8,256]{3,2,1,0:T(8,128)S(1)}, u32[]{:S(2)}, u32[]{:S(2)}) %collective-permute-start.10) | collective-permute-done | bytes 262176 | tf_op jit(solution)/shard_map/ppermute | solution.py:82
  84.4 6.8 %collective-permute-done.4 = f32[16,2,8,256]{3,2,1,0:T(8,128)S(1)} collective-permute-done((f32[16,2,8,256]{3,2,1,0:T(8,128)S(1)}, f32[16,2,8,256]{3,2,1,0:T(8,128)S(1)}, u32[]{:S(2)}, u32[]{:S(2)}) %collective-permute-start.4) | collective-permute-done | bytes 262176 | tf_op jit(solution)/shard_map/ppermute | solution.py:81
  91.2 2.5 %collective-permute-start.5 = (f32[16,2,8,256]{3,2,1,0:T(8,128)S(1)}, f32[16,2,8,256]{3,2,1,0:T(8,128)S(1)}, u32[]{:S(2)}, u32[]{:S(2)}) collective-permute-start(f32[16,2,8,256]{3,2,1,0:T(8,128)S(1)} %add.420), channel_id=1, source_target_pairs={{0,2},{2,4},{4,6},{6,7},{7,5},{5,3},{3,1},{1,0},{8,10},{10,12},{12... | collective-permute-start | bytes 786440 | tf_op jit(solution)/shard_map/ppermute | solution.py:81
  95.7 7.9 %collective-permute-done.5 = f32[16,2,8,256]{3,2,1,0:T(8,128)S(1)} collective-permute-done((f32[16,2,8,256]{3,2,1,0:T(8,128)S(1)}, f32[16,2,8,256]{3,2,1,0:T(8,128)S(1)}, u32[]{:S(2)}, u32[]{:S(2)}) %collective-permute-start.5) | collective-permute-done | bytes 262176 | tf_op jit(solution)/shard_map/ppermute | solution.py:81
  103.8 2.1 %collective-permute-start.13 = (f32[16,2,8,256]{3,2,1,0:T(8,128)S(1)}, f32[16,2,8,256]{3,2,1,0:T(8,128)S(1)}, u32[]{:S(2)}, u32[]{:S(2)}) collective-permute-start(f32[16,2,8,256]{3,2,1,0:T(8,128)S(1)} %add.488), channel_id=1, source_target_pairs={{2,0},{4,2},{6,4},{7,6},{5,7},{3,5},{1,3},{0,1},{10,8},{12,10},{14... | collective-permute-start | bytes 786440 | tf_op jit(solution)/shard_map/ppermute | solution.py:82
  106.5 4.0 %collective-permute-done.6 = f32[16,2,8,256]{3,2,1,0:T(8,128)S(1)} collective-permute-done((f32[16,2,8,256]{3,2,1,0:T(8,128)S(1)}, f32[16,2,8,256]{3,2,1,0:T(8,128)S(1)}, u32[]{:S(2)}, u32[]{:S(2)}) %collective-permute-start.6) | collective-permute-done | bytes 262176 | tf_op jit(solution)/shard_map/ppermute | solution.py:81
  110.6 2.1 %collective-permute-start.14 = (f32[16,2,8,256]{3,2,1,0:T(8,128)S(1)}, f32[16,2,8,256]{3,2,1,0:T(8,128)S(1)}, u32[]{:S(2)}, u32[]{:S(2)}) collective-permute-start(f32[16,2,8,256]{3,2,1,0:T(8,128)S(1)} %add.497), channel_id=1, source_target_pairs={{2,0},{4,2},{6,4},{7,6},{5,7},{3,5},{1,3},{0,1},{10,8},{12,10},{14... | collective-permute-start | bytes 786440 | tf_op jit(solution)/shard_map/ppermute | solution.py:82
  113.4 7.8 %collective-permute-done.7 = f32[16,2,8,256]{3,2,1,0:T(8,128)S(1)} collective-permute-done((f32[16,2,8,256]{3,2,1,0:T(8,128)S(1)}, f32[16,2,8,256]{3,2,1,0:T(8,128)S(1)}, u32[]{:S(2)}, u32[]{:S(2)}) %collective-permute-start.7) | collective-permute-done | bytes 262176 | tf_op jit(solution)/shard_map/ppermute | solution.py:81
  121.3 0.9 collective-permute-done.14
  122.3 1.7 %collective-permute-start.15 = (f32[16,2,8,256]{3,2,1,0:T(8,128)S(1)}, f32[16,2,8,256]{3,2,1,0:T(8,128)S(1)}, u32[]{:S(2)}, u32[]{:S(2)}) collective-permute-start(f32[16,2,8,256]{3,2,1,0:T(8,128)S(1)} %add.506), channel_id=1, source_target_pairs={{2,0},{4,2},{6,4},{7,6},{5,7},{3,5},{1,3},{0,1},{10,8},{12,10},{14... | collective-permute-start | bytes 786440 | tf_op jit(solution)/shard_map/ppermute | solution.py:82
  124.8 3.8 %collective-permute-done.8 = f32[16,2,8,256]{3,2,1,0:T(8,128)S(1)} collective-permute-done((f32[16,2,8,256]{3,2,1,0:T(8,128)S(1)}, f32[16,2,8,256]{3,2,1,0:T(8,128)S(1)}, u32[]{:S(2)}, u32[]{:S(2)}) %collective-permute-start.8) | collective-permute-done | bytes 262176 | tf_op jit(solution)/shard_map/ppermute | solution.py:81
  128.6 2.8 %collective-permute-done.15 = f32[16,2,8,256]{3,2,1,0:T(8,128)S(1)} collective-permute-done((f32[16,2,8,256]{3,2,1,0:T(8,128)S(1)}, f32[16,2,8,256]{3,2,1,0:T(8,128)S(1)}, u32[]{:S(2)}, u32[]{:S(2)}) %collective-permute-start.15) | collective-permute-done | bytes 262176 | tf_op jit(solution)/shard_map/ppermute | solution.py:82
  131.7 1.9 %pad_maximum_fusion.1 = f32[48,2,8,256]{3,2,1,0:T(8,128)} fusion(f32[16,2,8,256]{3,2,1,0:T(8,128)} %reduce-scatter.2.cloned.1.call-done, f32[16,2,8,256]{3,2,1,0:T(8,128)S(1)} %add.515, f32[16,2,8,256]{3,2,1,0:T(8,128)S(1)} %add.444), kind=kLoop, calls=%fused_computation.107 | loop fusion | flops 393216 | bytes 1572864 | tf_op jit(solution)/shard_map/concatenate | solution.py:85
  (79 shorter events, 15.7 us)
Async XLA Ops:
  6.5 125.1 %reduce-scatter.2.cloned.1.call-start = ((), (), s32[]{:S(2)}) async-start(), calls=%async_computation.1 | async-start | bytes 2359296 | tf_op jit(solution)/shard_map/reduce_scatter | solution.py:76
  6.5 30.3 %collective-permute-start = (bf16[384,2048]{1,0:T(8,128)(2,1)}, bf16[384,2048]{1,0:T(8,128)(2,1)}, u32[]{:S(2)}, u32[]{:S(2)}) collective-permute-start(bf16[384,2048]{1,0:T(8,128)(2,1)} %param.7), channel_id=1, source_target_pairs={{0,8},{8,0},{1,9},{9,1},{2,10},{10,2},{3,11},{11,3},{4,12},{12,4},... | collective-permute-start | bytes 4718600 | tf_op jit(solution)/shard_map/ppermute | solution.py:20
  7.0 28.4 %collective-permute-start.1 = (bf16[2048,256]{1,0:T(8,128)(2,1)}, bf16[2048,256]{1,0:T(8,128)(2,1)S(1)}, u32[]{:S(2)}, u32[]{:S(2)}) collective-permute-start(bf16[2048,256]{1,0:T(8,128)(2,1)} %param.8), channel_id=1, source_target_pairs={{0,16},{16,0},{1,17},{17,1},{2,18},{18,2},{3,19},{19,3},{4,20},{20... | collective-permute-start | bytes 3145736 | tf_op jit(solution)/shard_map/ppermute | solution.py:20
  34.3 2.5 %copy-start = (bf16[384,2048]{1,0:T(8,128)(2,1)S(1)}, bf16[384,2048]{1,0:T(8,128)(2,1)}, u32[]{:S(2)}) copy-start(bf16[384,2048]{1,0:T(8,128)(2,1)} %param.7) | copy-start | bytes 4718596
  35.3 11.5 %copy-start.13 = (f32[2,8,4096]{2,1,0:T(8,128)}, f32[2,8,4096]{2,1,0:T(8,128)S(1)}, u32[]{:S(2)}) copy-start(f32[2,8,4096]{2,1,0:T(8,128)S(1)} %pad_maximum_fusion.2) | copy-start | bytes 786436
  36.8 10.0 %copy-start.1 = (bf16[2048,256]{1,0:T(8,128)(2,1)}, bf16[2048,256]{1,0:T(8,128)(2,1)S(1)}, u32[]{:S(2)}) copy-start(bf16[2048,256]{1,0:T(8,128)(2,1)S(1)} %get-tuple-element.23) | copy-start | bytes 3145732
  36.8 10.0 %copy-start.3 = (bf16[2048,256]{1,0:T(8,128)(2,1)}, bf16[2048,256]{1,0:T(8,128)(2,1)S(1)}, u32[]{:S(2)}) copy-start(bf16[2048,256]{1,0:T(8,128)(2,1)S(1)} %get-tuple-element.24) | copy-start | bytes 3145732
  42.0 21.5 %collective-permute-start.2 = (f32[16,2,8,256]{3,2,1,0:T(8,128)}, f32[16,2,8,256]{3,2,1,0:T(8,128)}, u32[]{:S(2)}, u32[]{:S(2)}) collective-permute-start(f32[16,2,8,256]{3,2,1,0:T(8,128)} %fusion.3), channel_id=1, source_target_pairs={{0,2},{2,4},{4,6},{6,7},{7,5},{5,3},{3,1},{1,0},{8,10},{10,12},{12... | collective-permute-start | bytes 786440 | tf_op jit(solution)/shard_map/ppermute | solution.py:81
  46.0 20.4 %collective-permute-start.9 = (f32[16,2,8,256]{3,2,1,0:T(8,128)}, f32[16,2,8,256]{3,2,1,0:T(8,128)}, u32[]{:S(2)}, u32[]{:S(2)}) collective-permute-start(f32[16,2,8,256]{3,2,1,0:T(8,128)} %fusion.11), channel_id=1, source_target_pairs={{2,0},{4,2},{6,4},{7,6},{5,7},{3,5},{1,3},{0,1},{10,8},{12,10},{14... | collective-permute-start | bytes 786440 | tf_op jit(solution)/shard_map/ppermute | solution.py:82
  54.2 2.6 %copy-start.2 = (bf16[2048,256]{1,0:T(8,128)(2,1)S(1)}, bf16[2048,256]{1,0:T(8,128)(2,1)}, u32[]{:S(2)}) copy-start(bf16[2048,256]{1,0:T(8,128)(2,1)} %copy-done.1) | copy-start | bytes 3145732
  54.2 2.6 %copy-start.4 = (bf16[2048,256]{1,0:T(8,128)(2,1)S(1)}, bf16[2048,256]{1,0:T(8,128)(2,1)}, u32[]{:S(2)}) copy-start(bf16[2048,256]{1,0:T(8,128)(2,1)} %copy-done.3) | copy-start | bytes 3145732
  54.3 2.6 %copy-start.10 = (f32[16,4096]{1,0:T(8,128)S(1)}, f32[16,4096]{1,0:T(8,128)}, u32[]{:S(2)}) copy-start(f32[16,4096]{1,0:T(8,128)} %get-tuple-element.10) | copy-start | bytes 786436
  54.3 2.6 %copy-start.14 = (f32[2,8,4096]{2,1,0:T(8,128)S(1)}, f32[2,8,4096]{2,1,0:T(8,128)}, u32[]{:S(2)}) copy-start(f32[2,8,4096]{2,1,0:T(8,128)} %copy-done.13) | copy-start | bytes 786436
  56.8 1.0 copy-start.9
  57.6 1.0 copy-start.8
  58.5 1.0 copy-start.6
  59.3 1.0 copy-start.12
  60.2 1.0 copy-start.11
  61.9 1.0 copy-start.7
  62.8 5.1 %copy-start.5 = (f32[16,4096]{1,0:T(8,128)S(1)}, f32[16,4096]{1,0:T(8,128)}, u32[]{:S(2)}) copy-start(f32[16,4096]{1,0:T(8,128)} %get-tuple-element.15) | copy-start | bytes 786436
  64.6 13.5 %collective-permute-start.3 = (f32[16,2,8,256]{3,2,1,0:T(8,128)S(1)}, f32[16,2,8,256]{3,2,1,0:T(8,128)S(1)}, u32[]{:S(2)}, u32[]{:S(2)}) collective-permute-start(f32[16,2,8,256]{3,2,1,0:T(8,128)S(1)} %add.408), channel_id=1, source_target_pairs={{0,2},{2,4},{4,6},{6,7},{7,5},{5,3},{3,1},{1,0},{8,10},{10,12},{12... | collective-permute-start | bytes 786440 | tf_op jit(solution)/shard_map/ppermute | solution.py:81
  67.4 16.2 %collective-permute-start.10 = (f32[16,2,8,256]{3,2,1,0:T(8,128)S(1)}, f32[16,2,8,256]{3,2,1,0:T(8,128)S(1)}, u32[]{:S(2)}, u32[]{:S(2)}) collective-permute-start(f32[16,2,8,256]{3,2,1,0:T(8,128)S(1)} %add.461), channel_id=1, source_target_pairs={{2,0},{4,2},{6,4},{7,6},{5,7},{3,5},{1,3},{0,1},{10,8},{12,10},{14... | collective-permute-start | bytes 786440 | tf_op jit(solution)/shard_map/ppermute | solution.py:82
  78.1 13.1 %collective-permute-start.4 = (f32[16,2,8,256]{3,2,1,0:T(8,128)S(1)}, f32[16,2,8,256]{3,2,1,0:T(8,128)S(1)}, u32[]{:S(2)}, u32[]{:S(2)}) collective-permute-start(f32[16,2,8,256]{3,2,1,0:T(8,128)S(1)} %add.414), channel_id=1, source_target_pairs={{0,2},{2,4},{4,6},{6,7},{7,5},{5,3},{3,1},{1,0},{8,10},{10,12},{12... | collective-permute-start | bytes 786440 | tf_op jit(solution)/shard_map/ppermute | solution.py:81
  83.6 10.5 %collective-permute-start.11 = (f32[16,2,8,256]{3,2,1,0:T(8,128)S(1)}, f32[16,2,8,256]{3,2,1,0:T(8,128)S(1)}, u32[]{:S(2)}, u32[]{:S(2)}) collective-permute-start(f32[16,2,8,256]{3,2,1,0:T(8,128)S(1)} %add.470), channel_id=1, source_target_pairs={{2,0},{4,2},{6,4},{7,6},{5,7},{3,5},{1,3},{0,1},{10,8},{12,10},{14... | collective-permute-start | bytes 786440 | tf_op jit(solution)/shard_map/ppermute | solution.py:82
  91.2 12.4 %collective-permute-start.5 = (f32[16,2,8,256]{3,2,1,0:T(8,128)S(1)}, f32[16,2,8,256]{3,2,1,0:T(8,128)S(1)}, u32[]{:S(2)}, u32[]{:S(2)}) collective-permute-start(f32[16,2,8,256]{3,2,1,0:T(8,128)S(1)} %add.420), channel_id=1, source_target_pairs={{0,2},{2,4},{4,6},{6,7},{7,5},{5,3},{3,1},{1,0},{8,10},{10,12},{12... | collective-permute-start | bytes 786440 | tf_op jit(solution)/shard_map/ppermute | solution.py:81
  94.2 9.5 %collective-permute-start.12 = (f32[16,2,8,256]{3,2,1,0:T(8,128)S(1)}, f32[16,2,8,256]{3,2,1,0:T(8,128)S(1)}, u32[]{:S(2)}, u32[]{:S(2)}) collective-permute-start(f32[16,2,8,256]{3,2,1,0:T(8,128)S(1)} %add.479), channel_id=1, source_target_pairs={{2,0},{4,2},{6,4},{7,6},{5,7},{3,5},{1,3},{0,1},{10,8},{12,10},{14... | collective-permute-start | bytes 786440 | tf_op jit(solution)/shard_map/ppermute | solution.py:82
  103.6 6.8 %collective-permute-start.6 = (f32[16,2,8,256]{3,2,1,0:T(8,128)S(1)}, f32[16,2,8,256]{3,2,1,0:T(8,128)S(1)}, u32[]{:S(2)}, u32[]{:S(2)}) collective-permute-start(f32[16,2,8,256]{3,2,1,0:T(8,128)S(1)} %add.426), channel_id=1, source_target_pairs={{0,2},{2,4},{4,6},{6,7},{7,5},{5,3},{3,1},{1,0},{8,10},{10,12},{12... | collective-permute-start | bytes 786440 | tf_op jit(solution)/shard_map/ppermute | solution.py:81
  103.8 6.8 %collective-permute-start.13 = (f32[16,2,8,256]{3,2,1,0:T(8,128)S(1)}, f32[16,2,8,256]{3,2,1,0:T(8,128)S(1)}, u32[]{:S(2)}, u32[]{:S(2)}) collective-permute-start(f32[16,2,8,256]{3,2,1,0:T(8,128)S(1)} %add.488), channel_id=1, source_target_pairs={{2,0},{4,2},{6,4},{7,6},{5,7},{3,5},{1,3},{0,1},{10,8},{12,10},{14... | collective-permute-start | bytes 786440 | tf_op jit(solution)/shard_map/ppermute | solution.py:82
  110.5 10.7 %collective-permute-start.7 = (f32[16,2,8,256]{3,2,1,0:T(8,128)S(1)}, f32[16,2,8,256]{3,2,1,0:T(8,128)S(1)}, u32[]{:S(2)}, u32[]{:S(2)}) collective-permute-start(f32[16,2,8,256]{3,2,1,0:T(8,128)S(1)} %add.432), channel_id=1, source_target_pairs={{0,2},{2,4},{4,6},{6,7},{7,5},{5,3},{3,1},{1,0},{8,10},{10,12},{12... | collective-permute-start | bytes 786440 | tf_op jit(solution)/shard_map/ppermute | solution.py:81
  110.6 11.6 %collective-permute-start.14 = (f32[16,2,8,256]{3,2,1,0:T(8,128)S(1)}, f32[16,2,8,256]{3,2,1,0:T(8,128)S(1)}, u32[]{:S(2)}, u32[]{:S(2)}) collective-permute-start(f32[16,2,8,256]{3,2,1,0:T(8,128)S(1)} %add.497), channel_id=1, source_target_pairs={{2,0},{4,2},{6,4},{7,6},{5,7},{3,5},{1,3},{0,1},{10,8},{12,10},{14... | collective-permute-start | bytes 786440 | tf_op jit(solution)/shard_map/ppermute | solution.py:82
  121.3 7.3 %collective-permute-start.8 = (f32[16,2,8,256]{3,2,1,0:T(8,128)S(1)}, f32[16,2,8,256]{3,2,1,0:T(8,128)S(1)}, u32[]{:S(2)}, u32[]{:S(2)}) collective-permute-start(f32[16,2,8,256]{3,2,1,0:T(8,128)S(1)} %add.438), channel_id=1, source_target_pairs={{0,2},{2,4},{4,6},{6,7},{7,5},{5,3},{3,1},{1,0},{8,10},{10,12},{12... | collective-permute-start | bytes 786440 | tf_op jit(solution)/shard_map/ppermute | solution.py:81
  122.3 9.1 %collective-permute-start.15 = (f32[16,2,8,256]{3,2,1,0:T(8,128)S(1)}, f32[16,2,8,256]{3,2,1,0:T(8,128)S(1)}, u32[]{:S(2)}, u32[]{:S(2)}) collective-permute-start(f32[16,2,8,256]{3,2,1,0:T(8,128)S(1)} %add.506), channel_id=1, source_target_pairs={{2,0},{4,2},{6,4},{7,6},{5,7},{3,5},{1,3},{0,1},{10,8},{12,10},{14... | collective-permute-start | bytes 786440 | tf_op jit(solution)/shard_map/ppermute | solution.py:82
Sparse Core Ops, SparseCore 0:
  54.4 77.2 reduce-scatter.1

commit v8 on v6

--- a/solution.py
+++ b/solution.py
@@ -44,11 +44,6 @@
         receiver_block = gather_blocks(receivers, "evt", sizes["evt"], 1)
         width = excitations.shape[1] // 2
         first_source = gather_blocks(excitations[:, :width], "sta", sizes["sta"], 0)
-        second_local, _ = lax.optimization_barrier((excitations[:, width:], first_source))
-        if sizes["sta"] == 2:
-            second_far = swap_pair(second_local, "sta")
-        else:
-            second_far = lax.all_gather(second_local, "sta", axis=0, tiled=True)
         row_count, block_modes = receiver_block.shape
         real_weight, imag_weight = resonance(
             mode_freqs[None, :], mode_damping[None, :], sample_freqs[:, None]
@@ -90,7 +85,15 @@
             )
 
         steps = mode_count - 1
-        first = ring_step(0, start(first_source), first_source)
+        first = start(first_source)
+        second_local, first_ahead, first_behind = lax.optimization_barrier(
+            (excitations[:, width:], first[0], first[1])
+        )
+        if sizes["sta"] == 2:
+            second_far = swap_pair(second_local, "sta")
+        else:
+            second_far = lax.all_gather(second_local, "sta", axis=0, tiled=True)
+        first = ring_step(0, (first_ahead, first_behind), first_source)
         held, second_far, _, _ = lax.optimization_barrier(
             (receiver_block, second_far, first[0], first[1])
         )

time: 112 us -> 118 us (1.054)
  waiting for transfers between devices: 15.4 us -> 20.1 us
    ppermute x14, waiting for transfers between devices: 8.59 us -> 12.2 us  [ring_step(): behind = lax.ppermute(sent_behind, 'mode', counter)]
  transfers between devices with their start and end apart: 31 -> 31, of which waited for: 12 -> 15; matrix products, arithmetic and copies ran while one was open for 38% -> 32% of each run, Pallas kernels for 0% -> 0%
where the time goes in v8:
time: 118 us; the launch traced here: 117 us
  starting transfers between devices  32.4 us (27%)
  matrix products  31.3 us (27%)
  between operations  21.3 us (18%)
  waiting for transfers between devices  20.1 us (17%)
  other arithmetic  7.49 us (6%)
  local copies, waits for them, and re-layouts  4.35 us (4%)
    dot_general x32, matrix products, partial_rows(): jnp.dot(weighted.reshape(-1, block_modes), source_block, preferred_elemen...  31.3 us
    ppermute x14, starting transfers between devices, ring_step(): behind = lax.ppermute(sent_behind, 'mode', counter)  22.4 us
    ppermute x14, waiting for transfers between devices, ring_step(): behind = lax.ppermute(sent_behind, 'mode', counter)  12.2 us
    ppermute x14, waiting for transfers between devices, ring_step(): ahead = lax.ppermute(sent_ahead, 'mode', clockwise)  7.88 us
    ppermute x14, starting transfers between devices, ring_step(): ahead = lax.ppermute(sent_ahead, 'mode', clockwise)  6.73 us
    ppermute x3, starting transfers between devices, swap_pair(): return lax.ppermute(local, axis_name, [(0, 1), (1, 0)])  3.24 us
    select_n x2, other arithmetic, gather_blocks(): first = jnp.where(index == 0, local, other)  2.77 us
  transfers between devices with their start and end apart: 31, of which 15 were waited for; matrix products, arithmetic and copies ran while one was open for 32% of the time, Pallas kernels for 0%

profile of v8, /device:TPU:0, one launch (start us, length us, event | category | flops | bytes accessed | tf_op | source)
XLA Modules:
  0.0 116.9 jit_solution(8732707359524012973)
XLA Ops:
  0.5 1.1 slice.6
  1.5 2.7 %collective-permute-start.1 = (bf16[2048,128]{1,0:T(8,128)(2,1)S(1)}, bf16[2048,128]{1,0:T(8,128)(2,1)}, u32[]{:S(2)}, u32[]{:S(2)}) collective-permute-start(bf16[2048,128]{1,0:T(8,128)(2,1)S(1)} %slice.6), channel_id=1, source_target_pairs={{0,16},{16,0},{1,17},{17,1},{2,18},{18,2},{3,19},{19,3},{4,20},{20... | collective-permute-start | bytes 1572872 | tf_op jit(solution)/shard_map/ppermute | solution.py:20
  5.9 1.2 %dynamic_slice.163 = s32[1]{0:T(128)} dynamic-slice(s32[8]{0:T(128)} %constant.218.clone, s32[]{:T(128)S(6)} %select_n.268), dynamic_slice_sizes={1} | dynamic-slice | bytes 12 | tf_op jit(solution)/shard_map/dynamic_slice | solution.py:55
  17.9 2.0 %fusion.139 = (s32[1]{0:T(128)}, s32[1]{0:T(128)}, s32[1]{0:T(128)}, s32[1]{0:T(128)}, s32[1]{0:T(128)}, /*index=5*/s32[1]{0:T(128)}, s32[1]{0:T(128)}, s32[1]{0...) fusion(s32[8]{0:T(128)} %constant.217.clone, ...), kind=kLoop, calls=%fused_computation.218 | loop fusion | bytes 192 | tf_op jit(solution)/shard_map/dynamic_slice | solution.py:68
  29.8 1.1 broadcast_select_fusion.5
  31.1 1.6 %broadcast_select_fusion.1 = (bf16[384,2048]{1,0:T(8,128)(2,1)S(1)}, bf16[384,2048]{1,0:T(8,128)(2,1)S(1)}) fusion(bf16[384,2048]{1,0:T(8,128)(2,1)S(1)} %copy-done.1, bf16[384,2048]{1,0:T(8,128)(2,1)} %collective-permute-done, pred[]{:T(512)S(6)} %eq.43), kind=kLoop, calls=%fused_computation.134 | loop fusion | flops 1572864 | bytes 6291457 | tf_op jit(solution)/shard_map/jit(_where)/select_n | solution.py:28
  35.1 1.5 %collective-permute-start.3 = (f32[24,2,8,128]{3,2,1,0:T(8,128)S(1)}, f32[24,2,8,128]{3,2,1,0:T(8,128)S(1)}, u32[]{:S(2)}, u32[]{:S(2)}) collective-permute-start(f32[24,2,8,128]{3,2,1,0:T(8,128)S(1)} %fusion.1), channel_id=1, source_target_pairs={{2,0},{4,2},{6,4},{7,6},{5,7},{3,5},{1,3},{0,1},{10,8},{12,10},{14... | collective-permute-start | bytes 589832 | tf_op jit(solution)/shard_map/ppermute | solution.py:81
  37.4 4.8 %collective-permute-done.3 = f32[24,2,8,128]{3,2,1,0:T(8,128)S(1)} collective-permute-done((f32[24,2,8,128]{3,2,1,0:T(8,128)S(1)}, f32[24,2,8,128]{3,2,1,0:T(8,128)S(1)}, u32[]{:S(2)}, u32[]{:S(2)}) %collective-permute-start.3) | collective-permute-done | bytes 196640 | tf_op jit(solution)/shard_map/ppermute | solution.py:81
  44.3 1.6 %collective-permute-start.5 = (f32[24,2,8,128]{3,2,1,0:T(8,128)S(1)}, f32[24,2,8,128]{3,2,1,0:T(8,128)S(1)}, u32[]{:S(2)}, u32[]{:S(2)}) collective-permute-start(f32[24,2,8,128]{3,2,1,0:T(8,128)S(1)} %fusion.98), channel_id=1, source_target_pairs={{2,0},{4,2},{6,4},{7,6},{5,7},{3,5},{1,3},{0,1},{10,8},{12,10},{14... | collective-permute-start | bytes 589832 | tf_op jit(solution)/shard_map/ppermute | solution.py:81
  48.4 1.9 %collective-permute-done.5 = f32[24,2,8,128]{3,2,1,0:T(8,128)S(1)} collective-permute-done((f32[24,2,8,128]{3,2,1,0:T(8,128)S(1)}, f32[24,2,8,128]{3,2,1,0:T(8,128)S(1)}, u32[]{:S(2)}, u32[]{:S(2)}) %collective-permute-start.5) | collective-permute-done | bytes 196640 | tf_op jit(solution)/shard_map/ppermute | solution.py:81
  50.3 1.3 %collective-permute-done.4 = f32[24,2,8,128]{3,2,1,0:T(8,128)S(1)} collective-permute-done((f32[24,2,8,128]{3,2,1,0:T(8,128)S(1)}, f32[24,2,8,128]{3,2,1,0:T(8,128)S(1)}, u32[]{:S(2)}, u32[]{:S(2)}) %collective-permute-start.4) | collective-permute-done | bytes 196640 | tf_op jit(solution)/shard_map/ppermute | solution.py:80
  51.6 1.6 %collective-permute-start.7 = (f32[24,2,8,128]{3,2,1,0:T(8,128)S(1)}, f32[24,2,8,128]{3,2,1,0:T(8,128)S(1)}, u32[]{:S(2)}, u32[]{:S(2)}) collective-permute-start(f32[24,2,8,128]{3,2,1,0:T(8,128)S(1)} %add.552), channel_id=1, source_target_pairs={{2,0},{4,2},{6,4},{7,6},{5,7},{3,5},{1,3},{0,1},{10,8},{12,10},{14... | collective-permute-start | bytes 589832 | tf_op jit(solution)/shard_map/ppermute | solution.py:81
  54.8 1.0 fusion.6
  57.0 1.0 fusion.15
  58.0 1.6 %collective-permute-start.17 = (f32[24,2,8,128]{3,2,1,0:T(8,128)S(1)}, f32[24,2,8,128]{3,2,1,0:T(8,128)S(1)}, u32[]{:S(2)}, u32[]{:S(2)}) collective-permute-start(f32[24,2,8,128]{3,2,1,0:T(8,128)S(1)} %fusion.16), channel_id=1, source_target_pairs={{2,0},{4,2},{6,4},{7,6},{5,7},{3,5},{1,3},{0,1},{10,8},{12,10},{14... | collective-permute-start | bytes 589832 | tf_op jit(solution)/shard_map/ppermute | solution.py:81
  60.2 1.6 %collective-permute-start.9 = (f32[24,2,8,128]{3,2,1,0:T(8,128)S(1)}, f32[24,2,8,128]{3,2,1,0:T(8,128)S(1)}, u32[]{:S(2)}, u32[]{:S(2)}) collective-permute-start(f32[24,2,8,128]{3,2,1,0:T(8,128)S(1)} %add.567), channel_id=1, source_target_pairs={{2,0},{4,2},{6,4},{7,6},{5,7},{3,5},{1,3},{0,1},{10,8},{12,10},{14... | collective-permute-start | bytes 589832 | tf_op jit(solution)/shard_map/ppermute | solution.py:81
  66.7 1.6 %collective-permute-start.19 = (f32[24,2,8,128]{3,2,1,0:T(8,128)S(1)}, f32[24,2,8,128]{3,2,1,0:T(8,128)S(1)}, u32[]{:S(2)}, u32[]{:S(2)}) collective-permute-start(f32[24,2,8,128]{3,2,1,0:T(8,128)S(1)} %fusion.96), channel_id=1, source_target_pairs={{2,0},{4,2},{6,4},{7,6},{5,7},{3,5},{1,3},{0,1},{10,8},{12,10},{14... | collective-permute-start | bytes 589832 | tf_op jit(solution)/shard_map/ppermute | solution.py:81
  70.8 1.6 %collective-permute-start.11 = (f32[24,2,8,128]{3,2,1,0:T(8,128)S(1)}, f32[24,2,8,128]{3,2,1,0:T(8,128)S(1)}, u32[]{:S(2)}, u32[]{:S(2)}) collective-permute-start(f32[24,2,8,128]{3,2,1,0:T(8,128)S(1)} %add.582), channel_id=1, source_target_pairs={{2,0},{4,2},{6,4},{7,6},{5,7},{3,5},{1,3},{0,1},{10,8},{12,10},{14... | collective-permute-start | bytes 589832 | tf_op jit(solution)/shard_map/ppermute | solution.py:81
  75.1 1.6 %collective-permute-start.21 = (f32[24,2,8,128]{3,2,1,0:T(8,128)S(1)}, f32[24,2,8,128]{3,2,1,0:T(8,128)S(1)}, u32[]{:S(2)}, u32[]{:S(2)}) collective-permute-start(f32[24,2,8,128]{3,2,1,0:T(8,128)S(1)} %add.622), channel_id=1, source_target_pairs={{2,0},{4,2},{6,4},{7,6},{5,7},{3,5},{1,3},{0,1},{10,8},{12,10},{14... | collective-permute-start | bytes 589832 | tf_op jit(solution)/shard_map/ppermute | solution.py:81
  79.6 1.6 %collective-permute-start.13 = (f32[24,2,8,128]{3,2,1,0:T(8,128)S(1)}, f32[24,2,8,128]{3,2,1,0:T(8,128)S(1)}, u32[]{:S(2)}, u32[]{:S(2)}) collective-permute-start(f32[24,2,8,128]{3,2,1,0:T(8,128)S(1)} %add.597), channel_id=1, source_target_pairs={{2,0},{4,2},{6,4},{7,6},{5,7},{3,5},{1,3},{0,1},{10,8},{12,10},{14... | collective-permute-start | bytes 589832 | tf_op jit(solution)/shard_map/ppermute | solution.py:81
  84.4 1.5 %collective-permute-start.23 = (f32[24,2,8,128]{3,2,1,0:T(8,128)S(1)}, f32[24,2,8,128]{3,2,1,0:T(8,128)S(1)}, u32[]{:S(2)}, u32[]{:S(2)}) collective-permute-start(f32[24,2,8,128]{3,2,1,0:T(8,128)S(1)} %add.624), channel_id=1, source_target_pairs={{2,0},{4,2},{6,4},{7,6},{5,7},{3,5},{1,3},{0,1},{10,8},{12,10},{14... | collective-permute-start | bytes 589832 | tf_op jit(solution)/shard_map/ppermute | solution.py:81
  89.6 1.5 %collective-permute-start.29 = (f32[24,2,8,128]{3,2,1,0:T(8,128)S(1)}, f32[24,2,8,128]{3,2,1,0:T(8,128)S(1)}, u32[]{:S(2)}, u32[]{:S(2)}) collective-permute-start(f32[24,2,8,128]{3,2,1,0:T(8,128)S(1)} %add.612), channel_id=1, source_target_pairs={{2,0},{4,2},{6,4},{7,6},{5,7},{3,5},{1,3},{0,1},{10,8},{12,10},{14... | collective-permute-start | bytes 589832 | tf_op jit(solution)/shard_map/ppermute | solution.py:81
  93.6 1.9 %collective-permute-start.25 = (f32[24,2,8,128]{3,2,1,0:T(8,128)S(1)}, f32[24,2,8,128]{3,2,1,0:T(8,128)S(1)}, u32[]{:S(2)}, u32[]{:S(2)}) collective-permute-start(f32[24,2,8,128]{3,2,1,0:T(8,128)S(1)} %add.626), channel_id=1, source_target_pairs={{2,0},{4,2},{6,4},{7,6},{5,7},{3,5},{1,3},{0,1},{10,8},{12,10},{14... | collective-permute-start | bytes 589832 | tf_op jit(solution)/shard_map/ppermute | solution.py:81
  97.8 3.0 %collective-permute-done.25 = f32[24,2,8,128]{3,2,1,0:T(8,128)S(1)} collective-permute-done((f32[24,2,8,128]{3,2,1,0:T(8,128)S(1)}, f32[24,2,8,128]{3,2,1,0:T(8,128)S(1)}, u32[]{:S(2)}, u32[]{:S(2)}) %collective-permute-start.25) | collective-permute-done | bytes 196640 | tf_op jit(solution)/shard_map/ppermute | solution.py:81
  100.8 1.4 %collective-permute-done.24 = f32[24,2,8,128]{3,2,1,0:T(8,128)S(1)} collective-permute-done((f32[24,2,8,128]{3,2,1,0:T(8,128)S(1)}, f32[24,2,8,128]{3,2,1,0:T(8,128)S(1)}, u32[]{:S(2)}, u32[]{:S(2)}) %collective-permute-start.24) | collective-permute-done | bytes 196640 | tf_op jit(solution)/shard_map/ppermute | solution.py:80
  102.4 1.5 %collective-permute-start.27 = (f32[24,2,8,128]{3,2,1,0:T(8,128)S(1)}, f32[24,2,8,128]{3,2,1,0:T(8,128)S(1)}, u32[]{:S(2)}, u32[]{:S(2)}) collective-permute-start(f32[24,2,8,128]{3,2,1,0:T(8,128)S(1)} %add.628), channel_id=1, source_target_pairs={{2,0},{4,2},{6,4},{7,6},{5,7},{3,5},{1,3},{0,1},{10,8},{12,10},{14... | collective-permute-start | bytes 589832 | tf_op jit(solution)/shard_map/ppermute | solution.py:81
  104.5 1.0 fusion.28
  106.4 2.0 %collective-permute-done.27 = f32[24,2,8,128]{3,2,1,0:T(8,128)S(1)} collective-permute-done((f32[24,2,8,128]{3,2,1,0:T(8,128)S(1)}, f32[24,2,8,128]{3,2,1,0:T(8,128)S(1)}, u32[]{:S(2)}, u32[]{:S(2)}) %collective-permute-start.27) | collective-permute-done | bytes 196640 | tf_op jit(solution)/shard_map/ppermute | solution.py:81
  108.4 1.1 collective-permute-done.26
  110.3 1.5 %collective-permute-start.30 = (f32[24,2,8,128]{3,2,1,0:T(8,128)S(1)}, f32[24,2,8,128]{3,2,1,0:T(8,128)S(1)}, u32[]{:S(2)}, u32[]{:S(2)}) collective-permute-start(f32[24,2,8,128]{3,2,1,0:T(8,128)S(1)} %add.630), channel_id=1, source_target_pairs={{2,0},{4,2},{6,4},{7,6},{5,7},{3,5},{1,3},{0,1},{10,8},{12,10},{14... | collective-permute-start | bytes 589832 | tf_op jit(solution)/shard_map/ppermute | solution.py:81
  111.7 1.0 fusion.29
  113.7 1.7 %collective-permute-done.28 = f32[24,2,8,128]{3,2,1,0:T(8,128)S(1)} collective-permute-done((f32[24,2,8,128]{3,2,1,0:T(8,128)S(1)}, f32[24,2,8,128]{3,2,1,0:T(8,128)S(1)}, u32[]{:S(2)}, u32[]{:S(2)}) %collective-permute-start.28) | collective-permute-done | bytes 196640 | tf_op jit(solution)/shard_map/ppermute | solution.py:80
  (119 shorter events, 42.3 us)
Async XLA Ops:
  0.0 29.8 %copy-start = (bf16[2048,256]{1,0:T(8,128)(2,1)S(1)}, bf16[2048,256]{1,0:T(8,128)(2,1)}, u32[]{:S(2)}) copy-start(bf16[2048,256]{1,0:T(8,128)(2,1)} %param.8) | copy-start | bytes 3145732
  0.0 31.1 %collective-permute-start = (bf16[384,2048]{1,0:T(8,128)(2,1)}, bf16[384,2048]{1,0:T(8,128)(2,1)}, u32[]{:S(2)}, u32[]{:S(2)}) collective-permute-start(bf16[384,2048]{1,0:T(8,128)(2,1)} %param.7), channel_id=1, source_target_pairs={{0,8},{8,0},{1,9},{9,1},{2,10},{10,2},{3,11},{11,3},{4,12},{12,4},... | collective-permute-start | bytes 4718600 | tf_op jit(solution)/shard_map/ppermute | solution.py:20
  1.5 28.3 %collective-permute-start.1 = (bf16[2048,128]{1,0:T(8,128)(2,1)S(1)}, bf16[2048,128]{1,0:T(8,128)(2,1)}, u32[]{:S(2)}, u32[]{:S(2)}) collective-permute-start(bf16[2048,128]{1,0:T(8,128)(2,1)S(1)} %slice.6), channel_id=1, source_target_pairs={{0,16},{16,0},{1,17},{17,1},{2,18},{18,2},{3,19},{19,3},{4,20},{20... | collective-permute-start | bytes 1572872 | tf_op jit(solution)/shard_map/ppermute | solution.py:20
  35.1 7.0 %collective-permute-start.3 = (f32[24,2,8,128]{3,2,1,0:T(8,128)S(1)}, f32[24,2,8,128]{3,2,1,0:T(8,128)S(1)}, u32[]{:S(2)}, u32[]{:S(2)}) collective-permute-start(f32[24,2,8,128]{3,2,1,0:T(8,128)S(1)} %fusion.1), channel_id=1, source_target_pairs={{2,0},{4,2},{6,4},{7,6},{5,7},{3,5},{1,3},{0,1},{10,8},{12,10},{14... | collective-permute-start | bytes 589832 | tf_op jit(solution)/shard_map/ppermute | solution.py:81
  36.6 6.7 %collective-permute-start.2 = (f32[24,2,8,128]{3,2,1,0:T(8,128)S(1)}, f32[24,2,8,128]{3,2,1,0:T(8,128)S(1)}, u32[]{:S(2)}, u32[]{:S(2)}) collective-permute-start(f32[24,2,8,128]{3,2,1,0:T(8,128)S(1)} %fusion), channel_id=1, source_target_pairs={{0,2},{2,4},{4,6},{6,7},{7,5},{5,3},{3,1},{1,0},{8,10},{10,12},{12... | collective-permute-start | bytes 589832 | tf_op jit(solution)/shard_map/ppermute | solution.py:80
  37.2 18.6 %collective-permute-start.15 = (bf16[2048,128]{1,0:T(8,128)(2,1)S(1)}, bf16[2048,128]{1,0:T(8,128)(2,1)S(1)}, u32[]{:S(2)}, u32[]{:S(2)}) collective-permute-start(bf16[2048,128]{1,0:T(8,128)(2,1)S(1)} %get-tuple-element.95), channel_id=1, source_target_pairs={{0,16},{16,0},{1,17},{17,1},{2,18},{18,2},{3,19},{19,3},{4,20},{20... | collective-permute-start | bytes 1572872 | tf_op jit(solution)/shard_map/ppermute | solution.py:20
  44.3 6.0 %collective-permute-start.5 = (f32[24,2,8,128]{3,2,1,0:T(8,128)S(1)}, f32[24,2,8,128]{3,2,1,0:T(8,128)S(1)}, u32[]{:S(2)}, u32[]{:S(2)}) collective-permute-start(f32[24,2,8,128]{3,2,1,0:T(8,128)S(1)} %fusion.98), channel_id=1, source_target_pairs={{2,0},{4,2},{6,4},{7,6},{5,7},{3,5},{1,3},{0,1},{10,8},{12,10},{14... | collective-permute-start | bytes 589832 | tf_op jit(solution)/shard_map/ppermute | solution.py:81
  45.9 5.7 %collective-permute-start.4 = (f32[24,2,8,128]{3,2,1,0:T(8,128)S(1)}, f32[24,2,8,128]{3,2,1,0:T(8,128)S(1)}, u32[]{:S(2)}, u32[]{:S(2)}) collective-permute-start(f32[24,2,8,128]{3,2,1,0:T(8,128)S(1)} %fusion.99), channel_id=1, source_target_pairs={{0,2},{2,4},{4,6},{6,7},{7,5},{5,3},{3,1},{1,0},{8,10},{10,12},{12... | collective-permute-start | bytes 589832 | tf_op jit(solution)/shard_map/ppermute | solution.py:80
  51.6 8.5 %collective-permute-start.7 = (f32[24,2,8,128]{3,2,1,0:T(8,128)S(1)}, f32[24,2,8,128]{3,2,1,0:T(8,128)S(1)}, u32[]{:S(2)}, u32[]{:S(2)}) collective-permute-start(f32[24,2,8,128]{3,2,1,0:T(8,128)S(1)} %add.552), channel_id=1, source_target_pairs={{2,0},{4,2},{6,4},{7,6},{5,7},{3,5},{1,3},{0,1},{10,8},{12,10},{14... | collective-permute-start | bytes 589832 | tf_op jit(solution)/shard_map/ppermute | solution.py:81
  53.3 6.9 %collective-permute-start.6 = (f32[24,2,8,128]{3,2,1,0:T(8,128)S(1)}, f32[24,2,8,128]{3,2,1,0:T(8,128)S(1)}, u32[]{:S(2)}, u32[]{:S(2)}) collective-permute-start(f32[24,2,8,128]{3,2,1,0:T(8,128)S(1)} %add.543), channel_id=1, source_target_pairs={{0,2},{2,4},{4,6},{6,7},{7,5},{5,3},{3,1},{1,0},{8,10},{10,12},{12... | collective-permute-start | bytes 589832 | tf_op jit(solution)/shard_map/ppermute | solution.py:80
  58.0 6.3 %collective-permute-start.17 = (f32[24,2,8,128]{3,2,1,0:T(8,128)S(1)}, f32[24,2,8,128]{3,2,1,0:T(8,128)S(1)}, u32[]{:S(2)}, u32[]{:S(2)}) collective-permute-start(f32[24,2,8,128]{3,2,1,0:T(8,128)S(1)} %fusion.16), channel_id=1, source_target_pairs={{2,0},{4,2},{6,4},{7,6},{5,7},{3,5},{1,3},{0,1},{10,8},{12,10},{14... | collective-permute-start | bytes 589832 | tf_op jit(solution)/shard_map/ppermute | solution.py:81
  59.7 6.0 %collective-permute-start.16 = (f32[24,2,8,128]{3,2,1,0:T(8,128)S(1)}, f32[24,2,8,128]{3,2,1,0:T(8,128)S(1)}, u32[]{:S(2)}, u32[]{:S(2)}) collective-permute-start(f32[24,2,8,128]{3,2,1,0:T(8,128)S(1)} %fusion.15), channel_id=1, source_target_pairs={{0,2},{2,4},{4,6},{6,7},{7,5},{5,3},{3,1},{1,0},{8,10},{10,12},{12... | collective-permute-start | bytes 589832 | tf_op jit(solution)/shard_map/ppermute | solution.py:80
  60.2 10.5 %collective-permute-start.9 = (f32[24,2,8,128]{3,2,1,0:T(8,128)S(1)}, f32[24,2,8,128]{3,2,1,0:T(8,128)S(1)}, u32[]{:S(2)}, u32[]{:S(2)}) collective-permute-start(f32[24,2,8,128]{3,2,1,0:T(8,128)S(1)} %add.567), channel_id=1, source_target_pairs={{2,0},{4,2},{6,4},{7,6},{5,7},{3,5},{1,3},{0,1},{10,8},{12,10},{14... | collective-permute-start | bytes 589832 | tf_op jit(solution)/shard_map/ppermute | solution.py:81
  61.8 9.0 %collective-permute-start.8 = (f32[24,2,8,128]{3,2,1,0:T(8,128)S(1)}, f32[24,2,8,128]{3,2,1,0:T(8,128)S(1)}, u32[]{:S(2)}, u32[]{:S(2)}) collective-permute-start(f32[24,2,8,128]{3,2,1,0:T(8,128)S(1)} %add.558), channel_id=1, source_target_pairs={{0,2},{2,4},{4,6},{6,7},{7,5},{5,3},{3,1},{1,0},{8,10},{10,12},{12... | collective-permute-start | bytes 589832 | tf_op jit(solution)/shard_map/ppermute | solution.py:80
  66.7 8.2 %collective-permute-start.19 = (f32[24,2,8,128]{3,2,1,0:T(8,128)S(1)}, f32[24,2,8,128]{3,2,1,0:T(8,128)S(1)}, u32[]{:S(2)}, u32[]{:S(2)}) collective-permute-start(f32[24,2,8,128]{3,2,1,0:T(8,128)S(1)} %fusion.96), channel_id=1, source_target_pairs={{2,0},{4,2},{6,4},{7,6},{5,7},{3,5},{1,3},{0,1},{10,8},{12,10},{14... | collective-permute-start | bytes 589832 | tf_op jit(solution)/shard_map/ppermute | solution.py:81
  68.3 6.7 %collective-permute-start.18 = (f32[24,2,8,128]{3,2,1,0:T(8,128)S(1)}, f32[24,2,8,128]{3,2,1,0:T(8,128)S(1)}, u32[]{:S(2)}, u32[]{:S(2)}) collective-permute-start(f32[24,2,8,128]{3,2,1,0:T(8,128)S(1)} %fusion.97), channel_id=1, source_target_pairs={{0,2},{2,4},{4,6},{6,7},{7,5},{5,3},{3,1},{1,0},{8,10},{10,12},{12... | collective-permute-start | bytes 589832 | tf_op jit(solution)/shard_map/ppermute | solution.py:80
  70.8 8.3 %collective-permute-start.11 = (f32[24,2,8,128]{3,2,1,0:T(8,128)S(1)}, f32[24,2,8,128]{3,2,1,0:T(8,128)S(1)}, u32[]{:S(2)}, u32[]{:S(2)}) collective-permute-start(f32[24,2,8,128]{3,2,1,0:T(8,128)S(1)} %add.582), channel_id=1, source_target_pairs={{2,0},{4,2},{6,4},{7,6},{5,7},{3,5},{1,3},{0,1},{10,8},{12,10},{14... | collective-permute-start | bytes 589832 | tf_op jit(solution)/shard_map/ppermute | solution.py:81
  72.4 7.2 %collective-permute-start.10 = (f32[24,2,8,128]{3,2,1,0:T(8,128)S(1)}, f32[24,2,8,128]{3,2,1,0:T(8,128)S(1)}, u32[]{:S(2)}, u32[]{:S(2)}) collective-permute-start(f32[24,2,8,128]{3,2,1,0:T(8,128)S(1)} %add.573), channel_id=1, source_target_pairs={{0,2},{2,4},{4,6},{6,7},{7,5},{5,3},{3,1},{1,0},{8,10},{10,12},{12... | collective-permute-start | bytes 589832 | tf_op jit(solution)/shard_map/ppermute | solution.py:80
  75.1 8.7 %collective-permute-start.21 = (f32[24,2,8,128]{3,2,1,0:T(8,128)S(1)}, f32[24,2,8,128]{3,2,1,0:T(8,128)S(1)}, u32[]{:S(2)}, u32[]{:S(2)}) collective-permute-start(f32[24,2,8,128]{3,2,1,0:T(8,128)S(1)} %add.622), channel_id=1, source_target_pairs={{2,0},{4,2},{6,4},{7,6},{5,7},{3,5},{1,3},{0,1},{10,8},{12,10},{14... | collective-permute-start | bytes 589832 | tf_op jit(solution)/shard_map/ppermute | solution.py:81
  76.7 7.6 %collective-permute-start.20 = (f32[24,2,8,128]{3,2,1,0:T(8,128)S(1)}, f32[24,2,8,128]{3,2,1,0:T(8,128)S(1)}, u32[]{:S(2)}, u32[]{:S(2)}) collective-permute-start(f32[24,2,8,128]{3,2,1,0:T(8,128)S(1)} %add.621), channel_id=1, source_target_pairs={{0,2},{2,4},{4,6},{6,7},{7,5},{5,3},{3,1},{1,0},{8,10},{10,12},{12... | collective-permute-start | bytes 589832 | tf_op jit(solution)/shard_map/ppermute | solution.py:80
  79.6 8.8 %collective-permute-start.13 = (f32[24,2,8,128]{3,2,1,0:T(8,128)S(1)}, f32[24,2,8,128]{3,2,1,0:T(8,128)S(1)}, u32[]{:S(2)}, u32[]{:S(2)}) collective-permute-start(f32[24,2,8,128]{3,2,1,0:T(8,128)S(1)} %add.597), channel_id=1, source_target_pairs={{2,0},{4,2},{6,4},{7,6},{5,7},{3,5},{1,3},{0,1},{10,8},{12,10},{14... | collective-permute-start | bytes 589832 | tf_op jit(solution)/shard_map/ppermute | solution.py:81
  81.2 7.8 %collective-permute-start.12 = (f32[24,2,8,128]{3,2,1,0:T(8,128)S(1)}, f32[24,2,8,128]{3,2,1,0:T(8,128)S(1)}, u32[]{:S(2)}, u32[]{:S(2)}) collective-permute-start(f32[24,2,8,128]{3,2,1,0:T(8,128)S(1)} %add.588), channel_id=1, source_target_pairs={{0,2},{2,4},{4,6},{6,7},{7,5},{5,3},{3,1},{1,0},{8,10},{10,12},{12... | collective-permute-start | bytes 589832 | tf_op jit(solution)/shard_map/ppermute | solution.py:80
  84.4 8.8 %collective-permute-start.23 = (f32[24,2,8,128]{3,2,1,0:T(8,128)S(1)}, f32[24,2,8,128]{3,2,1,0:T(8,128)S(1)}, u32[]{:S(2)}, u32[]{:S(2)}) collective-permute-start(f32[24,2,8,128]{3,2,1,0:T(8,128)S(1)} %add.624), channel_id=1, source_target_pairs={{2,0},{4,2},{6,4},{7,6},{5,7},{3,5},{1,3},{0,1},{10,8},{12,10},{14... | collective-permute-start | bytes 589832 | tf_op jit(solution)/shard_map/ppermute | solution.py:81
  85.9 7.7 %collective-permute-start.22 = (f32[24,2,8,128]{3,2,1,0:T(8,128)S(1)}, f32[24,2,8,128]{3,2,1,0:T(8,128)S(1)}, u32[]{:S(2)}, u32[]{:S(2)}) collective-permute-start(f32[24,2,8,128]{3,2,1,0:T(8,128)S(1)} %add.623), channel_id=1, source_target_pairs={{0,2},{2,4},{4,6},{6,7},{7,5},{5,3},{3,1},{1,0},{8,10},{10,12},{12... | collective-permute-start | bytes 589832 | tf_op jit(solution)/shard_map/ppermute | solution.py:80
  89.1 8.6 %collective-permute-start.14 = (f32[24,2,8,128]{3,2,1,0:T(8,128)S(1)}, f32[24,2,8,128]{3,2,1,0:T(8,128)S(1)}, u32[]{:S(2)}, u32[]{:S(2)}) collective-permute-start(f32[24,2,8,128]{3,2,1,0:T(8,128)S(1)} %add.603), channel_id=1, source_target_pairs={{0,2},{2,4},{4,6},{6,7},{7,5},{5,3},{3,1},{1,0},{8,10},{10,12},{12... | collective-permute-start | bytes 589832 | tf_op jit(solution)/shard_map/ppermute | solution.py:80
  89.6 8.1 %collective-permute-start.29 = (f32[24,2,8,128]{3,2,1,0:T(8,128)S(1)}, f32[24,2,8,128]{3,2,1,0:T(8,128)S(1)}, u32[]{:S(2)}, u32[]{:S(2)}) collective-permute-start(f32[24,2,8,128]{3,2,1,0:T(8,128)S(1)} %add.612), channel_id=1, source_target_pairs={{2,0},{4,2},{6,4},{7,6},{5,7},{3,5},{1,3},{0,1},{10,8},{12,10},{14... | collective-permute-start | bytes 589832 | tf_op jit(solution)/shard_map/ppermute | solution.py:81
  93.6 7.2 %collective-permute-start.25 = (f32[24,2,8,128]{3,2,1,0:T(8,128)S(1)}, f32[24,2,8,128]{3,2,1,0:T(8,128)S(1)}, u32[]{:S(2)}, u32[]{:S(2)}) collective-permute-start(f32[24,2,8,128]{3,2,1,0:T(8,128)S(1)} %add.626), channel_id=1, source_target_pairs={{2,0},{4,2},{6,4},{7,6},{5,7},{3,5},{1,3},{0,1},{10,8},{12,10},{14... | collective-permute-start | bytes 589832 | tf_op jit(solution)/shard_map/ppermute | solution.py:81
  95.5 6.7 %collective-permute-start.24 = (f32[24,2,8,128]{3,2,1,0:T(8,128)S(1)}, f32[24,2,8,128]{3,2,1,0:T(8,128)S(1)}, u32[]{:S(2)}, u32[]{:S(2)}) collective-permute-start(f32[24,2,8,128]{3,2,1,0:T(8,128)S(1)} %add.625), channel_id=1, source_target_pairs={{0,2},{2,4},{4,6},{6,7},{7,5},{5,3},{3,1},{1,0},{8,10},{10,12},{12... | collective-permute-start | bytes 589832 | tf_op jit(solution)/shard_map/ppermute | solution.py:80
  102.4 6.0 %collective-permute-start.27 = (f32[24,2,8,128]{3,2,1,0:T(8,128)S(1)}, f32[24,2,8,128]{3,2,1,0:T(8,128)S(1)}, u32[]{:S(2)}, u32[]{:S(2)}) collective-permute-start(f32[24,2,8,128]{3,2,1,0:T(8,128)S(1)} %add.628), channel_id=1, source_target_pairs={{2,0},{4,2},{6,4},{7,6},{5,7},{3,5},{1,3},{0,1},{10,8},{12,10},{14... | collective-permute-start | bytes 589832 | tf_op jit(solution)/shard_map/ppermute | solution.py:81
  103.9 5.7 %collective-permute-start.26 = (f32[24,2,8,128]{3,2,1,0:T(8,128)S(1)}, f32[24,2,8,128]{3,2,1,0:T(8,128)S(1)}, u32[]{:S(2)}, u32[]{:S(2)}) collective-permute-start(f32[24,2,8,128]{3,2,1,0:T(8,128)S(1)} %add.627), channel_id=1, source_target_pairs={{0,2},{2,4},{4,6},{6,7},{7,5},{5,3},{3,1},{1,0},{8,10},{10,12},{12... | collective-permute-start | bytes 589832 | tf_op jit(solution)/shard_map/ppermute | solution.py:80
  109.7 5.7 %collective-permute-start.28 = (f32[24,2,8,128]{3,2,1,0:T(8,128)S(1)}, f32[24,2,8,128]{3,2,1,0:T(8,128)S(1)}, u32[]{:S(2)}, u32[]{:S(2)}) collective-permute-start(f32[24,2,8,128]{3,2,1,0:T(8,128)S(1)} %add.629), channel_id=1, source_target_pairs={{0,2},{2,4},{4,6},{6,7},{7,5},{5,3},{3,1},{1,0},{8,10},{10,12},{12... | collective-permute-start | bytes 589832 | tf_op jit(solution)/shard_map/ppermute | solution.py:80
  110.3 5.7 %collective-permute-start.30 = (f32[24,2,8,128]{3,2,1,0:T(8,128)S(1)}, f32[24,2,8,128]{3,2,1,0:T(8,128)S(1)}, u32[]{:S(2)}, u32[]{:S(2)}) collective-permute-start(f32[24,2,8,128]{3,2,1,0:T(8,128)S(1)} %add.630), channel_id=1, source_target_pairs={{2,0},{4,2},{6,4},{7,6},{5,7},{3,5},{1,3},{0,1},{10,8},{12,10},{14... | collective-permute-start | bytes 589832 | tf_op jit(solution)/shard_map/ppermute | solution.py:81
  (1 other events, 18.0 us)

commit v9 on v8

--- a/solution.py
+++ b/solution.py
@@ -41,18 +41,23 @@
 
     def per_device(receivers, excitations, mode_freqs, mode_damping, sample_freqs):
         mode = lax.axis_index("mode")
+        real_weight, imag_weight = resonance(
+            mode_freqs[None, :], mode_damping[None, :], sample_freqs[:, None]
+        )
+        weights = jnp.stack([real_weight, imag_weight], axis=0)
+        if mode_count % 2:
+            position = mode
+        else:
+            position = jnp.where(mode % 2 == 0, mode // 2, mode_count - 1 - mode // 2)
+        receivers, excitations, weights, position = lax.optimization_barrier(
+            (receivers, excitations, weights, position)
+        )
         receiver_block = gather_blocks(receivers, "evt", sizes["evt"], 1)
         width = excitations.shape[1] // 2
         first_source = gather_blocks(excitations[:, :width], "sta", sizes["sta"], 0)
         row_count, block_modes = receiver_block.shape
-        real_weight, imag_weight = resonance(
-            mode_freqs[None, :], mode_damping[None, :], sample_freqs[:, None]
-        )
-        weights = jnp.stack([real_weight, imag_weight], axis=0)
         chunk = row_count // mode_count
         half = chunk // 2
-        order_table = jnp.asarray(order, dtype=jnp.int32)
-        position = jnp.asarray(position_of, dtype=jnp.int32)[mode]
 
         def partial_rows(owner, part, source_block, receiver_block=receiver_block):
             start = owner * chunk + part * half
@@ -65,7 +70,10 @@
             return product.reshape(half, 2, sample_freqs.shape[0], source_block.shape[1])
 
         def owner_at(offset):
-            return order_table[(position + offset) % mode_count]
+            place = (position + offset) % mode_count
+            if mode_count % 2:
+                return place
+            return jnp.where(place < mode_count // 2, 2 * place, 2 * (mode_count - 1 - place) + 1)
 
         def start(source, held=receiver_block):
             return (

time: 118 us -> 105 us (0.89)
  between operations: 21.3 us -> 0.68 us
  waiting for transfers between devices: 20.1 us -> 29.9 us
  local copies, waits for them, and re-layouts: 4.35 us -> 1.09 us
  starting transfers between devices: 32.4 us -> 34 us
    ppermute x3, waiting for transfers between devices: 0.01 us -> 12.7 us  [swap_pair(): return lax.ppermute(local, axis_name, [(0, 1), (1, 0)])]
    dynamic_slice x2 -> x0, local copies, waits for them, and re-layouts: 3.26 us -> none  [the longest x1 2.02 us: owner_at(): return order_table[(position + offset) % mode_count]]
    ppermute x14, waiting for transfers between devices: 12.2 us -> 9.17 us  [ring_step(): behind = lax.ppermute(sent_behind, 'mode', counter)]
    ppermute x3, starting transfers between devices: 3.24 us -> 4.86 us  [swap_pair(): return lax.ppermute(local, axis_name, [(0, 1), (1, 0)])]
    ppermute x14, starting transfers between devices: 6.73 us -> 5.5 us  [ring_step(): ahead = lax.ppermute(sent_ahead, 'mode', clockwise)]
    ppermute x14, starting transfers between devices: 22.4 us -> 23.6 us  [ring_step(): behind = lax.ppermute(sent_behind, 'mode', counter)]
where the time goes in v9:
time: 105 us
  starting transfers between devices  34 us (32%)
  matrix products  31.4 us (30%)
  waiting for transfers between devices  29.9 us (28%)
  other arithmetic  7.51 us (7%)
  local copies, waits for them, and re-layouts  1.09 us (1%)
    dot_general x32, matrix products, partial_rows(): jnp.dot(weighted.reshape(-1, block_modes), source_block, preferred_elemen...  31.4 us
    ppermute x14, starting transfers between devices, ring_step(): behind = lax.ppermute(sent_behind, 'mode', counter)  23.6 us
    ppermute x3, waiting for transfers between devices, swap_pair(): return lax.ppermute(local, axis_name, [(0, 1), (1, 0)])  12.7 us
    ppermute x14, waiting for transfers between devices, ring_step(): behind = lax.ppermute(sent_behind, 'mode', counter)  9.17 us
    ppermute x14, waiting for transfers between devices, ring_step(): ahead = lax.ppermute(sent_ahead, 'mode', clockwise)  8.07 us
    ppermute x14, starting transfers between devices, ring_step(): ahead = lax.ppermute(sent_ahead, 'mode', clockwise)  5.5 us
    ppermute x3, starting transfers between devices, swap_pair(): return lax.ppermute(local, axis_name, [(0, 1), (1, 0)])  4.86 us
    select_n x2, other arithmetic, gather_blocks(): first = jnp.where(index == 0, local, other)  2.76 us
  transfers between devices with their start and end apart: 31, of which 15 were waited for; matrix products, arithmetic and copies ran while one was open for 32% of the time, Pallas kernels for 0%

profile of v9, /device:TPU:0, one launch (start us, length us, event | category | flops | bytes accessed | tf_op | source)
XLA Modules:
  0.0 104.6 jit_solution(9146271746511758632)
XLA Ops:
  2.2 1.1 %slice.6 = bf16[2048,128]{1,0:T(8,128)(2,1)S(1)} slice(bf16[2048,256]{1,0:T(8,128)(2,1)} %param.6), slice={[0:2048], [0:128]} | slice | bytes 1048576 | tf_op jit(solution)/shard_map/slice | solution.py:57
  3.3 2.6 %collective-permute-start.1 = (bf16[2048,128]{1,0:T(8,128)(2,1)S(1)}, bf16[2048,128]{1,0:T(8,128)(2,1)}, u32[]{:S(2)}, u32[]{:S(2)}) collective-permute-start(bf16[2048,128]{1,0:T(8,128)(2,1)S(1)} %slice.6), channel_id=1, source_target_pairs={{0,16},{16,0},{1,17},{17,1},{2,18},{18,2},{3,19},{19,3},{4,20},{20... | collective-permute-start | bytes 1572872 | tf_op jit(solution)/shard_map/ppermute | solution.py:20
  5.9 12.7 %collective-permute-done.1 = bf16[2048,128]{1,0:T(8,128)(2,1)} collective-permute-done((bf16[2048,128]{1,0:T(8,128)(2,1)S(1)}, bf16[2048,128]{1,0:T(8,128)(2,1)}, u32[]{:S(2)}, u32[]{:S(2)}) %collective-permute-start.1) | collective-permute-done | bytes 524320 | tf_op jit(solution)/shard_map/ppermute | solution.py:20
  18.6 1.1 %broadcast_select_fusion.5 = (bf16[2048,128]{1,0:T(8,128)(2,1)S(1)}, bf16[2048,128]{1,0:T(8,128)(2,1)S(1)}, bf16[2048,128]{1,0:T(8,128)(2,1)S(1)}) fusion(bf16[2048,128]{1,0:T(8,128)(2,1)} %collective-permute-done.1, pred[]{:T(512)S(6)} %eq.49, bf16[2048,256]{1,0:T(8,128)(2,1)S(1)} %copy-done), kind=kLoop, calls=%fused_computation.177 | loop fusion | flops 524288 | bytes 3145729 | tf_op jit(solution)/shard_map/jit(_where)/select_n | solution.py:28
  19.9 1.6 %broadcast_select_fusion.1 = (bf16[384,2048]{1,0:T(8,128)(2,1)S(1)}, bf16[384,2048]{1,0:T(8,128)(2,1)S(1)}) fusion(bf16[384,2048]{1,0:T(8,128)(2,1)S(1)} %copy-done.1, bf16[384,2048]{1,0:T(8,128)(2,1)} %collective-permute-done, pred[]{:T(512)S(6)} %eq.47), kind=kLoop, calls=%fused_computation.134 | loop fusion | flops 1572864 | bytes 6291457 | tf_op jit(solution)/shard_map/jit(_where)/select_n | solution.py:28
  23.9 1.8 %collective-permute-start.3 = (f32[24,2,8,128]{3,2,1,0:T(8,128)S(1)}, f32[24,2,8,128]{3,2,1,0:T(8,128)S(1)}, u32[]{:S(2)}, u32[]{:S(2)}) collective-permute-start(f32[24,2,8,128]{3,2,1,0:T(8,128)S(1)} %fusion.1), channel_id=1, source_target_pairs={{2,0},{4,2},{6,4},{7,6},{5,7},{3,5},{1,3},{0,1},{10,8},{12,10},{14... | collective-permute-start | bytes 589832 | tf_op jit(solution)/shard_map/ppermute | solution.py:89
  26.0 1.7 %collective-permute-start.15 = (bf16[2048,128]{1,0:T(8,128)(2,1)S(1)}, bf16[2048,128]{1,0:T(8,128)(2,1)S(1)}, u32[]{:S(2)}, u32[]{:S(2)}) collective-permute-start(bf16[2048,128]{1,0:T(8,128)(2,1)S(1)} %get-tuple-element.103), channel_id=1, source_target_pairs={{0,16},{16,0},{1,17},{17,1},{2,18},{18,2},{3,19},{19,3},{4,20},{20... | collective-permute-start | bytes 1572872 | tf_op jit(solution)/shard_map/ppermute | solution.py:20
  27.8 2.9 %collective-permute-done.3 = f32[24,2,8,128]{3,2,1,0:T(8,128)S(1)} collective-permute-done((f32[24,2,8,128]{3,2,1,0:T(8,128)S(1)}, f32[24,2,8,128]{3,2,1,0:T(8,128)S(1)}, u32[]{:S(2)}, u32[]{:S(2)}) %collective-permute-start.3) | collective-permute-done | bytes 196640 | tf_op jit(solution)/shard_map/ppermute | solution.py:89
  30.6 1.0 fusion.98
  31.9 1.0 fusion.99
  32.9 1.6 %collective-permute-start.5 = (f32[24,2,8,128]{3,2,1,0:T(8,128)S(1)}, f32[24,2,8,128]{3,2,1,0:T(8,128)S(1)}, u32[]{:S(2)}, u32[]{:S(2)}) collective-permute-start(f32[24,2,8,128]{3,2,1,0:T(8,128)S(1)} %fusion.98), channel_id=1, source_target_pairs={{2,0},{4,2},{6,4},{7,6},{5,7},{3,5},{1,3},{0,1},{10,8},{12,10},{14... | collective-permute-start | bytes 589832 | tf_op jit(solution)/shard_map/ppermute | solution.py:89
  37.0 1.6 %collective-permute-done.5 = f32[24,2,8,128]{3,2,1,0:T(8,128)S(1)} collective-permute-done((f32[24,2,8,128]{3,2,1,0:T(8,128)S(1)}, f32[24,2,8,128]{3,2,1,0:T(8,128)S(1)}, u32[]{:S(2)}, u32[]{:S(2)}) %collective-permute-start.5) | collective-permute-done | bytes 196640 | tf_op jit(solution)/shard_map/ppermute | solution.py:89
  38.6 1.6 %collective-permute-done.4 = f32[24,2,8,128]{3,2,1,0:T(8,128)S(1)} collective-permute-done((f32[24,2,8,128]{3,2,1,0:T(8,128)S(1)}, f32[24,2,8,128]{3,2,1,0:T(8,128)S(1)}, u32[]{:S(2)}, u32[]{:S(2)}) %collective-permute-start.4) | collective-permute-done | bytes 196640 | tf_op jit(solution)/shard_map/ppermute | solution.py:88
  40.2 1.6 %collective-permute-start.7 = (f32[24,2,8,128]{3,2,1,0:T(8,128)S(1)}, f32[24,2,8,128]{3,2,1,0:T(8,128)S(1)}, u32[]{:S(2)}, u32[]{:S(2)}) collective-permute-start(f32[24,2,8,128]{3,2,1,0:T(8,128)S(1)} %add.445), channel_id=1, source_target_pairs={{2,0},{4,2},{6,4},{7,6},{5,7},{3,5},{1,3},{0,1},{10,8},{12,10},{14... | collective-permute-start | bytes 589832 | tf_op jit(solution)/shard_map/ppermute | solution.py:89
  46.6 1.6 %collective-permute-start.17 = (f32[24,2,8,128]{3,2,1,0:T(8,128)S(1)}, f32[24,2,8,128]{3,2,1,0:T(8,128)S(1)}, u32[]{:S(2)}, u32[]{:S(2)}) collective-permute-start(f32[24,2,8,128]{3,2,1,0:T(8,128)S(1)} %fusion.16), channel_id=1, source_target_pairs={{2,0},{4,2},{6,4},{7,6},{5,7},{3,5},{1,3},{0,1},{10,8},{12,10},{14... | collective-permute-start | bytes 589832 | tf_op jit(solution)/shard_map/ppermute | solution.py:89
  48.8 1.6 %collective-permute-start.9 = (f32[24,2,8,128]{3,2,1,0:T(8,128)S(1)}, f32[24,2,8,128]{3,2,1,0:T(8,128)S(1)}, u32[]{:S(2)}, u32[]{:S(2)}) collective-permute-start(f32[24,2,8,128]{3,2,1,0:T(8,128)S(1)} %add.456), channel_id=1, source_target_pairs={{2,0},{4,2},{6,4},{7,6},{5,7},{3,5},{1,3},{0,1},{10,8},{12,10},{14... | collective-permute-start | bytes 589832 | tf_op jit(solution)/shard_map/ppermute | solution.py:89
  52.9 1.0 fusion.96
  53.9 1.0 fusion.97
  55.0 1.6 %collective-permute-start.19 = (f32[24,2,8,128]{3,2,1,0:T(8,128)S(1)}, f32[24,2,8,128]{3,2,1,0:T(8,128)S(1)}, u32[]{:S(2)}, u32[]{:S(2)}) collective-permute-start(f32[24,2,8,128]{3,2,1,0:T(8,128)S(1)} %fusion.96), channel_id=1, source_target_pairs={{2,0},{4,2},{6,4},{7,6},{5,7},{3,5},{1,3},{0,1},{10,8},{12,10},{14... | collective-permute-start | bytes 589832 | tf_op jit(solution)/shard_map/ppermute | solution.py:89
  59.1 1.7 %collective-permute-start.11 = (f32[24,2,8,128]{3,2,1,0:T(8,128)S(1)}, f32[24,2,8,128]{3,2,1,0:T(8,128)S(1)}, u32[]{:S(2)}, u32[]{:S(2)}) collective-permute-start(f32[24,2,8,128]{3,2,1,0:T(8,128)S(1)} %add.467), channel_id=1, source_target_pairs={{2,0},{4,2},{6,4},{7,6},{5,7},{3,5},{1,3},{0,1},{10,8},{12,10},{14... | collective-permute-start | bytes 589832 | tf_op jit(solution)/shard_map/ppermute | solution.py:89
  63.4 1.7 %collective-permute-start.21 = (f32[24,2,8,128]{3,2,1,0:T(8,128)S(1)}, f32[24,2,8,128]{3,2,1,0:T(8,128)S(1)}, u32[]{:S(2)}, u32[]{:S(2)}) collective-permute-start(f32[24,2,8,128]{3,2,1,0:T(8,128)S(1)} %add.498), channel_id=1, source_target_pairs={{2,0},{4,2},{6,4},{7,6},{5,7},{3,5},{1,3},{0,1},{10,8},{12,10},{14... | collective-permute-start | bytes 589832 | tf_op jit(solution)/shard_map/ppermute | solution.py:89
  67.7 1.7 %collective-permute-start.13 = (f32[24,2,8,128]{3,2,1,0:T(8,128)S(1)}, f32[24,2,8,128]{3,2,1,0:T(8,128)S(1)}, u32[]{:S(2)}, u32[]{:S(2)}) collective-permute-start(f32[24,2,8,128]{3,2,1,0:T(8,128)S(1)} %add.478), channel_id=1, source_target_pairs={{2,0},{4,2},{6,4},{7,6},{5,7},{3,5},{1,3},{0,1},{10,8},{12,10},{14... | collective-permute-start | bytes 589832 | tf_op jit(solution)/shard_map/ppermute | solution.py:89
  72.5 1.7 %collective-permute-start.23 = (f32[24,2,8,128]{3,2,1,0:T(8,128)S(1)}, f32[24,2,8,128]{3,2,1,0:T(8,128)S(1)}, u32[]{:S(2)}, u32[]{:S(2)}) collective-permute-start(f32[24,2,8,128]{3,2,1,0:T(8,128)S(1)} %add.500), channel_id=1, source_target_pairs={{2,0},{4,2},{6,4},{7,6},{5,7},{3,5},{1,3},{0,1},{10,8},{12,10},{14... | collective-permute-start | bytes 589832 | tf_op jit(solution)/shard_map/ppermute | solution.py:89
  77.7 1.6 %collective-permute-start.29 = (f32[24,2,8,128]{3,2,1,0:T(8,128)S(1)}, f32[24,2,8,128]{3,2,1,0:T(8,128)S(1)}, u32[]{:S(2)}, u32[]{:S(2)}) collective-permute-start(f32[24,2,8,128]{3,2,1,0:T(8,128)S(1)} %add.489), channel_id=1, source_target_pairs={{2,0},{4,2},{6,4},{7,6},{5,7},{3,5},{1,3},{0,1},{10,8},{12,10},{14... | collective-permute-start | bytes 589832 | tf_op jit(solution)/shard_map/ppermute | solution.py:89
  81.7 1.8 %collective-permute-start.25 = (f32[24,2,8,128]{3,2,1,0:T(8,128)S(1)}, f32[24,2,8,128]{3,2,1,0:T(8,128)S(1)}, u32[]{:S(2)}, u32[]{:S(2)}) collective-permute-start(f32[24,2,8,128]{3,2,1,0:T(8,128)S(1)} %add.502), channel_id=1, source_target_pairs={{2,0},{4,2},{6,4},{7,6},{5,7},{3,5},{1,3},{0,1},{10,8},{12,10},{14... | collective-permute-start | bytes 589832 | tf_op jit(solution)/shard_map/ppermute | solution.py:89
  85.8 2.5 %collective-permute-done.25 = f32[24,2,8,128]{3,2,1,0:T(8,128)S(1)} collective-permute-done((f32[24,2,8,128]{3,2,1,0:T(8,128)S(1)}, f32[24,2,8,128]{3,2,1,0:T(8,128)S(1)}, u32[]{:S(2)}, u32[]{:S(2)}) %collective-permute-start.25) | collective-permute-done | bytes 196640 | tf_op jit(solution)/shard_map/ppermute | solution.py:89
  88.3 1.6 %collective-permute-done.24 = f32[24,2,8,128]{3,2,1,0:T(8,128)S(1)} collective-permute-done((f32[24,2,8,128]{3,2,1,0:T(8,128)S(1)}, f32[24,2,8,128]{3,2,1,0:T(8,128)S(1)}, u32[]{:S(2)}, u32[]{:S(2)}) %collective-permute-start.24) | collective-permute-done | bytes 196640 | tf_op jit(solution)/shard_map/ppermute | solution.py:88
  90.0 1.8 %collective-permute-start.27 = (f32[24,2,8,128]{3,2,1,0:T(8,128)S(1)}, f32[24,2,8,128]{3,2,1,0:T(8,128)S(1)}, u32[]{:S(2)}, u32[]{:S(2)}) collective-permute-start(f32[24,2,8,128]{3,2,1,0:T(8,128)S(1)} %add.504), channel_id=1, source_target_pairs={{2,0},{4,2},{6,4},{7,6},{5,7},{3,5},{1,3},{0,1},{10,8},{12,10},{14... | collective-permute-start | bytes 589832 | tf_op jit(solution)/shard_map/ppermute | solution.py:89
  94.1 1.9 %collective-permute-done.27 = f32[24,2,8,128]{3,2,1,0:T(8,128)S(1)} collective-permute-done((f32[24,2,8,128]{3,2,1,0:T(8,128)S(1)}, f32[24,2,8,128]{3,2,1,0:T(8,128)S(1)}, u32[]{:S(2)}, u32[]{:S(2)}) %collective-permute-start.27) | collective-permute-done | bytes 196640 | tf_op jit(solution)/shard_map/ppermute | solution.py:89
  96.1 1.4 %collective-permute-done.26 = f32[24,2,8,128]{3,2,1,0:T(8,128)S(1)} collective-permute-done((f32[24,2,8,128]{3,2,1,0:T(8,128)S(1)}, f32[24,2,8,128]{3,2,1,0:T(8,128)S(1)}, u32[]{:S(2)}, u32[]{:S(2)}) %collective-permute-start.26) | collective-permute-done | bytes 196640 | tf_op jit(solution)/shard_map/ppermute | solution.py:88
  98.0 1.7 %collective-permute-start.30 = (f32[24,2,8,128]{3,2,1,0:T(8,128)S(1)}, f32[24,2,8,128]{3,2,1,0:T(8,128)S(1)}, u32[]{:S(2)}, u32[]{:S(2)}) collective-permute-start(f32[24,2,8,128]{3,2,1,0:T(8,128)S(1)} %add.506), channel_id=1, source_target_pairs={{2,0},{4,2},{6,4},{7,6},{5,7},{3,5},{1,3},{0,1},{10,8},{12,10},{14... | collective-permute-start | bytes 589832 | tf_op jit(solution)/shard_map/ppermute | solution.py:89
  101.7 1.7 %collective-permute-done.28 = f32[24,2,8,128]{3,2,1,0:T(8,128)S(1)} collective-permute-done((f32[24,2,8,128]{3,2,1,0:T(8,128)S(1)}, f32[24,2,8,128]{3,2,1,0:T(8,128)S(1)}, u32[]{:S(2)}, u32[]{:S(2)}) %collective-permute-start.28) | collective-permute-done | bytes 196640 | tf_op jit(solution)/shard_map/ppermute | solution.py:88
  (117 shorter events, 40.3 us)
Async XLA Ops:
  0.0 18.6 %copy-start = (bf16[2048,256]{1,0:T(8,128)(2,1)S(1)}, bf16[2048,256]{1,0:T(8,128)(2,1)}, u32[]{:S(2)}) copy-start(bf16[2048,256]{1,0:T(8,128)(2,1)} %param.6) | copy-start | bytes 3145732
  1.7 18.1 %collective-permute-start = (bf16[384,2048]{1,0:T(8,128)(2,1)}, bf16[384,2048]{1,0:T(8,128)(2,1)}, u32[]{:S(2)}, u32[]{:S(2)}) collective-permute-start(bf16[384,2048]{1,0:T(8,128)(2,1)} %param.5), channel_id=1, source_target_pairs={{0,8},{8,0},{1,9},{9,1},{2,10},{10,2},{3,11},{11,3},{4,12},{12,4},... | collective-permute-start | bytes 4718600 | tf_op jit(solution)/shard_map/ppermute | solution.py:20
  3.3 15.3 %collective-permute-start.1 = (bf16[2048,128]{1,0:T(8,128)(2,1)S(1)}, bf16[2048,128]{1,0:T(8,128)(2,1)}, u32[]{:S(2)}, u32[]{:S(2)}) collective-permute-start(bf16[2048,128]{1,0:T(8,128)(2,1)S(1)} %slice.6), channel_id=1, source_target_pairs={{0,16},{16,0},{1,17},{17,1},{2,18},{18,2},{3,19},{19,3},{4,20},{20... | collective-permute-start | bytes 1572872 | tf_op jit(solution)/shard_map/ppermute | solution.py:20
  23.9 6.8 %collective-permute-start.3 = (f32[24,2,8,128]{3,2,1,0:T(8,128)S(1)}, f32[24,2,8,128]{3,2,1,0:T(8,128)S(1)}, u32[]{:S(2)}, u32[]{:S(2)}) collective-permute-start(f32[24,2,8,128]{3,2,1,0:T(8,128)S(1)} %fusion.1), channel_id=1, source_target_pairs={{2,0},{4,2},{6,4},{7,6},{5,7},{3,5},{1,3},{0,1},{10,8},{12,10},{14... | collective-permute-start | bytes 589832 | tf_op jit(solution)/shard_map/ppermute | solution.py:89
  25.6 6.2 %collective-permute-start.2 = (f32[24,2,8,128]{3,2,1,0:T(8,128)S(1)}, f32[24,2,8,128]{3,2,1,0:T(8,128)S(1)}, u32[]{:S(2)}, u32[]{:S(2)}) collective-permute-start(f32[24,2,8,128]{3,2,1,0:T(8,128)S(1)} %fusion), channel_id=1, source_target_pairs={{0,2},{2,4},{4,6},{6,7},{7,5},{5,3},{3,1},{1,0},{8,10},{10,12},{12... | collective-permute-start | bytes 589832 | tf_op jit(solution)/shard_map/ppermute | solution.py:88
  26.0 18.4 %collective-permute-start.15 = (bf16[2048,128]{1,0:T(8,128)(2,1)S(1)}, bf16[2048,128]{1,0:T(8,128)(2,1)S(1)}, u32[]{:S(2)}, u32[]{:S(2)}) collective-permute-start(bf16[2048,128]{1,0:T(8,128)(2,1)S(1)} %get-tuple-element.103), channel_id=1, source_target_pairs={{0,16},{16,0},{1,17},{17,1},{2,18},{18,2},{3,19},{19,3},{4,20},{20... | collective-permute-start | bytes 1572872 | tf_op jit(solution)/shard_map/ppermute | solution.py:20
  32.9 5.7 %collective-permute-start.5 = (f32[24,2,8,128]{3,2,1,0:T(8,128)S(1)}, f32[24,2,8,128]{3,2,1,0:T(8,128)S(1)}, u32[]{:S(2)}, u32[]{:S(2)}) collective-permute-start(f32[24,2,8,128]{3,2,1,0:T(8,128)S(1)} %fusion.98), channel_id=1, source_target_pairs={{2,0},{4,2},{6,4},{7,6},{5,7},{3,5},{1,3},{0,1},{10,8},{12,10},{14... | collective-permute-start | bytes 589832 | tf_op jit(solution)/shard_map/ppermute | solution.py:89
  34.5 5.7 %collective-permute-start.4 = (f32[24,2,8,128]{3,2,1,0:T(8,128)S(1)}, f32[24,2,8,128]{3,2,1,0:T(8,128)S(1)}, u32[]{:S(2)}, u32[]{:S(2)}) collective-permute-start(f32[24,2,8,128]{3,2,1,0:T(8,128)S(1)} %fusion.99), channel_id=1, source_target_pairs={{0,2},{2,4},{4,6},{6,7},{7,5},{5,3},{3,1},{1,0},{8,10},{10,12},{12... | collective-permute-start | bytes 589832 | tf_op jit(solution)/shard_map/ppermute | solution.py:88
  40.2 8.5 %collective-permute-start.7 = (f32[24,2,8,128]{3,2,1,0:T(8,128)S(1)}, f32[24,2,8,128]{3,2,1,0:T(8,128)S(1)}, u32[]{:S(2)}, u32[]{:S(2)}) collective-permute-start(f32[24,2,8,128]{3,2,1,0:T(8,128)S(1)} %add.445), channel_id=1, source_target_pairs={{2,0},{4,2},{6,4},{7,6},{5,7},{3,5},{1,3},{0,1},{10,8},{12,10},{14... | collective-permute-start | bytes 589832 | tf_op jit(solution)/shard_map/ppermute | solution.py:89
  41.8 6.9 %collective-permute-start.6 = (f32[24,2,8,128]{3,2,1,0:T(8,128)S(1)}, f32[24,2,8,128]{3,2,1,0:T(8,128)S(1)}, u32[]{:S(2)}, u32[]{:S(2)}) collective-permute-start(f32[24,2,8,128]{3,2,1,0:T(8,128)S(1)} %add.439), channel_id=1, source_target_pairs={{0,2},{2,4},{4,6},{6,7},{7,5},{5,3},{3,1},{1,0},{8,10},{10,12},{12... | collective-permute-start | bytes 589832 | tf_op jit(solution)/shard_map/ppermute | solution.py:88
  46.6 6.3 %collective-permute-start.17 = (f32[24,2,8,128]{3,2,1,0:T(8,128)S(1)}, f32[24,2,8,128]{3,2,1,0:T(8,128)S(1)}, u32[]{:S(2)}, u32[]{:S(2)}) collective-permute-start(f32[24,2,8,128]{3,2,1,0:T(8,128)S(1)} %fusion.16), channel_id=1, source_target_pairs={{2,0},{4,2},{6,4},{7,6},{5,7},{3,5},{1,3},{0,1},{10,8},{12,10},{14... | collective-permute-start | bytes 589832 | tf_op jit(solution)/shard_map/ppermute | solution.py:89
  48.2 5.7 %collective-permute-start.16 = (f32[24,2,8,128]{3,2,1,0:T(8,128)S(1)}, f32[24,2,8,128]{3,2,1,0:T(8,128)S(1)}, u32[]{:S(2)}, u32[]{:S(2)}) collective-permute-start(f32[24,2,8,128]{3,2,1,0:T(8,128)S(1)} %fusion.15), channel_id=1, source_target_pairs={{0,2},{2,4},{4,6},{6,7},{7,5},{5,3},{3,1},{1,0},{8,10},{10,12},{12... | collective-permute-start | bytes 589832 | tf_op jit(solution)/shard_map/ppermute | solution.py:88
  48.8 10.3 %collective-permute-start.9 = (f32[24,2,8,128]{3,2,1,0:T(8,128)S(1)}, f32[24,2,8,128]{3,2,1,0:T(8,128)S(1)}, u32[]{:S(2)}, u32[]{:S(2)}) collective-permute-start(f32[24,2,8,128]{3,2,1,0:T(8,128)S(1)} %add.456), channel_id=1, source_target_pairs={{2,0},{4,2},{6,4},{7,6},{5,7},{3,5},{1,3},{0,1},{10,8},{12,10},{14... | collective-permute-start | bytes 589832 | tf_op jit(solution)/shard_map/ppermute | solution.py:89
  50.4 8.7 %collective-permute-start.8 = (f32[24,2,8,128]{3,2,1,0:T(8,128)S(1)}, f32[24,2,8,128]{3,2,1,0:T(8,128)S(1)}, u32[]{:S(2)}, u32[]{:S(2)}) collective-permute-start(f32[24,2,8,128]{3,2,1,0:T(8,128)S(1)} %add.450), channel_id=1, source_target_pairs={{0,2},{2,4},{4,6},{6,7},{7,5},{5,3},{3,1},{1,0},{8,10},{10,12},{12... | collective-permute-start | bytes 589832 | tf_op jit(solution)/shard_map/ppermute | solution.py:88
  55.0 8.2 %collective-permute-start.19 = (f32[24,2,8,128]{3,2,1,0:T(8,128)S(1)}, f32[24,2,8,128]{3,2,1,0:T(8,128)S(1)}, u32[]{:S(2)}, u32[]{:S(2)}) collective-permute-start(f32[24,2,8,128]{3,2,1,0:T(8,128)S(1)} %fusion.96), channel_id=1, source_target_pairs={{2,0},{4,2},{6,4},{7,6},{5,7},{3,5},{1,3},{0,1},{10,8},{12,10},{14... | collective-permute-start | bytes 589832 | tf_op jit(solution)/shard_map/ppermute | solution.py:89
  56.6 6.6 %collective-permute-start.18 = (f32[24,2,8,128]{3,2,1,0:T(8,128)S(1)}, f32[24,2,8,128]{3,2,1,0:T(8,128)S(1)}, u32[]{:S(2)}, u32[]{:S(2)}) collective-permute-start(f32[24,2,8,128]{3,2,1,0:T(8,128)S(1)} %fusion.97), channel_id=1, source_target_pairs={{0,2},{2,4},{4,6},{6,7},{7,5},{5,3},{3,1},{1,0},{8,10},{10,12},{12... | collective-permute-start | bytes 589832 | tf_op jit(solution)/shard_map/ppermute | solution.py:88
  59.1 8.3 %collective-permute-start.11 = (f32[24,2,8,128]{3,2,1,0:T(8,128)S(1)}, f32[24,2,8,128]{3,2,1,0:T(8,128)S(1)}, u32[]{:S(2)}, u32[]{:S(2)}) collective-permute-start(f32[24,2,8,128]{3,2,1,0:T(8,128)S(1)} %add.467), channel_id=1, source_target_pairs={{2,0},{4,2},{6,4},{7,6},{5,7},{3,5},{1,3},{0,1},{10,8},{12,10},{14... | collective-permute-start | bytes 589832 | tf_op jit(solution)/shard_map/ppermute | solution.py:89
  60.8 6.9 %collective-permute-start.10 = (f32[24,2,8,128]{3,2,1,0:T(8,128)S(1)}, f32[24,2,8,128]{3,2,1,0:T(8,128)S(1)}, u32[]{:S(2)}, u32[]{:S(2)}) collective-permute-start(f32[24,2,8,128]{3,2,1,0:T(8,128)S(1)} %add.461), channel_id=1, source_target_pairs={{0,2},{2,4},{4,6},{6,7},{7,5},{5,3},{3,1},{1,0},{8,10},{10,12},{12... | collective-permute-start | bytes 589832 | tf_op jit(solution)/shard_map/ppermute | solution.py:88
  63.4 8.4 %collective-permute-start.21 = (f32[24,2,8,128]{3,2,1,0:T(8,128)S(1)}, f32[24,2,8,128]{3,2,1,0:T(8,128)S(1)}, u32[]{:S(2)}, u32[]{:S(2)}) collective-permute-start(f32[24,2,8,128]{3,2,1,0:T(8,128)S(1)} %add.498), channel_id=1, source_target_pairs={{2,0},{4,2},{6,4},{7,6},{5,7},{3,5},{1,3},{0,1},{10,8},{12,10},{14... | collective-permute-start | bytes 589832 | tf_op jit(solution)/shard_map/ppermute | solution.py:89
  65.0 7.4 %collective-permute-start.20 = (f32[24,2,8,128]{3,2,1,0:T(8,128)S(1)}, f32[24,2,8,128]{3,2,1,0:T(8,128)S(1)}, u32[]{:S(2)}, u32[]{:S(2)}) collective-permute-start(f32[24,2,8,128]{3,2,1,0:T(8,128)S(1)} %add.497), channel_id=1, source_target_pairs={{0,2},{2,4},{4,6},{6,7},{7,5},{5,3},{3,1},{1,0},{8,10},{10,12},{12... | collective-permute-start | bytes 589832 | tf_op jit(solution)/shard_map/ppermute | solution.py:88
  67.7 8.9 %collective-permute-start.13 = (f32[24,2,8,128]{3,2,1,0:T(8,128)S(1)}, f32[24,2,8,128]{3,2,1,0:T(8,128)S(1)}, u32[]{:S(2)}, u32[]{:S(2)}) collective-permute-start(f32[24,2,8,128]{3,2,1,0:T(8,128)S(1)} %add.478), channel_id=1, source_target_pairs={{2,0},{4,2},{6,4},{7,6},{5,7},{3,5},{1,3},{0,1},{10,8},{12,10},{14... | collective-permute-start | bytes 589832 | tf_op jit(solution)/shard_map/ppermute | solution.py:89
  69.4 7.8 %collective-permute-start.12 = (f32[24,2,8,128]{3,2,1,0:T(8,128)S(1)}, f32[24,2,8,128]{3,2,1,0:T(8,128)S(1)}, u32[]{:S(2)}, u32[]{:S(2)}) collective-permute-start(f32[24,2,8,128]{3,2,1,0:T(8,128)S(1)} %add.472), channel_id=1, source_target_pairs={{0,2},{2,4},{4,6},{6,7},{7,5},{5,3},{3,1},{1,0},{8,10},{10,12},{12... | collective-permute-start | bytes 589832 | tf_op jit(solution)/shard_map/ppermute | solution.py:88
  72.5 8.8 %collective-permute-start.23 = (f32[24,2,8,128]{3,2,1,0:T(8,128)S(1)}, f32[24,2,8,128]{3,2,1,0:T(8,128)S(1)}, u32[]{:S(2)}, u32[]{:S(2)}) collective-permute-start(f32[24,2,8,128]{3,2,1,0:T(8,128)S(1)} %add.500), channel_id=1, source_target_pairs={{2,0},{4,2},{6,4},{7,6},{5,7},{3,5},{1,3},{0,1},{10,8},{12,10},{14... | collective-permute-start | bytes 589832 | tf_op jit(solution)/shard_map/ppermute | solution.py:89
  74.3 7.3 %collective-permute-start.22 = (f32[24,2,8,128]{3,2,1,0:T(8,128)S(1)}, f32[24,2,8,128]{3,2,1,0:T(8,128)S(1)}, u32[]{:S(2)}, u32[]{:S(2)}) collective-permute-start(f32[24,2,8,128]{3,2,1,0:T(8,128)S(1)} %add.499), channel_id=1, source_target_pairs={{0,2},{2,4},{4,6},{6,7},{7,5},{5,3},{3,1},{1,0},{8,10},{10,12},{12... | collective-permute-start | bytes 589832 | tf_op jit(solution)/shard_map/ppermute | solution.py:88
  77.2 8.6 %collective-permute-start.14 = (f32[24,2,8,128]{3,2,1,0:T(8,128)S(1)}, f32[24,2,8,128]{3,2,1,0:T(8,128)S(1)}, u32[]{:S(2)}, u32[]{:S(2)}) collective-permute-start(f32[24,2,8,128]{3,2,1,0:T(8,128)S(1)} %add.483), channel_id=1, source_target_pairs={{0,2},{2,4},{4,6},{6,7},{7,5},{5,3},{3,1},{1,0},{8,10},{10,12},{12... | collective-permute-start | bytes 589832 | tf_op jit(solution)/shard_map/ppermute | solution.py:88
  77.7 8.1 %collective-permute-start.29 = (f32[24,2,8,128]{3,2,1,0:T(8,128)S(1)}, f32[24,2,8,128]{3,2,1,0:T(8,128)S(1)}, u32[]{:S(2)}, u32[]{:S(2)}) collective-permute-start(f32[24,2,8,128]{3,2,1,0:T(8,128)S(1)} %add.489), channel_id=1, source_target_pairs={{2,0},{4,2},{6,4},{7,6},{5,7},{3,5},{1,3},{0,1},{10,8},{12,10},{14... | collective-permute-start | bytes 589832 | tf_op jit(solution)/shard_map/ppermute | solution.py:89
  81.7 6.6 %collective-permute-start.25 = (f32[24,2,8,128]{3,2,1,0:T(8,128)S(1)}, f32[24,2,8,128]{3,2,1,0:T(8,128)S(1)}, u32[]{:S(2)}, u32[]{:S(2)}) collective-permute-start(f32[24,2,8,128]{3,2,1,0:T(8,128)S(1)} %add.502), channel_id=1, source_target_pairs={{2,0},{4,2},{6,4},{7,6},{5,7},{3,5},{1,3},{0,1},{10,8},{12,10},{14... | collective-permute-start | bytes 589832 | tf_op jit(solution)/shard_map/ppermute | solution.py:89
  83.5 6.5 %collective-permute-start.24 = (f32[24,2,8,128]{3,2,1,0:T(8,128)S(1)}, f32[24,2,8,128]{3,2,1,0:T(8,128)S(1)}, u32[]{:S(2)}, u32[]{:S(2)}) collective-permute-start(f32[24,2,8,128]{3,2,1,0:T(8,128)S(1)} %add.501), channel_id=1, source_target_pairs={{0,2},{2,4},{4,6},{6,7},{7,5},{5,3},{3,1},{1,0},{8,10},{10,12},{12... | collective-permute-start | bytes 589832 | tf_op jit(solution)/shard_map/ppermute | solution.py:88
  90.0 6.0 %collective-permute-start.27 = (f32[24,2,8,128]{3,2,1,0:T(8,128)S(1)}, f32[24,2,8,128]{3,2,1,0:T(8,128)S(1)}, u32[]{:S(2)}, u32[]{:S(2)}) collective-permute-start(f32[24,2,8,128]{3,2,1,0:T(8,128)S(1)} %add.504), channel_id=1, source_target_pairs={{2,0},{4,2},{6,4},{7,6},{5,7},{3,5},{1,3},{0,1},{10,8},{12,10},{14... | collective-permute-start | bytes 589832 | tf_op jit(solution)/shard_map/ppermute | solution.py:89
  91.8 5.7 %collective-permute-start.26 = (f32[24,2,8,128]{3,2,1,0:T(8,128)S(1)}, f32[24,2,8,128]{3,2,1,0:T(8,128)S(1)}, u32[]{:S(2)}, u32[]{:S(2)}) collective-permute-start(f32[24,2,8,128]{3,2,1,0:T(8,128)S(1)} %add.503), channel_id=1, source_target_pairs={{0,2},{2,4},{4,6},{6,7},{7,5},{5,3},{3,1},{1,0},{8,10},{10,12},{12... | collective-permute-start | bytes 589832 | tf_op jit(solution)/shard_map/ppermute | solution.py:88
  97.6 5.7 %collective-permute-start.28 = (f32[24,2,8,128]{3,2,1,0:T(8,128)S(1)}, f32[24,2,8,128]{3,2,1,0:T(8,128)S(1)}, u32[]{:S(2)}, u32[]{:S(2)}) collective-permute-start(f32[24,2,8,128]{3,2,1,0:T(8,128)S(1)} %add.505), channel_id=1, source_target_pairs={{0,2},{2,4},{4,6},{6,7},{7,5},{5,3},{3,1},{1,0},{8,10},{10,12},{12... | collective-permute-start | bytes 589832 | tf_op jit(solution)/shard_map/ppermute | solution.py:88
  98.0 5.7 %collective-permute-start.30 = (f32[24,2,8,128]{3,2,1,0:T(8,128)S(1)}, f32[24,2,8,128]{3,2,1,0:T(8,128)S(1)}, u32[]{:S(2)}, u32[]{:S(2)}) collective-permute-start(f32[24,2,8,128]{3,2,1,0:T(8,128)S(1)} %add.506), channel_id=1, source_target_pairs={{2,0},{4,2},{6,4},{7,6},{5,7},{3,5},{1,3},{0,1},{10,8},{12,10},{14... | collective-permute-start | bytes 589832 | tf_op jit(solution)/shard_map/ppermute | solution.py:89
  (1 other events, 16.5 us)

commit v10 on v5

--- a/solution.py
+++ b/solution.py
@@ -41,17 +41,22 @@
 
     def per_device(receivers, excitations, mode_freqs, mode_damping, sample_freqs):
         mode = lax.axis_index("mode")
-        receiver_block = lax.all_gather(receivers, "evt", axis=1, tiled=True)
-        source_block = gather_blocks(excitations, "sta", sizes["sta"], 0)
-        row_count, block_modes = receiver_block.shape
         real_weight, imag_weight = resonance(
             mode_freqs[None, :], mode_damping[None, :], sample_freqs[:, None]
         )
         weights = jnp.stack([real_weight, imag_weight], axis=0)
+        if mode_count % 2:
+            position = mode
+        else:
+            position = jnp.where(mode % 2 == 0, mode // 2, mode_count - 1 - mode // 2)
+        receivers, excitations, weights, position = lax.optimization_barrier(
+            (receivers, excitations, weights, position)
+        )
+        receiver_block = gather_blocks(receivers, "evt", sizes["evt"], 1)
+        source_block = gather_blocks(excitations, "sta", sizes["sta"], 0)
+        row_count, block_modes = receiver_block.shape
         chunk = row_count // mode_count
         half = chunk // 2
-        order_table = jnp.asarray(order, dtype=jnp.int32)
-        position = jnp.asarray(position_of, dtype=jnp.int32)[mode]
 
         def partial_rows(owner, part):
             start = owner * chunk + part * half
@@ -64,7 +69,10 @@
             return product.reshape(half, 2, sample_freqs.shape[0], source_block.shape[1])
 
         def owner_at(offset):
-            return order_table[(position + offset) % mode_count]
+            place = (position + offset) % mode_count
+            if mode_count % 2:
+                return place
+            return jnp.where(place < mode_count // 2, 2 * place, 2 * (mode_count - 1 - place) + 1)
 
         ahead = partial_rows(owner_at(-1), 0)
         behind = partial_rows(owner_at(1), 1)

time: 119 us -> 104 us (0.87)
  between operations: 34.2 us -> 0.26 us
  waiting for transfers between devices: 40.1 us -> 64.8 us
  local copies, waits for them, and re-layouts: 3.25 us -> 0.01 us
  other arithmetic: 7.01 us -> 5.58 us
    ppermute x1 -> x2, waiting for transfers between devices: 0.01 us -> 23.5 us  [swap_pair(): return lax.ppermute(local, axis_name, [(0, 1), (1, 0)])]
    dynamic_slice x2 -> x0, local copies, waits for them, and re-layouts: 3.25 us -> none  [the longest x1 2.01 us: owner_at(): return order_table[(position + offset) % mode_count]]
    ppermute x7, waiting for transfers between devices: 4.3 us -> 7.25 us  [per_device(): behind = lax.ppermute(behind, 'mode', counter)]
    convert_element_type x1 -> x3, other arithmetic: 2.54 us -> 0.61 us  [partial_rows(): widened = rows.astype(jnp.float32)]
    ppermute x7, starting transfers between devices: 4.08 us -> 2.84 us  [per_device(): behind = lax.ppermute(behind, 'mode', counter)]
    ppermute x1 -> x2, starting transfers between devices: 3.03 us -> 3.03 us  [swap_pair(): return lax.ppermute(local, axis_name, [(0, 1), (1, 0)])]
  transfers between devices with their start and end apart: 16 -> 16, of which waited for: 14 -> 15; matrix products, arithmetic and copies ran while one was open for 18% -> 17% of each run, Pallas kernels for 0% -> 0%
where the time goes in v10:
time: 104 us
  waiting for transfers between devices  64.8 us (62%)
  starting transfers between devices  17.4 us (17%)
  matrix products  15.6 us (15%)
  other arithmetic  5.58 us (5%)
    ppermute x7, waiting for transfers between devices, per_device(): ahead = lax.ppermute(ahead, 'mode', clockwise)  34 us
    ppermute x2, waiting for transfers between devices, swap_pair(): return lax.ppermute(local, axis_name, [(0, 1), (1, 0)])  23.5 us
    dot_general x16, matrix products, partial_rows(): jnp.dot(weighted.reshape(-1, block_modes), source_block, preferred_elemen...  15.6 us
    ppermute x7, starting transfers between devices, per_device(): ahead = lax.ppermute(ahead, 'mode', clockwise)  11.5 us
    ppermute x7, waiting for transfers between devices, per_device(): behind = lax.ppermute(behind, 'mode', counter)  7.25 us
    ppermute x2, starting transfers between devices, swap_pair(): return lax.ppermute(local, axis_name, [(0, 1), (1, 0)])  3.03 us
    ppermute x7, starting transfers between devices, per_device(): behind = lax.ppermute(behind, 'mode', counter)  2.84 us
  transfers between devices with their start and end apart: 16, of which 15 were waited for; matrix products, arithmetic and copies ran while one was open for 17% of the time, Pallas kernels for 0%

profile of v10, /device:TPU:0, one launch (start us, length us, event | category | flops | bytes accessed | tf_op | source)
XLA Modules:
  0.0 103.6 jit_solution(9335284960916783746)
XLA Ops:
  1.7 3.0 %collective-permute-start.1 = (bf16[2048,256]{1,0:T(8,128)(2,1)}, bf16[2048,256]{1,0:T(8,128)(2,1)}, u32[]{:S(2)}, u32[]{:S(2)}) collective-permute-start(bf16[2048,256]{1,0:T(8,128)(2,1)} %param.6), channel_id=1, source_target_pairs={{0,16},{16,0},{1,17},{17,1},{2,18},{18,2},{3,19},{19,3},{4,20},{20... | collective-permute-start | bytes 3145736 | tf_op jit(solution)/shard_map/ppermute | solution.py:20
  4.8 23.5 %collective-permute-done.1 = bf16[2048,256]{1,0:T(8,128)(2,1)} collective-permute-done((bf16[2048,256]{1,0:T(8,128)(2,1)}, bf16[2048,256]{1,0:T(8,128)(2,1)}, u32[]{:S(2)}, u32[]{:S(2)}) %collective-permute-start.1) | collective-permute-done | bytes 1048608 | tf_op jit(solution)/shard_map/ppermute | solution.py:20
  28.2 1.4 %broadcast_select_fusion.3 = (bf16[2048,256]{1,0:T(8,128)(2,1)S(1)}, bf16[2048,256]{1,0:T(8,128)(2,1)S(1)}) fusion(bf16[2048,256]{1,0:T(8,128)(2,1)S(1)} %copy-done.1, bf16[2048,256]{1,0:T(8,128)(2,1)} %collective-permute-done.1, pred[]{:T(512)S(6)} %eq.31), kind=kLoop, calls=%fused_computation.100 | loop fusion | flops 1048576 | bytes 4194305 | tf_op jit(solution)/shard_map/jit(_where)/select_n | solution.py:28
  30.1 1.0 fusion
  31.1 1.8 %collective-permute-start.2 = (f32[24,2,8,256]{3,2,1,0:T(8,128)S(1)}, f32[24,2,8,256]{3,2,1,0:T(8,128)S(1)}, u32[]{:S(2)}, u32[]{:S(2)}) collective-permute-start(f32[24,2,8,256]{3,2,1,0:T(8,128)S(1)} %fusion), channel_id=1, source_target_pairs={{0,2},{2,4},{4,6},{6,7},{7,5},{5,3},{3,1},{1,0},{8,10},{10,12},{12... | collective-permute-start | bytes 1179656 | tf_op jit(solution)/shard_map/ppermute | solution.py:80
  33.2 1.0 fusion.8
  34.6 1.0 fusion.1
  35.6 1.0 fusion.9
  36.5 4.9 %collective-permute-done.2 = f32[24,2,8,256]{3,2,1,0:T(8,128)S(1)} collective-permute-done((f32[24,2,8,256]{3,2,1,0:T(8,128)S(1)}, f32[24,2,8,256]{3,2,1,0:T(8,128)S(1)}, u32[]{:S(2)}, u32[]{:S(2)}) %collective-permute-start.2) | collective-permute-done | bytes 393248 | tf_op jit(solution)/shard_map/ppermute | solution.py:80
  41.5 1.5 %collective-permute-start.3 = (f32[24,2,8,256]{3,2,1,0:T(8,128)S(1)}, f32[24,2,8,256]{3,2,1,0:T(8,128)S(1)}, u32[]{:S(2)}, u32[]{:S(2)}) collective-permute-start(f32[24,2,8,256]{3,2,1,0:T(8,128)S(1)} %add.309), channel_id=1, source_target_pairs={{0,2},{2,4},{4,6},{6,7},{7,5},{5,3},{3,1},{1,0},{8,10},{10,12},{12... | collective-permute-start | bytes 1179656 | tf_op jit(solution)/shard_map/ppermute | solution.py:80
  45.5 1.0 fusion.10
  46.5 4.4 %collective-permute-done.3 = f32[24,2,8,256]{3,2,1,0:T(8,128)S(1)} collective-permute-done((f32[24,2,8,256]{3,2,1,0:T(8,128)S(1)}, f32[24,2,8,256]{3,2,1,0:T(8,128)S(1)}, u32[]{:S(2)}, u32[]{:S(2)}) %collective-permute-start.3) | collective-permute-done | bytes 393248 | tf_op jit(solution)/shard_map/ppermute | solution.py:80
  51.0 1.3 %collective-permute-start.4 = (f32[24,2,8,256]{3,2,1,0:T(8,128)S(1)}, f32[24,2,8,256]{3,2,1,0:T(8,128)S(1)}, u32[]{:S(2)}, u32[]{:S(2)}) collective-permute-start(f32[24,2,8,256]{3,2,1,0:T(8,128)S(1)} %add.314), channel_id=1, source_target_pairs={{0,2},{2,4},{4,6},{6,7},{7,5},{5,3},{3,1},{1,0},{8,10},{10,12},{12... | collective-permute-start | bytes 1179656 | tf_op jit(solution)/shard_map/ppermute | solution.py:80
  53.8 1.0 fusion.3
  54.8 1.0 fusion.11
  55.8 4.4 %collective-permute-done.4 = f32[24,2,8,256]{3,2,1,0:T(8,128)S(1)} collective-permute-done((f32[24,2,8,256]{3,2,1,0:T(8,128)S(1)}, f32[24,2,8,256]{3,2,1,0:T(8,128)S(1)}, u32[]{:S(2)}, u32[]{:S(2)}) %collective-permute-start.4) | collective-permute-done | bytes 393248 | tf_op jit(solution)/shard_map/ppermute | solution.py:80
  60.3 1.3 %collective-permute-start.5 = (f32[24,2,8,256]{3,2,1,0:T(8,128)S(1)}, f32[24,2,8,256]{3,2,1,0:T(8,128)S(1)}, u32[]{:S(2)}, u32[]{:S(2)}) collective-permute-start(f32[24,2,8,256]{3,2,1,0:T(8,128)S(1)} %add.319), channel_id=1, source_target_pairs={{0,2},{2,4},{4,6},{6,7},{7,5},{5,3},{3,1},{1,0},{8,10},{10,12},{12... | collective-permute-start | bytes 1179656 | tf_op jit(solution)/shard_map/ppermute | solution.py:80
  63.1 1.0 fusion.4
  65.1 4.8 %collective-permute-done.5 = f32[24,2,8,256]{3,2,1,0:T(8,128)S(1)} collective-permute-done((f32[24,2,8,256]{3,2,1,0:T(8,128)S(1)}, f32[24,2,8,256]{3,2,1,0:T(8,128)S(1)}, u32[]{:S(2)}, u32[]{:S(2)}) %collective-permute-start.5) | collective-permute-done | bytes 393248 | tf_op jit(solution)/shard_map/ppermute | solution.py:80
  69.9 1.6 %collective-permute-start.6 = (f32[24,2,8,256]{3,2,1,0:T(8,128)S(1)}, f32[24,2,8,256]{3,2,1,0:T(8,128)S(1)}, u32[]{:S(2)}, u32[]{:S(2)}) collective-permute-start(f32[24,2,8,256]{3,2,1,0:T(8,128)S(1)} %add.324), channel_id=1, source_target_pairs={{0,2},{2,4},{4,6},{6,7},{7,5},{5,3},{3,1},{1,0},{8,10},{10,12},{12... | collective-permute-start | bytes 1179656 | tf_op jit(solution)/shard_map/ppermute | solution.py:80
  72.7 1.0 fusion.5
  73.7 1.0 fusion.13
  74.7 5.6 %collective-permute-done.6 = f32[24,2,8,256]{3,2,1,0:T(8,128)S(1)} collective-permute-done((f32[24,2,8,256]{3,2,1,0:T(8,128)S(1)}, f32[24,2,8,256]{3,2,1,0:T(8,128)S(1)}, u32[]{:S(2)}, u32[]{:S(2)}) %collective-permute-start.6) | collective-permute-done | bytes 393248 | tf_op jit(solution)/shard_map/ppermute | solution.py:80
  80.4 1.8 %collective-permute-start.7 = (f32[24,2,8,256]{3,2,1,0:T(8,128)S(1)}, f32[24,2,8,256]{3,2,1,0:T(8,128)S(1)}, u32[]{:S(2)}, u32[]{:S(2)}) collective-permute-start(f32[24,2,8,256]{3,2,1,0:T(8,128)S(1)} %add.329), channel_id=1, source_target_pairs={{0,2},{2,4},{4,6},{6,7},{7,5},{5,3},{3,1},{1,0},{8,10},{10,12},{12... | collective-permute-start | bytes 1179656 | tf_op jit(solution)/shard_map/ppermute | solution.py:80
  83.2 1.0 fusion.6
  84.2 1.0 fusion.14
  85.2 6.6 %collective-permute-done.7 = f32[24,2,8,256]{3,2,1,0:T(8,128)S(1)} collective-permute-done((f32[24,2,8,256]{3,2,1,0:T(8,128)S(1)}, f32[24,2,8,256]{3,2,1,0:T(8,128)S(1)}, u32[]{:S(2)}, u32[]{:S(2)}) %collective-permute-start.7) | collective-permute-done | bytes 393248 | tf_op jit(solution)/shard_map/ppermute | solution.py:80
  91.8 2.1 %collective-permute-start.8 = (f32[24,2,8,256]{3,2,1,0:T(8,128)S(1)}, f32[24,2,8,256]{3,2,1,0:T(8,128)S(1)}, u32[]{:S(2)}, u32[]{:S(2)}) collective-permute-start(f32[24,2,8,256]{3,2,1,0:T(8,128)S(1)} %add.334), channel_id=1, source_target_pairs={{0,2},{2,4},{4,6},{6,7},{7,5},{5,3},{3,1},{1,0},{8,10},{10,12},{12... | collective-permute-start | bytes 1179656 | tf_op jit(solution)/shard_map/ppermute | solution.py:80
  95.0 1.0 fusion.7
  96.0 1.0 fusion.15
  97.0 3.4 %collective-permute-done.8 = f32[24,2,8,256]{3,2,1,0:T(8,128)S(1)} collective-permute-done((f32[24,2,8,256]{3,2,1,0:T(8,128)S(1)}, f32[24,2,8,256]{3,2,1,0:T(8,128)S(1)}, u32[]{:S(2)}, u32[]{:S(2)}) %collective-permute-start.8) | collective-permute-done | bytes 393248 | tf_op jit(solution)/shard_map/ppermute | solution.py:80
  100.4 2.2 %collective-permute-done.15 = f32[24,2,8,256]{3,2,1,0:T(8,128)S(1)} collective-permute-done((f32[24,2,8,256]{3,2,1,0:T(8,128)S(1)}, f32[24,2,8,256]{3,2,1,0:T(8,128)S(1)}, u32[]{:S(2)}, u32[]{:S(2)}) %collective-permute-start.15) | collective-permute-done | bytes 393248 | tf_op jit(solution)/shard_map/ppermute | solution.py:81
  (43 shorter events, 14.1 us)
Async XLA Ops:
  0.0 28.2 %copy-start.1 = (bf16[2048,256]{1,0:T(8,128)(2,1)S(1)}, bf16[2048,256]{1,0:T(8,128)(2,1)}, u32[]{:S(2)}) copy-start(bf16[2048,256]{1,0:T(8,128)(2,1)} %param.6) | copy-start | bytes 3145732
  1.7 26.5 %collective-permute-start.1 = (bf16[2048,256]{1,0:T(8,128)(2,1)}, bf16[2048,256]{1,0:T(8,128)(2,1)}, u32[]{:S(2)}, u32[]{:S(2)}) collective-permute-start(bf16[2048,256]{1,0:T(8,128)(2,1)} %param.6), channel_id=1, source_target_pairs={{0,16},{16,0},{1,17},{17,1},{2,18},{18,2},{3,19},{19,3},{4,20},{20... | collective-permute-start | bytes 3145736 | tf_op jit(solution)/shard_map/ppermute | solution.py:20
  4.7 24.9 %collective-permute-start = (bf16[384,2048]{1,0:T(8,128)(2,1)}, bf16[384,2048]{1,0:T(8,128)(2,1)S(1)}, u32[]{:S(2)}, u32[]{:S(2)}) collective-permute-start(bf16[384,2048]{1,0:T(8,128)(2,1)} %param.5), channel_id=1, source_target_pairs={{0,8},{8,0},{1,9},{9,1},{2,10},{10,2},{3,11},{11,3},{4,12},{12,4},... | collective-permute-start | bytes 4718600 | tf_op jit(solution)/shard_map/ppermute | solution.py:20
  4.7 24.9 %copy-start = (bf16[384,2048]{1,0:T(8,128)(2,1)S(1)}, bf16[384,2048]{1,0:T(8,128)(2,1)}, u32[]{:S(2)}) copy-start(bf16[384,2048]{1,0:T(8,128)(2,1)} %param.5) | copy-start | bytes 4718596
  31.1 10.4 %collective-permute-start.2 = (f32[24,2,8,256]{3,2,1,0:T(8,128)S(1)}, f32[24,2,8,256]{3,2,1,0:T(8,128)S(1)}, u32[]{:S(2)}, u32[]{:S(2)}) collective-permute-start(f32[24,2,8,256]{3,2,1,0:T(8,128)S(1)} %fusion), channel_id=1, source_target_pairs={{0,2},{2,4},{4,6},{6,7},{7,5},{5,3},{3,1},{1,0},{8,10},{10,12},{12... | collective-permute-start | bytes 1179656 | tf_op jit(solution)/shard_map/ppermute | solution.py:80
  34.1 9.8 %collective-permute-start.9 = (f32[24,2,8,256]{3,2,1,0:T(8,128)S(1)}, f32[24,2,8,256]{3,2,1,0:T(8,128)S(1)}, u32[]{:S(2)}, u32[]{:S(2)}) collective-permute-start(f32[24,2,8,256]{3,2,1,0:T(8,128)S(1)} %fusion.8), channel_id=1, source_target_pairs={{2,0},{4,2},{6,4},{7,6},{5,7},{3,5},{1,3},{0,1},{10,8},{12,10},{14... | collective-permute-start | bytes 1179656 | tf_op jit(solution)/shard_map/ppermute | solution.py:81
  41.5 9.4 %collective-permute-start.3 = (f32[24,2,8,256]{3,2,1,0:T(8,128)S(1)}, f32[24,2,8,256]{3,2,1,0:T(8,128)S(1)}, u32[]{:S(2)}, u32[]{:S(2)}) collective-permute-start(f32[24,2,8,256]{3,2,1,0:T(8,128)S(1)} %add.309), channel_id=1, source_target_pairs={{0,2},{2,4},{4,6},{6,7},{7,5},{5,3},{3,1},{1,0},{8,10},{10,12},{12... | collective-permute-start | bytes 1179656 | tf_op jit(solution)/shard_map/ppermute | solution.py:80
  44.0 9.2 %collective-permute-start.10 = (f32[24,2,8,256]{3,2,1,0:T(8,128)S(1)}, f32[24,2,8,256]{3,2,1,0:T(8,128)S(1)}, u32[]{:S(2)}, u32[]{:S(2)}) collective-permute-start(f32[24,2,8,256]{3,2,1,0:T(8,128)S(1)} %add.350), channel_id=1, source_target_pairs={{2,0},{4,2},{6,4},{7,6},{5,7},{3,5},{1,3},{0,1},{10,8},{12,10},{14... | collective-permute-start | bytes 1179656 | tf_op jit(solution)/shard_map/ppermute | solution.py:81
  51.0 9.2 %collective-permute-start.4 = (f32[24,2,8,256]{3,2,1,0:T(8,128)S(1)}, f32[24,2,8,256]{3,2,1,0:T(8,128)S(1)}, u32[]{:S(2)}, u32[]{:S(2)}) collective-permute-start(f32[24,2,8,256]{3,2,1,0:T(8,128)S(1)} %add.314), channel_id=1, source_target_pairs={{0,2},{2,4},{4,6},{6,7},{7,5},{5,3},{3,1},{1,0},{8,10},{10,12},{12... | collective-permute-start | bytes 1179656 | tf_op jit(solution)/shard_map/ppermute | solution.py:80
  53.2 9.0 %collective-permute-start.11 = (f32[24,2,8,256]{3,2,1,0:T(8,128)S(1)}, f32[24,2,8,256]{3,2,1,0:T(8,128)S(1)}, u32[]{:S(2)}, u32[]{:S(2)}) collective-permute-start(f32[24,2,8,256]{3,2,1,0:T(8,128)S(1)} %add.356), channel_id=1, source_target_pairs={{2,0},{4,2},{6,4},{7,6},{5,7},{3,5},{1,3},{0,1},{10,8},{12,10},{14... | collective-permute-start | bytes 1179656 | tf_op jit(solution)/shard_map/ppermute | solution.py:81
  60.3 9.6 %collective-permute-start.5 = (f32[24,2,8,256]{3,2,1,0:T(8,128)S(1)}, f32[24,2,8,256]{3,2,1,0:T(8,128)S(1)}, u32[]{:S(2)}, u32[]{:S(2)}) collective-permute-start(f32[24,2,8,256]{3,2,1,0:T(8,128)S(1)} %add.319), channel_id=1, source_target_pairs={{0,2},{2,4},{4,6},{6,7},{7,5},{5,3},{3,1},{1,0},{8,10},{10,12},{12... | collective-permute-start | bytes 1179656 | tf_op jit(solution)/shard_map/ppermute | solution.py:80
  62.3 10.0 %collective-permute-start.12 = (f32[24,2,8,256]{3,2,1,0:T(8,128)S(1)}, f32[24,2,8,256]{3,2,1,0:T(8,128)S(1)}, u32[]{:S(2)}, u32[]{:S(2)}) collective-permute-start(f32[24,2,8,256]{3,2,1,0:T(8,128)S(1)} %add.362), channel_id=1, source_target_pairs={{2,0},{4,2},{6,4},{7,6},{5,7},{3,5},{1,3},{0,1},{10,8},{12,10},{14... | collective-permute-start | bytes 1179656 | tf_op jit(solution)/shard_map/ppermute | solution.py:81
  69.9 10.4 %collective-permute-start.6 = (f32[24,2,8,256]{3,2,1,0:T(8,128)S(1)}, f32[24,2,8,256]{3,2,1,0:T(8,128)S(1)}, u32[]{:S(2)}, u32[]{:S(2)}) collective-permute-start(f32[24,2,8,256]{3,2,1,0:T(8,128)S(1)} %add.324), channel_id=1, source_target_pairs={{0,2},{2,4},{4,6},{6,7},{7,5},{5,3},{3,1},{1,0},{8,10},{10,12},{12... | collective-permute-start | bytes 1179656 | tf_op jit(solution)/shard_map/ppermute | solution.py:80
  72.4 10.7 %collective-permute-start.13 = (f32[24,2,8,256]{3,2,1,0:T(8,128)S(1)}, f32[24,2,8,256]{3,2,1,0:T(8,128)S(1)}, u32[]{:S(2)}, u32[]{:S(2)}) collective-permute-start(f32[24,2,8,256]{3,2,1,0:T(8,128)S(1)} %add.368), channel_id=1, source_target_pairs={{2,0},{4,2},{6,4},{7,6},{5,7},{3,5},{1,3},{0,1},{10,8},{12,10},{14... | collective-permute-start | bytes 1179656 | tf_op jit(solution)/shard_map/ppermute | solution.py:81
  80.4 11.4 %collective-permute-start.7 = (f32[24,2,8,256]{3,2,1,0:T(8,128)S(1)}, f32[24,2,8,256]{3,2,1,0:T(8,128)S(1)}, u32[]{:S(2)}, u32[]{:S(2)}) collective-permute-start(f32[24,2,8,256]{3,2,1,0:T(8,128)S(1)} %add.329), channel_id=1, source_target_pairs={{0,2},{2,4},{4,6},{6,7},{7,5},{5,3},{3,1},{1,0},{8,10},{10,12},{12... | collective-permute-start | bytes 1179656 | tf_op jit(solution)/shard_map/ppermute | solution.py:80
  83.2 11.6 %collective-permute-start.14 = (f32[24,2,8,256]{3,2,1,0:T(8,128)S(1)}, f32[24,2,8,256]{3,2,1,0:T(8,128)S(1)}, u32[]{:S(2)}, u32[]{:S(2)}) collective-permute-start(f32[24,2,8,256]{3,2,1,0:T(8,128)S(1)} %add.374), channel_id=1, source_target_pairs={{2,0},{4,2},{6,4},{7,6},{5,7},{3,5},{1,3},{0,1},{10,8},{12,10},{14... | collective-permute-start | bytes 1179656 | tf_op jit(solution)/shard_map/ppermute | solution.py:81
  91.8 8.5 %collective-permute-start.8 = (f32[24,2,8,256]{3,2,1,0:T(8,128)S(1)}, f32[24,2,8,256]{3,2,1,0:T(8,128)S(1)}, u32[]{:S(2)}, u32[]{:S(2)}) collective-permute-start(f32[24,2,8,256]{3,2,1,0:T(8,128)S(1)} %add.334), channel_id=1, source_target_pairs={{0,2},{2,4},{4,6},{6,7},{7,5},{5,3},{3,1},{1,0},{8,10},{10,12},{12... | collective-permute-start | bytes 1179656 | tf_op jit(solution)/shard_map/ppermute | solution.py:80
  94.8 7.8 %collective-permute-start.15 = (f32[24,2,8,256]{3,2,1,0:T(8,128)S(1)}, f32[24,2,8,256]{3,2,1,0:T(8,128)S(1)}, u32[]{:S(2)}, u32[]{:S(2)}) collective-permute-start(f32[24,2,8,256]{3,2,1,0:T(8,128)S(1)} %add.380), channel_id=1, source_target_pairs={{2,0},{4,2},{6,4},{7,6},{5,7},{3,5},{1,3},{0,1},{10,8},{12,10},{14... | collective-permute-start | bytes 1179656 | tf_op jit(solution)/shard_map/ppermute | solution.py:81

commit v11 on v9

--- a/solution.py
+++ b/solution.py
@@ -81,27 +81,28 @@
                 partial_rows(owner_at(1), 1, source, held),
             )
 
-        def ring_step(step, sums, source):
-            held, gated, sent_ahead, sent_behind = lax.optimization_barrier(
-                (receiver_block, source, sums[0], sums[1])
+        def send(sums):
+            return (
+                lax.ppermute(sums[0], "mode", clockwise),
+                lax.ppermute(sums[1], "mode", counter),
             )
-            ahead = lax.ppermute(sent_ahead, "mode", clockwise)
-            behind = lax.ppermute(sent_behind, "mode", counter)
+
+        def add(step, sums, source, held):
             return (
-                ahead + partial_rows(owner_at(-step - 2), 0, gated, held),
-                behind + partial_rows(owner_at(step + 2), 1, gated, held),
+                sums[0] + partial_rows(owner_at(-step - 2), 0, source, held),
+                sums[1] + partial_rows(owner_at(step + 2), 1, source, held),
             )
 
         steps = mode_count - 1
-        first = start(first_source)
-        second_local, first_ahead, first_behind = lax.optimization_barrier(
-            (excitations[:, width:], first[0], first[1])
-        )
+        second_local, _ = lax.optimization_barrier((excitations[:, width:], first_source))
         if sizes["sta"] == 2:
             second_far = swap_pair(second_local, "sta")
         else:
             second_far = lax.all_gather(second_local, "sta", axis=0, tiled=True)
-        first = ring_step(0, (first_ahead, first_behind), first_source)
+        held, gated, ahead, behind = lax.optimization_barrier(
+            (receiver_block, first_source, *start(first_source))
+        )
+        first = add(0, send((ahead, behind)), gated, held)
         held, second_far, _, _ = lax.optimization_barrier(
             (receiver_block, second_far, first[0], first[1])
         )
@@ -118,9 +119,18 @@
             second_source = second_far
         second = start(second_source, held)
         for step in range(1, steps):
-            first = ring_step(step, first, first_source)
-            second = ring_step(step - 1, second, second_source)
-        second = ring_step(steps - 1, second, second_source)
+            held, gated, later, a1, b1, a2, b2 = lax.optimization_barrier(
+                (receiver_block, first_source, second_source, *first, *second)
+            )
+            ahead, behind = send(
+                (jnp.concatenate([a1, a2], axis=3), jnp.concatenate([b1, b2], axis=3))
+            )
+            first = add(step, (ahead[..., :width], behind[..., :width]), gated, held)
+            second = add(step - 1, (ahead[..., width:], behind[..., width:]), later, held)
+        held, later, a2, b2 = lax.optimization_barrier(
+            (receiver_block, second_source, *second)
+        )
+        second = add(steps - 1, send((a2, b2)), later, held)
         rows = [jnp.concatenate(parts, axis=3) for parts in zip(first, second)]
         return jnp.concatenate(rows, axis=0)
 

time: 105 us -> 116 us (1.10)
  waiting for transfers between devices: 29.9 us -> 52.1 us
  starting transfers between devices: 34 us -> 22.6 us
    ppermute x28 -> x16, waiting for transfers between devices: 17.2 us -> 39.4 us  [the longest x8 31.6 us: send(): lax.ppermute(sums[1], 'mode', counter)]
    ppermute x28 -> x16, starting transfers between devices: 29.1 us -> 17.6 us  [the longest x8 13.6 us: send(): lax.ppermute(sums[1], 'mode', counter)]
  transfers between devices with their start and end apart: 31 -> 19, of which waited for: 15 -> 15; matrix products, arithmetic and copies ran while one was open for 32% -> 24% of each run, Pallas kernels for 0% -> 0%
where the time goes in v11:
time: 116 us; the launch traced here: 115 us
  waiting for transfers between devices  52.1 us (45%)
  matrix products  31.6 us (27%)
  starting transfers between devices  22.6 us (19%)
  other arithmetic  7.32 us (6%)
    ppermute x8, waiting for transfers between devices, send(): lax.ppermute(sums[1], 'mode', counter)  31.6 us
    dot_general x32, matrix products, partial_rows(): jnp.dot(weighted.reshape(-1, block_modes), source_block, preferred_elemen...  31.6 us
    ppermute x8, starting transfers between devices, send(): lax.ppermute(sums[1], 'mode', counter)  13.6 us
    ppermute x3, waiting for transfers between devices, swap_pair(): return lax.ppermute(local, axis_name, [(0, 1), (1, 0)])  12.7 us
    ppermute x8, waiting for transfers between devices, send(): lax.ppermute(sums[0], 'mode', clockwise)  7.8 us
    ppermute x3, starting transfers between devices, swap_pair(): return lax.ppermute(local, axis_name, [(0, 1), (1, 0)])  4.92 us
    ppermute x8, starting transfers between devices, send(): lax.ppermute(sums[0], 'mode', clockwise)  4.03 us
    select_n x2, other arithmetic, gather_blocks(): first = jnp.where(index == 0, local, other)  2.76 us
  transfers between devices with their start and end apart: 19, of which 15 were waited for; matrix products, arithmetic and copies ran while one was open for 24% of the time, Pallas kernels for 0%

profile of v11, /device:TPU:0, one launch (start us, length us, event | category | flops | bytes accessed | tf_op | source)
XLA Modules:
  0.0 115.2 jit_solution(10791530513511655962)
XLA Ops:
  2.2 1.1 slice.78
  3.3 2.6 %collective-permute-start.1 = (bf16[2048,128]{1,0:T(8,128)(2,1)S(1)}, bf16[2048,128]{1,0:T(8,128)(2,1)}, u32[]{:S(2)}, u32[]{:S(2)}) collective-permute-start(bf16[2048,128]{1,0:T(8,128)(2,1)S(1)} %slice.78), channel_id=1, source_target_pairs={{0,16},{16,0},{1,17},{17,1},{2,18},{18,2},{3,19},{19,3},{4,20},{20... | collective-permute-start | bytes 1572872 | tf_op jit(solution)/shard_map/ppermute | solution.py:20
  5.9 12.7 %collective-permute-done.1 = bf16[2048,128]{1,0:T(8,128)(2,1)} collective-permute-done((bf16[2048,128]{1,0:T(8,128)(2,1)S(1)}, bf16[2048,128]{1,0:T(8,128)(2,1)}, u32[]{:S(2)}, u32[]{:S(2)}) %collective-permute-start.1) | collective-permute-done | bytes 524320 | tf_op jit(solution)/shard_map/ppermute | solution.py:20
  18.6 1.1 broadcast_select_fusion.5
  19.8 1.8 %collective-permute-start.2 = (bf16[2048,128]{1,0:T(8,128)(2,1)S(1)}, bf16[2048,128]{1,0:T(8,128)(2,1)S(1)}, u32[]{:S(2)}, u32[]{:S(2)}) collective-permute-start(bf16[2048,128]{1,0:T(8,128)(2,1)S(1)} %get-tuple-element.64), channel_id=1, source_target_pairs={{0,16},{16,0},{1,17},{17,1},{2,18},{18,2},{3,19},{19,3},{4,20},{20... | collective-permute-start | bytes 1572872 | tf_op jit(solution)/shard_map/ppermute | solution.py:20
  21.6 1.6 %broadcast_select_fusion.1 = (bf16[384,2048]{1,0:T(8,128)(2,1)S(1)}, bf16[384,2048]{1,0:T(8,128)(2,1)S(1)}) fusion(bf16[384,2048]{1,0:T(8,128)(2,1)S(1)} %copy-done.1, bf16[384,2048]{1,0:T(8,128)(2,1)} %collective-permute-done, pred[]{:T(512)S(6)} %eq.47), kind=kLoop, calls=%fused_computation.134 | loop fusion | flops 1572864 | bytes 6291457 | tf_op jit(solution)/shard_map/jit(_where)/select_n | solution.py:28
  25.7 1.5 %collective-permute-start.4 = (f32[24,2,8,128]{3,2,1,0:T(8,128)S(1)}, f32[24,2,8,128]{3,2,1,0:T(8,128)S(1)}, u32[]{:S(2)}, u32[]{:S(2)}) collective-permute-start(f32[24,2,8,128]{3,2,1,0:T(8,128)S(1)} %fusion.1), channel_id=1, source_target_pairs={{2,0},{4,2},{6,4},{7,6},{5,7},{3,5},{1,3},{0,1},{10,8},{12,10},{14... | collective-permute-start | bytes 589832 | tf_op jit(solution)/shard_map/ppermute | solution.py:87
  27.8 4.2 %collective-permute-done.4 = f32[24,2,8,128]{3,2,1,0:T(8,128)S(1)} collective-permute-done((f32[24,2,8,128]{3,2,1,0:T(8,128)S(1)}, f32[24,2,8,128]{3,2,1,0:T(8,128)S(1)}, u32[]{:S(2)}, u32[]{:S(2)}) %collective-permute-start.4) | collective-permute-done | bytes 196640 | tf_op jit(solution)/shard_map/ppermute | solution.py:87
  32.0 1.0 fusion.98
  33.2 1.0 fusion.99
  36.4 1.6 %collective-permute-start.6 = (f32[24,2,8,256]{3,2,1,0:T(8,128)S(1)}, f32[24,2,8,256]{3,2,1,0:T(8,128)S(1)}, u32[]{:S(2)}, u32[]{:S(2)}) collective-permute-start(f32[24,2,8,256]{3,2,1,0:T(8,128)S(1)} %pad_maximum_fusion.4), channel_id=1, source_target_pairs={{2,0},{4,2},{6,4},{7,6},{5,7},{3,5},{1,3},{0,1},{10,8},{12,10},{14... | collective-permute-start | bytes 1179656 | tf_op jit(solution)/shard_map/ppermute | solution.py:87
  40.7 5.3 %collective-permute-done.6 = f32[24,2,8,256]{3,2,1,0:T(8,128)S(1)} collective-permute-done((f32[24,2,8,256]{3,2,1,0:T(8,128)S(1)}, f32[24,2,8,256]{3,2,1,0:T(8,128)S(1)}, u32[]{:S(2)}, u32[]{:S(2)}) %collective-permute-start.6) | collective-permute-done | bytes 393248 | tf_op jit(solution)/shard_map/ppermute | solution.py:87
  46.0 1.0 slice_add_fusion.20
  48.2 1.6 %collective-permute-start.8 = (f32[24,2,8,256]{3,2,1,0:T(8,128)S(1)}, f32[24,2,8,256]{3,2,1,0:T(8,128)S(1)}, u32[]{:S(2)}, u32[]{:S(2)}) collective-permute-start(f32[24,2,8,256]{3,2,1,0:T(8,128)S(1)} %pad_maximum_fusion.6), channel_id=1, source_target_pairs={{2,0},{4,2},{6,4},{7,6},{5,7},{3,5},{1,3},{0,1},{10,8},{12,10},{14... | collective-permute-start | bytes 1179656 | tf_op jit(solution)/shard_map/ppermute | solution.py:87
  52.6 4.1 %collective-permute-done.8 = f32[24,2,8,256]{3,2,1,0:T(8,128)S(1)} collective-permute-done((f32[24,2,8,256]{3,2,1,0:T(8,128)S(1)}, f32[24,2,8,256]{3,2,1,0:T(8,128)S(1)}, u32[]{:S(2)}, u32[]{:S(2)}) %collective-permute-start.8) | collective-permute-done | bytes 393248 | tf_op jit(solution)/shard_map/ppermute | solution.py:87
  56.7 1.0 slice_add_fusion.16
  58.9 1.7 %collective-permute-start.10 = (f32[24,2,8,256]{3,2,1,0:T(8,128)S(1)}, f32[24,2,8,256]{3,2,1,0:T(8,128)S(1)}, u32[]{:S(2)}, u32[]{:S(2)}) collective-permute-start(f32[24,2,8,256]{3,2,1,0:T(8,128)S(1)} %pad_maximum_fusion.8), channel_id=1, source_target_pairs={{2,0},{4,2},{6,4},{7,6},{5,7},{3,5},{1,3},{0,1},{10,8},{12,10},{14... | collective-permute-start | bytes 1179656 | tf_op jit(solution)/shard_map/ppermute | solution.py:87
  63.1 3.6 %collective-permute-done.10 = f32[24,2,8,256]{3,2,1,0:T(8,128)S(1)} collective-permute-done((f32[24,2,8,256]{3,2,1,0:T(8,128)S(1)}, f32[24,2,8,256]{3,2,1,0:T(8,128)S(1)}, u32[]{:S(2)}, u32[]{:S(2)}) %collective-permute-start.10) | collective-permute-done | bytes 393248 | tf_op jit(solution)/shard_map/ppermute | solution.py:87
  66.7 1.0 slice_add_fusion.12
  69.5 1.8 %collective-permute-start.12 = (f32[24,2,8,256]{3,2,1,0:T(8,128)S(1)}, f32[24,2,8,256]{3,2,1,0:T(8,128)S(1)}, u32[]{:S(2)}, u32[]{:S(2)}) collective-permute-start(f32[24,2,8,256]{3,2,1,0:T(8,128)S(1)} %pad_maximum_fusion.10), channel_id=1, source_target_pairs={{2,0},{4,2},{6,4},{7,6},{5,7},{3,5},{1,3},{0,1},{10,8},{12,10},{14... | collective-permute-start | bytes 1179656 | tf_op jit(solution)/shard_map/ppermute | solution.py:87
  74.0 3.7 %collective-permute-done.12 = f32[24,2,8,256]{3,2,1,0:T(8,128)S(1)} collective-permute-done((f32[24,2,8,256]{3,2,1,0:T(8,128)S(1)}, f32[24,2,8,256]{3,2,1,0:T(8,128)S(1)}, u32[]{:S(2)}, u32[]{:S(2)}) %collective-permute-start.12) | collective-permute-done | bytes 393248 | tf_op jit(solution)/shard_map/ppermute | solution.py:87
  78.6 1.5 %collective-permute-done.11 = f32[24,2,8,256]{3,2,1,0:T(8,128)S(1)} collective-permute-done((f32[24,2,8,256]{3,2,1,0:T(8,128)S(1)}, f32[24,2,8,256]{3,2,1,0:T(8,128)S(1)}, u32[]{:S(2)}, u32[]{:S(2)}) %collective-permute-start.11) | collective-permute-done | bytes 393248 | tf_op jit(solution)/shard_map/ppermute | solution.py:86
  81.2 2.0 %collective-permute-start.14 = (f32[24,2,8,256]{3,2,1,0:T(8,128)S(1)}, f32[24,2,8,256]{3,2,1,0:T(8,128)S(1)}, u32[]{:S(2)}, u32[]{:S(2)}) collective-permute-start(f32[24,2,8,256]{3,2,1,0:T(8,128)S(1)} %pad_maximum_fusion.12), channel_id=1, source_target_pairs={{2,0},{4,2},{6,4},{7,6},{5,7},{3,5},{1,3},{0,1},{10,8},{12,10},{14... | collective-permute-start | bytes 1179656 | tf_op jit(solution)/shard_map/ppermute | solution.py:87
  85.5 5.5 %collective-permute-done.14 = f32[24,2,8,256]{3,2,1,0:T(8,128)S(1)} collective-permute-done((f32[24,2,8,256]{3,2,1,0:T(8,128)S(1)}, f32[24,2,8,256]{3,2,1,0:T(8,128)S(1)}, u32[]{:S(2)}, u32[]{:S(2)}) %collective-permute-start.14) | collective-permute-done | bytes 393248 | tf_op jit(solution)/shard_map/ppermute | solution.py:87
  91.0 1.0 slice_add_fusion.4
  92.0 1.6 %collective-permute-done.13 = f32[24,2,8,256]{3,2,1,0:T(8,128)S(1)} collective-permute-done((f32[24,2,8,256]{3,2,1,0:T(8,128)S(1)}, f32[24,2,8,256]{3,2,1,0:T(8,128)S(1)}, u32[]{:S(2)}, u32[]{:S(2)}) %collective-permute-start.13) | collective-permute-done | bytes 393248 | tf_op jit(solution)/shard_map/ppermute | solution.py:86
  94.6 1.2 %collective-permute-start.16 = (f32[24,2,8,256]{3,2,1,0:T(8,128)S(1)}, f32[24,2,8,256]{3,2,1,0:T(8,128)S(1)}, u32[]{:S(2)}, u32[]{:S(2)}) collective-permute-start(f32[24,2,8,256]{3,2,1,0:T(8,128)S(1)} %pad_maximum_fusion.14), channel_id=1, source_target_pairs={{2,0},{4,2},{6,4},{7,6},{5,7},{3,5},{1,3},{0,1},{10,8},{12,10},{14... | collective-permute-start | bytes 1179656 | tf_op jit(solution)/shard_map/ppermute | solution.py:87
  95.8 1.2 %collective-permute-start.15 = (f32[24,2,8,256]{3,2,1,0:T(8,128)S(1)}, f32[24,2,8,256]{3,2,1,0:T(8,128)S(1)}, u32[]{:S(2)}, u32[]{:S(2)}) collective-permute-start(f32[24,2,8,256]{3,2,1,0:T(8,128)S(1)} %pad_maximum_fusion.13), channel_id=1, source_target_pairs={{0,2},{2,4},{4,6},{6,7},{7,5},{5,3},{3,1},{1,0},{8,10},{10,12},{12... | collective-permute-start | bytes 1179656 | tf_op jit(solution)/shard_map/ppermute | solution.py:86
  99.1 5.4 %collective-permute-done.16 = f32[24,2,8,256]{3,2,1,0:T(8,128)S(1)} collective-permute-done((f32[24,2,8,256]{3,2,1,0:T(8,128)S(1)}, f32[24,2,8,256]{3,2,1,0:T(8,128)S(1)}, u32[]{:S(2)}, u32[]{:S(2)}) %collective-permute-start.16) | collective-permute-done | bytes 393248 | tf_op jit(solution)/shard_map/ppermute | solution.py:87
  106.6 2.1 %collective-permute-start.18 = (f32[24,2,8,128]{3,2,1,0:T(8,128)S(1)}, f32[24,2,8,128]{3,2,1,0:T(8,128)S(1)}, u32[]{:S(2)}, u32[]{:S(2)}) collective-permute-start(f32[24,2,8,128]{3,2,1,0:T(8,128)S(1)} %get-tuple-element.118), channel_id=1, source_target_pairs={{2,0},{4,2},{6,4},{7,6},{5,7},{3,5},{1,3},{0,1},{10,8},{12,10},{14... | collective-permute-start | bytes 589832 | tf_op jit(solution)/shard_map/ppermute | solution.py:87
  108.7 3.5 %collective-permute-done.17 = f32[24,2,8,128]{3,2,1,0:T(8,128)S(1)} collective-permute-done((f32[24,2,8,128]{3,2,1,0:T(8,128)S(1)}, f32[24,2,8,128]{3,2,1,0:T(8,128)S(1)}, u32[]{:S(2)}, u32[]{:S(2)}) %collective-permute-start.17) | collective-permute-done | bytes 196640 | tf_op jit(solution)/shard_map/ppermute | solution.py:86
  113.2 1.0 fusion.96
  (75 shorter events, 33.7 us)
Async XLA Ops:
  0.0 18.6 %copy-start = (bf16[2048,256]{1,0:T(8,128)(2,1)S(1)}, bf16[2048,256]{1,0:T(8,128)(2,1)}, u32[]{:S(2)}) copy-start(bf16[2048,256]{1,0:T(8,128)(2,1)} %param.6) | copy-start | bytes 3145732
  1.7 19.9 %collective-permute-start = (bf16[384,2048]{1,0:T(8,128)(2,1)}, bf16[384,2048]{1,0:T(8,128)(2,1)}, u32[]{:S(2)}, u32[]{:S(2)}) collective-permute-start(bf16[384,2048]{1,0:T(8,128)(2,1)} %param.5), channel_id=1, source_target_pairs={{0,8},{8,0},{1,9},{9,1},{2,10},{10,2},{3,11},{11,3},{4,12},{12,4},... | collective-permute-start | bytes 4718600 | tf_op jit(solution)/shard_map/ppermute | solution.py:20
  3.3 18.3 %copy-start.1 = (bf16[384,2048]{1,0:T(8,128)(2,1)S(1)}, bf16[384,2048]{1,0:T(8,128)(2,1)}, u32[]{:S(2)}) copy-start(bf16[384,2048]{1,0:T(8,128)(2,1)} %param.5) | copy-start | bytes 4718596
  3.3 15.3 %collective-permute-start.1 = (bf16[2048,128]{1,0:T(8,128)(2,1)S(1)}, bf16[2048,128]{1,0:T(8,128)(2,1)}, u32[]{:S(2)}, u32[]{:S(2)}) collective-permute-start(bf16[2048,128]{1,0:T(8,128)(2,1)S(1)} %slice.78), channel_id=1, source_target_pairs={{0,16},{16,0},{1,17},{17,1},{2,18},{18,2},{3,19},{19,3},{4,20},{20... | collective-permute-start | bytes 1572872 | tf_op jit(solution)/shard_map/ppermute | solution.py:20
  19.8 14.3 %collective-permute-start.2 = (bf16[2048,128]{1,0:T(8,128)(2,1)S(1)}, bf16[2048,128]{1,0:T(8,128)(2,1)S(1)}, u32[]{:S(2)}, u32[]{:S(2)}) collective-permute-start(bf16[2048,128]{1,0:T(8,128)(2,1)S(1)} %get-tuple-element.64), channel_id=1, source_target_pairs={{0,16},{16,0},{1,17},{17,1},{2,18},{18,2},{3,19},{19,3},{4,20},{20... | collective-permute-start | bytes 1572872 | tf_op jit(solution)/shard_map/ppermute | solution.py:20
  25.7 6.3 %collective-permute-start.4 = (f32[24,2,8,128]{3,2,1,0:T(8,128)S(1)}, f32[24,2,8,128]{3,2,1,0:T(8,128)S(1)}, u32[]{:S(2)}, u32[]{:S(2)}) collective-permute-start(f32[24,2,8,128]{3,2,1,0:T(8,128)S(1)} %fusion.1), channel_id=1, source_target_pairs={{2,0},{4,2},{6,4},{7,6},{5,7},{3,5},{1,3},{0,1},{10,8},{12,10},{14... | collective-permute-start | bytes 589832 | tf_op jit(solution)/shard_map/ppermute | solution.py:87
  27.2 6.0 %collective-permute-start.3 = (f32[24,2,8,128]{3,2,1,0:T(8,128)S(1)}, f32[24,2,8,128]{3,2,1,0:T(8,128)S(1)}, u32[]{:S(2)}, u32[]{:S(2)}) collective-permute-start(f32[24,2,8,128]{3,2,1,0:T(8,128)S(1)} %fusion), channel_id=1, source_target_pairs={{0,2},{2,4},{4,6},{6,7},{7,5},{5,3},{3,1},{1,0},{8,10},{10,12},{12... | collective-permute-start | bytes 589832 | tf_op jit(solution)/shard_map/ppermute | solution.py:86
  36.4 9.6 %collective-permute-start.6 = (f32[24,2,8,256]{3,2,1,0:T(8,128)S(1)}, f32[24,2,8,256]{3,2,1,0:T(8,128)S(1)}, u32[]{:S(2)}, u32[]{:S(2)}) collective-permute-start(f32[24,2,8,256]{3,2,1,0:T(8,128)S(1)} %pad_maximum_fusion.4), channel_id=1, source_target_pairs={{2,0},{4,2},{6,4},{7,6},{5,7},{3,5},{1,3},{0,1},{10,8},{12,10},{14... | collective-permute-start | bytes 1179656 | tf_op jit(solution)/shard_map/ppermute | solution.py:87
  38.1 9.0 %collective-permute-start.5 = (f32[24,2,8,256]{3,2,1,0:T(8,128)S(1)}, f32[24,2,8,256]{3,2,1,0:T(8,128)S(1)}, u32[]{:S(2)}, u32[]{:S(2)}) collective-permute-start(f32[24,2,8,256]{3,2,1,0:T(8,128)S(1)} %pad_maximum_fusion.3), channel_id=1, source_target_pairs={{0,2},{2,4},{4,6},{6,7},{7,5},{5,3},{3,1},{1,0},{8,10},{10,12},{12... | collective-permute-start | bytes 1179656 | tf_op jit(solution)/shard_map/ppermute | solution.py:86
  48.2 8.5 %collective-permute-start.8 = (f32[24,2,8,256]{3,2,1,0:T(8,128)S(1)}, f32[24,2,8,256]{3,2,1,0:T(8,128)S(1)}, u32[]{:S(2)}, u32[]{:S(2)}) collective-permute-start(f32[24,2,8,256]{3,2,1,0:T(8,128)S(1)} %pad_maximum_fusion.6), channel_id=1, source_target_pairs={{2,0},{4,2},{6,4},{7,6},{5,7},{3,5},{1,3},{0,1},{10,8},{12,10},{14... | collective-permute-start | bytes 1179656 | tf_op jit(solution)/shard_map/ppermute | solution.py:87
  49.8 8.0 %collective-permute-start.7 = (f32[24,2,8,256]{3,2,1,0:T(8,128)S(1)}, f32[24,2,8,256]{3,2,1,0:T(8,128)S(1)}, u32[]{:S(2)}, u32[]{:S(2)}) collective-permute-start(f32[24,2,8,256]{3,2,1,0:T(8,128)S(1)} %pad_maximum_fusion.5), channel_id=1, source_target_pairs={{0,2},{2,4},{4,6},{6,7},{7,5},{5,3},{3,1},{1,0},{8,10},{10,12},{12... | collective-permute-start | bytes 1179656 | tf_op jit(solution)/shard_map/ppermute | solution.py:86
  58.9 7.8 %collective-permute-start.10 = (f32[24,2,8,256]{3,2,1,0:T(8,128)S(1)}, f32[24,2,8,256]{3,2,1,0:T(8,128)S(1)}, u32[]{:S(2)}, u32[]{:S(2)}) collective-permute-start(f32[24,2,8,256]{3,2,1,0:T(8,128)S(1)} %pad_maximum_fusion.8), channel_id=1, source_target_pairs={{2,0},{4,2},{6,4},{7,6},{5,7},{3,5},{1,3},{0,1},{10,8},{12,10},{14... | collective-permute-start | bytes 1179656 | tf_op jit(solution)/shard_map/ppermute | solution.py:87
  60.6 7.8 %collective-permute-start.9 = (f32[24,2,8,256]{3,2,1,0:T(8,128)S(1)}, f32[24,2,8,256]{3,2,1,0:T(8,128)S(1)}, u32[]{:S(2)}, u32[]{:S(2)}) collective-permute-start(f32[24,2,8,256]{3,2,1,0:T(8,128)S(1)} %pad_maximum_fusion.7), channel_id=1, source_target_pairs={{0,2},{2,4},{4,6},{6,7},{7,5},{5,3},{3,1},{1,0},{8,10},{10,12},{12... | collective-permute-start | bytes 1179656 | tf_op jit(solution)/shard_map/ppermute | solution.py:86
  69.5 8.2 %collective-permute-start.12 = (f32[24,2,8,256]{3,2,1,0:T(8,128)S(1)}, f32[24,2,8,256]{3,2,1,0:T(8,128)S(1)}, u32[]{:S(2)}, u32[]{:S(2)}) collective-permute-start(f32[24,2,8,256]{3,2,1,0:T(8,128)S(1)} %pad_maximum_fusion.10), channel_id=1, source_target_pairs={{2,0},{4,2},{6,4},{7,6},{5,7},{3,5},{1,3},{0,1},{10,8},{12,10},{14... | collective-permute-start | bytes 1179656 | tf_op jit(solution)/shard_map/ppermute | solution.py:87
  71.3 8.9 %collective-permute-start.11 = (f32[24,2,8,256]{3,2,1,0:T(8,128)S(1)}, f32[24,2,8,256]{3,2,1,0:T(8,128)S(1)}, u32[]{:S(2)}, u32[]{:S(2)}) collective-permute-start(f32[24,2,8,256]{3,2,1,0:T(8,128)S(1)} %pad_maximum_fusion.9), channel_id=1, source_target_pairs={{0,2},{2,4},{4,6},{6,7},{7,5},{5,3},{3,1},{1,0},{8,10},{10,12},{12... | collective-permute-start | bytes 1179656 | tf_op jit(solution)/shard_map/ppermute | solution.py:86
  81.2 9.7 %collective-permute-start.14 = (f32[24,2,8,256]{3,2,1,0:T(8,128)S(1)}, f32[24,2,8,256]{3,2,1,0:T(8,128)S(1)}, u32[]{:S(2)}, u32[]{:S(2)}) collective-permute-start(f32[24,2,8,256]{3,2,1,0:T(8,128)S(1)} %pad_maximum_fusion.12), channel_id=1, source_target_pairs={{2,0},{4,2},{6,4},{7,6},{5,7},{3,5},{1,3},{0,1},{10,8},{12,10},{14... | collective-permute-start | bytes 1179656 | tf_op jit(solution)/shard_map/ppermute | solution.py:87
  83.3 10.2 %collective-permute-start.13 = (f32[24,2,8,256]{3,2,1,0:T(8,128)S(1)}, f32[24,2,8,256]{3,2,1,0:T(8,128)S(1)}, u32[]{:S(2)}, u32[]{:S(2)}) collective-permute-start(f32[24,2,8,256]{3,2,1,0:T(8,128)S(1)} %pad_maximum_fusion.11), channel_id=1, source_target_pairs={{0,2},{2,4},{4,6},{6,7},{7,5},{5,3},{3,1},{1,0},{8,10},{10,12},{12... | collective-permute-start | bytes 1179656 | tf_op jit(solution)/shard_map/ppermute | solution.py:86
  94.6 9.9 %collective-permute-start.16 = (f32[24,2,8,256]{3,2,1,0:T(8,128)S(1)}, f32[24,2,8,256]{3,2,1,0:T(8,128)S(1)}, u32[]{:S(2)}, u32[]{:S(2)}) collective-permute-start(f32[24,2,8,256]{3,2,1,0:T(8,128)S(1)} %pad_maximum_fusion.14), channel_id=1, source_target_pairs={{2,0},{4,2},{6,4},{7,6},{5,7},{3,5},{1,3},{0,1},{10,8},{12,10},{14... | collective-permute-start | bytes 1179656 | tf_op jit(solution)/shard_map/ppermute | solution.py:87
  95.8 9.7 %collective-permute-start.15 = (f32[24,2,8,256]{3,2,1,0:T(8,128)S(1)}, f32[24,2,8,256]{3,2,1,0:T(8,128)S(1)}, u32[]{:S(2)}, u32[]{:S(2)}) collective-permute-start(f32[24,2,8,256]{3,2,1,0:T(8,128)S(1)} %pad_maximum_fusion.13), channel_id=1, source_target_pairs={{0,2},{2,4},{4,6},{6,7},{7,5},{5,3},{3,1},{1,0},{8,10},{10,12},{12... | collective-permute-start | bytes 1179656 | tf_op jit(solution)/shard_map/ppermute | solution.py:86
  106.5 5.7 %collective-permute-start.17 = (f32[24,2,8,128]{3,2,1,0:T(8,128)S(1)}, f32[24,2,8,128]{3,2,1,0:T(8,128)S(1)}, u32[]{:S(2)}, u32[]{:S(2)}) collective-permute-start(f32[24,2,8,128]{3,2,1,0:T(8,128)S(1)} %get-tuple-element.115), channel_id=1, source_target_pairs={{0,2},{2,4},{4,6},{6,7},{7,5},{5,3},{3,1},{1,0},{8,10},{10,12},{12... | collective-permute-start | bytes 589832 | tf_op jit(solution)/shard_map/ppermute | solution.py:86
  106.6 6.6 %collective-permute-start.18 = (f32[24,2,8,128]{3,2,1,0:T(8,128)S(1)}, f32[24,2,8,128]{3,2,1,0:T(8,128)S(1)}, u32[]{:S(2)}, u32[]{:S(2)}) collective-permute-start(f32[24,2,8,128]{3,2,1,0:T(8,128)S(1)} %get-tuple-element.118), channel_id=1, source_target_pairs={{2,0},{4,2},{6,4},{7,6},{5,7},{3,5},{1,3},{0,1},{10,8},{12,10},{14... | collective-permute-start | bytes 589832 | tf_op jit(solution)/shard_map/ppermute | solution.py:87

commit v12 on v10

--- a/solution.py
+++ b/solution.py
@@ -56,9 +56,9 @@
         source_block = gather_blocks(excitations, "sta", sizes["sta"], 0)
         row_count, block_modes = receiver_block.shape
         chunk = row_count // mode_count
-        half = chunk // 2
+        half = chunk // 4
 
-        def partial_rows(owner, part):
+        def partial_rows(owner, part, receiver_block=receiver_block):
             start = owner * chunk + part * half
             rows = lax.dynamic_slice_in_dim(receiver_block, start, half, axis=0)
             widened = rows.astype(jnp.float32)
@@ -74,14 +74,18 @@
                 return place
             return jnp.where(place < mode_count // 2, 2 * place, 2 * (mode_count - 1 - place) + 1)
 
-        ahead = partial_rows(owner_at(-1), 0)
-        behind = partial_rows(owner_at(1), 1)
+        ahead = [partial_rows(owner_at(-1), part) for part in (0, 1)]
+        behind = [partial_rows(owner_at(1), part) for part in (2, 3)]
         for step in range(mode_count - 1):
-            ahead = lax.ppermute(ahead, "mode", clockwise)
-            behind = lax.ppermute(behind, "mode", counter)
-            ahead = ahead + partial_rows(owner_at(-step - 2), 0)
-            behind = behind + partial_rows(owner_at(step + 2), 1)
-        return jnp.concatenate([ahead, behind], axis=0)
+            for i in range(2):
+                held, sent_ahead, sent_behind = lax.optimization_barrier(
+                    (receiver_block, ahead[i], behind[i])
+                )
+                ahead[i] = lax.ppermute(sent_ahead, "mode", clockwise)
+                behind[i] = lax.ppermute(sent_behind, "mode", counter)
+                ahead[i] = ahead[i] + partial_rows(owner_at(-step - 2), i, held)
+                behind[i] = behind[i] + partial_rows(owner_at(step + 2), 2 + i, held)
+        return jnp.concatenate(ahead + behind, axis=0)
 
     return per_device
 

time: 104 us -> 103 us (level)
  waiting for transfers between devices: 64.8 us -> 44.2 us
  starting transfers between devices: 17.4 us -> 32.5 us
  matrix products: 15.6 us -> 18.8 us
  other arithmetic: 5.58 us -> 6.97 us
    ppermute x14 -> x28, waiting for transfers between devices: 41.3 us -> 20.7 us  [the longest x14 14.2 us: per_device(): behind[i] = lax.ppermute(sent_behind, 'mode', counter)]
    ppermute x14 -> x28, starting transfers between devices: 14.3 us -> 29.5 us  [the longest x14 21 us: per_device(): ahead[i] = lax.ppermute(sent_ahead, 'mode', clockwise)]
    dot_general x16 -> x32, matrix products: 15.6 us -> 18.8 us  [partial_rows(): jnp.dot(weighted.reshape(-1, block_modes), source_block, preferred_elemen...]
  transfers between devices with their start and end apart: 16 -> 30, of which waited for: 15 -> 18; matrix products, arithmetic and copies ran while one was open for 17% -> 20% of each run, Pallas kernels for 0% -> 0%
where the time goes in v12:
time: 103 us
  waiting for transfers between devices  44.2 us (43%)
  starting transfers between devices  32.5 us (32%)
  matrix products  18.8 us (18%)
  other arithmetic  6.97 us (7%)
    ppermute x2, waiting for transfers between devices, swap_pair(): return lax.ppermute(local, axis_name, [(0, 1), (1, 0)])  23.5 us
    ppermute x14, starting transfers between devices, per_device(): ahead[i] = lax.ppermute(sent_ahead, 'mode', clockwise)  21 us
    dot_general x32, matrix products, partial_rows(): jnp.dot(weighted.reshape(-1, block_modes), source_block, preferred_elemen...  18.8 us
    ppermute x14, waiting for transfers between devices, per_device(): behind[i] = lax.ppermute(sent_behind, 'mode', counter)  14.2 us
    ppermute x14, starting transfers between devices, per_device(): behind[i] = lax.ppermute(sent_behind, 'mode', counter)  8.51 us
    ppermute x14, waiting for transfers between devices, per_device(): ahead[i] = lax.ppermute(sent_ahead, 'mode', clockwise)  6.46 us
    ppermute x2, starting transfers between devices, swap_pair(): return lax.ppermute(local, axis_name, [(0, 1), (1, 0)])  3.03 us
  transfers between devices with their start and end apart: 30, of which 18 were waited for; matrix products, arithmetic and copies ran while one was open for 20% of the time, Pallas kernels for 0%

profile of v12, /device:TPU:0, one launch (start us, length us, event | category | flops | bytes accessed | tf_op | source)
XLA Modules:
  0.0 103.0 jit_solution(8368780833493442547)
XLA Ops:
  1.8 3.0 %collective-permute-start.1 = (bf16[2048,256]{1,0:T(8,128)(2,1)}, bf16[2048,256]{1,0:T(8,128)(2,1)}, u32[]{:S(2)}, u32[]{:S(2)}) collective-permute-start(bf16[2048,256]{1,0:T(8,128)(2,1)} %param.6), channel_id=1, source_target_pairs={{0,16},{16,0},{1,17},{17,1},{2,18},{18,2},{3,19},{19,3},{4,20},{20... | collective-permute-start | bytes 3145736 | tf_op jit(solution)/shard_map/ppermute | solution.py:20
  4.8 23.5 %collective-permute-done.1 = bf16[2048,256]{1,0:T(8,128)(2,1)} collective-permute-done((bf16[2048,256]{1,0:T(8,128)(2,1)}, bf16[2048,256]{1,0:T(8,128)(2,1)}, u32[]{:S(2)}, u32[]{:S(2)}) %collective-permute-start.1) | collective-permute-done | bytes 1048608 | tf_op jit(solution)/shard_map/ppermute | solution.py:20
  28.3 1.7 %broadcast_select_fusion.3 = (bf16[2048,256]{1,0:T(8,128)(2,1)S(1)}, bf16[2048,256]{1,0:T(8,128)(2,1)S(1)}) fusion(bf16[2048,256]{1,0:T(8,128)(2,1)} %param.6, bf16[2048,256]{1,0:T(8,128)(2,1)} %collective-permute-done.1, pred[]{:T(512)S(6)} %eq.47), kind=kLoop, calls=%fused_computation.145 | loop fusion | flops 1048576 | bytes 4194305 | tf_op jit(solution)/shard_map/jit(_where)/select_n | solution.py:28
  32.2 1.8 %collective-permute-start.15 = (f32[12,2,8,256]{3,2,1,0:T(8,128)S(1)}, f32[12,2,8,256]{3,2,1,0:T(8,128)S(1)}, u32[]{:S(2)}, u32[]{:S(2)}) collective-permute-start(f32[12,2,8,256]{3,2,1,0:T(8,128)S(1)} %fusion.15), channel_id=1, source_target_pairs={{0,2},{2,4},{4,6},{6,7},{7,5},{5,3},{3,1},{1,0},{8,10},{10,12},{12... | collective-permute-start | bytes 589832 | tf_op jit(solution)/shard_map/ppermute | solution.py:84
  35.5 1.8 %collective-permute-start.2 = (f32[12,2,8,256]{3,2,1,0:T(8,128)S(1)}, f32[12,2,8,256]{3,2,1,0:T(8,128)S(1)}, u32[]{:S(2)}, u32[]{:S(2)}) collective-permute-start(f32[12,2,8,256]{3,2,1,0:T(8,128)S(1)} %fusion), channel_id=1, source_target_pairs={{0,2},{2,4},{4,6},{6,7},{7,5},{5,3},{3,1},{1,0},{8,10},{10,12},{12... | collective-permute-start | bytes 589832 | tf_op jit(solution)/shard_map/ppermute | solution.py:84
  37.7 2.1 %collective-permute-done.15 = f32[12,2,8,256]{3,2,1,0:T(8,128)S(1)} collective-permute-done((f32[12,2,8,256]{3,2,1,0:T(8,128)S(1)}, f32[12,2,8,256]{3,2,1,0:T(8,128)S(1)}, u32[]{:S(2)}, u32[]{:S(2)}) %collective-permute-start.15) | collective-permute-done | bytes 196640 | tf_op jit(solution)/shard_map/ppermute | solution.py:84
  40.5 1.0 %collective-permute-done.16 = f32[12,2,8,256]{3,2,1,0:T(8,128)S(1)} collective-permute-done((f32[12,2,8,256]{3,2,1,0:T(8,128)S(1)}, f32[12,2,8,256]{3,2,1,0:T(8,128)S(1)}, u32[]{:S(2)}, u32[]{:S(2)}) %collective-permute-start.16) | collective-permute-done | bytes 196640 | tf_op jit(solution)/shard_map/ppermute | solution.py:85
  42.1 1.6 %collective-permute-start.17 = (f32[12,2,8,256]{3,2,1,0:T(8,128)S(1)}, f32[12,2,8,256]{3,2,1,0:T(8,128)S(1)}, u32[]{:S(2)}, u32[]{:S(2)}) collective-permute-start(f32[12,2,8,256]{3,2,1,0:T(8,128)S(1)} %fusion.97), channel_id=1, source_target_pairs={{0,2},{2,4},{4,6},{6,7},{7,5},{5,3},{3,1},{1,0},{8,10},{10,12},{12... | collective-permute-start | bytes 589832 | tf_op jit(solution)/shard_map/ppermute | solution.py:84
  46.7 1.6 %collective-permute-start.4 = (f32[12,2,8,256]{3,2,1,0:T(8,128)S(1)}, f32[12,2,8,256]{3,2,1,0:T(8,128)S(1)}, u32[]{:S(2)}, u32[]{:S(2)}) collective-permute-start(f32[12,2,8,256]{3,2,1,0:T(8,128)S(1)} %fusion.99), channel_id=1, source_target_pairs={{0,2},{2,4},{4,6},{6,7},{7,5},{5,3},{3,1},{1,0},{8,10},{10,12},{12... | collective-permute-start | bytes 589832 | tf_op jit(solution)/shard_map/ppermute | solution.py:84
  50.1 1.2 %collective-permute-done.18 = f32[12,2,8,256]{3,2,1,0:T(8,128)S(1)} collective-permute-done((f32[12,2,8,256]{3,2,1,0:T(8,128)S(1)}, f32[12,2,8,256]{3,2,1,0:T(8,128)S(1)}, u32[]{:S(2)}, u32[]{:S(2)}) %collective-permute-start.18) | collective-permute-done | bytes 196640 | tf_op jit(solution)/shard_map/ppermute | solution.py:85
  51.3 1.7 %collective-permute-start.19 = (f32[12,2,8,256]{3,2,1,0:T(8,128)S(1)}, f32[12,2,8,256]{3,2,1,0:T(8,128)S(1)}, u32[]{:S(2)}, u32[]{:S(2)}) collective-permute-start(f32[12,2,8,256]{3,2,1,0:T(8,128)S(1)} %add.611), channel_id=1, source_target_pairs={{0,2},{2,4},{4,6},{6,7},{7,5},{5,3},{3,1},{1,0},{8,10},{10,12},{12... | collective-permute-start | bytes 589832 | tf_op jit(solution)/shard_map/ppermute | solution.py:84
  54.7 1.0 %collective-permute-done.5 = f32[12,2,8,256]{3,2,1,0:T(8,128)S(1)} collective-permute-done((f32[12,2,8,256]{3,2,1,0:T(8,128)S(1)}, f32[12,2,8,256]{3,2,1,0:T(8,128)S(1)}, u32[]{:S(2)}, u32[]{:S(2)}) %collective-permute-start.5) | collective-permute-done | bytes 196640 | tf_op jit(solution)/shard_map/ppermute | solution.py:85
  55.7 1.6 %collective-permute-start.6 = (f32[12,2,8,256]{3,2,1,0:T(8,128)S(1)}, f32[12,2,8,256]{3,2,1,0:T(8,128)S(1)}, u32[]{:S(2)}, u32[]{:S(2)}) collective-permute-start(f32[12,2,8,256]{3,2,1,0:T(8,128)S(1)} %add.543), channel_id=1, source_target_pairs={{0,2},{2,4},{4,6},{6,7},{7,5},{5,3},{3,1},{1,0},{8,10},{10,12},{12... | collective-permute-start | bytes 589832 | tf_op jit(solution)/shard_map/ppermute | solution.py:84
  59.4 1.3 %collective-permute-done.20 = f32[12,2,8,256]{3,2,1,0:T(8,128)S(1)} collective-permute-done((f32[12,2,8,256]{3,2,1,0:T(8,128)S(1)}, f32[12,2,8,256]{3,2,1,0:T(8,128)S(1)}, u32[]{:S(2)}, u32[]{:S(2)}) %collective-permute-start.20) | collective-permute-done | bytes 196640 | tf_op jit(solution)/shard_map/ppermute | solution.py:85
  60.7 1.4 %collective-permute-start.21 = (f32[12,2,8,256]{3,2,1,0:T(8,128)S(1)}, f32[12,2,8,256]{3,2,1,0:T(8,128)S(1)}, u32[]{:S(2)}, u32[]{:S(2)}) collective-permute-start(f32[12,2,8,256]{3,2,1,0:T(8,128)S(1)} %add.617), channel_id=1, source_target_pairs={{0,2},{2,4},{4,6},{6,7},{7,5},{5,3},{3,1},{1,0},{8,10},{10,12},{12... | collective-permute-start | bytes 589832 | tf_op jit(solution)/shard_map/ppermute | solution.py:84
  64.9 1.8 %collective-permute-start.8 = (f32[12,2,8,256]{3,2,1,0:T(8,128)S(1)}, f32[12,2,8,256]{3,2,1,0:T(8,128)S(1)}, u32[]{:S(2)}, u32[]{:S(2)}) collective-permute-start(f32[12,2,8,256]{3,2,1,0:T(8,128)S(1)} %add.554), channel_id=1, source_target_pairs={{0,2},{2,4},{4,6},{6,7},{7,5},{5,3},{3,1},{1,0},{8,10},{10,12},{12... | collective-permute-start | bytes 589832 | tf_op jit(solution)/shard_map/ppermute | solution.py:84
  68.6 1.4 %collective-permute-done.22 = f32[12,2,8,256]{3,2,1,0:T(8,128)S(1)} collective-permute-done((f32[12,2,8,256]{3,2,1,0:T(8,128)S(1)}, f32[12,2,8,256]{3,2,1,0:T(8,128)S(1)}, u32[]{:S(2)}, u32[]{:S(2)}) %collective-permute-start.22) | collective-permute-done | bytes 196640 | tf_op jit(solution)/shard_map/ppermute | solution.py:85
  70.0 1.2 %collective-permute-start.23 = (f32[12,2,8,256]{3,2,1,0:T(8,128)S(1)}, f32[12,2,8,256]{3,2,1,0:T(8,128)S(1)}, u32[]{:S(2)}, u32[]{:S(2)}) collective-permute-start(f32[12,2,8,256]{3,2,1,0:T(8,128)S(1)} %add.623), channel_id=1, source_target_pairs={{0,2},{2,4},{4,6},{6,7},{7,5},{5,3},{3,1},{1,0},{8,10},{10,12},{12... | collective-permute-start | bytes 589832 | tf_op jit(solution)/shard_map/ppermute | solution.py:84
  73.3 0.9 collective-permute-done.9
  74.3 1.5 %collective-permute-start.10 = (f32[12,2,8,256]{3,2,1,0:T(8,128)S(1)}, f32[12,2,8,256]{3,2,1,0:T(8,128)S(1)}, u32[]{:S(2)}, u32[]{:S(2)}) collective-permute-start(f32[12,2,8,256]{3,2,1,0:T(8,128)S(1)} %add.565), channel_id=1, source_target_pairs={{0,2},{2,4},{4,6},{6,7},{7,5},{5,3},{3,1},{1,0},{8,10},{10,12},{12... | collective-permute-start | bytes 589832 | tf_op jit(solution)/shard_map/ppermute | solution.py:84
  77.7 1.3 %collective-permute-done.24 = f32[12,2,8,256]{3,2,1,0:T(8,128)S(1)} collective-permute-done((f32[12,2,8,256]{3,2,1,0:T(8,128)S(1)}, f32[12,2,8,256]{3,2,1,0:T(8,128)S(1)}, u32[]{:S(2)}, u32[]{:S(2)}) %collective-permute-start.24) | collective-permute-done | bytes 196640 | tf_op jit(solution)/shard_map/ppermute | solution.py:85
  79.0 1.2 %collective-permute-start.25 = (f32[12,2,8,256]{3,2,1,0:T(8,128)S(1)}, f32[12,2,8,256]{3,2,1,0:T(8,128)S(1)}, u32[]{:S(2)}, u32[]{:S(2)}) collective-permute-start(f32[12,2,8,256]{3,2,1,0:T(8,128)S(1)} %add.629), channel_id=1, source_target_pairs={{0,2},{2,4},{4,6},{6,7},{7,5},{5,3},{3,1},{1,0},{8,10},{10,12},{12... | collective-permute-start | bytes 589832 | tf_op jit(solution)/shard_map/ppermute | solution.py:84
  82.4 1.0 collective-permute-done.11
  83.4 1.2 %collective-permute-start.12 = (f32[12,2,8,256]{3,2,1,0:T(8,128)S(1)}, f32[12,2,8,256]{3,2,1,0:T(8,128)S(1)}, u32[]{:S(2)}, u32[]{:S(2)}) collective-permute-start(f32[12,2,8,256]{3,2,1,0:T(8,128)S(1)} %add.576), channel_id=1, source_target_pairs={{0,2},{2,4},{4,6},{6,7},{7,5},{5,3},{3,1},{1,0},{8,10},{10,12},{12... | collective-permute-start | bytes 589832 | tf_op jit(solution)/shard_map/ppermute | solution.py:84
  85.3 1.0 collective-permute-start.13
  86.9 1.2 %collective-permute-done.26 = f32[12,2,8,256]{3,2,1,0:T(8,128)S(1)} collective-permute-done((f32[12,2,8,256]{3,2,1,0:T(8,128)S(1)}, f32[12,2,8,256]{3,2,1,0:T(8,128)S(1)}, u32[]{:S(2)}, u32[]{:S(2)}) %collective-permute-start.26) | collective-permute-done | bytes 196640 | tf_op jit(solution)/shard_map/ppermute | solution.py:85
  90.3 2.4 %collective-permute-done.13 = f32[12,2,8,256]{3,2,1,0:T(8,128)S(1)} collective-permute-done((f32[12,2,8,256]{3,2,1,0:T(8,128)S(1)}, f32[12,2,8,256]{3,2,1,0:T(8,128)S(1)}, u32[]{:S(2)}, u32[]{:S(2)}) %collective-permute-start.13) | collective-permute-done | bytes 196640 | tf_op jit(solution)/shard_map/ppermute | solution.py:85
  94.2 1.4 %collective-permute-start.27 = (f32[12,2,8,256]{3,2,1,0:T(8,128)S(1)}, f32[12,2,8,256]{3,2,1,0:T(8,128)S(1)}, u32[]{:S(2)}, u32[]{:S(2)}) collective-permute-start(f32[12,2,8,256]{3,2,1,0:T(8,128)S(1)} %add.635), channel_id=1, source_target_pairs={{0,2},{2,4},{4,6},{6,7},{7,5},{5,3},{3,1},{1,0},{8,10},{10,12},{12... | collective-permute-start | bytes 589832 | tf_op jit(solution)/shard_map/ppermute | solution.py:84
  96.2 1.1 %collective-permute-start.14 = (f32[12,2,8,256]{3,2,1,0:T(8,128)S(1)}, f32[12,2,8,256]{3,2,1,0:T(8,128)S(1)}, u32[]{:S(2)}, u32[]{:S(2)}) collective-permute-start(f32[12,2,8,256]{3,2,1,0:T(8,128)S(1)} %add.587), channel_id=1, source_target_pairs={{0,2},{2,4},{4,6},{6,7},{7,5},{5,3},{3,1},{1,0},{8,10},{10,12},{12... | collective-permute-start | bytes 589832 | tf_op jit(solution)/shard_map/ppermute | solution.py:84
  98.5 1.4 %collective-permute-done.27 = f32[12,2,8,256]{3,2,1,0:T(8,128)S(1)} collective-permute-done((f32[12,2,8,256]{3,2,1,0:T(8,128)S(1)}, f32[12,2,8,256]{3,2,1,0:T(8,128)S(1)}, u32[]{:S(2)}, u32[]{:S(2)}) %collective-permute-start.27) | collective-permute-done | bytes 196640 | tf_op jit(solution)/shard_map/ppermute | solution.py:84
  100.0 2.1 %collective-permute-done.14 = f32[12,2,8,256]{3,2,1,0:T(8,128)S(1)} collective-permute-done((f32[12,2,8,256]{3,2,1,0:T(8,128)S(1)}, f32[12,2,8,256]{3,2,1,0:T(8,128)S(1)}, u32[]{:S(2)}, u32[]{:S(2)}) %collective-permute-start.14) | collective-permute-done | bytes 196640 | tf_op jit(solution)/shard_map/ppermute | solution.py:84
  102.1 0.9 pad_maximum_fusion.1
  (108 shorter events, 33.0 us)
Async XLA Ops:
  0.0 30.0 %copy-start = (bf16[384,2048]{1,0:T(8,128)(2,1)S(1)}, bf16[384,2048]{1,0:T(8,128)(2,1)}, u32[]{:S(2)}) copy-start(bf16[384,2048]{1,0:T(8,128)(2,1)} %param.5) | copy-start | bytes 4718596
  1.8 26.5 %collective-permute-start.1 = (bf16[2048,256]{1,0:T(8,128)(2,1)}, bf16[2048,256]{1,0:T(8,128)(2,1)}, u32[]{:S(2)}, u32[]{:S(2)}) collective-permute-start(bf16[2048,256]{1,0:T(8,128)(2,1)} %param.6), channel_id=1, source_target_pairs={{0,16},{16,0},{1,17},{17,1},{2,18},{18,2},{3,19},{19,3},{4,20},{20... | collective-permute-start | bytes 3145736 | tf_op jit(solution)/shard_map/ppermute | solution.py:20
  4.8 25.2 %collective-permute-start = (bf16[384,2048]{1,0:T(8,128)(2,1)}, bf16[384,2048]{1,0:T(8,128)(2,1)S(1)}, u32[]{:S(2)}, u32[]{:S(2)}) collective-permute-start(bf16[384,2048]{1,0:T(8,128)(2,1)} %param.5), channel_id=1, source_target_pairs={{0,8},{8,0},{1,9},{9,1},{2,10},{10,2},{3,11},{11,3},{4,12},{12,4},... | collective-permute-start | bytes 4718600 | tf_op jit(solution)/shard_map/ppermute | solution.py:20
  32.2 7.6 %collective-permute-start.15 = (f32[12,2,8,256]{3,2,1,0:T(8,128)S(1)}, f32[12,2,8,256]{3,2,1,0:T(8,128)S(1)}, u32[]{:S(2)}, u32[]{:S(2)}) collective-permute-start(f32[12,2,8,256]{3,2,1,0:T(8,128)S(1)} %fusion.15), channel_id=1, source_target_pairs={{0,2},{2,4},{4,6},{6,7},{7,5},{5,3},{3,1},{1,0},{8,10},{10,12},{12... | collective-permute-start | bytes 589832 | tf_op jit(solution)/shard_map/ppermute | solution.py:84
  34.1 7.4 %collective-permute-start.16 = (f32[12,2,8,256]{3,2,1,0:T(8,128)S(1)}, f32[12,2,8,256]{3,2,1,0:T(8,128)S(1)}, u32[]{:S(2)}, u32[]{:S(2)}) collective-permute-start(f32[12,2,8,256]{3,2,1,0:T(8,128)S(1)} %fusion.16), channel_id=1, source_target_pairs={{2,0},{4,2},{6,4},{7,6},{5,7},{3,5},{1,3},{0,1},{10,8},{12,10},{14... | collective-permute-start | bytes 589832 | tf_op jit(solution)/shard_map/ppermute | solution.py:85
  35.5 9.4 %collective-permute-start.2 = (f32[12,2,8,256]{3,2,1,0:T(8,128)S(1)}, f32[12,2,8,256]{3,2,1,0:T(8,128)S(1)}, u32[]{:S(2)}, u32[]{:S(2)}) collective-permute-start(f32[12,2,8,256]{3,2,1,0:T(8,128)S(1)} %fusion), channel_id=1, source_target_pairs={{0,2},{2,4},{4,6},{6,7},{7,5},{5,3},{3,1},{1,0},{8,10},{10,12},{12... | collective-permute-start | bytes 589832 | tf_op jit(solution)/shard_map/ppermute | solution.py:84
  37.3 8.7 %collective-permute-start.3 = (f32[12,2,8,256]{3,2,1,0:T(8,128)S(1)}, f32[12,2,8,256]{3,2,1,0:T(8,128)S(1)}, u32[]{:S(2)}, u32[]{:S(2)}) collective-permute-start(f32[12,2,8,256]{3,2,1,0:T(8,128)S(1)} %fusion.1), channel_id=1, source_target_pairs={{2,0},{4,2},{6,4},{7,6},{5,7},{3,5},{1,3},{0,1},{10,8},{12,10},{14... | collective-permute-start | bytes 589832 | tf_op jit(solution)/shard_map/ppermute | solution.py:85
  42.1 7.9 %collective-permute-start.17 = (f32[12,2,8,256]{3,2,1,0:T(8,128)S(1)}, f32[12,2,8,256]{3,2,1,0:T(8,128)S(1)}, u32[]{:S(2)}, u32[]{:S(2)}) collective-permute-start(f32[12,2,8,256]{3,2,1,0:T(8,128)S(1)} %fusion.97), channel_id=1, source_target_pairs={{0,2},{2,4},{4,6},{6,7},{7,5},{5,3},{3,1},{1,0},{8,10},{10,12},{12... | collective-permute-start | bytes 589832 | tf_op jit(solution)/shard_map/ppermute | solution.py:84
  43.7 7.5 %collective-permute-start.18 = (f32[12,2,8,256]{3,2,1,0:T(8,128)S(1)}, f32[12,2,8,256]{3,2,1,0:T(8,128)S(1)}, u32[]{:S(2)}, u32[]{:S(2)}) collective-permute-start(f32[12,2,8,256]{3,2,1,0:T(8,128)S(1)} %fusion.96), channel_id=1, source_target_pairs={{2,0},{4,2},{6,4},{7,6},{5,7},{3,5},{1,3},{0,1},{10,8},{12,10},{14... | collective-permute-start | bytes 589832 | tf_op jit(solution)/shard_map/ppermute | solution.py:85
  46.7 7.4 %collective-permute-start.4 = (f32[12,2,8,256]{3,2,1,0:T(8,128)S(1)}, f32[12,2,8,256]{3,2,1,0:T(8,128)S(1)}, u32[]{:S(2)}, u32[]{:S(2)}) collective-permute-start(f32[12,2,8,256]{3,2,1,0:T(8,128)S(1)} %fusion.99), channel_id=1, source_target_pairs={{0,2},{2,4},{4,6},{6,7},{7,5},{5,3},{3,1},{1,0},{8,10},{10,12},{12... | collective-permute-start | bytes 589832 | tf_op jit(solution)/shard_map/ppermute | solution.py:84
  48.9 6.8 %collective-permute-start.5 = (f32[12,2,8,256]{3,2,1,0:T(8,128)S(1)}, f32[12,2,8,256]{3,2,1,0:T(8,128)S(1)}, u32[]{:S(2)}, u32[]{:S(2)}) collective-permute-start(f32[12,2,8,256]{3,2,1,0:T(8,128)S(1)} %fusion.98), channel_id=1, source_target_pairs={{2,0},{4,2},{6,4},{7,6},{5,7},{3,5},{1,3},{0,1},{10,8},{12,10},{14... | collective-permute-start | bytes 589832 | tf_op jit(solution)/shard_map/ppermute | solution.py:85
  51.3 8.0 %collective-permute-start.19 = (f32[12,2,8,256]{3,2,1,0:T(8,128)S(1)}, f32[12,2,8,256]{3,2,1,0:T(8,128)S(1)}, u32[]{:S(2)}, u32[]{:S(2)}) collective-permute-start(f32[12,2,8,256]{3,2,1,0:T(8,128)S(1)} %add.611), channel_id=1, source_target_pairs={{0,2},{2,4},{4,6},{6,7},{7,5},{5,3},{3,1},{1,0},{8,10},{10,12},{12... | collective-permute-start | bytes 589832 | tf_op jit(solution)/shard_map/ppermute | solution.py:84
  52.9 7.8 %collective-permute-start.20 = (f32[12,2,8,256]{3,2,1,0:T(8,128)S(1)}, f32[12,2,8,256]{3,2,1,0:T(8,128)S(1)}, u32[]{:S(2)}, u32[]{:S(2)}) collective-permute-start(f32[12,2,8,256]{3,2,1,0:T(8,128)S(1)} %add.614), channel_id=1, source_target_pairs={{2,0},{4,2},{6,4},{7,6},{5,7},{3,5},{1,3},{0,1},{10,8},{12,10},{14... | collective-permute-start | bytes 589832 | tf_op jit(solution)/shard_map/ppermute | solution.py:85
  55.7 7.7 %collective-permute-start.6 = (f32[12,2,8,256]{3,2,1,0:T(8,128)S(1)}, f32[12,2,8,256]{3,2,1,0:T(8,128)S(1)}, u32[]{:S(2)}, u32[]{:S(2)}) collective-permute-start(f32[12,2,8,256]{3,2,1,0:T(8,128)S(1)} %add.543), channel_id=1, source_target_pairs={{0,2},{2,4},{4,6},{6,7},{7,5},{5,3},{3,1},{1,0},{8,10},{10,12},{12... | collective-permute-start | bytes 589832 | tf_op jit(solution)/shard_map/ppermute | solution.py:84
  58.0 6.9 %collective-permute-start.7 = (f32[12,2,8,256]{3,2,1,0:T(8,128)S(1)}, f32[12,2,8,256]{3,2,1,0:T(8,128)S(1)}, u32[]{:S(2)}, u32[]{:S(2)}) collective-permute-start(f32[12,2,8,256]{3,2,1,0:T(8,128)S(1)} %add.549), channel_id=1, source_target_pairs={{2,0},{4,2},{6,4},{7,6},{5,7},{3,5},{1,3},{0,1},{10,8},{12,10},{14... | collective-permute-start | bytes 589832 | tf_op jit(solution)/shard_map/ppermute | solution.py:85
  60.7 7.8 %collective-permute-start.21 = (f32[12,2,8,256]{3,2,1,0:T(8,128)S(1)}, f32[12,2,8,256]{3,2,1,0:T(8,128)S(1)}, u32[]{:S(2)}, u32[]{:S(2)}) collective-permute-start(f32[12,2,8,256]{3,2,1,0:T(8,128)S(1)} %add.617), channel_id=1, source_target_pairs={{0,2},{2,4},{4,6},{6,7},{7,5},{5,3},{3,1},{1,0},{8,10},{10,12},{12... | collective-permute-start | bytes 589832 | tf_op jit(solution)/shard_map/ppermute | solution.py:84
  62.2 7.8 %collective-permute-start.22 = (f32[12,2,8,256]{3,2,1,0:T(8,128)S(1)}, f32[12,2,8,256]{3,2,1,0:T(8,128)S(1)}, u32[]{:S(2)}, u32[]{:S(2)}) collective-permute-start(f32[12,2,8,256]{3,2,1,0:T(8,128)S(1)} %add.620), channel_id=1, source_target_pairs={{2,0},{4,2},{6,4},{7,6},{5,7},{3,5},{1,3},{0,1},{10,8},{12,10},{14... | collective-permute-start | bytes 589832 | tf_op jit(solution)/shard_map/ppermute | solution.py:85
  64.9 7.8 %collective-permute-start.8 = (f32[12,2,8,256]{3,2,1,0:T(8,128)S(1)}, f32[12,2,8,256]{3,2,1,0:T(8,128)S(1)}, u32[]{:S(2)}, u32[]{:S(2)}) collective-permute-start(f32[12,2,8,256]{3,2,1,0:T(8,128)S(1)} %add.554), channel_id=1, source_target_pairs={{0,2},{2,4},{4,6},{6,7},{7,5},{5,3},{3,1},{1,0},{8,10},{10,12},{12... | collective-permute-start | bytes 589832 | tf_op jit(solution)/shard_map/ppermute | solution.py:84
  67.4 6.8 %collective-permute-start.9 = (f32[12,2,8,256]{3,2,1,0:T(8,128)S(1)}, f32[12,2,8,256]{3,2,1,0:T(8,128)S(1)}, u32[]{:S(2)}, u32[]{:S(2)}) collective-permute-start(f32[12,2,8,256]{3,2,1,0:T(8,128)S(1)} %add.560), channel_id=1, source_target_pairs={{2,0},{4,2},{6,4},{7,6},{5,7},{3,5},{1,3},{0,1},{10,8},{12,10},{14... | collective-permute-start | bytes 589832 | tf_op jit(solution)/shard_map/ppermute | solution.py:85
  70.0 7.7 %collective-permute-start.23 = (f32[12,2,8,256]{3,2,1,0:T(8,128)S(1)}, f32[12,2,8,256]{3,2,1,0:T(8,128)S(1)}, u32[]{:S(2)}, u32[]{:S(2)}) collective-permute-start(f32[12,2,8,256]{3,2,1,0:T(8,128)S(1)} %add.623), channel_id=1, source_target_pairs={{0,2},{2,4},{4,6},{6,7},{7,5},{5,3},{3,1},{1,0},{8,10},{10,12},{12... | collective-permute-start | bytes 589832 | tf_op jit(solution)/shard_map/ppermute | solution.py:84
  71.2 7.8 %collective-permute-start.24 = (f32[12,2,8,256]{3,2,1,0:T(8,128)S(1)}, f32[12,2,8,256]{3,2,1,0:T(8,128)S(1)}, u32[]{:S(2)}, u32[]{:S(2)}) collective-permute-start(f32[12,2,8,256]{3,2,1,0:T(8,128)S(1)} %add.626), channel_id=1, source_target_pairs={{2,0},{4,2},{6,4},{7,6},{5,7},{3,5},{1,3},{0,1},{10,8},{12,10},{14... | collective-permute-start | bytes 589832 | tf_op jit(solution)/shard_map/ppermute | solution.py:85
  74.3 7.5 %collective-permute-start.10 = (f32[12,2,8,256]{3,2,1,0:T(8,128)S(1)}, f32[12,2,8,256]{3,2,1,0:T(8,128)S(1)}, u32[]{:S(2)}, u32[]{:S(2)}) collective-permute-start(f32[12,2,8,256]{3,2,1,0:T(8,128)S(1)} %add.565), channel_id=1, source_target_pairs={{0,2},{2,4},{4,6},{6,7},{7,5},{5,3},{3,1},{1,0},{8,10},{10,12},{12... | collective-permute-start | bytes 589832 | tf_op jit(solution)/shard_map/ppermute | solution.py:84
  76.4 7.0 %collective-permute-start.11 = (f32[12,2,8,256]{3,2,1,0:T(8,128)S(1)}, f32[12,2,8,256]{3,2,1,0:T(8,128)S(1)}, u32[]{:S(2)}, u32[]{:S(2)}) collective-permute-start(f32[12,2,8,256]{3,2,1,0:T(8,128)S(1)} %add.571), channel_id=1, source_target_pairs={{2,0},{4,2},{6,4},{7,6},{5,7},{3,5},{1,3},{0,1},{10,8},{12,10},{14... | collective-permute-start | bytes 589832 | tf_op jit(solution)/shard_map/ppermute | solution.py:85
  79.0 7.8 %collective-permute-start.25 = (f32[12,2,8,256]{3,2,1,0:T(8,128)S(1)}, f32[12,2,8,256]{3,2,1,0:T(8,128)S(1)}, u32[]{:S(2)}, u32[]{:S(2)}) collective-permute-start(f32[12,2,8,256]{3,2,1,0:T(8,128)S(1)} %add.629), channel_id=1, source_target_pairs={{0,2},{2,4},{4,6},{6,7},{7,5},{5,3},{3,1},{1,0},{8,10},{10,12},{12... | collective-permute-start | bytes 589832 | tf_op jit(solution)/shard_map/ppermute | solution.py:84
  80.3 7.8 %collective-permute-start.26 = (f32[12,2,8,256]{3,2,1,0:T(8,128)S(1)}, f32[12,2,8,256]{3,2,1,0:T(8,128)S(1)}, u32[]{:S(2)}, u32[]{:S(2)}) collective-permute-start(f32[12,2,8,256]{3,2,1,0:T(8,128)S(1)} %add.632), channel_id=1, source_target_pairs={{2,0},{4,2},{6,4},{7,6},{5,7},{3,5},{1,3},{0,1},{10,8},{12,10},{14... | collective-permute-start | bytes 589832 | tf_op jit(solution)/shard_map/ppermute | solution.py:85
  83.4 6.3 %collective-permute-start.12 = (f32[12,2,8,256]{3,2,1,0:T(8,128)S(1)}, f32[12,2,8,256]{3,2,1,0:T(8,128)S(1)}, u32[]{:S(2)}, u32[]{:S(2)}) collective-permute-start(f32[12,2,8,256]{3,2,1,0:T(8,128)S(1)} %add.576), channel_id=1, source_target_pairs={{0,2},{2,4},{4,6},{6,7},{7,5},{5,3},{3,1},{1,0},{8,10},{10,12},{12... | collective-permute-start | bytes 589832 | tf_op jit(solution)/shard_map/ppermute | solution.py:84
  85.3 7.5 %collective-permute-start.13 = (f32[12,2,8,256]{3,2,1,0:T(8,128)S(1)}, f32[12,2,8,256]{3,2,1,0:T(8,128)S(1)}, u32[]{:S(2)}, u32[]{:S(2)}) collective-permute-start(f32[12,2,8,256]{3,2,1,0:T(8,128)S(1)} %add.582), channel_id=1, source_target_pairs={{2,0},{4,2},{6,4},{7,6},{5,7},{3,5},{1,3},{0,1},{10,8},{12,10},{14... | collective-permute-start | bytes 589832 | tf_op jit(solution)/shard_map/ppermute | solution.py:85
  88.1 9.7 %collective-permute-start.29 = (f32[12,2,8,256]{3,2,1,0:T(8,128)S(1)}, f32[12,2,8,256]{3,2,1,0:T(8,128)S(1)}, u32[]{:S(2)}, u32[]{:S(2)}) collective-permute-start(f32[12,2,8,256]{3,2,1,0:T(8,128)S(1)} %add.638), channel_id=1, source_target_pairs={{2,0},{4,2},{6,4},{7,6},{5,7},{3,5},{1,3},{0,1},{10,8},{12,10},{14... | collective-permute-start | bytes 589832 | tf_op jit(solution)/shard_map/ppermute | solution.py:85
  92.8 5.7 %collective-permute-start.28 = (f32[12,2,8,256]{3,2,1,0:T(8,128)S(1)}, f32[12,2,8,256]{3,2,1,0:T(8,128)S(1)}, u32[]{:S(2)}, u32[]{:S(2)}) collective-permute-start(f32[12,2,8,256]{3,2,1,0:T(8,128)S(1)} %add.593), channel_id=1, source_target_pairs={{2,0},{4,2},{6,4},{7,6},{5,7},{3,5},{1,3},{0,1},{10,8},{12,10},{14... | collective-permute-start | bytes 589832 | tf_op jit(solution)/shard_map/ppermute | solution.py:85
  94.2 5.7 %collective-permute-start.27 = (f32[12,2,8,256]{3,2,1,0:T(8,128)S(1)}, f32[12,2,8,256]{3,2,1,0:T(8,128)S(1)}, u32[]{:S(2)}, u32[]{:S(2)}) collective-permute-start(f32[12,2,8,256]{3,2,1,0:T(8,128)S(1)} %add.635), channel_id=1, source_target_pairs={{0,2},{2,4},{4,6},{6,7},{7,5},{5,3},{3,1},{1,0},{8,10},{10,12},{12... | collective-permute-start | bytes 589832 | tf_op jit(solution)/shard_map/ppermute | solution.py:84
  96.2 5.9 %collective-permute-start.14 = (f32[12,2,8,256]{3,2,1,0:T(8,128)S(1)}, f32[12,2,8,256]{3,2,1,0:T(8,128)S(1)}, u32[]{:S(2)}, u32[]{:S(2)}) collective-permute-start(f32[12,2,8,256]{3,2,1,0:T(8,128)S(1)} %add.587), channel_id=1, source_target_pairs={{0,2},{2,4},{4,6},{6,7},{7,5},{5,3},{3,1},{1,0},{8,10},{10,12},{12... | collective-permute-start | bytes 589832 | tf_op jit(solution)/shard_map/ppermute | solution.py:84

commit v13 on v10

--- a/solution.py
+++ b/solution.py
@@ -52,21 +52,50 @@
         receivers, excitations, weights, position = lax.optimization_barrier(
             (receivers, excitations, weights, position)
         )
-        receiver_block = gather_blocks(receivers, "evt", sizes["evt"], 1)
-        source_block = gather_blocks(excitations, "sta", sizes["sta"], 0)
-        row_count, block_modes = receiver_block.shape
+        if sizes["sta"] == 2 and sizes["evt"] == 2:
+            sta = lax.axis_index("sta")
+            same = sta == lax.axis_index("evt")
+            other_receivers = swap_pair(receivers, "evt")
+            block_modes = receivers.shape[1]
+            pieces = [
+                (
+                    jnp.where(same, receivers, other_receivers),
+                    lax.dynamic_slice_in_dim(weights, sta * block_modes, block_modes, axis=2),
+                    excitations,
+                ),
+                (
+                    jnp.where(same, other_receivers, receivers),
+                    lax.dynamic_slice_in_dim(weights, (1 - sta) * block_modes, block_modes, axis=2),
+                    swap_pair(excitations, "sta"),
+                ),
+            ]
+        else:
+            pieces = [
+                (
+                    gather_blocks(receivers, "evt", sizes["evt"], 1),
+                    weights,
+                    gather_blocks(excitations, "sta", sizes["sta"], 0),
+                )
+            ]
+        row_count = receivers.shape[0]
+        events = excitations.shape[1]
         chunk = row_count // mode_count
         half = chunk // 2
 
-        def partial_rows(owner, part):
+        def partial_rows(owner, part, held=pieces):
             start = owner * chunk + part * half
-            rows = lax.dynamic_slice_in_dim(receiver_block, start, half, axis=0)
-            widened = rows.astype(jnp.float32)
-            weighted = (widened[:, None, None, :] * weights[None]).astype(jnp.bfloat16)
-            product = jnp.dot(
-                weighted.reshape(-1, block_modes), source_block, preferred_element_type=jnp.float32
-            )
-            return product.reshape(half, 2, sample_freqs.shape[0], source_block.shape[1])
+            total = None
+            for receiver_block, piece_weights, source_block in held:
+                rows = lax.dynamic_slice_in_dim(receiver_block, start, half, axis=0)
+                widened = rows.astype(jnp.float32)
+                weighted = (widened[:, None, None, :] * piece_weights[None]).astype(jnp.bfloat16)
+                product = jnp.dot(
+                    weighted.reshape(-1, receiver_block.shape[1]),
+                    source_block,
+                    preferred_element_type=jnp.float32,
+                )
+                total = product if total is None else total + product
+            return total.reshape(half, 2, sample_freqs.shape[0], events)
 
         def owner_at(offset):
             place = (position + offset) % mode_count
@@ -77,10 +106,11 @@
         ahead = partial_rows(owner_at(-1), 0)
         behind = partial_rows(owner_at(1), 1)
         for step in range(mode_count - 1):
+            held, ahead, behind = lax.optimization_barrier((pieces, ahead, behind))
             ahead = lax.ppermute(ahead, "mode", clockwise)
             behind = lax.ppermute(behind, "mode", counter)
-            ahead = ahead + partial_rows(owner_at(-step - 2), 0)
-            behind = behind + partial_rows(owner_at(step + 2), 1)
+            ahead = ahead + partial_rows(owner_at(-step - 2), 0, held)
+            behind = behind + partial_rows(owner_at(step + 2), 1, held)
         return jnp.concatenate([ahead, behind], axis=0)
 
     return per_device

time: 104 us -> 110 us (1.058)
  other arithmetic: 5.58 us -> 15.4 us
  waiting for transfers between devices: 64.8 us -> 56.3 us
  matrix products: 15.6 us -> 18.5 us
  starting transfers between devices: 17.4 us -> 18.5 us
    convert_element_type x0 -> x16, other arithmetic: none -> 9.87 us  [partial_rows(): (widened[:, None, None, :] * piece_weights[None]).astype(jnp.bfloat16)]
    ppermute x7, waiting for transfers between devices: 34 us -> 26.3 us  [per_device(): ahead = lax.ppermute(ahead, 'mode', clockwise)]
    ppermute x2, waiting for transfers between devices: 23.5 us -> 19.2 us  [swap_pair(): return lax.ppermute(local, axis_name, [(0, 1), (1, 0)])]
    ppermute x7, waiting for transfers between devices: 7.25 us -> 10.8 us  [per_device(): behind = lax.ppermute(behind, 'mode', counter)]
    ppermute x7, starting transfers between devices: 2.84 us -> 6.04 us  [per_device(): behind = lax.ppermute(behind, 'mode', counter)]
    dot_general x16 -> x32, matrix products: 15.6 us -> 18.5 us  [partial_rows(): jnp.dot(weighted.reshape(-1, receiver_block.shape[1]), source_block, pref...]
    ppermute x7, starting transfers between devices: 11.5 us -> 9.38 us  [per_device(): ahead = lax.ppermute(ahead, 'mode', clockwise)]
  transfers between devices with their start and end apart: 16 -> 16, of which waited for: 15 -> 16; matrix products, arithmetic and copies ran while one was open for 17% -> 27% of each run, Pallas kernels for 0% -> 0%
where the time goes in v13:
time: 110 us
  waiting for transfers between devices  56.3 us (51%)
  starting transfers between devices  18.5 us (17%)
  matrix products  18.5 us (17%)
  other arithmetic  15.4 us (14%)
    ppermute x7, waiting for transfers between devices, per_device(): ahead = lax.ppermute(ahead, 'mode', clockwise)  26.3 us
    ppermute x2, waiting for transfers between devices, swap_pair(): return lax.ppermute(local, axis_name, [(0, 1), (1, 0)])  19.2 us
    dot_general x32, matrix products, partial_rows(): jnp.dot(weighted.reshape(-1, receiver_block.shape[1]), source_block, pref...  18.5 us
    ppermute x7, waiting for transfers between devices, per_device(): behind = lax.ppermute(behind, 'mode', counter)  10.8 us
    convert_element_type x16, other arithmetic, partial_rows(): (widened[:, None, None, :] * piece_weights[None]).astype(jnp.bfloat16)  9.87 us
    ppermute x7, starting transfers between devices, per_device(): ahead = lax.ppermute(ahead, 'mode', clockwise)  9.38 us
    ppermute x7, starting transfers between devices, per_device(): behind = lax.ppermute(behind, 'mode', counter)  6.04 us
    ppermute x2, starting transfers between devices, swap_pair(): return lax.ppermute(local, axis_name, [(0, 1), (1, 0)])  3.11 us
  transfers between devices with their start and end apart: 16, of which 16 were waited for; matrix products, arithmetic and copies ran while one was open for 27% of the time, Pallas kernels for 0%

profile of v13, /device:TPU:0, one launch (start us, length us, event | category | flops | bytes accessed | tf_op | source)
XLA Modules:
  0.0 109.9 jit_solution(7399792874785043429)
XLA Ops:
  0.0 0.9 mul.617
  0.9 0.9 fusion.2
  2.3 2.6 %collective-permute-start.1 = (bf16[2048,256]{1,0:T(8,128)(2,1)}, bf16[2048,256]{1,0:T(8,128)(2,1)S(1)}, u32[]{:S(2)}, u32[]{:S(2)}) collective-permute-start(bf16[2048,256]{1,0:T(8,128)(2,1)} %param.6), channel_id=1, source_target_pairs={{0,16},{16,0},{1,17},{17,1},{2,18},{18,2},{3,19},{19,3},{4,20},{20... | collective-permute-start | bytes 3145736 | tf_op jit(solution)/shard_map/ppermute | solution.py:20
  4.9 0.8 collective-permute-done
  5.7 1.6 %broadcast_select_fusion = (bf16[384,2048]{1,0:T(8,128)(2,1)S(1)}, bf16[384,2048]{1,0:T(8,128)(2,1)S(1)}) fusion(bf16[384,2048]{1,0:T(8,128)(2,1)} %collective-permute-done, bf16[384,2048]{1,0:T(8,128)(2,1)S(1)} %copy-done.1, pred[]{:T(512)S(6)} %eq.24), kind=kLoop, calls=%fused_computation.32 | loop fusion | flops 1572864 | bytes 6291457 | tf_op jit(solution)/shard_map/jit(_where)/select_n | solution.py:67
  10.4 18.5 %collective-permute-done.1 = bf16[2048,256]{1,0:T(8,128)(2,1)S(1)} collective-permute-done((bf16[2048,256]{1,0:T(8,128)(2,1)}, bf16[2048,256]{1,0:T(8,128)(2,1)S(1)}, u32[]{:S(2)}, u32[]{:S(2)}) %collective-permute-start.1) | collective-permute-done | bytes 1048608 | tf_op jit(solution)/shard_map/ppermute | solution.py:20
  30.0 1.9 %collective-permute-start.2 = (f32[24,2,8,256]{3,2,1,0:T(8,128)S(1)}, f32[24,2,8,256]{3,2,1,0:T(8,128)S(1)}, u32[]{:S(2)}, u32[]{:S(2)}) collective-permute-start(f32[24,2,8,256]{3,2,1,0:T(8,128)S(1)} %bitcast.159), channel_id=1, source_target_pairs={{0,2},{2,4},{4,6},{6,7},{7,5},{5,3},{3,1},{1,0},{8,10},{10,12},{12... | collective-permute-start | bytes 1179656 | tf_op jit(solution)/shard_map/ppermute | solution.py:110
  35.8 5.1 %collective-permute-done.2 = f32[24,2,8,256]{3,2,1,0:T(8,128)S(1)} collective-permute-done((f32[24,2,8,256]{3,2,1,0:T(8,128)S(1)}, f32[24,2,8,256]{3,2,1,0:T(8,128)S(1)}, u32[]{:S(2)}, u32[]{:S(2)}) %collective-permute-start.2) | collective-permute-done | bytes 393248 | tf_op jit(solution)/shard_map/ppermute | solution.py:110
  41.0 1.4 %collective-permute-done.3 = f32[24,2,8,256]{3,2,1,0:T(8,128)S(1)} collective-permute-done((f32[24,2,8,256]{3,2,1,0:T(8,128)S(1)}, f32[24,2,8,256]{3,2,1,0:T(8,128)S(1)}, u32[]{:S(2)}, u32[]{:S(2)}) %collective-permute-start.3) | collective-permute-done | bytes 393248 | tf_op jit(solution)/shard_map/ppermute | solution.py:111
  42.4 1.6 %collective-permute-start.4 = (f32[24,2,8,256]{3,2,1,0:T(8,128)S(1)}, f32[24,2,8,256]{3,2,1,0:T(8,128)S(1)}, u32[]{:S(2)}, u32[]{:S(2)}) collective-permute-start(f32[24,2,8,256]{3,2,1,0:T(8,128)S(1)} %add.389), channel_id=1, source_target_pairs={{0,2},{2,4},{4,6},{6,7},{7,5},{5,3},{3,1},{1,0},{8,10},{10,12},{12... | collective-permute-start | bytes 1179656 | tf_op jit(solution)/shard_map/ppermute | solution.py:110
  48.3 3.7 %collective-permute-done.4 = f32[24,2,8,256]{3,2,1,0:T(8,128)S(1)} collective-permute-done((f32[24,2,8,256]{3,2,1,0:T(8,128)S(1)}, f32[24,2,8,256]{3,2,1,0:T(8,128)S(1)}, u32[]{:S(2)}, u32[]{:S(2)}) %collective-permute-start.4) | collective-permute-done | bytes 393248 | tf_op jit(solution)/shard_map/ppermute | solution.py:110
  52.0 1.4 %collective-permute-done.5 = f32[24,2,8,256]{3,2,1,0:T(8,128)S(1)} collective-permute-done((f32[24,2,8,256]{3,2,1,0:T(8,128)S(1)}, f32[24,2,8,256]{3,2,1,0:T(8,128)S(1)}, u32[]{:S(2)}, u32[]{:S(2)}) %collective-permute-start.5) | collective-permute-done | bytes 393248 | tf_op jit(solution)/shard_map/ppermute | solution.py:111
  53.5 1.6 %collective-permute-start.6 = (f32[24,2,8,256]{3,2,1,0:T(8,128)S(1)}, f32[24,2,8,256]{3,2,1,0:T(8,128)S(1)}, u32[]{:S(2)}, u32[]{:S(2)}) collective-permute-start(f32[24,2,8,256]{3,2,1,0:T(8,128)S(1)} %add.402), channel_id=1, source_target_pairs={{0,2},{2,4},{4,6},{6,7},{7,5},{5,3},{3,1},{1,0},{8,10},{10,12},{12... | collective-permute-start | bytes 1179656 | tf_op jit(solution)/shard_map/ppermute | solution.py:110
  55.2 0.7 collective-permute-start.7
  59.4 2.3 %collective-permute-done.6 = f32[24,2,8,256]{3,2,1,0:T(8,128)S(1)} collective-permute-done((f32[24,2,8,256]{3,2,1,0:T(8,128)S(1)}, f32[24,2,8,256]{3,2,1,0:T(8,128)S(1)}, u32[]{:S(2)}, u32[]{:S(2)}) %collective-permute-start.6) | collective-permute-done | bytes 393248 | tf_op jit(solution)/shard_map/ppermute | solution.py:110
  61.8 1.5 %collective-permute-done.7 = f32[24,2,8,256]{3,2,1,0:T(8,128)S(1)} collective-permute-done((f32[24,2,8,256]{3,2,1,0:T(8,128)S(1)}, f32[24,2,8,256]{3,2,1,0:T(8,128)S(1)}, u32[]{:S(2)}, u32[]{:S(2)}) %collective-permute-start.7) | collective-permute-done | bytes 393248 | tf_op jit(solution)/shard_map/ppermute | solution.py:111
  63.4 2.2 %collective-permute-start.8 = (f32[24,2,8,256]{3,2,1,0:T(8,128)S(1)}, f32[24,2,8,256]{3,2,1,0:T(8,128)S(1)}, u32[]{:S(2)}, u32[]{:S(2)}) collective-permute-start(f32[24,2,8,256]{3,2,1,0:T(8,128)S(1)} %add.415), channel_id=1, source_target_pairs={{0,2},{2,4},{4,6},{6,7},{7,5},{5,3},{3,1},{1,0},{8,10},{10,12},{12... | collective-permute-start | bytes 1179656 | tf_op jit(solution)/shard_map/ppermute | solution.py:110
  69.3 3.3 %collective-permute-done.8 = f32[24,2,8,256]{3,2,1,0:T(8,128)S(1)} collective-permute-done((f32[24,2,8,256]{3,2,1,0:T(8,128)S(1)}, f32[24,2,8,256]{3,2,1,0:T(8,128)S(1)}, u32[]{:S(2)}, u32[]{:S(2)}) %collective-permute-start.8) | collective-permute-done | bytes 393248 | tf_op jit(solution)/shard_map/ppermute | solution.py:110
  72.7 2.8 %collective-permute-done.9 = f32[24,2,8,256]{3,2,1,0:T(8,128)S(1)} collective-permute-done((f32[24,2,8,256]{3,2,1,0:T(8,128)S(1)}, f32[24,2,8,256]{3,2,1,0:T(8,128)S(1)}, u32[]{:S(2)}, u32[]{:S(2)}) %collective-permute-start.9) | collective-permute-done | bytes 393248 | tf_op jit(solution)/shard_map/ppermute | solution.py:111
  75.6 0.8 collective-permute-start.10
  76.4 1.4 %collective-permute-start.11 = (f32[24,2,8,256]{3,2,1,0:T(8,128)S(1)}, f32[24,2,8,256]{3,2,1,0:T(8,128)S(1)}, u32[]{:S(2)}, u32[]{:S(2)}) collective-permute-start(f32[24,2,8,256]{3,2,1,0:T(8,128)S(1)} %add.435), channel_id=1, source_target_pairs={{2,0},{4,2},{6,4},{7,6},{5,7},{3,5},{1,3},{0,1},{10,8},{12,10},{14... | collective-permute-start | bytes 1179656 | tf_op jit(solution)/shard_map/ppermute | solution.py:111
  81.4 5.2 %collective-permute-done.10 = f32[24,2,8,256]{3,2,1,0:T(8,128)S(1)} collective-permute-done((f32[24,2,8,256]{3,2,1,0:T(8,128)S(1)}, f32[24,2,8,256]{3,2,1,0:T(8,128)S(1)}, u32[]{:S(2)}, u32[]{:S(2)}) %collective-permute-start.10) | collective-permute-done | bytes 393248 | tf_op jit(solution)/shard_map/ppermute | solution.py:110
  86.6 0.9 collective-permute-done.11
  87.6 0.7 collective-permute-start.12
  88.4 1.6 %collective-permute-start.13 = (f32[24,2,8,256]{3,2,1,0:T(8,128)S(1)}, f32[24,2,8,256]{3,2,1,0:T(8,128)S(1)}, u32[]{:S(2)}, u32[]{:S(2)}) collective-permute-start(f32[24,2,8,256]{3,2,1,0:T(8,128)S(1)} %add.448), channel_id=1, source_target_pairs={{2,0},{4,2},{6,4},{7,6},{5,7},{3,5},{1,3},{0,1},{10,8},{12,10},{14... | collective-permute-start | bytes 1179656 | tf_op jit(solution)/shard_map/ppermute | solution.py:111
  91.2 0.6 multiply_convert_fusion.5
  93.6 5.1 %collective-permute-done.12 = f32[24,2,8,256]{3,2,1,0:T(8,128)S(1)} collective-permute-done((f32[24,2,8,256]{3,2,1,0:T(8,128)S(1)}, f32[24,2,8,256]{3,2,1,0:T(8,128)S(1)}, u32[]{:S(2)}, u32[]{:S(2)}) %collective-permute-start.12) | collective-permute-done | bytes 393248 | tf_op jit(solution)/shard_map/ppermute | solution.py:110
  98.8 0.7 collective-permute-done.13
  99.5 1.6 %collective-permute-start.15 = (f32[24,2,8,256]{3,2,1,0:T(8,128)S(1)}, f32[24,2,8,256]{3,2,1,0:T(8,128)S(1)}, u32[]{:S(2)}, u32[]{:S(2)}) collective-permute-start(f32[24,2,8,256]{3,2,1,0:T(8,128)S(1)} %add.461), channel_id=1, source_target_pairs={{2,0},{4,2},{6,4},{7,6},{5,7},{3,5},{1,3},{0,1},{10,8},{12,10},{14... | collective-permute-start | bytes 1179656 | tf_op jit(solution)/shard_map/ppermute | solution.py:111
  105.3 2.0 %collective-permute-done.15 = f32[24,2,8,256]{3,2,1,0:T(8,128)S(1)} collective-permute-done((f32[24,2,8,256]{3,2,1,0:T(8,128)S(1)}, f32[24,2,8,256]{3,2,1,0:T(8,128)S(1)}, u32[]{:S(2)}, u32[]{:S(2)}) %collective-permute-start.15) | collective-permute-done | bytes 393248 | tf_op jit(solution)/shard_map/ppermute | solution.py:111
  107.4 1.6 %collective-permute-done.14 = f32[24,2,8,256]{3,2,1,0:T(8,128)S(1)} collective-permute-done((f32[24,2,8,256]{3,2,1,0:T(8,128)S(1)}, f32[24,2,8,256]{3,2,1,0:T(8,128)S(1)}, u32[]{:S(2)}, u32[]{:S(2)}) %collective-permute-start.14) | collective-permute-done | bytes 393248 | tf_op jit(solution)/shard_map/ppermute | solution.py:110
  109.0 0.9 pad_maximum_fusion
  (87 shorter events, 31.6 us)
Async XLA Ops:
  0.0 5.7 %copy-start.1 = (bf16[384,2048]{1,0:T(8,128)(2,1)S(1)}, bf16[384,2048]{1,0:T(8,128)(2,1)}, u32[]{:S(2)}) copy-start(bf16[384,2048]{1,0:T(8,128)(2,1)} %param.5) | copy-start | bytes 4718596
  1.8 3.9 %collective-permute-start = (bf16[384,2048]{1,0:T(8,128)(2,1)}, bf16[384,2048]{1,0:T(8,128)(2,1)}, u32[]{:S(2)}, u32[]{:S(2)}) collective-permute-start(bf16[384,2048]{1,0:T(8,128)(2,1)} %param.5), channel_id=1, source_target_pairs={{0,8},{8,0},{1,9},{9,1},{2,10},{10,2},{3,11},{11,3},{4,12},{12,4},... | collective-permute-start | bytes 4718600 | tf_op jit(solution)/shard_map/ppermute | solution.py:20
  2.3 26.6 %collective-permute-start.1 = (bf16[2048,256]{1,0:T(8,128)(2,1)}, bf16[2048,256]{1,0:T(8,128)(2,1)S(1)}, u32[]{:S(2)}, u32[]{:S(2)}) collective-permute-start(bf16[2048,256]{1,0:T(8,128)(2,1)} %param.6), channel_id=1, source_target_pairs={{0,16},{16,0},{1,17},{17,1},{2,18},{18,2},{3,19},{19,3},{4,20},{20... | collective-permute-start | bytes 3145736 | tf_op jit(solution)/shard_map/ppermute | solution.py:20
  7.4 1.2 %copy-start = (bf16[2048,256]{1,0:T(8,128)(2,1)S(1)}, bf16[2048,256]{1,0:T(8,128)(2,1)}, u32[]{:S(2)}) copy-start(bf16[2048,256]{1,0:T(8,128)(2,1)} %param.6) | copy-start | bytes 3145732
  30.0 10.9 %collective-permute-start.2 = (f32[24,2,8,256]{3,2,1,0:T(8,128)S(1)}, f32[24,2,8,256]{3,2,1,0:T(8,128)S(1)}, u32[]{:S(2)}, u32[]{:S(2)}) collective-permute-start(f32[24,2,8,256]{3,2,1,0:T(8,128)S(1)} %bitcast.159), channel_id=1, source_target_pairs={{0,2},{2,4},{4,6},{6,7},{7,5},{5,3},{3,1},{1,0},{8,10},{10,12},{12... | collective-permute-start | bytes 1179656 | tf_op jit(solution)/shard_map/ppermute | solution.py:110
  32.0 10.4 %collective-permute-start.3 = (f32[24,2,8,256]{3,2,1,0:T(8,128)S(1)}, f32[24,2,8,256]{3,2,1,0:T(8,128)S(1)}, u32[]{:S(2)}, u32[]{:S(2)}) collective-permute-start(f32[24,2,8,256]{3,2,1,0:T(8,128)S(1)} %bitcast.158), channel_id=1, source_target_pairs={{2,0},{4,2},{6,4},{7,6},{5,7},{3,5},{1,3},{0,1},{10,8},{12,10},{14... | collective-permute-start | bytes 1179656 | tf_op jit(solution)/shard_map/ppermute | solution.py:111
  42.4 9.5 %collective-permute-start.4 = (f32[24,2,8,256]{3,2,1,0:T(8,128)S(1)}, f32[24,2,8,256]{3,2,1,0:T(8,128)S(1)}, u32[]{:S(2)}, u32[]{:S(2)}) collective-permute-start(f32[24,2,8,256]{3,2,1,0:T(8,128)S(1)} %add.389), channel_id=1, source_target_pairs={{0,2},{2,4},{4,6},{6,7},{7,5},{5,3},{3,1},{1,0},{8,10},{10,12},{12... | collective-permute-start | bytes 1179656 | tf_op jit(solution)/shard_map/ppermute | solution.py:110
  44.2 9.2 %collective-permute-start.5 = (f32[24,2,8,256]{3,2,1,0:T(8,128)S(1)}, f32[24,2,8,256]{3,2,1,0:T(8,128)S(1)}, u32[]{:S(2)}, u32[]{:S(2)}) collective-permute-start(f32[24,2,8,256]{3,2,1,0:T(8,128)S(1)} %add.396), channel_id=1, source_target_pairs={{2,0},{4,2},{6,4},{7,6},{5,7},{3,5},{1,3},{0,1},{10,8},{12,10},{14... | collective-permute-start | bytes 1179656 | tf_op jit(solution)/shard_map/ppermute | solution.py:111
  53.5 8.3 %collective-permute-start.6 = (f32[24,2,8,256]{3,2,1,0:T(8,128)S(1)}, f32[24,2,8,256]{3,2,1,0:T(8,128)S(1)}, u32[]{:S(2)}, u32[]{:S(2)}) collective-permute-start(f32[24,2,8,256]{3,2,1,0:T(8,128)S(1)} %add.402), channel_id=1, source_target_pairs={{0,2},{2,4},{4,6},{6,7},{7,5},{5,3},{3,1},{1,0},{8,10},{10,12},{12... | collective-permute-start | bytes 1179656 | tf_op jit(solution)/shard_map/ppermute | solution.py:110
  55.2 8.2 %collective-permute-start.7 = (f32[24,2,8,256]{3,2,1,0:T(8,128)S(1)}, f32[24,2,8,256]{3,2,1,0:T(8,128)S(1)}, u32[]{:S(2)}, u32[]{:S(2)}) collective-permute-start(f32[24,2,8,256]{3,2,1,0:T(8,128)S(1)} %add.409), channel_id=1, source_target_pairs={{2,0},{4,2},{6,4},{7,6},{5,7},{3,5},{1,3},{0,1},{10,8},{12,10},{14... | collective-permute-start | bytes 1179656 | tf_op jit(solution)/shard_map/ppermute | solution.py:111
  63.4 9.2 %collective-permute-start.8 = (f32[24,2,8,256]{3,2,1,0:T(8,128)S(1)}, f32[24,2,8,256]{3,2,1,0:T(8,128)S(1)}, u32[]{:S(2)}, u32[]{:S(2)}) collective-permute-start(f32[24,2,8,256]{3,2,1,0:T(8,128)S(1)} %add.415), channel_id=1, source_target_pairs={{0,2},{2,4},{4,6},{6,7},{7,5},{5,3},{3,1},{1,0},{8,10},{10,12},{12... | collective-permute-start | bytes 1179656 | tf_op jit(solution)/shard_map/ppermute | solution.py:110
  65.7 9.8 %collective-permute-start.9 = (f32[24,2,8,256]{3,2,1,0:T(8,128)S(1)}, f32[24,2,8,256]{3,2,1,0:T(8,128)S(1)}, u32[]{:S(2)}, u32[]{:S(2)}) collective-permute-start(f32[24,2,8,256]{3,2,1,0:T(8,128)S(1)} %add.422), channel_id=1, source_target_pairs={{2,0},{4,2},{6,4},{7,6},{5,7},{3,5},{1,3},{0,1},{10,8},{12,10},{14... | collective-permute-start | bytes 1179656 | tf_op jit(solution)/shard_map/ppermute | solution.py:111
  75.6 11.0 %collective-permute-start.10 = (f32[24,2,8,256]{3,2,1,0:T(8,128)S(1)}, f32[24,2,8,256]{3,2,1,0:T(8,128)S(1)}, u32[]{:S(2)}, u32[]{:S(2)}) collective-permute-start(f32[24,2,8,256]{3,2,1,0:T(8,128)S(1)} %add.428), channel_id=1, source_target_pairs={{0,2},{2,4},{4,6},{6,7},{7,5},{5,3},{3,1},{1,0},{8,10},{10,12},{12... | collective-permute-start | bytes 1179656 | tf_op jit(solution)/shard_map/ppermute | solution.py:110
  76.4 11.1 %collective-permute-start.11 = (f32[24,2,8,256]{3,2,1,0:T(8,128)S(1)}, f32[24,2,8,256]{3,2,1,0:T(8,128)S(1)}, u32[]{:S(2)}, u32[]{:S(2)}) collective-permute-start(f32[24,2,8,256]{3,2,1,0:T(8,128)S(1)} %add.435), channel_id=1, source_target_pairs={{2,0},{4,2},{6,4},{7,6},{5,7},{3,5},{1,3},{0,1},{10,8},{12,10},{14... | collective-permute-start | bytes 1179656 | tf_op jit(solution)/shard_map/ppermute | solution.py:111
  87.6 11.1 %collective-permute-start.12 = (f32[24,2,8,256]{3,2,1,0:T(8,128)S(1)}, f32[24,2,8,256]{3,2,1,0:T(8,128)S(1)}, u32[]{:S(2)}, u32[]{:S(2)}) collective-permute-start(f32[24,2,8,256]{3,2,1,0:T(8,128)S(1)} %add.441), channel_id=1, source_target_pairs={{0,2},{2,4},{4,6},{6,7},{7,5},{5,3},{3,1},{1,0},{8,10},{10,12},{12... | collective-permute-start | bytes 1179656 | tf_op jit(solution)/shard_map/ppermute | solution.py:110
  88.4 11.0 %collective-permute-start.13 = (f32[24,2,8,256]{3,2,1,0:T(8,128)S(1)}, f32[24,2,8,256]{3,2,1,0:T(8,128)S(1)}, u32[]{:S(2)}, u32[]{:S(2)}) collective-permute-start(f32[24,2,8,256]{3,2,1,0:T(8,128)S(1)} %add.448), channel_id=1, source_target_pairs={{2,0},{4,2},{6,4},{7,6},{5,7},{3,5},{1,3},{0,1},{10,8},{12,10},{14... | collective-permute-start | bytes 1179656 | tf_op jit(solution)/shard_map/ppermute | solution.py:111
  99.5 7.8 %collective-permute-start.15 = (f32[24,2,8,256]{3,2,1,0:T(8,128)S(1)}, f32[24,2,8,256]{3,2,1,0:T(8,128)S(1)}, u32[]{:S(2)}, u32[]{:S(2)}) collective-permute-start(f32[24,2,8,256]{3,2,1,0:T(8,128)S(1)} %add.461), channel_id=1, source_target_pairs={{2,0},{4,2},{6,4},{7,6},{5,7},{3,5},{1,3},{0,1},{10,8},{12,10},{14... | collective-permute-start | bytes 1179656 | tf_op jit(solution)/shard_map/ppermute | solution.py:111
  101.1 7.8 %collective-permute-start.14 = (f32[24,2,8,256]{3,2,1,0:T(8,128)S(1)}, f32[24,2,8,256]{3,2,1,0:T(8,128)S(1)}, u32[]{:S(2)}, u32[]{:S(2)}) collective-permute-start(f32[24,2,8,256]{3,2,1,0:T(8,128)S(1)} %add.454), channel_id=1, source_target_pairs={{0,2},{2,4},{4,6},{6,7},{7,5},{5,3},{3,1},{1,0},{8,10},{10,12},{12... | collective-permute-start | bytes 1179656 | tf_op jit(solution)/shard_map/ppermute | solution.py:110

commit v14 on v10

--- a/solution.py
+++ b/solution.py
@@ -52,15 +52,30 @@
         receivers, excitations, weights, position = lax.optimization_barrier(
             (receivers, excitations, weights, position)
         )
-        receiver_block = gather_blocks(receivers, "evt", sizes["evt"], 1)
-        source_block = gather_blocks(excitations, "sta", sizes["sta"], 0)
-        row_count, block_modes = receiver_block.shape
+        row_count = receivers.shape[0]
         chunk = row_count // mode_count
         half = chunk // 2
 
-        def partial_rows(owner, part):
-            start = owner * chunk + part * half
-            rows = lax.dynamic_slice_in_dim(receiver_block, start, half, axis=0)
+        def owner_at(offset):
+            place = (position + offset) % mode_count
+            if mode_count % 2:
+                return place
+            return jnp.where(place < mode_count // 2, 2 * place, 2 * (mode_count - 1 - place) + 1)
+
+        first_rows = jnp.concatenate(
+            [
+                lax.dynamic_slice_in_dim(receivers, owner_at(-1) * chunk, half, axis=0),
+                lax.dynamic_slice_in_dim(receivers, owner_at(1) * chunk + half, half, axis=0),
+            ],
+            axis=0,
+        )
+        first_block = gather_blocks(first_rows, "evt", sizes["evt"], 1)
+        source_block = gather_blocks(excitations, "sta", sizes["sta"], 0)
+        later_receivers, source_block = lax.optimization_barrier((receivers, source_block))
+        receiver_block = gather_blocks(later_receivers, "evt", sizes["evt"], 1)
+        block_modes = receiver_block.shape[1]
+
+        def weighted_product(rows):
             widened = rows.astype(jnp.float32)
             weighted = (widened[:, None, None, :] * weights[None]).astype(jnp.bfloat16)
             product = jnp.dot(
@@ -68,14 +83,12 @@
             )
             return product.reshape(half, 2, sample_freqs.shape[0], source_block.shape[1])
 
-        def owner_at(offset):
-            place = (position + offset) % mode_count
-            if mode_count % 2:
-                return place
-            return jnp.where(place < mode_count // 2, 2 * place, 2 * (mode_count - 1 - place) + 1)
+        def partial_rows(owner, part):
+            start = owner * chunk + part * half
+            return weighted_product(lax.dynamic_slice_in_dim(receiver_block, start, half, axis=0))
 
-        ahead = partial_rows(owner_at(-1), 0)
-        behind = partial_rows(owner_at(1), 1)
+        ahead = weighted_product(first_block[:half])
+        behind = weighted_product(first_block[half:])
         for step in range(mode_count - 1):
             ahead = lax.ppermute(ahead, "mode", clockwise)
             behind = lax.ppermute(behind, "mode", counter)

time: 104 us -> 105 us (level)
  local copies, waits for them, and re-layouts: 0.01 us -> 2.21 us
  waiting for transfers between devices: 64.8 us -> 62.7 us
  other arithmetic: 5.58 us -> 4.45 us
    ppermute x7, waiting for transfers between devices: 34 us -> 5.97 us  [per_device(): ahead = lax.ppermute(ahead, 'mode', clockwise)]
    ppermute x7, waiting for transfers between devices: 7.25 us -> 34.9 us  [per_device(): behind = lax.ppermute(behind, 'mode', counter)]
    ppermute x7, starting transfers between devices: 2.84 us -> 11.6 us  [per_device(): behind = lax.ppermute(behind, 'mode', counter)]
    ppermute x7, starting transfers between devices: 11.5 us -> 3.49 us  [per_device(): ahead = lax.ppermute(ahead, 'mode', clockwise)]
    ppermute x2 -> x3, waiting for transfers between devices: 23.5 us -> 21.9 us  [swap_pair(): return lax.ppermute(local, axis_name, [(0, 1), (1, 0)])]
    unnamed x4, local copies, waits for them, and re-layouts: 0.01 us -> 1.26 us
    select_n x2 -> x3, other arithmetic: 1.57 us -> 0.42 us  [gather_blocks(): first = jnp.where(index == 0, local, other)]
    ppermute x2 -> x3, starting transfers between devices: 3.03 us -> 3.11 us  [swap_pair(): return lax.ppermute(local, axis_name, [(0, 1), (1, 0)])]
  transfers between devices with their start and end apart: 16 -> 17, of which waited for: 15 -> 14; matrix products, arithmetic and copies ran while one was open for 17% -> 18% of each run, Pallas kernels for 0% -> 0%
where the time goes in v14:
time: 105 us; the launch traced here: 104 us
  waiting for transfers between devices  62.7 us (60%)
  starting transfers between devices  18.2 us (17%)
  matrix products  15.8 us (15%)
  other arithmetic  4.45 us (4%)
  local copies, waits for them, and re-layouts  2.21 us (2%)
    ppermute x7, waiting for transfers between devices, per_device(): behind = lax.ppermute(behind, 'mode', counter)  34.9 us
    ppermute x3, waiting for transfers between devices, swap_pair(): return lax.ppermute(local, axis_name, [(0, 1), (1, 0)])  21.9 us
    dot_general x16, matrix products, weighted_product(): jnp.dot(weighted.reshape(-1, block_modes), source_block, preferred_elemen...  15.8 us
    ppermute x7, starting transfers between devices, per_device(): behind = lax.ppermute(behind, 'mode', counter)  11.6 us
    ppermute x7, waiting for transfers between devices, per_device(): ahead = lax.ppermute(ahead, 'mode', clockwise)  5.97 us
    ppermute x7, starting transfers between devices, per_device(): ahead = lax.ppermute(ahead, 'mode', clockwise)  3.49 us
    ppermute x3, starting transfers between devices, swap_pair(): return lax.ppermute(local, axis_name, [(0, 1), (1, 0)])  3.11 us
  transfers between devices with their start and end apart: 17, of which 14 were waited for; matrix products, arithmetic and copies ran while one was open for 18% of the time, Pallas kernels for 0%

profile of v14, /device:TPU:0, one launch (start us, length us, event | category | flops | bytes accessed | tf_op | source)
XLA Modules:
  0.0 104.2 jit_solution(9496848700927321844)
XLA Ops:
  1.7 3.0 %collective-permute-start.1 = (bf16[2048,256]{1,0:T(8,128)(2,1)}, bf16[2048,256]{1,0:T(8,128)(2,1)S(1)}, u32[]{:S(2)}, u32[]{:S(2)}) collective-permute-start(bf16[2048,256]{1,0:T(8,128)(2,1)} %param.6), channel_id=1, source_target_pairs={{0,16},{16,0},{1,17},{17,1},{2,18},{18,2},{3,19},{19,3},{4,20},{20... | collective-permute-start | bytes 3145736 | tf_op jit(solution)/shard_map/ppermute | solution.py:20
  6.2 21.9 %collective-permute-done.1 = bf16[2048,256]{1,0:T(8,128)(2,1)S(1)} collective-permute-done((bf16[2048,256]{1,0:T(8,128)(2,1)}, bf16[2048,256]{1,0:T(8,128)(2,1)S(1)}, u32[]{:S(2)}, u32[]{:S(2)}) %collective-permute-start.1) | collective-permute-done | bytes 1048608 | tf_op jit(solution)/shard_map/ppermute | solution.py:20
  28.4 1.3 %copy-done = bf16[384,2048]{1,0:T(8,128)(2,1)S(1)} copy-done((bf16[384,2048]{1,0:T(8,128)(2,1)S(1)}, bf16[384,2048]{1,0:T(8,128)(2,1)}, u32[]{:S(2)}) %copy-start) | copy-done | bytes 1572888
  29.8 1.0 fusion.8
  30.8 1.8 %collective-permute-start.10 = (f32[24,2,8,256]{3,2,1,0:T(8,128)S(1)}, f32[24,2,8,256]{3,2,1,0:T(8,128)S(1)}, u32[]{:S(2)}, u32[]{:S(2)}) collective-permute-start(f32[24,2,8,256]{3,2,1,0:T(8,128)S(1)} %fusion.8), channel_id=1, source_target_pairs={{2,0},{4,2},{6,4},{7,6},{5,7},{3,5},{1,3},{0,1},{10,8},{12,10},{14... | collective-permute-start | bytes 1179656 | tf_op jit(solution)/shard_map/ppermute | solution.py:94
  32.6 1.0 fusion
  34.4 8.0 %collective-permute-done.10 = f32[24,2,8,256]{3,2,1,0:T(8,128)S(1)} collective-permute-done((f32[24,2,8,256]{3,2,1,0:T(8,128)S(1)}, f32[24,2,8,256]{3,2,1,0:T(8,128)S(1)}, u32[]{:S(2)}, u32[]{:S(2)}) %collective-permute-start.10) | collective-permute-done | bytes 393248 | tf_op jit(solution)/shard_map/ppermute | solution.py:94
  42.5 1.0 fusion.64
  43.5 1.7 %collective-permute-start.11 = (f32[24,2,8,256]{3,2,1,0:T(8,128)S(1)}, f32[24,2,8,256]{3,2,1,0:T(8,128)S(1)}, u32[]{:S(2)}, u32[]{:S(2)}) collective-permute-start(f32[24,2,8,256]{3,2,1,0:T(8,128)S(1)} %fusion.64), channel_id=1, source_target_pairs={{2,0},{4,2},{6,4},{7,6},{5,7},{3,5},{1,3},{0,1},{10,8},{12,10},{14... | collective-permute-start | bytes 1179656 | tf_op jit(solution)/shard_map/ppermute | solution.py:94
  45.4 1.0 fusion.67
  46.9 1.0 fusion.10
  47.9 1.0 fusion.2
  48.9 5.4 %collective-permute-done.11 = f32[24,2,8,256]{3,2,1,0:T(8,128)S(1)} collective-permute-done((f32[24,2,8,256]{3,2,1,0:T(8,128)S(1)}, f32[24,2,8,256]{3,2,1,0:T(8,128)S(1)}, u32[]{:S(2)}, u32[]{:S(2)}) %collective-permute-start.11) | collective-permute-done | bytes 393248 | tf_op jit(solution)/shard_map/ppermute | solution.py:94
  54.4 1.7 %collective-permute-start.12 = (f32[24,2,8,256]{3,2,1,0:T(8,128)S(1)}, f32[24,2,8,256]{3,2,1,0:T(8,128)S(1)}, u32[]{:S(2)}, u32[]{:S(2)}) collective-permute-start(f32[24,2,8,256]{3,2,1,0:T(8,128)S(1)} %add.356), channel_id=1, source_target_pairs={{2,0},{4,2},{6,4},{7,6},{5,7},{3,5},{1,3},{0,1},{10,8},{12,10},{14... | collective-permute-start | bytes 1179656 | tf_op jit(solution)/shard_map/ppermute | solution.py:94
  57.5 1.0 fusion.11
  58.5 1.0 fusion.3
  59.4 4.9 %collective-permute-done.12 = f32[24,2,8,256]{3,2,1,0:T(8,128)S(1)} collective-permute-done((f32[24,2,8,256]{3,2,1,0:T(8,128)S(1)}, f32[24,2,8,256]{3,2,1,0:T(8,128)S(1)}, u32[]{:S(2)}, u32[]{:S(2)}) %collective-permute-start.12) | collective-permute-done | bytes 393248 | tf_op jit(solution)/shard_map/ppermute | solution.py:94
  64.4 1.6 %collective-permute-start.13 = (f32[24,2,8,256]{3,2,1,0:T(8,128)S(1)}, f32[24,2,8,256]{3,2,1,0:T(8,128)S(1)}, u32[]{:S(2)}, u32[]{:S(2)}) collective-permute-start(f32[24,2,8,256]{3,2,1,0:T(8,128)S(1)} %add.362), channel_id=1, source_target_pairs={{2,0},{4,2},{6,4},{7,6},{5,7},{3,5},{1,3},{0,1},{10,8},{12,10},{14... | collective-permute-start | bytes 1179656 | tf_op jit(solution)/shard_map/ppermute | solution.py:94
  67.3 1.0 fusion.12
  68.3 1.0 fusion.4
  69.3 4.3 %collective-permute-done.13 = f32[24,2,8,256]{3,2,1,0:T(8,128)S(1)} collective-permute-done((f32[24,2,8,256]{3,2,1,0:T(8,128)S(1)}, f32[24,2,8,256]{3,2,1,0:T(8,128)S(1)}, u32[]{:S(2)}, u32[]{:S(2)}) %collective-permute-start.13) | collective-permute-done | bytes 393248 | tf_op jit(solution)/shard_map/ppermute | solution.py:94
  73.7 1.6 %collective-permute-start.14 = (f32[24,2,8,256]{3,2,1,0:T(8,128)S(1)}, f32[24,2,8,256]{3,2,1,0:T(8,128)S(1)}, u32[]{:S(2)}, u32[]{:S(2)}) collective-permute-start(f32[24,2,8,256]{3,2,1,0:T(8,128)S(1)} %add.368), channel_id=1, source_target_pairs={{2,0},{4,2},{6,4},{7,6},{5,7},{3,5},{1,3},{0,1},{10,8},{12,10},{14... | collective-permute-start | bytes 1179656 | tf_op jit(solution)/shard_map/ppermute | solution.py:94
  76.6 1.0 fusion.13
  78.6 4.3 %collective-permute-done.14 = f32[24,2,8,256]{3,2,1,0:T(8,128)S(1)} collective-permute-done((f32[24,2,8,256]{3,2,1,0:T(8,128)S(1)}, f32[24,2,8,256]{3,2,1,0:T(8,128)S(1)}, u32[]{:S(2)}, u32[]{:S(2)}) %collective-permute-start.14) | collective-permute-done | bytes 393248 | tf_op jit(solution)/shard_map/ppermute | solution.py:94
  82.9 1.6 %collective-permute-start.15 = (f32[24,2,8,256]{3,2,1,0:T(8,128)S(1)}, f32[24,2,8,256]{3,2,1,0:T(8,128)S(1)}, u32[]{:S(2)}, u32[]{:S(2)}) collective-permute-start(f32[24,2,8,256]{3,2,1,0:T(8,128)S(1)} %add.374), channel_id=1, source_target_pairs={{2,0},{4,2},{6,4},{7,6},{5,7},{3,5},{1,3},{0,1},{10,8},{12,10},{14... | collective-permute-start | bytes 1179656 | tf_op jit(solution)/shard_map/ppermute | solution.py:94
  86.9 1.0 fusion.6
  87.9 5.0 %collective-permute-done.15 = f32[24,2,8,256]{3,2,1,0:T(8,128)S(1)} collective-permute-done((f32[24,2,8,256]{3,2,1,0:T(8,128)S(1)}, f32[24,2,8,256]{3,2,1,0:T(8,128)S(1)}, u32[]{:S(2)}, u32[]{:S(2)}) %collective-permute-start.15) | collective-permute-done | bytes 393248 | tf_op jit(solution)/shard_map/ppermute | solution.py:94
  93.0 1.7 %collective-permute-start.16 = (f32[24,2,8,256]{3,2,1,0:T(8,128)S(1)}, f32[24,2,8,256]{3,2,1,0:T(8,128)S(1)}, u32[]{:S(2)}, u32[]{:S(2)}) collective-permute-start(f32[24,2,8,256]{3,2,1,0:T(8,128)S(1)} %add.380), channel_id=1, source_target_pairs={{2,0},{4,2},{6,4},{7,6},{5,7},{3,5},{1,3},{0,1},{10,8},{12,10},{14... | collective-permute-start | bytes 1179656 | tf_op jit(solution)/shard_map/ppermute | solution.py:94
  95.9 1.0 fusion.15
  96.9 1.0 fusion.7
  97.9 2.9 %collective-permute-done.16 = f32[24,2,8,256]{3,2,1,0:T(8,128)S(1)} collective-permute-done((f32[24,2,8,256]{3,2,1,0:T(8,128)S(1)}, f32[24,2,8,256]{3,2,1,0:T(8,128)S(1)}, u32[]{:S(2)}, u32[]{:S(2)}) %collective-permute-start.16) | collective-permute-done | bytes 393248 | tf_op jit(solution)/shard_map/ppermute | solution.py:94
  100.8 2.3 %collective-permute-done.9 = f32[24,2,8,256]{3,2,1,0:T(8,128)S(1)} collective-permute-done((f32[24,2,8,256]{3,2,1,0:T(8,128)S(1)}, f32[24,2,8,256]{3,2,1,0:T(8,128)S(1)}, u32[]{:S(2)}, u32[]{:S(2)}) %collective-permute-start.9) | collective-permute-done | bytes 393248 | tf_op jit(solution)/shard_map/ppermute | solution.py:93
  (48 shorter events, 14.6 us)
Async XLA Ops:
  0.0 28.1 %copy-start.1 = (bf16[2048,256]{1,0:T(8,128)(2,1)S(1)}, bf16[2048,256]{1,0:T(8,128)(2,1)}, u32[]{:S(2)}) copy-start(bf16[2048,256]{1,0:T(8,128)(2,1)} %param.6) | copy-start | bytes 3145732
  1.7 26.4 %collective-permute-start.1 = (bf16[2048,256]{1,0:T(8,128)(2,1)}, bf16[2048,256]{1,0:T(8,128)(2,1)S(1)}, u32[]{:S(2)}, u32[]{:S(2)}) collective-permute-start(bf16[2048,256]{1,0:T(8,128)(2,1)} %param.6), channel_id=1, source_target_pairs={{0,16},{16,0},{1,17},{17,1},{2,18},{18,2},{3,19},{19,3},{4,20},{20... | collective-permute-start | bytes 3145736 | tf_op jit(solution)/shard_map/ppermute | solution.py:20
  5.7 24.0 %collective-permute-start = (bf16[48,2048]{1,0:T(8,128)(2,1)S(1)}, bf16[48,2048]{1,0:T(8,128)(2,1)S(1)}, u32[]{:S(2)}, u32[]{:S(2)}) collective-permute-start(bf16[48,2048]{1,0:T(8,128)(2,1)S(1)} %pad_maximum_fusion.4), channel_id=1, source_target_pairs={{0,8},{8,0},{1,9},{9,1},{2,10},{10,2},{3,11},{11,3},{4,12},{12,4},... | collective-permute-start | bytes 589832 | tf_op jit(solution)/shard_map/ppermute | solution.py:20
  28.3 1.4 %copy-start = (bf16[384,2048]{1,0:T(8,128)(2,1)S(1)}, bf16[384,2048]{1,0:T(8,128)(2,1)}, u32[]{:S(2)}) copy-start(bf16[384,2048]{1,0:T(8,128)(2,1)} %param.5) | copy-start | bytes 4718596
  29.7 4.3 %collective-permute-start.3 = (bf16[384,2048]{1,0:T(8,128)(2,1)S(1)}, bf16[384,2048]{1,0:T(8,128)(2,1)S(1)}, u32[]{:S(2)}, u32[]{:S(2)}) collective-permute-start(bf16[384,2048]{1,0:T(8,128)(2,1)S(1)} %copy-done), channel_id=1, source_target_pairs={{0,8},{8,0},{1,9},{9,1},{2,10},{10,2},{3,11},{11,3},{4,12},{12,4},... | collective-permute-start | bytes 4718600 | tf_op jit(solution)/shard_map/ppermute | solution.py:20
  30.8 11.6 %collective-permute-start.10 = (f32[24,2,8,256]{3,2,1,0:T(8,128)S(1)}, f32[24,2,8,256]{3,2,1,0:T(8,128)S(1)}, u32[]{:S(2)}, u32[]{:S(2)}) collective-permute-start(f32[24,2,8,256]{3,2,1,0:T(8,128)S(1)} %fusion.8), channel_id=1, source_target_pairs={{2,0},{4,2},{6,4},{7,6},{5,7},{3,5},{1,3},{0,1},{10,8},{12,10},{14... | collective-permute-start | bytes 1179656 | tf_op jit(solution)/shard_map/ppermute | solution.py:94
  33.6 11.8 %collective-permute-start.2 = (f32[24,2,8,256]{3,2,1,0:T(8,128)S(1)}, f32[24,2,8,256]{3,2,1,0:T(8,128)S(1)}, u32[]{:S(2)}, u32[]{:S(2)}) collective-permute-start(f32[24,2,8,256]{3,2,1,0:T(8,128)S(1)} %fusion), channel_id=1, source_target_pairs={{0,2},{2,4},{4,6},{6,7},{7,5},{5,3},{3,1},{1,0},{8,10},{10,12},{12... | collective-permute-start | bytes 1179656 | tf_op jit(solution)/shard_map/ppermute | solution.py:93
  43.5 10.8 %collective-permute-start.11 = (f32[24,2,8,256]{3,2,1,0:T(8,128)S(1)}, f32[24,2,8,256]{3,2,1,0:T(8,128)S(1)}, u32[]{:S(2)}, u32[]{:S(2)}) collective-permute-start(f32[24,2,8,256]{3,2,1,0:T(8,128)S(1)} %fusion.64), channel_id=1, source_target_pairs={{2,0},{4,2},{6,4},{7,6},{5,7},{3,5},{1,3},{0,1},{10,8},{12,10},{14... | collective-permute-start | bytes 1179656 | tf_op jit(solution)/shard_map/ppermute | solution.py:94
  46.4 10.5 %collective-permute-start.4 = (f32[24,2,8,256]{3,2,1,0:T(8,128)S(1)}, f32[24,2,8,256]{3,2,1,0:T(8,128)S(1)}, u32[]{:S(2)}, u32[]{:S(2)}) collective-permute-start(f32[24,2,8,256]{3,2,1,0:T(8,128)S(1)} %fusion.67), channel_id=1, source_target_pairs={{0,2},{2,4},{4,6},{6,7},{7,5},{5,3},{3,1},{1,0},{8,10},{10,12},{12... | collective-permute-start | bytes 1179656 | tf_op jit(solution)/shard_map/ppermute | solution.py:93
  54.4 10.0 %collective-permute-start.12 = (f32[24,2,8,256]{3,2,1,0:T(8,128)S(1)}, f32[24,2,8,256]{3,2,1,0:T(8,128)S(1)}, u32[]{:S(2)}, u32[]{:S(2)}) collective-permute-start(f32[24,2,8,256]{3,2,1,0:T(8,128)S(1)} %add.356), channel_id=1, source_target_pairs={{2,0},{4,2},{6,4},{7,6},{5,7},{3,5},{1,3},{0,1},{10,8},{12,10},{14... | collective-permute-start | bytes 1179656 | tf_op jit(solution)/shard_map/ppermute | solution.py:94
  57.0 9.6 %collective-permute-start.5 = (f32[24,2,8,256]{3,2,1,0:T(8,128)S(1)}, f32[24,2,8,256]{3,2,1,0:T(8,128)S(1)}, u32[]{:S(2)}, u32[]{:S(2)}) collective-permute-start(f32[24,2,8,256]{3,2,1,0:T(8,128)S(1)} %add.319), channel_id=1, source_target_pairs={{0,2},{2,4},{4,6},{6,7},{7,5},{5,3},{3,1},{1,0},{8,10},{10,12},{12... | collective-permute-start | bytes 1179656 | tf_op jit(solution)/shard_map/ppermute | solution.py:93
  64.4 9.2 %collective-permute-start.13 = (f32[24,2,8,256]{3,2,1,0:T(8,128)S(1)}, f32[24,2,8,256]{3,2,1,0:T(8,128)S(1)}, u32[]{:S(2)}, u32[]{:S(2)}) collective-permute-start(f32[24,2,8,256]{3,2,1,0:T(8,128)S(1)} %add.362), channel_id=1, source_target_pairs={{2,0},{4,2},{6,4},{7,6},{5,7},{3,5},{1,3},{0,1},{10,8},{12,10},{14... | collective-permute-start | bytes 1179656 | tf_op jit(solution)/shard_map/ppermute | solution.py:94
  66.7 9.4 %collective-permute-start.6 = (f32[24,2,8,256]{3,2,1,0:T(8,128)S(1)}, f32[24,2,8,256]{3,2,1,0:T(8,128)S(1)}, u32[]{:S(2)}, u32[]{:S(2)}) collective-permute-start(f32[24,2,8,256]{3,2,1,0:T(8,128)S(1)} %add.324), channel_id=1, source_target_pairs={{0,2},{2,4},{4,6},{6,7},{7,5},{5,3},{3,1},{1,0},{8,10},{10,12},{12... | collective-permute-start | bytes 1179656 | tf_op jit(solution)/shard_map/ppermute | solution.py:93
  73.7 9.2 %collective-permute-start.14 = (f32[24,2,8,256]{3,2,1,0:T(8,128)S(1)}, f32[24,2,8,256]{3,2,1,0:T(8,128)S(1)}, u32[]{:S(2)}, u32[]{:S(2)}) collective-permute-start(f32[24,2,8,256]{3,2,1,0:T(8,128)S(1)} %add.368), channel_id=1, source_target_pairs={{2,0},{4,2},{6,4},{7,6},{5,7},{3,5},{1,3},{0,1},{10,8},{12,10},{14... | collective-permute-start | bytes 1179656 | tf_op jit(solution)/shard_map/ppermute | solution.py:94
  76.1 9.2 %collective-permute-start.7 = (f32[24,2,8,256]{3,2,1,0:T(8,128)S(1)}, f32[24,2,8,256]{3,2,1,0:T(8,128)S(1)}, u32[]{:S(2)}, u32[]{:S(2)}) collective-permute-start(f32[24,2,8,256]{3,2,1,0:T(8,128)S(1)} %add.329), channel_id=1, source_target_pairs={{0,2},{2,4},{4,6},{6,7},{7,5},{5,3},{3,1},{1,0},{8,10},{10,12},{12... | collective-permute-start | bytes 1179656 | tf_op jit(solution)/shard_map/ppermute | solution.py:93
  82.9 9.9 %collective-permute-start.15 = (f32[24,2,8,256]{3,2,1,0:T(8,128)S(1)}, f32[24,2,8,256]{3,2,1,0:T(8,128)S(1)}, u32[]{:S(2)}, u32[]{:S(2)}) collective-permute-start(f32[24,2,8,256]{3,2,1,0:T(8,128)S(1)} %add.374), channel_id=1, source_target_pairs={{2,0},{4,2},{6,4},{7,6},{5,7},{3,5},{1,3},{0,1},{10,8},{12,10},{14... | collective-permute-start | bytes 1179656 | tf_op jit(solution)/shard_map/ppermute | solution.py:94
  85.3 9.9 %collective-permute-start.8 = (f32[24,2,8,256]{3,2,1,0:T(8,128)S(1)}, f32[24,2,8,256]{3,2,1,0:T(8,128)S(1)}, u32[]{:S(2)}, u32[]{:S(2)}) collective-permute-start(f32[24,2,8,256]{3,2,1,0:T(8,128)S(1)} %add.334), channel_id=1, source_target_pairs={{0,2},{2,4},{4,6},{6,7},{7,5},{5,3},{3,1},{1,0},{8,10},{10,12},{12... | collective-permute-start | bytes 1179656 | tf_op jit(solution)/shard_map/ppermute | solution.py:93
  93.0 7.8 %collective-permute-start.16 = (f32[24,2,8,256]{3,2,1,0:T(8,128)S(1)}, f32[24,2,8,256]{3,2,1,0:T(8,128)S(1)}, u32[]{:S(2)}, u32[]{:S(2)}) collective-permute-start(f32[24,2,8,256]{3,2,1,0:T(8,128)S(1)} %add.380), channel_id=1, source_target_pairs={{2,0},{4,2},{6,4},{7,6},{5,7},{3,5},{1,3},{0,1},{10,8},{12,10},{14... | collective-permute-start | bytes 1179656 | tf_op jit(solution)/shard_map/ppermute | solution.py:94
  95.3 7.8 %collective-permute-start.9 = (f32[24,2,8,256]{3,2,1,0:T(8,128)S(1)}, f32[24,2,8,256]{3,2,1,0:T(8,128)S(1)}, u32[]{:S(2)}, u32[]{:S(2)}) collective-permute-start(f32[24,2,8,256]{3,2,1,0:T(8,128)S(1)} %add.339), channel_id=1, source_target_pairs={{0,2},{2,4},{4,6},{6,7},{7,5},{5,3},{3,1},{1,0},{8,10},{10,12},{12... | collective-permute-start | bytes 1179656 | tf_op jit(solution)/shard_map/ppermute | solution.py:93
